TPU v7x, 32 devices: a whole 2x2x4 slice. The times are simulated.
32 devices in a mesh: dp: 4 (over x, core), pipe: 2 (over y), tensor: 4 (over z).
Axes of the slice: x: 2, y: 2, z: 4, core: 2. Of those that a mesh axis runs over, the one named last changes fastest.
Arguments:
- layer_input: bfloat16 [4, 2, 512, 8192], P('dp', 'pipe', None, 'tensor'), may hold values from -40 to 40
- output_grad: bfloat16 [4, 2, 512, 8192], P('dp', 'pipe', None, 'tensor'), may hold values from -6 to 6
- kv_grad: bfloat16 [4, 2, 512, 2048], P('dp', 'pipe', None, 'tensor'), may hold values from -6 to 6
- norm_gain: bfloat16 [2, 8192], P('pipe', 'tensor'), may hold values from 0.5 to 1.5
- kv_weight: bfloat16 [2, 8192, 2048], P('pipe', 'tensor'), may hold values from -0.0625 to 0.0625
Outputs:
- upstream_grad: bfloat16 [4, 2, 512, 8192], P('dp', 'pipe', None, 'tensor')
- kv_weight_grad: bfloat16 [2, 8192, 2048], P('pipe', 'tensor', 'dp')
- gain_grad: float32 [2, 8192], P('pipe', 'tensor')
All inputs are finite; a program needn't handle non-finite values.
Results may differ from a plain program's by a relative error of at most 0.009.
Values may be sent and summed in bfloat16 or wider, within the bound.
No kernel may reach another device: no remote copies, remote signals or barrier semaphores. Data moves between devices by JAX's collectives and lax.ppermute only.
A program may use at most 128 MiB of HBM per device.

v0:
```python
import jax
import jax.numpy as jnp
from jax import lax
from jax.sharding import PartitionSpec as P

D = 8192


def from_behind(block, axis, distance):
    devices = range(lax.axis_size(axis))
    route = [(i - distance, i) for i in devices if i - distance in devices]
    return lax.ppermute(block, axis, route)


def on_device(layer_input, output_grad, kv_grad, norm_gain, kv_weight):
    rows = layer_input[0, 0]
    grad_out = output_grad[0, 0]
    grad_kv = kv_grad[0, 0]
    gain_f = norm_gain[0].astype(jnp.float32)
    weight = kv_weight[0]
    values = rows.astype(jnp.float32)
    local_squares = jnp.sum(values * values, axis=1, keepdims=True)
    total_squares = lax.psum(local_squares, "tensor")
    rstd = lax.rsqrt(total_squares / D + 1e-05)
    normed = values * rstd
    hidden = (normed * gain_f).astype(jnp.bfloat16)
    piece = lax.all_gather(grad_kv, "tensor", axis=1, tiled=True)
    row_total = lax.dot_general(
        piece, weight, (((1,), (1,)), ((), ())), preferred_element_type=jnp.float32
    )
    term = lax.dot_general(
        hidden, piece, (((0,), (0,)), ((), ())), preferred_element_type=jnp.float32
    )
    weight_total = term
    wgrad = weight_total
    scaled = gain_f * row_total
    local_dot = jnp.sum(scaled * normed, axis=1, keepdims=True)
    mean_term = lax.psum(local_dot, "tensor") / D
    input_grad = (grad_out.astype(jnp.float32) + rstd * (scaled - normed * mean_term)).astype(
        jnp.bfloat16
    )
    upstream = from_behind(input_grad, "pipe", -1)
    gain_part = jnp.sum(row_total * normed, axis=0)
    gain_total = lax.psum(gain_part, "dp")
    weight_total = lax.psum_scatter(
        wgrad.astype(jnp.bfloat16), "dp", scatter_dimension=1, tiled=True
    )
    return (upstream[None, None], weight_total[None], gain_total[None])


def solution(mesh):
    in_specs = (
        P("dp", "pipe", None, "tensor"),
        P("dp", "pipe", None, "tensor"),
        P("dp", "pipe", None, "tensor"),
        P("pipe", "tensor"),
        P("pipe", "tensor", None),
    )
    out_specs = (P("dp", "pipe", None, "tensor"), P("pipe", "tensor", "dp"), P("pipe", "tensor"))
    return jax.shard_map(
        on_device, mesh=mesh, in_specs=in_specs, out_specs=out_specs, check_vma=False
    )
```

profile of v0, /device:TPU:0, one launch (start us, length us, event | category | flops | bytes accessed | tf_op | source)
XLA Modules:
  0.0 152.9 jit_solution(5806783644709270451)
XLA Ops:
  7.2 0.0 all-gather.3.cloned.1.call-start
  7.2 0.7 all-gather.3.cloned.1.call-update
  7.9 0.0 reduce-scatter.2.cloned.1.call-start
  7.9 0.7 mul.69
  8.7 2.1 %fusion.13 = f32[512]{0:T(512)S(1)} fusion(bf16[1,1,512,2048]{3,2,1,0:T(8,128)(2,1)} %param.5), kind=kLoop, calls=%fused_computation.16 | loop fusion | flops 3145216 | bytes 2099200 | tf_op jit(solution)/shard_map/reduce_sum | solution.py:22
  10.7 13.7 %psum.21 = f32[512,1]{0,1:T(1,128)S(1)} all-reduce(f32[512,1]{0,1:T(1,128)S(1)} %bitcast.37), channel_id=1, replica_groups=mesh['dp'=4,'pipe'=2,'tensor'=4] {'tensor'}, use_global_device_ids=true, to_apply=%region_1.0 | all-reduce | flops 512 | bytes 4096 | tf_op jit(solution)/shard_map/psum | solution.py:23
  24.4 33.9 %all-gather.3.cloned.1.call-done = bf16[1,1,512,2048]{3,2,1,0:T(8,128)(2,1)} async-done(((bf16[1,1,512,512]{3,2,1,0:T(8,128)(2,1)}), bf16[1,1,512,2048]{3,2,1,0:T(8,128)(2,1)}) %all-gather.3.cloned.1.call-update) | async-done | bytes 2097168 | tf_op jit(solution)/shard_map/all_gather | solution.py:27
  58.3 10.1 %convolution_convert_fusion = bf16[2048,2048]{1,0:T(8,128)(2,1)} fusion(bf16[1,1,512,2048]{3,2,1,0:T(8,128)(2,1)} %param.5, bf16[1,1,512,2048]{3,2,1,0:T(8,128)(2,1)} %all-gather.3.cloned.1.call-done, f32[2048]{0:T(1024)S(1)} %bitcast.34, f32[512]{0:T(512)S(1)} %bitcast.39), kind=kOutput, calls=%fused_computation.2 | convolution fusion | flops 4303355904 | bytes 12593152 | tf_op jit(solution)/shard_map/dot_general | solution.py:31
  68.4 0.0 copy-start
  68.4 0.0 reduce-scatter.2.cloned.1.call-update
  68.4 1.6 %copy-done = bf16[1,1,512,2048]{3,2,1,0:T(8,128)(2,1)S(1)} copy-done((bf16[1,1,512,2048]{3,2,1,0:T(8,128)(2,1)S(1)}, bf16[1,1,512,2048]{3,2,1,0:T(8,128)(2,1)}, u32[]{:S(2)}) %copy-start) | copy-done | bytes 2097176
  70.0 11.8 %fusion.12 = (f32[2048]{0:T(1024)S(1)}, f32[512]{0:T(512)S(1)}, f32[512,2048]{1,0:T(8,128)}) fusion(bf16[1,1,512,2048]{3,2,1,0:T(8,128)(2,1)S(1)} %copy-done, f32[512]{0:T(512)S(1)} %bitcast.40, f32[2048]{0:T(1024)S(1)} %bitcast.35, bf16[1,2048,2048]{2,1,0:T(8,128)(2,1)} %param.9, bf16[1,1,512,2048]{3,2,1,0:T(8,128)(2,1)} %all-gather.3.cloned.1.call-done), kind=kOutput, calls=%fused_computation.15 | convolution fusion | flops 4302304768 | bytes 16797696 | tf_op jit(solution)/shard_map/dot_general | solution.py:28
  81.8 9.0 %psum.22 = f32[512,1]{0,1:T(1,128)S(1)} all-reduce(f32[512,1]{0,1:T(1,128)S(1)} %bitcast.43), channel_id=1, replica_groups=mesh['dp'=4,'pipe'=2,'tensor'=4] {'tensor'}, use_global_device_ids=true, to_apply=%region_3.0 | all-reduce | flops 512 | bytes 4096 | tf_op jit(solution)/shard_map/psum | solution.py:38
  90.8 5.7 %fusion.10 = bf16[512,2048]{1,0:T(8,128)(2,1)} fusion(f32[512,2048]{1,0:T(8,128)} %get-tuple-element.5, bf16[1,1,512,2048]{3,2,1,0:T(8,128)(2,1)} %param.6, bf16[1,1,512,2048]{3,2,1,0:T(8,128)(2,1)S(1)} %copy-done, f32[512]{0:T(512)S(1)} %bitcast.42, f32[2048]{0:T(1024)S(1)} %bitcast.36, f32[512]{0:T(512)S(1)} %bitcast.41), kind=kLoop, calls=%fused_computation.13 | loop fusion | flops 9437184 | bytes 10498048 | tf_op jit(solution)/shard_map/convert_element_type | solution.py:39
  96.5 1.3 collective-permute-start
  97.8 7.0 %psum.23 = f32[1,2048]{1,0:T(1,128)} all-reduce(f32[1,2048]{1,0:T(1,128)S(1)} %bitcast.38), channel_id=1, replica_groups=mesh['dp'=4,'pipe'=2,'tensor'=4] {'dp'}, use_global_device_ids=true, to_apply=%region_6.0 | all-reduce | flops 2048 | bytes 16384 | tf_op jit(solution)/shard_map/psum | solution.py:44
  104.8 39.9 %collective-permute-done = bf16[512,2048]{1,0:T(8,128)(2,1)S(1)} collective-permute-done((bf16[512,2048]{1,0:T(8,128)(2,1)}, bf16[512,2048]{1,0:T(8,128)(2,1)S(1)}, u32[]{:S(2)}, u32[]{:S(2)}) %collective-permute-start) | collective-permute-done | bytes 2097184 | tf_op jit(solution)/shard_map/ppermute | solution.py:12
  144.7 0.0 reduce-scatter.2.cloned.1.call-done
  144.7 1.3 copy.9
  (2 shorter events, 0.0 us)
Async XLA Ops:
  7.2 51.1 %all-gather.3.cloned.1.call-start = ((), (), s32[]{:S(2)}) async-start(), calls=%async_computation.2 | async-start | bytes 2621440 | tf_op jit(solution)/shard_map/all_gather | solution.py:27
  7.9 136.8 %reduce-scatter.2.cloned.1.call-start = ((), (), s32[]{:S(2)}) async-start(), calls=%async_computation.1 | async-start | bytes 10485760 | tf_op jit(solution)/shard_map/reduce_scatter | solution.py:45
  68.4 1.6 %copy-start = (bf16[1,1,512,2048]{3,2,1,0:T(8,128)(2,1)S(1)}, bf16[1,1,512,2048]{3,2,1,0:T(8,128)(2,1)}, u32[]{:S(2)}) copy-start(bf16[1,1,512,2048]{3,2,1,0:T(8,128)(2,1)} %param.5) | copy-start | bytes 6291460
  96.5 48.2 %collective-permute-start = (bf16[512,2048]{1,0:T(8,128)(2,1)}, bf16[512,2048]{1,0:T(8,128)(2,1)S(1)}, u32[]{:S(2)}, u32[]{:S(2)}) collective-permute-start(bf16[512,2048]{1,0:T(8,128)(2,1)} %fusion.10), channel_id=1, source_target_pairs={{4,0},{5,1},{6,2},{7,3},{12,8},{13,9},{14,10},{15,11},{20,16},{21,... | collective-permute-start | bytes 6291464 | tf_op jit(solution)/shard_map/ppermute | solution.py:12
Sparse Core Ops, SparseCore 0:
  9.6 48.6 all-gather.2
  68.5 70.6 reduce-scatter.1
where the time goes:
time: 153 us
  waiting for transfers between devices  74.5 us (49%)
  blocking collectives  29.6 us (19%)
  matrix products  21.9 us (14%)
  between operations  14.1 us (9%)
  other arithmetic  8.53 us (6%)
  local copies, waits for them, and re-layouts  2.89 us (2%)
    ppermute x1, waiting for transfers between devices, from_behind(): return lax.ppermute(block, axis, route)  39.9 us
    all_gather x1, waiting for transfers between devices, on_device(): piece = lax.all_gather(grad_kv, 'tensor', axis=1, tiled=True)  33.9 us
    psum x1, blocking collectives, on_device(): total_squares = lax.psum(local_squares, 'tensor')  13.7 us
    dot_general x1, matrix products, on_device(): lax.dot_general(piece, weight, (((1,), (1,)), ((), ())), preferred_elemen...  11.8 us
    dot_general x1, matrix products, on_device(): lax.dot_general(hidden, piece, (((0,), (0,)), ((), ())), preferred_elemen...  10.1 us
    psum x1, blocking collectives, on_device(): mean_term = lax.psum(local_dot, 'tensor') / D  8.96 us
    psum x1, blocking collectives, on_device(): gain_total = lax.psum(gain_part, 'dp')  7.03 us
    convert_element_type x1, other arithmetic, on_device(): (grad_out.astype(jnp.float32) + rstd * (scaled - normed * mean_term)).ast...  5.73 us
  transfers between devices with their start and end apart: 3, of which 2 were waited for; matrix products, arithmetic and copies ran while one was open for 13% of the time, Pallas kernels for 0%

commit v1 on v0

v1 whole, which is shorter than its diff:
```python
import jax
import jax.numpy as jnp
from jax import lax
from jax.sharding import PartitionSpec as P

EPS = 1e-05
CHUNKS = 2


def from_behind(block, axis, distance):
    devices = range(lax.axis_size(axis))
    route = [(i - distance, i) for i in devices if i - distance in devices]
    return lax.ppermute(block, axis, route)


def shifted(block, axis, shift):
    n = lax.axis_size(axis)
    return lax.ppermute(block, axis, [(i, (i + shift) % n) for i in range(n)])


def to_partner(block):
    n = lax.axis_size("dp")
    return lax.ppermute(block, "dp", [(i, i ^ 1) for i in range(n)])


def summed_over(part, axis):
    return jnp.sum(lax.all_gather(part, axis, axis=0), axis=0)


def gather_columns(block):
    n = lax.axis_size("tensor")
    me = lax.axis_index("tensor")
    rows, width = block.shape
    full = jnp.zeros((rows, width * n), block.dtype)
    full = lax.dynamic_update_slice(full, block, (0, me * width))
    for d in range(1, n):
        piece = shifted(block, "tensor", d)
        full = lax.dynamic_update_slice(full, piece, (0, ((me - d) % n) * width))
    return full


def on_device(layer_input, output_grad, kv_grad, norm_gain, kv_weight):
    rows = layer_input[0, 0]
    grad_out = output_grad[0, 0]
    grad_kv = kv_grad[0, 0]
    gain_f = norm_gain[0].astype(jnp.float32)
    weight = kv_weight[0]
    seq, d_local = rows.shape
    d_model = d_local * lax.axis_size("tensor")
    n_dp = lax.axis_size("dp")
    me = lax.axis_index("dp")
    kv = grad_kv.shape[1] * lax.axis_size("tensor")
    kv_block = kv // n_dp
    shifts = [2 * d for d in range(1, n_dp // 2)]

    rows_outer = [shifted(rows, "dp", s) for s in shifts]
    rows_partner = to_partner(rows)
    rows_partner_outer = [to_partner(r) for r in rows_outer]

    values = rows.astype(jnp.float32)
    total_squares = summed_over(jnp.sum(values * values, axis=1), "tensor")
    rstd = lax.rsqrt(total_squares / d_model + EPS)
    rstd_outer = [shifted(rstd, "dp", s) for s in shifts]
    rstd_partner = to_partner(rstd)
    rstd_partner_outer = [to_partner(r) for r in rstd_outer]
    normed = values * rstd[:, None]

    def hidden_of(x, r):
        return ((x.astype(jnp.float32) * r[:, None]) * gain_f).astype(jnp.bfloat16)

    def kv_cols(full, owner):
        return lax.dynamic_slice_in_dim(full, owner * kv_block, kv_block, axis=1)

    step = seq // CHUNKS
    inputs_grad = []
    gain_part = jnp.zeros((d_local,), jnp.float32)
    kv_own, kv_outer, kv_partner, kv_partner_outer = [], [], [], []
    for c in range(CHUNKS):
        lo = c * step
        piece = gather_columns(grad_kv[lo:lo + step])
        kv_own.append(kv_cols(piece, me))
        outer = []
        for s in shifts:
            dest = (me + s) % n_dp
            pair = jnp.concatenate([kv_cols(piece, dest), kv_cols(piece, dest ^ 1)], axis=1)
            outer.append(shifted(pair, "dp", s))
        kv_outer.append([o[:, :kv_block] for o in outer])
        kv_partner.append(to_partner(kv_cols(piece, me ^ 1)))
        kv_partner_outer.append([to_partner(o[:, kv_block:]) for o in outer])

        row_total = lax.dot_general(
            piece, weight, (((1,), (1,)), ((), ())), preferred_element_type=jnp.float32
        )
        normed_c = normed[lo:lo + step]
        scaled = gain_f * row_total
        mean_term = summed_over(jnp.sum(scaled * normed_c, axis=1), "tensor") / d_model
        input_grad = (
            grad_out[lo:lo + step].astype(jnp.float32)
            + rstd[lo:lo + step, None] * (scaled - normed_c * mean_term[:, None])
        ).astype(jnp.bfloat16)
        inputs_grad.append(from_behind(input_grad, "pipe", -1))
        gain_part = gain_part + jnp.sum(row_total * normed_c, axis=0)

    upstream = jnp.concatenate(inputs_grad, axis=0)
    gain_total = summed_over(gain_part, "dp")

    def weight_part(x, r, blocks):
        h = hidden_of(x, r)
        total = None
        for c, blk in enumerate(blocks):
            term = lax.dot_general(
                h[c * step:(c + 1) * step], blk, (((0,), (0,)), ((), ())),
                preferred_element_type=jnp.float32,
            )
            total = term if total is None else total + term
        return total

    wgrad = weight_part(rows, rstd, kv_own)
    wgrad = wgrad + weight_part(rows_partner, rstd_partner, kv_partner)
    for k in range(len(shifts)):
        wgrad = wgrad + weight_part(rows_outer[k], rstd_outer[k], [b[k] for b in kv_outer])
        wgrad = wgrad + weight_part(
            rows_partner_outer[k], rstd_partner_outer[k], [b[k] for b in kv_partner_outer]
        )
    weight_total = wgrad.astype(jnp.bfloat16)
    return (upstream[None, None], weight_total[None], gain_total[None])


def solution(mesh):
    in_specs = (
        P("dp", "pipe", None, "tensor"),
        P("dp", "pipe", None, "tensor"),
        P("dp", "pipe", None, "tensor"),
        P("pipe", "tensor"),
        P("pipe", "tensor", None),
    )
    out_specs = (P("dp", "pipe", None, "tensor"), P("pipe", "tensor", "dp"), P("pipe", "tensor"))
    return jax.shard_map(
        on_device, mesh=mesh, in_specs=in_specs, out_specs=out_specs, check_vma=False
    )
```

time: 153 us -> 200 us (1.31)
  blocking collectives: 29.6 us -> 57.7 us
  starting transfers between devices: 1.36 us -> 25.2 us
  between operations: 14.1 us -> 1.01 us
  waiting for transfers between devices: 74.5 us -> 62.2 us
  other arithmetic: 8.53 us -> 17.3 us
  matrix products: 21.9 us -> 30.2 us
  local copies, waits for them, and re-layouts: 2.89 us -> 5.97 us
    all_gather x0 -> x4, blocking collectives: none -> 57.7 us  [summed_over(): return jnp.sum(lax.all_gather(part, axis, axis=0), axis=0)]
    ppermute x0 -> x18, waiting for transfers between devices: none -> 39.2 us  [the longest x10 39.1 us: shifted(): return lax.ppermute(block, axis, [(i, (i + shift) % n) for i in range(n)])]
    all_gather x1 -> x0, waiting for transfers between devices: 33.9 us -> none  [on_device(): piece = lax.all_gather(grad_kv, 'tensor', axis=1, tiled=True)]
    psum x3 -> x0, blocking collectives: 29.6 us -> none  [the longest x1 13.7 us: on_device(): total_squares = lax.psum(local_squares, 'tensor')]
    ppermute x0 -> x18, starting transfers between devices: none -> 22.4 us  [the longest x10 20.9 us: shifted(): return lax.ppermute(block, axis, [(i, (i + shift) % n) for i in range(n)])]
    ppermute x1 -> x2, waiting for transfers between devices: 39.9 us -> 23 us  [from_behind(): return lax.ppermute(block, axis, route)]
    dot_general x1 -> x8, matrix products: 10.1 us -> 23.9 us  [weight_part(): lax.dot_general(h[c * step:(c + 1) * step], blk, (((0,), (0,)), ((), ()))...]
    convert_element_type x1 -> x2, other arithmetic: 5.73 us -> 11.3 us  [the longest x1 5.77 us: on_device(): input_grad = (grad_out[lo:lo + step].astype(jnp.float32) + rstd[lo:lo + s...]
  transfers between devices with their start and end apart: 3 -> 20, of which waited for: 2 -> 7; matrix products, arithmetic and copies ran while one was open for 13% -> 25% of each run, Pallas kernels for 0% -> 0%
where the time goes in v1:
time: 200 us
  waiting for transfers between devices  62.2 us (31%)
  blocking collectives  57.7 us (29%)
  matrix products  30.2 us (15%)
  starting transfers between devices  25.2 us (13%)
  other arithmetic  17.3 us (9%)
  local copies, waits for them, and re-layouts  5.97 us (3%)
    all_gather x4, blocking collectives, summed_over(): return jnp.sum(lax.all_gather(part, axis, axis=0), axis=0)  57.7 us
    ppermute x10, waiting for transfers between devices, shifted(): return lax.ppermute(block, axis, [(i, (i + shift) % n) for i in range(n)])  39.1 us
    dot_general x8, matrix products, weight_part(): lax.dot_general(h[c * step:(c + 1) * step], blk, (((0,), (0,)), ((), ()))...  23.9 us
    ppermute x2, waiting for transfers between devices, from_behind(): return lax.ppermute(block, axis, route)  23 us
    ppermute x10, starting transfers between devices, shifted(): return lax.ppermute(block, axis, [(i, (i + shift) % n) for i in range(n)])  20.9 us
    dot_general x2, matrix products, on_device(): lax.dot_general(piece, weight, (((1,), (1,)), ((), ())), preferred_elemen...  6.35 us
    convert_element_type x1, other arithmetic, on_device(): input_grad = (grad_out[lo:lo + step].astype(jnp.float32) + rstd[lo:lo + s...  5.77 us
    convert_element_type x1, other arithmetic, hidden_of(): return (x.astype(jnp.float32) * r[:, None] * gain_f).astype(jnp.bfloat16)  5.51 us
  transfers between devices with their start and end apart: 20, of which 7 were waited for; matrix products, arithmetic and copies ran while one was open for 25% of the time, Pallas kernels for 0%

profile of v1, /device:TPU:0, one launch (start us, length us, event | category | flops | bytes accessed | tf_op | source)
XLA Modules:
  0.0 199.6 jit_solution(5802457722451996849)
XLA Ops:
  0.6 3.0 %collective-permute-start.12 = (bf16[512,2048]{1,0:T(8,128)(2,1)}, bf16[512,2048]{1,0:T(8,128)(2,1)}, u32[]{:S(2)}, u32[]{:S(2)}) collective-permute-start(bf16[512,2048]{1,0:T(8,128)(2,1)} %bitcast.41), channel_id=1, source_target_pairs={{0,16},{8,24},{16,0},{24,8},{1,17},{9,25},{17,1},{25,9},{2,18},{10... | collective-permute-start | bytes 6291464 | tf_op jit(solution)/shard_map/ppermute | solution.py:18
  5.5 2.6 %collective-permute-start.5 = (bf16[256,512]{1,0:T(8,128)(2,1)}, bf16[256,512]{1,0:T(8,128)(2,1)S(1)}, u32[]{:S(2)}, u32[]{:S(2)}) collective-permute-start(bf16[256,512]{1,0:T(8,128)(2,1)} %get-tuple-element.20), channel_id=1, source_target_pairs={{0,2},{1,3},{2,0},{3,1},{4,6},{5,7},{6,4},{7,5},{8,10},{9,11},{10,... | collective-permute-start | bytes 786440 | tf_op jit(solution)/shard_map/ppermute | solution.py:18
  9.7 2.2 %collective-permute-start.6 = (bf16[256,512]{1,0:T(8,128)(2,1)}, bf16[256,512]{1,0:T(8,128)(2,1)S(1)}, u32[]{:S(2)}, u32[]{:S(2)}) collective-permute-start(bf16[256,512]{1,0:T(8,128)(2,1)} %get-tuple-element.20), channel_id=1, source_target_pairs={{0,3},{1,0},{2,1},{3,2},{4,7},{5,4},{6,5},{7,6},{8,11},{9,8},{10,9... | collective-permute-start | bytes 786440 | tf_op jit(solution)/shard_map/ppermute | solution.py:18
  14.0 24.6 %all-gather.4 = f32[4,1,512]{2,1,0:T(1,128)S(1)} all-gather(f32[1,1,512]{2,1,0:T(1,128)S(1)} %bitcast.46), channel_id=2, replica_groups=mesh['dp'=4,'pipe'=2,'tensor'=4] {'tensor'}, dimensions={0}, use_global_device_ids=true | all-gather | bytes 10240 | tf_op jit(solution)/shard_map/all_gather | solution.py:27
  39.0 10.6 %collective-permute-done.12 = bf16[512,2048]{1,0:T(8,128)(2,1)} collective-permute-done((bf16[512,2048]{1,0:T(8,128)(2,1)}, bf16[512,2048]{1,0:T(8,128)(2,1)}, u32[]{:S(2)}, u32[]{:S(2)}) %collective-permute-start.12) | collective-permute-done | bytes 2097184 | tf_op jit(solution)/shard_map/ppermute | solution.py:18
  49.7 2.9 %collective-permute-start.1 = (bf16[256,512]{1,0:T(8,128)(2,1)}, bf16[256,512]{1,0:T(8,128)(2,1)S(1)}, u32[]{:S(2)}, u32[]{:S(2)}) collective-permute-start(bf16[256,512]{1,0:T(8,128)(2,1)} %get-tuple-element.19), channel_id=1, source_target_pairs={{0,2},{1,3},{2,0},{3,1},{4,6},{5,7},{6,4},{7,5},{8,10},{9,11},{10,... | collective-permute-start | bytes 786440 | tf_op jit(solution)/shard_map/ppermute | solution.py:18
  54.3 2.3 %collective-permute-start.2 = (bf16[256,512]{1,0:T(8,128)(2,1)}, bf16[256,512]{1,0:T(8,128)(2,1)S(1)}, u32[]{:S(2)}, u32[]{:S(2)}) collective-permute-start(bf16[256,512]{1,0:T(8,128)(2,1)} %get-tuple-element.19), channel_id=1, source_target_pairs={{0,3},{1,0},{2,1},{3,2},{4,7},{5,4},{6,5},{7,6},{8,11},{9,8},{10,9... | collective-permute-start | bytes 786440 | tf_op jit(solution)/shard_map/ppermute | solution.py:18
  57.6 9.4 %collective-permute-done = bf16[256,512]{1,0:T(8,128)(2,1)S(1)} collective-permute-done((bf16[256,512]{1,0:T(8,128)(2,1)}, bf16[256,512]{1,0:T(8,128)(2,1)S(1)}, u32[]{:S(2)}, u32[]{:S(2)}) %collective-permute-start) | collective-permute-done | bytes 262176 | tf_op jit(solution)/shard_map/ppermute | solution.py:18
  68.5 2.8 %collective-permute-done.1 = bf16[256,512]{1,0:T(8,128)(2,1)S(1)} collective-permute-done((bf16[256,512]{1,0:T(8,128)(2,1)}, bf16[256,512]{1,0:T(8,128)(2,1)S(1)}, u32[]{:S(2)}, u32[]{:S(2)}) %collective-permute-start.1) | collective-permute-done | bytes 262176 | tf_op jit(solution)/shard_map/ppermute | solution.py:18
  73.0 7.1 %collective-permute-done.13 = f32[512]{0:T(512)S(1)} collective-permute-done((f32[512]{0:T(512)S(1)}, f32[512]{0:T(512)S(1)}, u32[]{:S(2)}, u32[]{:S(2)}) %collective-permute-start.13) | collective-permute-done | bytes 2080 | tf_op jit(solution)/shard_map/ppermute | solution.py:18
  83.2 2.4 %fusion = f32[256,2048]{1,0:T(8,128)S(1)} fusion(bf16[256,2048]{1,0:T(8,128)(2,1)S(1)} %constant_dynamic-update-slice_fusion, bf16[1,2048,2048]{2,1,0:T(8,128)(2,1)S(1)} %copy-done.13), kind=kOutput, calls=%fused_computation | convolution fusion | flops 2147483648 | bytes 11534336 | tf_op jit(solution)/shard_map/dot_general | solution.py:91
  86.4 9.2 %collective-permute-done.14 = bf16[256,1024]{1,0:T(8,128)(2,1)S(1)} collective-permute-done((bf16[256,1024]{1,0:T(8,128)(2,1)S(1)}, bf16[256,1024]{1,0:T(8,128)(2,1)S(1)}, u32[]{:S(2)}, u32[]{:S(2)}) %collective-permute-start.14) | collective-permute-done | bytes 524320 | tf_op jit(solution)/shard_map/ppermute | solution.py:18
  97.3 5.5 %multiply_convert_fusion.3 = (bf16[512,2048]{1,0:T(8,128)(2,1)S(1)}, f32[512,2048]{1,0:T(8,128)S(1)}, bf16[512,2048]{1,0:T(8,128)(2,1)}, bf16[512,2048]{1,0:T(8,128)(2,1)}, bf16[512,2048]{1,0:T(8,128)(2,1)}) fusion(f32[2048]{0:T(1024)S(1)} %bitcast.43, f32[512]{0:T(512)S(1)} %add_rsqrt_fusion, bf16[1,1,512,2048]{3,2,1,0:T(8,128)(2,1)S(1)} %copy-done.4, ...), kind=kLoop, calls=%fused_computation.11 | loop fusion | flops 16777216 | bytes 20987904 | tf_op jit(solution)/shard_map/convert_element_type | solution.py:69
  102.9 4.0 %multiply_reduce_fusion.1 = (f32[2048]{0:T(1024)S(1)}, f32[256]{0:T(256)S(1)}, f32[256]{0:T(256)S(1)}, f32[2048]{0:T(1024)S(1)}, f32[256,2048]{1,0:T(8,128)}) fusion(f32[512,2048]{1,0:T(8,128)S(1)} %get-tuple-element.12, f32[2048]{0:T(1024)S(1)} %bitcast.44, f32[256,2048]{1,0:T(8,128)S(1)} %fusion, bf16[256,2048]{1,0:T(8,128)(2,1)S(1)} %copy-done.6, ...), kind=kOutput, calls=%fused_computation.19 | convolution fusion | flops 2152721920 | bytes 17852416 | tf_op jit(solution)/shard_map/dot_general | solution.py:91
  106.8 18.8 %all-gather.5 = f32[4,1,256]{2,1,0:T(1,128)S(1)} all-gather(f32[1,1,256]{2,1,0:T(1,128)S(1)} %bitcast.49), channel_id=3, replica_groups=mesh['dp'=4,'pipe'=2,'tensor'=4] {'tensor'}, dimensions={0}, use_global_device_ids=true | all-gather | bytes 5120 | tf_op jit(solution)/shard_map/all_gather | solution.py:27
  125.7 9.0 %all-gather.6 = f32[4,1,256]{2,1,0:T(1,128)S(1)} all-gather(f32[1,1,256]{2,1,0:T(1,128)S(1)} %bitcast.48), channel_id=4, replica_groups=mesh['dp'=4,'pipe'=2,'tensor'=4] {'tensor'}, dimensions={0}, use_global_device_ids=true | all-gather | bytes 5120 | tf_op jit(solution)/shard_map/all_gather | solution.py:27
  134.8 5.2 %all-gather.3 = f32[8192]{0:T(1024)S(1)} all-gather(f32[2048]{0:T(1024)S(1)} %add.130), channel_id=5, replica_groups=mesh['dp'=4,'pipe'=2,'tensor'=4] {'dp'}, dimensions={0}, use_global_device_ids=true | all-gather | bytes 40960 | tf_op jit(solution)/shard_map/all_gather | solution.py:27
  140.6 5.8 %fusion.7 = (bf16[256,2048]{1,0:T(8,128)(2,1)}, bf16[256,2048]{1,0:T(8,128)(2,1)}) fusion(f32[256,2048]{1,0:T(8,128)} %get-tuple-element.26, f32[512,2048]{1,0:T(8,128)} %copy-done.2, f32[256]{0:T(256)S(1)} %broadcast_multiply_fusion.1, f32[2048]{0:T(1024)S(1)} %bitcast.45, f32[256]{0:T(256)S(1)} %get-tuple-element.24, bf16[1,1,512,2048]{3,2,1,0:T(8,128)(2,1)} %param.6, ...), kind=kLoop, calls=%fused_computation.17 | loop fusion | flops 7340032 | bytes 12595200 | tf_op jit(solution)/shard_map/convert_element_type | solution.py:100
  153.5 3.8 %fusion.21 = f32[2048,512]{1,0:T(8,128)} fusion(bf16[512,2048]{1,0:T(8,128)(2,1)S(1)} %get-tuple-element.11, bf16[256,2048]{1,0:T(8,128)(2,1)} %copy-done.5, s32[]{:T(128)S(6)} %select_n.66), kind=kOutput, calls=%fused_computation.35 | convolution fusion | flops 536870912 | bytes 5505028 | tf_op jit(solution)/shard_map/dot_general | solution.py:111
  157.3 3.7 %fusion.8 = f32[2048,512]{1,0:T(8,128)} fusion(bf16[256,512]{1,0:T(8,128)(2,1)} %collective-permute-done.19, bf16[512,2048]{1,0:T(8,128)(2,1)S(1)} %copy-done.3), kind=kOutput, calls=%fused_computation.22 | convolution fusion | flops 536870912 | bytes 5505024 | tf_op jit(solution)/shard_map/dot_general | solution.py:111
  160.9 3.7 %fusion.19 = f32[2048,512]{1,0:T(8,128)} fusion(bf16[512,2048]{1,0:T(8,128)(2,1)S(1)} %get-tuple-element.11, bf16[256,2048]{1,0:T(8,128)(2,1)} %copy-done.7, s32[]{:T(128)S(6)} %select_n.66), kind=kOutput, calls=%fused_computation.33 | convolution fusion | flops 536870912 | bytes 5505028 | tf_op jit(solution)/shard_map/dot_general | solution.py:111
  164.6 8.8 %fusion.5 = bf16[1,2048,512]{2,1,0:T(8,128)(2,1)} fusion(f32[2048,512]{1,0:T(8,128)} %fusion.8, bf16[256,512]{1,0:T(8,128)(2,1)} %collective-permute-done.18, f32[2048,512]{1,0:T(8,128)S(1)} %fusion.13, f32[2048,512]{1,0:T(8,128)S(1)} %fusion.11, f32[2048,512]{1,0:T(8,128)S(1)} %fusion.17, f32[2048,512]{1,0:T(8,128)S(1)} %fusion.15, ...), kind=kOutput, calls=%fused_computation.12 | convolution fusion | flops 545259520 | bytes 32768000 | tf_op jit(solution)/shard_map/dot_general | solution.py:111
  174.6 21.9 %collective-permute-done.7 = bf16[256,2048]{1,0:T(8,128)(2,1)} collective-permute-done((bf16[256,2048]{1,0:T(8,128)(2,1)}, bf16[256,2048]{1,0:T(8,128)(2,1)}, u32[]{:S(2)}, u32[]{:S(2)}) %collective-permute-start.7) | collective-permute-done | bytes 1048608 | tf_op jit(solution)/shard_map/ppermute | solution.py:13
  196.4 3.1 %maximum_bitcast_fusion = bf16[1,1,512,2048]{3,2,1,0:T(8,128)(2,1)} fusion(bf16[256,2048]{1,0:T(8,128)(2,1)} %collective-permute-done.7, bf16[256,2048]{1,0:T(8,128)(2,1)} %collective-permute-done.3), kind=kLoop, calls=%fused_computation.13 | loop fusion | flops 4194304 | bytes 4194304 | tf_op jit(solution)/shard_map/broadcast_in_dim | solution.py:126
  (90 shorter events, 26.2 us)
Async XLA Ops:
  0.6 38.1 %copy-start.9 = (bf16[1,1,512,512]{3,2,1,0:T(8,128)(2,1)S(1)}, bf16[1,1,512,512]{3,2,1,0:T(8,128)(2,1)}, u32[]{:S(2)}) copy-start(bf16[1,1,512,512]{3,2,1,0:T(8,128)(2,1)} %param.7) | copy-start | bytes 1572868
  0.6 49.0 %collective-permute-start.12 = (bf16[512,2048]{1,0:T(8,128)(2,1)}, bf16[512,2048]{1,0:T(8,128)(2,1)}, u32[]{:S(2)}, u32[]{:S(2)}) collective-permute-start(bf16[512,2048]{1,0:T(8,128)(2,1)} %bitcast.41), channel_id=1, source_target_pairs={{0,16},{8,24},{16,0},{24,8},{1,17},{9,25},{17,1},{25,9},{2,18},{10... | collective-permute-start | bytes 6291464 | tf_op jit(solution)/shard_map/ppermute | solution.py:18
  5.5 47.1 %collective-permute-start.5 = (bf16[256,512]{1,0:T(8,128)(2,1)}, bf16[256,512]{1,0:T(8,128)(2,1)S(1)}, u32[]{:S(2)}, u32[]{:S(2)}) collective-permute-start(bf16[256,512]{1,0:T(8,128)(2,1)} %get-tuple-element.20), channel_id=1, source_target_pairs={{0,2},{1,3},{2,0},{3,1},{4,6},{5,7},{6,4},{7,5},{8,10},{9,11},{10,... | collective-permute-start | bytes 786440 | tf_op jit(solution)/shard_map/ppermute | solution.py:18
  8.1 41.6 %collective-permute-start.4 = (bf16[256,512]{1,0:T(8,128)(2,1)}, bf16[256,512]{1,0:T(8,128)(2,1)S(1)}, u32[]{:S(2)}, u32[]{:S(2)}) collective-permute-start(bf16[256,512]{1,0:T(8,128)(2,1)} %get-tuple-element.20), channel_id=1, source_target_pairs={{0,1},{1,2},{2,3},{3,0},{4,5},{5,6},{6,7},{7,4},{8,9},{9,10},{10,1... | collective-permute-start | bytes 786440 | tf_op jit(solution)/shard_map/ppermute | solution.py:18
  9.7 44.6 %collective-permute-start.6 = (bf16[256,512]{1,0:T(8,128)(2,1)}, bf16[256,512]{1,0:T(8,128)(2,1)S(1)}, u32[]{:S(2)}, u32[]{:S(2)}) collective-permute-start(bf16[256,512]{1,0:T(8,128)(2,1)} %get-tuple-element.20), channel_id=1, source_target_pairs={{0,3},{1,0},{2,1},{3,2},{4,7},{5,4},{6,5},{7,6},{8,11},{9,8},{10,9... | collective-permute-start | bytes 786440 | tf_op jit(solution)/shard_map/ppermute | solution.py:18
  11.9 85.0 %collective-permute-start.8 = (bf16[512,2048]{1,0:T(8,128)(2,1)}, bf16[512,2048]{1,0:T(8,128)(2,1)}, u32[]{:S(2)}, u32[]{:S(2)}) collective-permute-start(bf16[512,2048]{1,0:T(8,128)(2,1)} %bitcast.42), channel_id=1, source_target_pairs={{0,8},{8,0},{16,24},{24,16},{1,9},{9,1},{17,25},{25,17},{2,10},{10... | collective-permute-start | bytes 6291464 | tf_op jit(solution)/shard_map/ppermute | solution.py:23
  14.0 35.6 %copy-start.12 = (bf16[1,2048]{1,0:T(2,128)(2,1)S(1)}, bf16[1,2048]{1,0:T(2,128)(2,1)}, u32[]{:S(2)}) copy-start(bf16[1,2048]{1,0:T(2,128)(2,1)} %param.8) | copy-start | bytes 12292
  49.6 47.7 %collective-permute-start.16 = (bf16[512,2048]{1,0:T(8,128)(2,1)}, bf16[512,2048]{1,0:T(8,128)(2,1)}, u32[]{:S(2)}, u32[]{:S(2)}) collective-permute-start(bf16[512,2048]{1,0:T(8,128)(2,1)} %collective-permute-done.12), channel_id=1, source_target_pairs={{0,8},{8,0},{16,24},{24,16},{1,9},{9,1},{17,25},{25,17},{2,10},{10... | collective-permute-start | bytes 6291464 | tf_op jit(solution)/shard_map/ppermute | solution.py:23
  49.7 21.6 %collective-permute-start.1 = (bf16[256,512]{1,0:T(8,128)(2,1)}, bf16[256,512]{1,0:T(8,128)(2,1)S(1)}, u32[]{:S(2)}, u32[]{:S(2)}) collective-permute-start(bf16[256,512]{1,0:T(8,128)(2,1)} %get-tuple-element.19), channel_id=1, source_target_pairs={{0,2},{1,3},{2,0},{3,1},{4,6},{5,7},{6,4},{7,5},{8,10},{9,11},{10,... | collective-permute-start | bytes 786440 | tf_op jit(solution)/shard_map/ppermute | solution.py:18
  52.6 30.7 %copy-start.13 = (bf16[1,2048,2048]{2,1,0:T(8,128)(2,1)S(1)}, bf16[1,2048,2048]{2,1,0:T(8,128)(2,1)}, u32[]{:S(2)}) copy-start(bf16[1,2048,2048]{2,1,0:T(8,128)(2,1)} %param.9) | copy-start | bytes 25165828
  52.6 14.4 %collective-permute-start = (bf16[256,512]{1,0:T(8,128)(2,1)}, bf16[256,512]{1,0:T(8,128)(2,1)S(1)}, u32[]{:S(2)}, u32[]{:S(2)}) collective-permute-start(bf16[256,512]{1,0:T(8,128)(2,1)} %get-tuple-element.19), channel_id=1, source_target_pairs={{0,1},{1,2},{2,3},{3,0},{4,5},{5,6},{6,7},{7,4},{8,9},{9,10},{10,1... | collective-permute-start | bytes 786440 | tf_op jit(solution)/shard_map/ppermute | solution.py:18
  54.3 25.8 %collective-permute-start.2 = (bf16[256,512]{1,0:T(8,128)(2,1)}, bf16[256,512]{1,0:T(8,128)(2,1)S(1)}, u32[]{:S(2)}, u32[]{:S(2)}) collective-permute-start(bf16[256,512]{1,0:T(8,128)(2,1)} %get-tuple-element.19), channel_id=1, source_target_pairs={{0,3},{1,0},{2,1},{3,2},{4,7},{5,4},{6,5},{7,6},{8,11},{9,8},{10,9... | collective-permute-start | bytes 786440 | tf_op jit(solution)/shard_map/ppermute | solution.py:18
  56.6 26.6 %copy-start.7 = (bf16[256,2048]{1,0:T(8,128)(2,1)}, bf16[256,2048]{1,0:T(8,128)(2,1)S(1)}, u32[]{:S(2)}) copy-start(bf16[256,2048]{1,0:T(8,128)(2,1)S(1)} %constant_dynamic-update-slice_fusion) | copy-start | bytes 3145732
  67.0 14.7 %collective-permute-start.15 = (bf16[256,1024]{1,0:T(8,128)(2,1)S(1)}, bf16[256,1024]{1,0:T(8,128)(2,1)S(1)}, u32[]{:S(2)}, u32[]{:S(2)}) collective-permute-start(bf16[256,1024]{1,0:T(8,128)(2,1)S(1)} %pad_maximum_fusion.1), channel_id=1, source_target_pairs={{0,16},{8,24},{16,0},{24,8},{1,17},{9,25},{17,1},{25,9},{2,18},{10... | collective-permute-start | bytes 1572872 | tf_op jit(solution)/shard_map/ppermute | solution.py:18
  71.3 8.8 %collective-permute-start.13 = (f32[512]{0:T(512)S(1)}, f32[512]{0:T(512)S(1)}, u32[]{:S(2)}, u32[]{:S(2)}) collective-permute-start(f32[512]{0:T(512)S(1)} %add_rsqrt_fusion), channel_id=1, source_target_pairs={{0,16},{8,24},{16,0},{24,8},{1,17},{9,25},{17,1},{25,9},{2,18},{10... | collective-permute-start | bytes 6152 | tf_op jit(solution)/shard_map/ppermute | solution.py:18
  80.1 16.2 %collective-permute-start.9 = (f32[512]{0:T(512)S(1)}, f32[512]{0:T(512)S(1)}, u32[]{:S(2)}, u32[]{:S(2)}) collective-permute-start(f32[512]{0:T(512)S(1)} %add_rsqrt_fusion), channel_id=1, source_target_pairs={{0,8},{8,0},{16,24},{24,16},{1,9},{9,1},{17,25},{25,17},{2,10},{10... | collective-permute-start | bytes 6152 | tf_op jit(solution)/shard_map/ppermute | solution.py:23
  80.1 16.7 %collective-permute-start.17 = (f32[512]{0:T(512)S(1)}, f32[512]{0:T(512)S(1)}, u32[]{:S(2)}, u32[]{:S(2)}) collective-permute-start(f32[512]{0:T(512)S(1)} %collective-permute-done.13), channel_id=1, source_target_pairs={{0,8},{8,0},{16,24},{24,16},{1,9},{9,1},{17,25},{25,17},{2,10},{10... | collective-permute-start | bytes 6152 | tf_op jit(solution)/shard_map/ppermute | solution.py:23
  81.7 13.9 %collective-permute-start.14 = (bf16[256,1024]{1,0:T(8,128)(2,1)S(1)}, bf16[256,1024]{1,0:T(8,128)(2,1)S(1)}, u32[]{:S(2)}, u32[]{:S(2)}) collective-permute-start(bf16[256,1024]{1,0:T(8,128)(2,1)S(1)} %pad_maximum_fusion), channel_id=1, source_target_pairs={{0,16},{8,24},{16,0},{24,8},{1,17},{9,25},{17,1},{25,9},{2,18},{10... | collective-permute-start | bytes 1572872 | tf_op jit(solution)/shard_map/ppermute | solution.py:18
  95.6 53.9 %collective-permute-start.11 = (bf16[256,512]{1,0:T(8,128)(2,1)}, bf16[256,512]{1,0:T(8,128)(2,1)S(1)}, u32[]{:S(2)}, u32[]{:S(2)}) collective-permute-start(bf16[256,512]{1,0:T(8,128)(2,1)} %get-tuple-element.13), channel_id=1, source_target_pairs={{0,8},{8,0},{16,24},{24,16},{1,9},{9,1},{17,25},{25,17},{2,10},{10... | collective-permute-start | bytes 786440 | tf_op jit(solution)/shard_map/ppermute | solution.py:23
  96.3 55.4 %collective-permute-start.10 = (bf16[256,512]{1,0:T(8,128)(2,1)}, bf16[256,512]{1,0:T(8,128)(2,1)}, u32[]{:S(2)}, u32[]{:S(2)}) collective-permute-start(bf16[256,512]{1,0:T(8,128)(2,1)} %get-tuple-element.16), channel_id=1, source_target_pairs={{0,8},{8,0},{16,24},{24,16},{1,9},{9,1},{17,25},{25,17},{2,10},{10... | collective-permute-start | bytes 786440 | tf_op jit(solution)/shard_map/ppermute | solution.py:23
  96.8 60.5 %collective-permute-start.19 = (bf16[256,512]{1,0:T(8,128)(2,1)}, bf16[256,512]{1,0:T(8,128)(2,1)}, u32[]{:S(2)}, u32[]{:S(2)}) collective-permute-start(bf16[256,512]{1,0:T(8,128)(2,1)} %slice.103), channel_id=1, source_target_pairs={{0,8},{8,0},{16,24},{24,16},{1,9},{9,1},{17,25},{25,17},{2,10},{10... | collective-permute-start | bytes 786440 | tf_op jit(solution)/shard_map/ppermute | solution.py:23
  96.9 67.7 %collective-permute-start.18 = (bf16[256,512]{1,0:T(8,128)(2,1)}, bf16[256,512]{1,0:T(8,128)(2,1)}, u32[]{:S(2)}, u32[]{:S(2)}) collective-permute-start(bf16[256,512]{1,0:T(8,128)(2,1)} %slice.101), channel_id=1, source_target_pairs={{0,8},{8,0},{16,24},{24,16},{1,9},{9,1},{17,25},{25,17},{2,10},{10... | collective-permute-start | bytes 786440 | tf_op jit(solution)/shard_map/ppermute | solution.py:23
  146.4 28.2 %collective-permute-start.3 = (bf16[256,2048]{1,0:T(8,128)(2,1)}, bf16[256,2048]{1,0:T(8,128)(2,1)}, u32[]{:S(2)}, u32[]{:S(2)}) collective-permute-start(bf16[256,2048]{1,0:T(8,128)(2,1)} %get-tuple-element.9), channel_id=1, source_target_pairs={{4,0},{5,1},{6,2},{7,3},{12,8},{13,9},{14,10},{15,11},{20,16},{21,... | collective-permute-start | bytes 3145736 | tf_op jit(solution)/shard_map/ppermute | solution.py:13
  149.5 47.0 %collective-permute-start.7 = (bf16[256,2048]{1,0:T(8,128)(2,1)}, bf16[256,2048]{1,0:T(8,128)(2,1)}, u32[]{:S(2)}, u32[]{:S(2)}) collective-permute-start(bf16[256,2048]{1,0:T(8,128)(2,1)} %get-tuple-element.10), channel_id=1, source_target_pairs={{4,0},{5,1},{6,2},{7,3},{12,8},{13,9},{14,10},{15,11},{20,16},{21,... | collective-permute-start | bytes 3145736 | tf_op jit(solution)/shard_map/ppermute | solution.py:13
  (10 other events, 61.7 us)

commit v2 on v1

v2 whole, which is shorter than its diff:
```python
import jax
import jax.numpy as jnp
from jax import lax
from jax.sharding import PartitionSpec as P

EPS = 1e-05
CHUNKS = 2


def from_behind(block, axis, distance):
    devices = range(lax.axis_size(axis))
    route = [(i - distance, i) for i in devices if i - distance in devices]
    return lax.ppermute(block, axis, route)


def shifted(block, axis, shift):
    n = lax.axis_size(axis)
    return lax.ppermute(block, axis, [(i, (i + shift) % n) for i in range(n)])


def to_partner(block):
    n = lax.axis_size("dp")
    return lax.ppermute(block, "dp", [(i, i ^ 1) for i in range(n)])


def gather_columns(block):
    n = lax.axis_size("tensor")
    me = lax.axis_index("tensor")
    rows, width = block.shape
    full = jnp.zeros((rows, width * n), block.dtype)
    full = lax.dynamic_update_slice(full, block, (0, me * width))
    for d in range(1, n):
        piece = shifted(block, "tensor", d)
        full = lax.dynamic_update_slice(full, piece, (0, ((me - d) % n) * width))
    return full


def on_device(layer_input, output_grad, kv_grad, norm_gain, kv_weight):
    rows = layer_input[0, 0]
    grad_out = output_grad[0, 0]
    grad_kv = kv_grad[0, 0]
    gain_f = norm_gain[0].astype(jnp.float32)
    weight = kv_weight[0]
    seq, d_local = rows.shape
    d_model = d_local * lax.axis_size("tensor")
    n_dp = lax.axis_size("dp")
    me = lax.axis_index("dp")
    kv = grad_kv.shape[1] * lax.axis_size("tensor")
    kv_block = kv // n_dp
    shifts = [2 * d for d in range(1, n_dp // 2)]

    values = rows.astype(jnp.float32)
    total_squares = lax.psum(jnp.sum(values * values, axis=1, keepdims=True), "tensor")
    rstd = lax.rsqrt(total_squares / d_model + EPS)
    normed = values * rstd
    hidden = (normed * gain_f).astype(jnp.bfloat16)

    hidden_outer = [shifted(hidden, "dp", s) for s in shifts]
    hidden_partner = to_partner(hidden)
    hidden_partner_outer = [to_partner(h) for h in hidden_outer]

    piece = gather_columns(grad_kv)

    def kv_cols(owner):
        return lax.dynamic_slice_in_dim(piece, owner * kv_block, kv_block, axis=1)

    kv_outer = []
    for s in shifts:
        dest = (me + s) % n_dp
        kv_outer.append(shifted(jnp.concatenate([kv_cols(dest), kv_cols(dest ^ 1)], axis=1), "dp", s))
    to_send = jnp.concatenate([kv_cols(me ^ 1)] + [o[:, kv_block:] for o in kv_outer], axis=1)
    kv_partner_all = to_partner(to_send)
    kv_partner = kv_partner_all[:, :kv_block]
    kv_partner_outer = [
        kv_partner_all[:, (k + 1) * kv_block:(k + 2) * kv_block] for k in range(len(shifts))
    ]

    step = seq // CHUNKS
    inputs_grad = []
    sent = []
    gain_part = jnp.zeros((d_local,), jnp.float32)
    block = piece[:step]
    for c in range(CHUNKS):
        lo = c * step
        row_total = lax.dot_general(
            block, weight, (((1,), (1,)), ((), ())),
            preferred_element_type=jnp.float32,
        )
        normed_c = normed[lo:lo + step]
        scaled = gain_f * row_total
        mean_term = lax.psum(jnp.sum(scaled * normed_c, axis=1, keepdims=True), "tensor") / d_model
        input_grad = (
            grad_out[lo:lo + step].astype(jnp.float32)
            + rstd[lo:lo + step] * (scaled - normed_c * mean_term)
        ).astype(jnp.bfloat16)
        inputs_grad.append(from_behind(input_grad, "pipe", -1))
        sent.append(input_grad)
        if c + 1 < CHUNKS:
            _, block = lax.optimization_barrier((input_grad, piece[lo + step:lo + 2 * step]))
        gain_part = gain_part + jnp.sum(row_total * normed_c, axis=0)

    upstream = jnp.concatenate(inputs_grad, axis=0)
    gain_total = lax.psum(gain_part, "dp")

    _, hidden_own = lax.optimization_barrier((sent, hidden))

    def term(h, blk):
        return lax.dot_general(h, blk, (((0,), (0,)), ((), ())), preferred_element_type=jnp.float32)

    wgrad = term(hidden_own, kv_cols(me))
    wgrad = wgrad + term(hidden_partner, kv_partner)
    for k in range(len(shifts)):
        wgrad = wgrad + term(hidden_outer[k], kv_outer[k][:, :kv_block])
        wgrad = wgrad + term(hidden_partner_outer[k], kv_partner_outer[k])
    weight_total = wgrad.astype(jnp.bfloat16)
    return (upstream[None, None], weight_total[None], gain_total[None])


def solution(mesh):
    in_specs = (
        P("dp", "pipe", None, "tensor"),
        P("dp", "pipe", None, "tensor"),
        P("dp", "pipe", None, "tensor"),
        P("pipe", "tensor"),
        P("pipe", "tensor", None),
    )
    out_specs = (P("dp", "pipe", None, "tensor"), P("pipe", "tensor", "dp"), P("pipe", "tensor"))
    return jax.shard_map(
        on_device, mesh=mesh, in_specs=in_specs, out_specs=out_specs, check_vma=False
    )
```

time: 200 us -> 166 us (0.83)
  waiting for transfers between devices: 62.2 us -> 28.8 us
  blocking collectives: 57.7 us -> 72.7 us
  starting transfers between devices: 25.2 us -> 12 us
  matrix products: 30.2 us -> 28 us
    psum x0 -> x4, blocking collectives: none -> 72.7 us  [the longest x1 33.4 us: on_device(): lax.psum(jnp.sum(values * values, axis=1, keepdims=True), 'tensor')]
    all_gather x4 -> x0, blocking collectives: 57.7 us -> none  [summed_over(): return jnp.sum(lax.all_gather(part, axis, axis=0), axis=0)]
    ppermute x10 -> x5, waiting for transfers between devices: 39.1 us -> 0.01 us  [shifted(): return lax.ppermute(block, axis, [(i, (i + shift) % n) for i in range(n)])]
    ppermute x10 -> x5, starting transfers between devices: 20.9 us -> 9.28 us  [shifted(): return lax.ppermute(block, axis, [(i, (i + shift) % n) for i in range(n)])]
    ppermute x2, waiting for transfers between devices: 23 us -> 28.8 us  [from_behind(): return lax.ppermute(block, axis, route)]
    dynamic_update_slice x6 -> x3, local copies, waits for them, and re-layouts: 0.14 us -> 2.47 us  [gather_columns(): full = lax.dynamic_update_slice(full, piece, (0, (me - d) % n * width))]
    convert_element_type x1 -> x2, other arithmetic: 5.77 us -> 8.09 us  [on_device(): input_grad = (grad_out[lo:lo + step].astype(jnp.float32) + rstd[lo:lo + s...]
    dot_general x10 -> x6, matrix products: 30.2 us -> 28 us  [the longest x2 14.5 us: on_device(): lax.dot_general(block, weight, (((1,), (1,)), ((), ())), preferred_elemen...]
  transfers between devices with their start and end apart: 20 -> 10, of which waited for: 7 -> 2; matrix products, arithmetic and copies ran while one was open for 25% -> 28% of each run, Pallas kernels for 0% -> 0%
where the time goes in v2:
time: 166 us
  blocking collectives  72.7 us (44%)
  waiting for transfers between devices  28.8 us (17%)
  matrix products  28 us (17%)
  other arithmetic  18.5 us (11%)
  starting transfers between devices  12 us (7%)
  local copies, waits for them, and re-layouts  4.62 us (3%)
    psum x1, blocking collectives, on_device(): lax.psum(jnp.sum(values * values, axis=1, keepdims=True), 'tensor')  33.4 us
    ppermute x2, waiting for transfers between devices, from_behind(): return lax.ppermute(block, axis, route)  28.8 us
    psum x2, blocking collectives, on_device(): lax.psum(jnp.sum(scaled * normed_c, axis=1, keepdims=True), 'tensor')  28.4 us
    dot_general x2, matrix products, on_device(): lax.dot_general(block, weight, (((1,), (1,)), ((), ())), preferred_elemen...  14.5 us
    dot_general x4, matrix products, term(): lax.dot_general(h, blk, (((0,), (0,)), ((), ())), preferred_element_type=...  13.5 us
    psum x1, blocking collectives, on_device(): gain_total = lax.psum(gain_part, 'dp')  10.9 us
    ppermute x5, starting transfers between devices, shifted(): return lax.ppermute(block, axis, [(i, (i + shift) % n) for i in range(n)])  9.28 us
    convert_element_type x2, other arithmetic, on_device(): input_grad = (grad_out[lo:lo + step].astype(jnp.float32) + rstd[lo:lo + s...  8.09 us
  transfers between devices with their start and end apart: 10, of which 2 were waited for; matrix products, arithmetic and copies ran while one was open for 28% of the time, Pallas kernels for 0%

profile of v2, /device:TPU:0, one launch (start us, length us, event | category | flops | bytes accessed | tf_op | source)
XLA Modules:
  0.0 165.5 jit_solution(766013093374667887)
XLA Ops:
  0.6 3.1 %collective-permute-start = (bf16[512,512]{1,0:T(8,128)(2,1)}, bf16[512,512]{1,0:T(8,128)(2,1)}, u32[]{:S(2)}, u32[]{:S(2)}) collective-permute-start(bf16[512,512]{1,0:T(8,128)(2,1)} %bitcast.42), channel_id=1, source_target_pairs={{0,1},{1,2},{2,3},{3,0},{4,5},{5,6},{6,7},{7,4},{8,9},{9,10},{10,1... | collective-permute-start | bytes 1572872 | tf_op jit(solution)/shard_map/ppermute | solution.py:18
  3.7 2.6 %collective-permute-start.1 = (bf16[512,512]{1,0:T(8,128)(2,1)}, bf16[512,512]{1,0:T(8,128)(2,1)}, u32[]{:S(2)}, u32[]{:S(2)}) collective-permute-start(bf16[512,512]{1,0:T(8,128)(2,1)} %bitcast.43), channel_id=1, source_target_pairs={{0,2},{1,3},{2,0},{3,1},{4,6},{5,7},{6,4},{7,5},{8,10},{9,11},{10,... | collective-permute-start | bytes 1572872 | tf_op jit(solution)/shard_map/ppermute | solution.py:18
  6.3 1.3 collective-permute-start.2
  8.4 2.1 %fusion.4 = f32[512]{0:T(512)S(1)} fusion(bf16[1,1,512,2048]{3,2,1,0:T(8,128)(2,1)} %param.5), kind=kLoop, calls=%fused_computation.6 | loop fusion | flops 3145216 | bytes 2099200 | tf_op jit(solution)/shard_map/reduce_sum | solution.py:53
  10.4 33.4 %psum.28 = f32[512,1]{0,1:T(1,128)S(1)} all-reduce(f32[512,1]{0,1:T(1,128)S(1)} %bitcast.52), channel_id=1, replica_groups=mesh['dp'=4,'pipe'=2,'tensor'=4] {'tensor'}, use_global_device_ids=true, to_apply=%region_1.0 | all-reduce | flops 512 | bytes 4096 | tf_op jit(solution)/shard_map/psum | solution.py:53
  43.8 3.3 %multiply_convert_fusion = (bf16[512,2048]{1,0:T(8,128)(2,1)}, f32[512,2048]{1,0:T(8,128)}) fusion(f32[2048]{0:T(1024)S(1)} %bitcast.45, f32[512]{0:T(512)S(1)} %bitcast.51, bf16[1,1,512,2048]{3,2,1,0:T(8,128)(2,1)S(1)} %copy-done.2), kind=kLoop, calls=%fused_computation.8 | loop fusion | flops 4194304 | bytes 8398848 | tf_op jit(solution)/shard_map/convert_element_type | solution.py:56
  47.1 1.5 collective-permute-start.8
  48.9 1.3 constant_dynamic-update-slice_fusion.2
  51.4 7.3 %multiply_reduce_fusion.1 = (f32[2048]{0:T(1024)S(1)}, f32[256]{0:T(256)S(1)}, f32[256,2048]{1,0:T(8,128)}) fusion(f32[512,2048]{1,0:T(8,128)S(1)} %copy-done, f32[2048]{0:T(1024)S(1)} %bitcast.46, bf16[1,2048,2048]{2,1,0:T(8,128)(2,1)} %param.9, bf16[512,2048]{1,0:T(8,128)(2,1)S(1)} %constant_dynamic-update-slice_fusion), kind=kOutput, calls=%fused_computation.16 | convolution fusion | flops 2150102784 | bytes 13648896 | tf_op jit(solution)/shard_map/dot_general | solution.py:85
  58.7 20.1 %psum.29 = f32[256,1]{0,1:T(1,128)S(1)} all-reduce(f32[256,1]{0,1:T(1,128)S(1)} %bitcast.58), channel_id=1, replica_groups=mesh['dp'=4,'pipe'=2,'tensor'=4] {'tensor'}, use_global_device_ids=true, to_apply=%region_3.4 | all-reduce | flops 256 | bytes 2048 | tf_op jit(solution)/shard_map/psum | solution.py:91
  78.8 4.0 %fusion.7 = bf16[256,2048]{1,0:T(8,128)(2,1)} fusion(f32[256,2048]{1,0:T(8,128)} %get-tuple-element.18, f32[512,2048]{1,0:T(8,128)} %get-tuple-element.12, f32[256]{0:T(256)S(1)} %bitcast.54, f32[2048]{0:T(1024)S(1)} %bitcast.47, f32[256]{0:T(256)S(1)} %bitcast.56, bf16[1,1,512,2048]{3,2,1,0:T(8,128)(2,1)} %param.6), kind=kLoop, calls=%fused_computation.14 | loop fusion | flops 3670016 | bytes 6301696 | tf_op jit(solution)/shard_map/convert_element_type | solution.py:95
  85.5 7.3 %multiply_reduce_fusion = (f32[2048]{0:T(1024)S(1)}, f32[256]{0:T(256)S(1)}, f32[256,2048]{1,0:T(8,128)}) fusion(f32[512,2048]{1,0:T(8,128)S(1)} %copy-done.1, f32[2048]{0:T(1024)S(1)} %bitcast.48, bf16[256,2048]{1,0:T(8,128)(2,1)S(1)} %slice.54, bf16[1,2048,2048]{2,1,0:T(8,128)(2,1)} %param.9), kind=kOutput, calls=%fused_computation.15 | convolution fusion | flops 2150102784 | bytes 13648896 | tf_op jit(solution)/shard_map/dot_general | solution.py:85
  92.8 8.3 %psum.30 = f32[256,1]{0,1:T(1,128)S(1)} all-reduce(f32[256,1]{0,1:T(1,128)S(1)} %bitcast.57), channel_id=1, replica_groups=mesh['dp'=4,'pipe'=2,'tensor'=4] {'tensor'}, use_global_device_ids=true, to_apply=%region_5.6 | all-reduce | flops 256 | bytes 2048 | tf_op jit(solution)/shard_map/psum | solution.py:91
  101.1 4.0 %fusion.6 = bf16[256,2048]{1,0:T(8,128)(2,1)} fusion(f32[256,2048]{1,0:T(8,128)} %get-tuple-element.19, f32[512,2048]{1,0:T(8,128)} %get-tuple-element.12, f32[256]{0:T(256)S(1)} %bitcast.53, f32[256]{0:T(256)S(1)} %bitcast.55, bf16[1,1,512,2048]{3,2,1,0:T(8,128)(2,1)} %param.6, f32[2048]{0:T(1024)S(1)} %bitcast.49), kind=kLoop, calls=%fused_computation.12 | loop fusion | flops 3670016 | bytes 6301696 | tf_op jit(solution)/shard_map/convert_element_type | solution.py:95
  105.2 1.3 collective-permute-start.4
  106.5 1.3 collective-permute-start.3
  107.9 10.9 %psum.31 = f32[1,2048]{1,0:T(1,128)} all-reduce(f32[1,2048]{1,0:T(1,128)S(1)} %bitcast.50), channel_id=1, replica_groups=mesh['dp'=4,'pipe'=2,'tensor'=4] {'dp'}, use_global_device_ids=true, to_apply=%region_8.9 | all-reduce | flops 2048 | bytes 16384 | tf_op jit(solution)/shard_map/psum | solution.py:103
  120.1 2.9 %fusion.14 = f32[2048,512]{1,0:T(8,128)S(1)} fusion(bf16[512,2048]{1,0:T(8,128)(2,1)} %get-tuple-element.6, bf16[512,2048]{1,0:T(8,128)(2,1)S(1)} %constant_dynamic-update-slice_fusion, s32[]{:T(128)S(6)} %select_n.50), kind=kOutput, calls=%fused_computation.27 | convolution fusion | flops 1073741824 | bytes 6815748 | tf_op jit(solution)/shard_map/dot_general | solution.py:108
  123.0 10.5 %collective-permute-done.4 = bf16[256,2048]{1,0:T(8,128)(2,1)} collective-permute-done((bf16[256,2048]{1,0:T(8,128)(2,1)}, bf16[256,2048]{1,0:T(8,128)(2,1)}, u32[]{:S(2)}, u32[]{:S(2)}) %collective-permute-start.4) | collective-permute-done | bytes 1048608 | tf_op jit(solution)/shard_map/ppermute | solution.py:13
  133.5 18.3 %collective-permute-done.3 = bf16[256,2048]{1,0:T(8,128)(2,1)} collective-permute-done((bf16[256,2048]{1,0:T(8,128)(2,1)}, bf16[256,2048]{1,0:T(8,128)(2,1)}, u32[]{:S(2)}, u32[]{:S(2)}) %collective-permute-start.3) | collective-permute-done | bytes 1048608 | tf_op jit(solution)/shard_map/ppermute | solution.py:13
  151.8 3.1 %maximum_bitcast_fusion = bf16[1,1,512,2048]{3,2,1,0:T(8,128)(2,1)} fusion(bf16[256,2048]{1,0:T(8,128)(2,1)} %collective-permute-done.4, bf16[256,2048]{1,0:T(8,128)(2,1)} %collective-permute-done.3), kind=kLoop, calls=%fused_computation.10 | loop fusion | flops 4194304 | bytes 4194304 | tf_op jit(solution)/shard_map/broadcast_in_dim | solution.py:116
  154.9 3.0 %fusion.10 = f32[2048,512]{1,0:T(8,128)S(1)} fusion(bf16[512,2048]{1,0:T(8,128)(2,1)} %collective-permute-done.8, bf16[512,1024]{1,0:T(8,128)(2,1)} %collective-permute-done.6), kind=kOutput, calls=%fused_computation.23 | convolution fusion | flops 1073741824 | bytes 6815744 | tf_op jit(solution)/shard_map/dot_general | solution.py:108
  157.9 2.9 %fusion.12 = f32[2048,512]{1,0:T(8,128)S(1)} fusion(bf16[512,2048]{1,0:T(8,128)(2,1)} %collective-permute-done.5, bf16[512,1024]{1,0:T(8,128)(2,1)S(1)} %collective-permute-done.7), kind=kOutput, calls=%fused_computation.25 | convolution fusion | flops 1073741824 | bytes 6815744 | tf_op jit(solution)/shard_map/dot_general | solution.py:108
  160.8 4.7 %fusion.5 = bf16[1,2048,512]{2,1,0:T(8,128)(2,1)} fusion(bf16[512,2048]{1,0:T(8,128)(2,1)} %collective-permute-done.9, f32[2048,512]{1,0:T(8,128)S(1)} %fusion.10, f32[2048,512]{1,0:T(8,128)S(1)} %fusion.14, f32[2048,512]{1,0:T(8,128)S(1)} %fusion.12, bf16[512,1024]{1,0:T(8,128)(2,1)S(1)} %collective-permute-done.7), kind=kOutput, calls=%fused_computation.9 | convolution fusion | flops 1077936128 | bytes 17301504 | tf_op jit(solution)/shard_map/dot_general | solution.py:108
  (35 shorter events, 6.3 us)
Async XLA Ops:
  0.6 43.2 %copy-start.2 = (bf16[1,1,512,2048]{3,2,1,0:T(8,128)(2,1)S(1)}, bf16[1,1,512,2048]{3,2,1,0:T(8,128)(2,1)}, u32[]{:S(2)}) copy-start(bf16[1,1,512,2048]{3,2,1,0:T(8,128)(2,1)} %param.5) | copy-start | bytes 6291460
  0.6 48.3 %collective-permute-start = (bf16[512,512]{1,0:T(8,128)(2,1)}, bf16[512,512]{1,0:T(8,128)(2,1)}, u32[]{:S(2)}, u32[]{:S(2)}) collective-permute-start(bf16[512,512]{1,0:T(8,128)(2,1)} %bitcast.42), channel_id=1, source_target_pairs={{0,1},{1,2},{2,3},{3,0},{4,5},{5,6},{6,7},{7,4},{8,9},{9,10},{10,1... | collective-permute-start | bytes 1572872 | tf_op jit(solution)/shard_map/ppermute | solution.py:18
  3.7 46.5 %collective-permute-start.1 = (bf16[512,512]{1,0:T(8,128)(2,1)}, bf16[512,512]{1,0:T(8,128)(2,1)}, u32[]{:S(2)}, u32[]{:S(2)}) collective-permute-start(bf16[512,512]{1,0:T(8,128)(2,1)} %bitcast.43), channel_id=1, source_target_pairs={{0,2},{1,3},{2,0},{3,1},{4,6},{5,7},{6,4},{7,5},{8,10},{9,11},{10,... | collective-permute-start | bytes 1572872 | tf_op jit(solution)/shard_map/ppermute | solution.py:18
  6.3 45.0 %collective-permute-start.2 = (bf16[512,512]{1,0:T(8,128)(2,1)}, bf16[512,512]{1,0:T(8,128)(2,1)S(1)}, u32[]{:S(2)}, u32[]{:S(2)}) collective-permute-start(bf16[512,512]{1,0:T(8,128)(2,1)} %bitcast.44), channel_id=1, source_target_pairs={{0,3},{1,0},{2,1},{3,2},{4,7},{5,4},{6,5},{7,6},{8,11},{9,8},{10,9... | collective-permute-start | bytes 1572872 | tf_op jit(solution)/shard_map/ppermute | solution.py:18
  47.1 1.8 %copy-start.3 = (bf16[1,1,512,512]{3,2,1,0:T(8,128)(2,1)S(1)}, bf16[1,1,512,512]{3,2,1,0:T(8,128)(2,1)}, u32[]{:S(2)}) copy-start(bf16[1,1,512,512]{3,2,1,0:T(8,128)(2,1)} %param.7) | copy-start | bytes 1572868
  47.1 60.7 %collective-permute-start.8 = (bf16[512,2048]{1,0:T(8,128)(2,1)}, bf16[512,2048]{1,0:T(8,128)(2,1)}, u32[]{:S(2)}, u32[]{:S(2)}) collective-permute-start(bf16[512,2048]{1,0:T(8,128)(2,1)} %get-tuple-element.6), channel_id=1, source_target_pairs={{0,16},{8,24},{16,0},{24,8},{1,17},{9,25},{17,1},{25,9},{2,18},{10... | collective-permute-start | bytes 6291464 | tf_op jit(solution)/shard_map/ppermute | solution.py:18
  48.6 109.3 %collective-permute-start.5 = (bf16[512,2048]{1,0:T(8,128)(2,1)}, bf16[512,2048]{1,0:T(8,128)(2,1)}, u32[]{:S(2)}, u32[]{:S(2)}) collective-permute-start(bf16[512,2048]{1,0:T(8,128)(2,1)} %get-tuple-element.6), channel_id=1, source_target_pairs={{0,8},{8,0},{16,24},{24,16},{1,9},{9,1},{17,25},{25,17},{2,10},{10... | collective-permute-start | bytes 6291464 | tf_op jit(solution)/shard_map/ppermute | solution.py:23
  48.8 2.6 %copy-start = (f32[512,2048]{1,0:T(8,128)S(1)}, f32[512,2048]{1,0:T(8,128)}, u32[]{:S(2)}) copy-start(f32[512,2048]{1,0:T(8,128)} %get-tuple-element.12) | copy-start | bytes 12582916
  83.0 2.6 %copy-start.1 = (f32[512,2048]{1,0:T(8,128)S(1)}, f32[512,2048]{1,0:T(8,128)}, u32[]{:S(2)}) copy-start(f32[512,2048]{1,0:T(8,128)} %get-tuple-element.12) | copy-start | bytes 12582916
  84.3 34.5 %collective-permute-start.6 = (bf16[512,1024]{1,0:T(8,128)(2,1)}, bf16[512,1024]{1,0:T(8,128)(2,1)}, u32[]{:S(2)}, u32[]{:S(2)}) collective-permute-start(bf16[512,1024]{1,0:T(8,128)(2,1)} %pad_maximum_fusion), channel_id=1, source_target_pairs={{0,16},{8,24},{16,0},{24,8},{1,17},{9,25},{17,1},{25,9},{2,18},{10... | collective-permute-start | bytes 3145736 | tf_op jit(solution)/shard_map/ppermute | solution.py:18
  105.2 28.3 %collective-permute-start.4 = (bf16[256,2048]{1,0:T(8,128)(2,1)}, bf16[256,2048]{1,0:T(8,128)(2,1)}, u32[]{:S(2)}, u32[]{:S(2)}) collective-permute-start(bf16[256,2048]{1,0:T(8,128)(2,1)} %fusion.6), channel_id=1, source_target_pairs={{4,0},{5,1},{6,2},{7,3},{12,8},{13,9},{14,10},{15,11},{20,16},{21,... | collective-permute-start | bytes 3145736 | tf_op jit(solution)/shard_map/ppermute | solution.py:13
  106.5 45.3 %collective-permute-start.3 = (bf16[256,2048]{1,0:T(8,128)(2,1)}, bf16[256,2048]{1,0:T(8,128)(2,1)}, u32[]{:S(2)}, u32[]{:S(2)}) collective-permute-start(bf16[256,2048]{1,0:T(8,128)(2,1)} %fusion.7), channel_id=1, source_target_pairs={{4,0},{5,1},{6,2},{7,3},{12,8},{13,9},{14,10},{15,11},{20,16},{21,... | collective-permute-start | bytes 3145736 | tf_op jit(solution)/shard_map/ppermute | solution.py:13
  107.8 53.0 %collective-permute-start.9 = (bf16[512,2048]{1,0:T(8,128)(2,1)}, bf16[512,2048]{1,0:T(8,128)(2,1)}, u32[]{:S(2)}, u32[]{:S(2)}) collective-permute-start(bf16[512,2048]{1,0:T(8,128)(2,1)} %collective-permute-done.8), channel_id=1, source_target_pairs={{0,8},{8,0},{16,24},{24,16},{1,9},{9,1},{17,25},{25,17},{2,10},{10... | collective-permute-start | bytes 6291464 | tf_op jit(solution)/shard_map/ppermute | solution.py:23
  120.0 37.9 %collective-permute-start.7 = (bf16[512,1024]{1,0:T(8,128)(2,1)S(1)}, bf16[512,1024]{1,0:T(8,128)(2,1)S(1)}, u32[]{:S(2)}, u32[]{:S(2)}) collective-permute-start(bf16[512,1024]{1,0:T(8,128)(2,1)S(1)} %pad_maximum_fusion.1), channel_id=1, source_target_pairs={{0,8},{8,0},{16,24},{24,16},{1,9},{9,1},{17,25},{25,17},{2,10},{10... | collective-permute-start | bytes 3145736 | tf_op jit(solution)/shard_map/ppermute | solution.py:23

commit v3 on v2

v3 whole, which is shorter than its diff:
```python
import jax
import jax.numpy as jnp
from jax import lax
from jax.sharding import PartitionSpec as P

EPS = 1e-05
CHUNKS = 2


def from_behind(block, axis, distance):
    devices = range(lax.axis_size(axis))
    route = [(i - distance, i) for i in devices if i - distance in devices]
    return lax.ppermute(block, axis, route)


def shifted(block, axis, shift):
    n = lax.axis_size(axis)
    return lax.ppermute(block, axis, [(i, (i + shift) % n) for i in range(n)])


def to_partner(block):
    n = lax.axis_size("dp")
    return lax.ppermute(block, "dp", [(i, i ^ 1) for i in range(n)])


def place(parts, axis):
    n = lax.axis_size(axis)
    me = lax.axis_index(axis)
    out = jnp.zeros((n,) + parts[0].shape, parts[0].dtype)
    for d, p in enumerate(parts):
        out = lax.dynamic_update_slice_in_dim(out, p[None], (me - d) % n, axis=0)
    return out


def summed(part, axis):
    n = lax.axis_size(axis)
    parts = [part] + [shifted(part, axis, d) for d in range(1, n)]
    return jnp.sum(place(parts, axis), axis=0)


def on_device(layer_input, output_grad, kv_grad, norm_gain, kv_weight):
    rows = layer_input[0, 0]
    grad_out = output_grad[0, 0]
    grad_kv = kv_grad[0, 0]
    gain_f = norm_gain[0].astype(jnp.float32)
    weight = kv_weight[0]
    seq, d_local = rows.shape
    n_t = lax.axis_size("tensor")
    d_model = d_local * n_t
    n_dp = lax.axis_size("dp")
    me = lax.axis_index("dp")
    width = grad_kv.shape[1]
    kv_block = width * n_t // n_dp
    shifts = [2 * d for d in range(1, n_dp // 2)]

    rows_outer = [shifted(rows, "dp", s) for s in shifts]
    rows_partner = to_partner(rows)
    rows_partner_outer = [to_partner(r) for r in rows_outer]

    values = rows.astype(jnp.float32)
    squares = jnp.sum(values * values, axis=1)

    t_me = lax.axis_index("tensor")
    piece = jnp.zeros((seq, width * n_t), grad_kv.dtype)
    piece = lax.dynamic_update_slice(piece, grad_kv, (0, t_me * width))
    square_parts = [squares]
    for d in range(1, n_t):
        blk, sq = shifted((grad_kv, squares), "tensor", d)
        piece = lax.dynamic_update_slice(piece, blk, (0, ((t_me - d) % n_t) * width))
        square_parts.append(sq)
    total_squares = jnp.sum(place(square_parts, "tensor"), axis=0)
    rstd = lax.rsqrt(total_squares / d_model + EPS)[:, None]
    normed = values * rstd

    def kv_cols(owner):
        return lax.dynamic_slice_in_dim(piece, owner * kv_block, kv_block, axis=1)

    kv_outer, rstd_outer = [], []
    for s in shifts:
        dest = (me + s) % n_dp
        pair = jnp.concatenate([kv_cols(dest), kv_cols(dest ^ 1)], axis=1)
        got_kv, got_rstd = shifted((pair, rstd), "dp", s)
        kv_outer.append(got_kv)
        rstd_outer.append(got_rstd)
    send_kv = jnp.concatenate([kv_cols(me ^ 1)] + [o[:, kv_block:] for o in kv_outer], axis=1)
    send_rstd = jnp.concatenate([rstd] + rstd_outer, axis=1)
    kv_partner_all, rstd_partner_all = to_partner((send_kv, send_rstd))

    step = seq // CHUNKS
    inputs_grad = []
    sent = []
    gain_part = jnp.zeros((d_local,), jnp.float32)
    block = piece[:step]
    for c in range(CHUNKS):
        lo = c * step
        row_total = lax.dot_general(
            block, weight, (((1,), (1,)), ((), ())), preferred_element_type=jnp.float32
        )
        normed_c = normed[lo:lo + step]
        scaled = gain_f * row_total
        mean_term = summed(jnp.sum(scaled * normed_c, axis=1), "tensor")[:, None] / d_model
        input_grad = (
            grad_out[lo:lo + step].astype(jnp.float32)
            + rstd[lo:lo + step] * (scaled - normed_c * mean_term)
        ).astype(jnp.bfloat16)
        inputs_grad.append(from_behind(input_grad, "pipe", -1))
        sent.append(input_grad)
        gain_part = gain_part + jnp.sum(row_total * normed_c, axis=0)
        if c + 1 < CHUNKS:
            _, block = lax.optimization_barrier((input_grad, piece[lo + step:lo + 2 * step]))

    upstream = jnp.concatenate(inputs_grad, axis=0)
    gain_total = summed(gain_part, "dp")

    _, rows_own = lax.optimization_barrier((sent, rows))

    def term(x, r, blk):
        h = ((x.astype(jnp.float32) * r) * gain_f).astype(jnp.bfloat16)
        return lax.dot_general(h, blk, (((0,), (0,)), ((), ())), preferred_element_type=jnp.float32)

    wgrad = term(rows_own, rstd, kv_cols(me))
    wgrad = wgrad + term(rows_partner, rstd_partner_all[:, :1], kv_partner_all[:, :kv_block])
    for k in range(len(shifts)):
        wgrad = wgrad + term(rows_outer[k], rstd_outer[k], kv_outer[k][:, :kv_block])
        wgrad = wgrad + term(
            rows_partner_outer[k],
            rstd_partner_all[:, k + 1:k + 2],
            kv_partner_all[:, (k + 1) * kv_block:(k + 2) * kv_block],
        )
    weight_total = wgrad.astype(jnp.bfloat16)
    return (upstream[None, None], weight_total[None], gain_total[None])


def solution(mesh):
    in_specs = (
        P("dp", "pipe", None, "tensor"),
        P("dp", "pipe", None, "tensor"),
        P("dp", "pipe", None, "tensor"),
        P("pipe", "tensor"),
        P("pipe", "tensor", None),
    )
    out_specs = (P("dp", "pipe", None, "tensor"), P("pipe", "tensor", "dp"), P("pipe", "tensor"))
    return jax.shard_map(
        on_device, mesh=mesh, in_specs=in_specs, out_specs=out_specs, check_vma=False
    )
```

time: 166 us -> 164 us (0.988)
  blocking collectives: 72.7 us -> 0 us
  waiting for transfers between devices: 28.8 us -> 78.6 us
  starting transfers between devices: 12 us -> 30.4 us
  local copies, waits for them, and re-layouts: 4.62 us -> 6.75 us
    psum x4 -> x0, blocking collectives: 72.7 us -> none  [the longest x1 33.4 us: on_device(): lax.psum(jnp.sum(values * values, axis=1, keepdims=True), 'tensor')]
    ppermute x5 -> x18, waiting for transfers between devices: 0.01 us -> 62.6 us  [shifted(): return lax.ppermute(block, axis, [(i, (i + shift) % n) for i in range(n)])]
    ppermute x5 -> x18, starting transfers between devices: 9.28 us -> 26.5 us  [shifted(): return lax.ppermute(block, axis, [(i, (i + shift) % n) for i in range(n)])]
    ppermute x2, waiting for transfers between devices: 28.8 us -> 16 us  [from_behind(): return lax.ppermute(block, axis, route)]
    dot_general x2, matrix products: 14.5 us -> 11.2 us  [on_device(): lax.dot_general(block, weight, (((1,), (1,)), ((), ())), preferred_elemen...]
    convert_element_type x1 -> x0, other arithmetic: 3.25 us -> none  [on_device(): hidden = (normed * gain_f).astype(jnp.bfloat16)]
    dot_general x4, matrix products: 13.5 us -> 15.9 us  [term(): lax.dot_general(h, blk, (((0,), (0,)), ((), ())), preferred_element_type=...]
    mul x0 -> x1, other arithmetic: none -> 2.08 us  [on_device(): normed = values * rstd]
  transfers between devices with their start and end apart: 10 -> 24, of which waited for: 2 -> 10; matrix products, arithmetic and copies ran while one was open for 28% -> 29% of each run, Pallas kernels for 0% -> 0%
where the time goes in v3:
time: 164 us; the launch traced here: 162 us
  waiting for transfers between devices  78.6 us (48%)
  starting transfers between devices  30.4 us (19%)
  matrix products  27.1 us (17%)
  other arithmetic  18.5 us (11%)
  local copies, waits for them, and re-layouts  6.75 us (4%)
    ppermute x18, waiting for transfers between devices, shifted(): return lax.ppermute(block, axis, [(i, (i + shift) % n) for i in range(n)])  62.6 us
    ppermute x18, starting transfers between devices, shifted(): return lax.ppermute(block, axis, [(i, (i + shift) % n) for i in range(n)])  26.5 us
    ppermute x2, waiting for transfers between devices, from_behind(): return lax.ppermute(block, axis, route)  16 us
    dot_general x4, matrix products, term(): lax.dot_general(h, blk, (((0,), (0,)), ((), ())), preferred_element_type=...  15.9 us
    dot_general x2, matrix products, on_device(): lax.dot_general(block, weight, (((1,), (1,)), ((), ())), preferred_elemen...  11.2 us
    convert_element_type x2, other arithmetic, on_device(): input_grad = (grad_out[lo:lo + step].astype(jnp.float32) + rstd[lo:lo + s...  8.26 us
  transfers between devices with their start and end apart: 24, of which 10 were waited for; matrix products, arithmetic and copies ran while one was open for 29% of the time, Pallas kernels for 0%

profile of v3, /device:TPU:0, one launch (start us, length us, event | category | flops | bytes accessed | tf_op | source)
XLA Modules:
  0.0 162.5 jit_solution(14563421027894792772)
XLA Ops:
  0.6 3.1 %collective-permute-start.3 = (bf16[512,512]{1,0:T(8,128)(2,1)}, bf16[512,512]{1,0:T(8,128)(2,1)}, u32[]{:S(2)}, u32[]{:S(2)}) collective-permute-start(bf16[512,512]{1,0:T(8,128)(2,1)} %bitcast.47), channel_id=1, source_target_pairs={{0,1},{1,2},{2,3},{3,0},{4,5},{5,6},{6,7},{7,4},{8,9},{9,10},{10,1... | collective-permute-start | bytes 1572872 | tf_op jit(solution)/shard_map/ppermute | solution.py:18
  3.7 2.6 %collective-permute-start.4 = (bf16[512,512]{1,0:T(8,128)(2,1)}, bf16[512,512]{1,0:T(8,128)(2,1)S(1)}, u32[]{:S(2)}, u32[]{:S(2)}) collective-permute-start(bf16[512,512]{1,0:T(8,128)(2,1)} %bitcast.48), channel_id=1, source_target_pairs={{0,2},{1,3},{2,0},{3,1},{4,6},{5,7},{6,4},{7,5},{8,10},{9,11},{10,... | collective-permute-start | bytes 1572872 | tf_op jit(solution)/shard_map/ppermute | solution.py:18
  6.3 2.1 %fusion.4 = f32[512]{0:T(512)S(1)} fusion(bf16[1,1,512,2048]{3,2,1,0:T(8,128)(2,1)} %param.5), kind=kLoop, calls=%fused_computation.6 | loop fusion | flops 3145216 | bytes 2099200 | tf_op jit(solution)/shard_map/reduce_sum | solution.py:61
  8.5 1.8 %collective-permute-start.1 = (f32[512]{0:T(512)S(1)}, f32[512]{0:T(512)S(1)}, u32[]{:S(2)}, u32[]{:S(2)}) collective-permute-start(f32[512]{0:T(512)S(1)} %fusion.4), channel_id=1, source_target_pairs={{0,2},{1,3},{2,0},{3,1},{4,6},{5,7},{6,4},{7,5},{8,10},{9,11},{10,... | collective-permute-start | bytes 6152 | tf_op jit(solution)/shard_map/ppermute | solution.py:18
  10.4 1.9 %collective-permute-start.2 = (f32[512]{0:T(512)S(1)}, f32[512]{0:T(512)S(1)}, u32[]{:S(2)}, u32[]{:S(2)}) collective-permute-start(f32[512]{0:T(512)S(1)} %fusion.4), channel_id=1, source_target_pairs={{0,3},{1,0},{2,1},{3,2},{4,7},{5,4},{6,5},{7,6},{8,11},{9,8},{10,9... | collective-permute-start | bytes 6152 | tf_op jit(solution)/shard_map/ppermute | solution.py:18
  12.8 16.5 %collective-permute-done = f32[512]{0:T(512)S(1)} collective-permute-done((f32[512]{0:T(512)S(1)}, f32[512]{0:T(512)S(1)}, u32[]{:S(2)}, u32[]{:S(2)}) %collective-permute-start) | collective-permute-done | bytes 2080 | tf_op jit(solution)/shard_map/ppermute | solution.py:18
  29.3 11.2 %collective-permute-done.1 = f32[512]{0:T(512)S(1)} collective-permute-done((f32[512]{0:T(512)S(1)}, f32[512]{0:T(512)S(1)}, u32[]{:S(2)}, u32[]{:S(2)}) %collective-permute-start.1) | collective-permute-done | bytes 2080 | tf_op jit(solution)/shard_map/ppermute | solution.py:18
  40.7 2.1 %convert_multiply_fusion = f32[512,2048]{1,0:T(8,128)S(1)} fusion(f32[512]{0:T(512)S(1)} %add_rsqrt_fusion, bf16[1,1,512,2048]{3,2,1,0:T(8,128)(2,1)} %param.5), kind=kLoop, calls=%fused_computation.4 | loop fusion | flops 2097152 | bytes 6293504 | tf_op jit(solution)/shard_map/mul | solution.py:73
  44.3 2.1 %collective-permute-done.15 = f32[512,1]{0,1:T(1,128)S(1)} collective-permute-done((f32[512,1]{0,1:T(1,128)S(1)}, f32[512,1]{0,1:T(1,128)S(1)}, u32[]{:S(2)}, u32[]{:S(2)}) %collective-permute-start.15) | collective-permute-done | bytes 2080 | tf_op jit(solution)/shard_map/ppermute | solution.py:18
  49.1 12.6 %collective-permute-done.5 = bf16[512,512]{1,0:T(8,128)(2,1)} collective-permute-done((bf16[512,512]{1,0:T(8,128)(2,1)S(1)}, bf16[512,512]{1,0:T(8,128)(2,1)}, u32[]{:S(2)}, u32[]{:S(2)}) %collective-permute-start.5) | collective-permute-done | bytes 524320 | tf_op jit(solution)/shard_map/ppermute | solution.py:18
  62.9 3.9 %multiply_reduce_fusion.1 = (f32[2048]{0:T(1024)S(1)}, f32[256]{0:T(256)S(1)}, f32[256,2048]{1,0:T(8,128)}) fusion(f32[512,2048]{1,0:T(8,128)S(1)} %convert_multiply_fusion, f32[2048]{0:T(1024)S(1)} %bitcast.50, bf16[1,2048,2048]{2,1,0:T(8,128)(2,1)S(1)} %copy-done.7, bf16[512,2048]{1,0:T(8,128)(2,1)S(1)} %constant_dynamic-update-slice_fusion), kind=kOutput, calls=%fused_computation.23 | convolution fusion | flops 2150102784 | bytes 13648896 | tf_op jit(solution)/shard_map/dot_general | solution.py:96
  66.8 2.1 %collective-permute-start.6 = (f32[256]{0:T(256)S(1)}, f32[256]{0:T(256)S(1)}, u32[]{:S(2)}, u32[]{:S(2)}) collective-permute-start(f32[256]{0:T(256)S(1)} %get-tuple-element.10), channel_id=1, source_target_pairs={{0,1},{1,2},{2,3},{3,0},{4,5},{5,6},{6,7},{7,4},{8,9},{9,10},{10,1... | collective-permute-start | bytes 3080 | tf_op jit(solution)/shard_map/ppermute | solution.py:18
  70.1 2.9 %collective-permute-start.8 = (f32[256]{0:T(256)S(1)}, f32[256]{0:T(256)S(1)}, u32[]{:S(2)}, u32[]{:S(2)}) collective-permute-start(f32[256]{0:T(256)S(1)} %get-tuple-element.10), channel_id=1, source_target_pairs={{0,3},{1,0},{2,1},{3,2},{4,7},{5,4},{6,5},{7,6},{8,11},{9,8},{10,9... | collective-permute-start | bytes 3080 | tf_op jit(solution)/shard_map/ppermute | solution.py:18
  75.3 4.2 %fusion.11 = bf16[256,2048]{1,0:T(8,128)(2,1)} fusion(f32[256,2048]{1,0:T(8,128)} %get-tuple-element.18, f32[512,2048]{1,0:T(8,128)} %copy-done, f32[256]{0:T(256)S(1)} %broadcast_multiply_fusion.1, f32[2048]{0:T(1024)S(1)} %bitcast.51, f32[256]{0:T(256)S(1)} %get-tuple-element.17, bf16[1,1,512,2048]{3,2,1,0:T(8,128)(2,1)} %param.6), kind=kLoop, calls=%fused_computation.21 | loop fusion | flops 3670016 | bytes 6301696 | tf_op jit(solution)/shard_map/convert_element_type | solution.py:105
  79.5 7.3 %multiply_reduce_fusion = (f32[2048]{0:T(1024)S(1)}, f32[256]{0:T(256)S(1)}, f32[256,2048]{1,0:T(8,128)}) fusion(f32[512,2048]{1,0:T(8,128)S(1)} %copy-done.1, f32[2048]{0:T(1024)S(1)} %bitcast.52, bf16[256,2048]{1,0:T(8,128)(2,1)S(1)} %copy-done.4, bf16[1,2048,2048]{2,1,0:T(8,128)(2,1)} %param.9), kind=kOutput, calls=%fused_computation.22 | convolution fusion | flops 2150102784 | bytes 13648896 | tf_op jit(solution)/shard_map/dot_general | solution.py:96
  86.9 3.7 %collective-permute-start.11 = (f32[256]{0:T(256)S(1)}, f32[256]{0:T(256)S(1)}, u32[]{:S(2)}, u32[]{:S(2)}) collective-permute-start(f32[256]{0:T(256)S(1)} %get-tuple-element.8), channel_id=1, source_target_pairs={{0,2},{1,3},{2,0},{3,1},{4,6},{5,7},{6,4},{7,5},{8,10},{9,11},{10,... | collective-permute-start | bytes 3080 | tf_op jit(solution)/shard_map/ppermute | solution.py:18
  94.2 4.0 %fusion.10 = bf16[256,2048]{1,0:T(8,128)(2,1)} fusion(f32[256,2048]{1,0:T(8,128)} %get-tuple-element.19, f32[512,2048]{1,0:T(8,128)} %copy-done, f32[256]{0:T(256)S(1)} %broadcast_multiply_fusion, f32[256]{0:T(256)S(1)} %get-tuple-element.16, bf16[1,1,512,2048]{3,2,1,0:T(8,128)(2,1)} %param.6, f32[2048]{0:T(1024)S(1)} %bitcast.53), kind=kLoop, calls=%fused_computation.19 | loop fusion | flops 3670016 | bytes 6301696 | tf_op jit(solution)/shard_map/convert_element_type | solution.py:105
  99.5 18.4 %collective-permute-done.21 = f32[2048]{0:T(1024)S(1)} collective-permute-done((f32[2048]{0:T(1024)S(1)}, f32[2048]{0:T(1024)S(1)}, u32[]{:S(2)}, u32[]{:S(2)}) %collective-permute-start.21) | collective-permute-done | bytes 8224 | tf_op jit(solution)/shard_map/ppermute | solution.py:18
  126.4 5.0 %fusion.5 = f32[2048,512]{1,0:T(8,128)} fusion(bf16[512,2048]{1,0:T(8,128)(2,1)} %bitcast.1, f32[2048]{0:T(1024)S(1)} %bitcast.54, f32[512]{0:T(512)S(1)} %add_rsqrt_fusion, bf16[512,2048]{1,0:T(8,128)(2,1)S(1)} %constant_dynamic-update-slice_fusion, s32[]{:T(128)S(6)} %select_n.129), kind=kOutput, calls=%fused_computation.12 | convolution fusion | flops 1077936128 | bytes 6825988 | tf_op jit(solution)/shard_map/dot_general | solution.py:119
  132.4 16.0 %collective-permute-done.13 = bf16[256,2048]{1,0:T(8,128)(2,1)} collective-permute-done((bf16[256,2048]{1,0:T(8,128)(2,1)}, bf16[256,2048]{1,0:T(8,128)(2,1)}, u32[]{:S(2)}, u32[]{:S(2)}) %collective-permute-start.13) | collective-permute-done | bytes 1048608 | tf_op jit(solution)/shard_map/ppermute | solution.py:13
  148.4 3.1 %maximum_bitcast_fusion = bf16[1,1,512,2048]{3,2,1,0:T(8,128)(2,1)} fusion(bf16[256,2048]{1,0:T(8,128)(2,1)} %collective-permute-done.13, bf16[256,2048]{1,0:T(8,128)(2,1)} %collective-permute-done.9), kind=kLoop, calls=%fused_computation.17 | loop fusion | flops 4194304 | bytes 4194304 | tf_op jit(solution)/shard_map/broadcast_in_dim | solution.py:131
  151.5 3.1 %fusion.7 = f32[2048,512]{1,0:T(8,128)S(1)} fusion(bf16[512,2048]{1,0:T(8,128)(2,1)} %collective-permute-done.19, f32[512]{0:T(512)S(1)} %bitcast.70, f32[2048]{0:T(1024)S(1)} %bitcast.55, bf16[512,1024]{1,0:T(8,128)(2,1)} %collective-permute-done.17), kind=kOutput, calls=%fused_computation.14 | convolution fusion | flops 1077936128 | bytes 6825984 | tf_op jit(solution)/shard_map/dot_general | solution.py:119
  154.6 3.1 %fusion.6 = f32[2048,512]{1,0:T(8,128)S(1)} fusion(bf16[512,2048]{1,0:T(8,128)(2,1)} %collective-permute-done.14, f32[512]{0:T(512)S(1)} %bitcast.71, f32[2048]{0:T(1024)S(1)} %bitcast.56, bf16[512,1024]{1,0:T(8,128)(2,1)S(1)} %collective-permute-done.18), kind=kOutput, calls=%fused_computation.13 | convolution fusion | flops 1077936128 | bytes 6825984 | tf_op jit(solution)/shard_map/dot_general | solution.py:119
  157.8 4.7 %fusion.9 = bf16[1,2048,512]{2,1,0:T(8,128)(2,1)} fusion(bf16[512,2048]{1,0:T(8,128)(2,1)} %collective-permute-done.20, f32[2048,512]{1,0:T(8,128)S(1)} %fusion.7, f32[2048,512]{1,0:T(8,128)S(1)} %copy-done.2, f32[2048,512]{1,0:T(8,128)S(1)} %fusion.6, f32[512]{0:T(512)S(1)} %bitcast.62, f32[2048]{0:T(1024)S(1)} %bitcast.57, ...), kind=kOutput, calls=%fused_computation.16 | convolution fusion | flops 1082130432 | bytes 17311744 | tf_op jit(solution)/shard_map/dot_general | solution.py:119
  (93 shorter events, 23.8 us)
Async XLA Ops:
  0.6 47.3 %collective-permute-start.3 = (bf16[512,512]{1,0:T(8,128)(2,1)}, bf16[512,512]{1,0:T(8,128)(2,1)}, u32[]{:S(2)}, u32[]{:S(2)}) collective-permute-start(bf16[512,512]{1,0:T(8,128)(2,1)} %bitcast.47), channel_id=1, source_target_pairs={{0,1},{1,2},{2,3},{3,0},{4,5},{5,6},{6,7},{7,4},{8,9},{9,10},{10,1... | collective-permute-start | bytes 1572872 | tf_op jit(solution)/shard_map/ppermute | solution.py:18
  3.7 45.3 %collective-permute-start.4 = (bf16[512,512]{1,0:T(8,128)(2,1)}, bf16[512,512]{1,0:T(8,128)(2,1)S(1)}, u32[]{:S(2)}, u32[]{:S(2)}) collective-permute-start(bf16[512,512]{1,0:T(8,128)(2,1)} %bitcast.48), channel_id=1, source_target_pairs={{0,2},{1,3},{2,0},{3,1},{4,6},{5,7},{6,4},{7,5},{8,10},{9,11},{10,... | collective-permute-start | bytes 1572872 | tf_op jit(solution)/shard_map/ppermute | solution.py:18
  8.4 20.9 %collective-permute-start = (f32[512]{0:T(512)S(1)}, f32[512]{0:T(512)S(1)}, u32[]{:S(2)}, u32[]{:S(2)}) collective-permute-start(f32[512]{0:T(512)S(1)} %fusion.4), channel_id=1, source_target_pairs={{0,1},{1,2},{2,3},{3,0},{4,5},{5,6},{6,7},{7,4},{8,9},{9,10},{10,1... | collective-permute-start | bytes 6152 | tf_op jit(solution)/shard_map/ppermute | solution.py:18
  8.5 32.0 %collective-permute-start.1 = (f32[512]{0:T(512)S(1)}, f32[512]{0:T(512)S(1)}, u32[]{:S(2)}, u32[]{:S(2)}) collective-permute-start(f32[512]{0:T(512)S(1)} %fusion.4), channel_id=1, source_target_pairs={{0,2},{1,3},{2,0},{3,1},{4,6},{5,7},{6,4},{7,5},{8,10},{9,11},{10,... | collective-permute-start | bytes 6152 | tf_op jit(solution)/shard_map/ppermute | solution.py:18
  10.4 30.2 %collective-permute-start.2 = (f32[512]{0:T(512)S(1)}, f32[512]{0:T(512)S(1)}, u32[]{:S(2)}, u32[]{:S(2)}) collective-permute-start(f32[512]{0:T(512)S(1)} %fusion.4), channel_id=1, source_target_pairs={{0,3},{1,0},{2,1},{3,2},{4,7},{5,4},{6,5},{7,6},{8,11},{9,8},{10,9... | collective-permute-start | bytes 6152 | tf_op jit(solution)/shard_map/ppermute | solution.py:18
  29.3 32.5 %collective-permute-start.5 = (bf16[512,512]{1,0:T(8,128)(2,1)S(1)}, bf16[512,512]{1,0:T(8,128)(2,1)}, u32[]{:S(2)}, u32[]{:S(2)}) collective-permute-start(bf16[512,512]{1,0:T(8,128)(2,1)S(1)} %bitcast.49), channel_id=1, source_target_pairs={{0,3},{1,0},{2,1},{3,2},{4,7},{5,4},{6,5},{7,6},{8,11},{9,8},{10,9... | collective-permute-start | bytes 1572872 | tf_op jit(solution)/shard_map/ppermute | solution.py:18
  40.5 114.1 %collective-permute-start.14 = (bf16[512,2048]{1,0:T(8,128)(2,1)}, bf16[512,2048]{1,0:T(8,128)(2,1)}, u32[]{:S(2)}, u32[]{:S(2)}) collective-permute-start(bf16[512,2048]{1,0:T(8,128)(2,1)} %bitcast.1), channel_id=1, source_target_pairs={{0,8},{8,0},{16,24},{24,16},{1,9},{9,1},{17,25},{25,17},{2,10},{10... | collective-permute-start | bytes 6291464 | tf_op jit(solution)/shard_map/ppermute | solution.py:23
  42.8 3.7 %collective-permute-start.15 = (f32[512,1]{0,1:T(1,128)S(1)}, f32[512,1]{0,1:T(1,128)S(1)}, u32[]{:S(2)}, u32[]{:S(2)}) collective-permute-start(f32[512,1]{0,1:T(1,128)S(1)} %bitcast.58), channel_id=1, source_target_pairs={{0,16},{8,24},{16,0},{24,8},{1,17},{9,25},{17,1},{25,9},{2,18},{10... | collective-permute-start | bytes 6152 | tf_op jit(solution)/shard_map/ppermute | solution.py:18
  46.4 72.8 %collective-permute-start.19 = (bf16[512,2048]{1,0:T(8,128)(2,1)}, bf16[512,2048]{1,0:T(8,128)(2,1)}, u32[]{:S(2)}, u32[]{:S(2)}) collective-permute-start(bf16[512,2048]{1,0:T(8,128)(2,1)} %bitcast.1), channel_id=1, source_target_pairs={{0,16},{8,24},{16,0},{24,8},{1,17},{9,25},{17,1},{25,9},{2,18},{10... | collective-permute-start | bytes 6291464 | tf_op jit(solution)/shard_map/ppermute | solution.py:18
  66.8 8.4 %collective-permute-start.6 = (f32[256]{0:T(256)S(1)}, f32[256]{0:T(256)S(1)}, u32[]{:S(2)}, u32[]{:S(2)}) collective-permute-start(f32[256]{0:T(256)S(1)} %get-tuple-element.10), channel_id=1, source_target_pairs={{0,1},{1,2},{2,3},{3,0},{4,5},{5,6},{6,7},{7,4},{8,9},{9,10},{10,1... | collective-permute-start | bytes 3080 | tf_op jit(solution)/shard_map/ppermute | solution.py:18
  68.9 6.3 %collective-permute-start.7 = (f32[256]{0:T(256)S(1)}, f32[256]{0:T(256)S(1)}, u32[]{:S(2)}, u32[]{:S(2)}) collective-permute-start(f32[256]{0:T(256)S(1)} %get-tuple-element.10), channel_id=1, source_target_pairs={{0,2},{1,3},{2,0},{3,1},{4,6},{5,7},{6,4},{7,5},{8,10},{9,11},{10,... | collective-permute-start | bytes 3080 | tf_op jit(solution)/shard_map/ppermute | solution.py:18
  70.1 5.1 %collective-permute-start.8 = (f32[256]{0:T(256)S(1)}, f32[256]{0:T(256)S(1)}, u32[]{:S(2)}, u32[]{:S(2)}) collective-permute-start(f32[256]{0:T(256)S(1)} %get-tuple-element.10), channel_id=1, source_target_pairs={{0,3},{1,0},{2,1},{3,2},{4,7},{5,4},{6,5},{7,6},{8,11},{9,8},{10,9... | collective-permute-start | bytes 3080 | tf_op jit(solution)/shard_map/ppermute | solution.py:18
  86.9 5.4 %collective-permute-start.10 = (f32[256]{0:T(256)S(1)}, f32[256]{0:T(256)S(1)}, u32[]{:S(2)}, u32[]{:S(2)}) collective-permute-start(f32[256]{0:T(256)S(1)} %get-tuple-element.8), channel_id=1, source_target_pairs={{0,1},{1,2},{2,3},{3,0},{4,5},{5,6},{6,7},{7,4},{8,9},{9,10},{10,1... | collective-permute-start | bytes 3080 | tf_op jit(solution)/shard_map/ppermute | solution.py:18
  86.9 5.4 %collective-permute-start.11 = (f32[256]{0:T(256)S(1)}, f32[256]{0:T(256)S(1)}, u32[]{:S(2)}, u32[]{:S(2)}) collective-permute-start(f32[256]{0:T(256)S(1)} %get-tuple-element.8), channel_id=1, source_target_pairs={{0,2},{1,3},{2,0},{3,1},{4,6},{5,7},{6,4},{7,5},{8,10},{9,11},{10,... | collective-permute-start | bytes 3080 | tf_op jit(solution)/shard_map/ppermute | solution.py:18
  90.5 3.6 %collective-permute-start.12 = (f32[256]{0:T(256)S(1)}, f32[256]{0:T(256)S(1)}, u32[]{:S(2)}, u32[]{:S(2)}) collective-permute-start(f32[256]{0:T(256)S(1)} %get-tuple-element.8), channel_id=1, source_target_pairs={{0,3},{1,0},{2,1},{3,2},{4,7},{5,4},{6,5},{7,6},{8,11},{9,8},{10,9... | collective-permute-start | bytes 3080 | tf_op jit(solution)/shard_map/ppermute | solution.py:18
  92.2 6.0 %collective-permute-start.16 = (f32[512,2]{0,1:T(2,128)S(1)}, f32[512,2]{0,1:T(2,128)S(1)}, u32[]{:S(2)}, u32[]{:S(2)}) collective-permute-start(f32[512,2]{0,1:T(2,128)S(1)} %pad_maximum_fusion.2), channel_id=1, source_target_pairs={{0,8},{8,0},{16,24},{24,16},{1,9},{9,1},{17,25},{25,17},{2,10},{10... | collective-permute-start | bytes 12296 | tf_op jit(solution)/shard_map/ppermute | solution.py:23
  92.3 27.1 %collective-permute-start.17 = (bf16[512,1024]{1,0:T(8,128)(2,1)}, bf16[512,1024]{1,0:T(8,128)(2,1)}, u32[]{:S(2)}, u32[]{:S(2)}) collective-permute-start(bf16[512,1024]{1,0:T(8,128)(2,1)} %pad_maximum_fusion), channel_id=1, source_target_pairs={{0,16},{8,24},{16,0},{24,8},{1,17},{9,25},{17,1},{25,9},{2,18},{10... | collective-permute-start | bytes 3145736 | tf_op jit(solution)/shard_map/ppermute | solution.py:18
  94.1 23.8 %collective-permute-start.21 = (f32[2048]{0:T(1024)S(1)}, f32[2048]{0:T(1024)S(1)}, u32[]{:S(2)}, u32[]{:S(2)}) collective-permute-start(f32[2048]{0:T(1024)S(1)} %add.172), channel_id=1, source_target_pairs={{0,8},{8,16},{16,24},{24,0},{1,9},{9,17},{17,25},{25,1},{2,10},{10... | collective-permute-start | bytes 24584 | tf_op jit(solution)/shard_map/ppermute | solution.py:18
  98.2 34.1 %collective-permute-start.9 = (bf16[256,2048]{1,0:T(8,128)(2,1)}, bf16[256,2048]{1,0:T(8,128)(2,1)}, u32[]{:S(2)}, u32[]{:S(2)}) collective-permute-start(bf16[256,2048]{1,0:T(8,128)(2,1)} %fusion.11), channel_id=1, source_target_pairs={{4,0},{5,1},{6,2},{7,3},{12,8},{13,9},{14,10},{15,11},{20,16},{21,... | collective-permute-start | bytes 3145736 | tf_op jit(solution)/shard_map/ppermute | solution.py:13
  117.9 30.5 %collective-permute-start.13 = (bf16[256,2048]{1,0:T(8,128)(2,1)}, bf16[256,2048]{1,0:T(8,128)(2,1)}, u32[]{:S(2)}, u32[]{:S(2)}) collective-permute-start(bf16[256,2048]{1,0:T(8,128)(2,1)} %fusion.10), channel_id=1, source_target_pairs={{4,0},{5,1},{6,2},{7,3},{12,8},{13,9},{14,10},{15,11},{20,16},{21,... | collective-permute-start | bytes 3145736 | tf_op jit(solution)/shard_map/ppermute | solution.py:13
  119.2 38.6 %collective-permute-start.20 = (bf16[512,2048]{1,0:T(8,128)(2,1)}, bf16[512,2048]{1,0:T(8,128)(2,1)}, u32[]{:S(2)}, u32[]{:S(2)}) collective-permute-start(bf16[512,2048]{1,0:T(8,128)(2,1)} %collective-permute-done.19), channel_id=1, source_target_pairs={{0,8},{8,0},{16,24},{24,16},{1,9},{9,1},{17,25},{25,17},{2,10},{10... | collective-permute-start | bytes 6291464 | tf_op jit(solution)/shard_map/ppermute | solution.py:23
  119.4 3.7 %collective-permute-start.22 = (f32[2048]{0:T(1024)S(1)}, f32[2048]{0:T(1024)S(1)}, u32[]{:S(2)}, u32[]{:S(2)}) collective-permute-start(f32[2048]{0:T(1024)S(1)} %add.172), channel_id=1, source_target_pairs={{0,16},{8,24},{16,0},{24,8},{1,17},{9,25},{17,1},{25,9},{2,18},{10... | collective-permute-start | bytes 24584 | tf_op jit(solution)/shard_map/ppermute | solution.py:18
  123.1 2.1 %collective-permute-start.23 = (f32[2048]{0:T(1024)S(1)}, f32[2048]{0:T(1024)S(1)}, u32[]{:S(2)}, u32[]{:S(2)}) collective-permute-start(f32[2048]{0:T(1024)S(1)} %add.172), channel_id=1, source_target_pairs={{0,24},{8,0},{16,8},{24,16},{1,25},{9,1},{17,9},{25,17},{2,26},{10... | collective-permute-start | bytes 24584 | tf_op jit(solution)/shard_map/ppermute | solution.py:18
  125.1 29.4 %collective-permute-start.18 = (bf16[512,1024]{1,0:T(8,128)(2,1)}, bf16[512,1024]{1,0:T(8,128)(2,1)S(1)}, u32[]{:S(2)}, u32[]{:S(2)}) collective-permute-start(bf16[512,1024]{1,0:T(8,128)(2,1)} %pad_maximum_fusion.1), channel_id=1, source_target_pairs={{0,8},{8,0},{16,24},{24,16},{1,9},{9,1},{17,25},{25,17},{2,10},{10... | collective-permute-start | bytes 3145736 | tf_op jit(solution)/shard_map/ppermute | solution.py:23
  (8 other events, 85.2 us)

commit v4 on v2

v4 whole, which is shorter than its diff:
```python
import jax
import jax.numpy as jnp
from jax import lax
from jax.sharding import PartitionSpec as P

EPS = 1e-05
CHUNKS = 2


def from_behind(block, axis, distance):
    devices = range(lax.axis_size(axis))
    route = [(i - distance, i) for i in devices if i - distance in devices]
    return lax.ppermute(block, axis, route)


def shifted(block, axis, shift):
    n = lax.axis_size(axis)
    return lax.ppermute(block, axis, [(i, (i + shift) % n) for i in range(n)])


def to_partner(block):
    n = lax.axis_size("dp")
    return lax.ppermute(block, "dp", [(i, i ^ 1) for i in range(n)])


def on_device(layer_input, output_grad, kv_grad, norm_gain, kv_weight):
    rows = layer_input[0, 0]
    grad_out = output_grad[0, 0]
    grad_kv = kv_grad[0, 0]
    gain_f = norm_gain[0].astype(jnp.float32)
    weight = kv_weight[0]
    seq, d_local = rows.shape
    d_model = d_local * lax.axis_size("tensor")
    n_dp = lax.axis_size("dp")
    me = lax.axis_index("dp")
    parity = me % 2
    kv_block = grad_kv.shape[1] * lax.axis_size("tensor") // n_dp
    groups = n_dp // 2

    values = rows.astype(jnp.float32)
    total_squares = lax.psum(jnp.sum(values * values, axis=1, keepdims=True), "tensor")
    rstd = lax.rsqrt(total_squares / d_model + EPS)
    normed = values * rstd
    hidden = (normed * gain_f).astype(jnp.bfloat16)
    hidden_partner = to_partner(hidden)

    piece = lax.all_gather(grad_kv, "tensor", axis=1, tiled=True)

    def cols_of(p):
        return jnp.concatenate(
            [lax.dynamic_slice_in_dim(piece, (2 * g + p) * kv_block, kv_block, axis=1) for g in range(groups)],
            axis=1,
        )

    cols_partner = to_partner(cols_of(1 - parity))
    cols_own = cols_of(parity)

    step = seq // CHUNKS
    inputs_grad = []
    gain_part = jnp.zeros((d_local,), jnp.float32)
    block = piece[:step]
    weight_total = None
    for c in range(CHUNKS):
        lo = c * step
        row_total = lax.dot_general(
            block, weight, (((1,), (1,)), ((), ())), preferred_element_type=jnp.float32
        )
        normed_c = normed[lo:lo + step]
        scaled = gain_f * row_total
        mean_term = lax.psum(jnp.sum(scaled * normed_c, axis=1, keepdims=True), "tensor") / d_model
        input_grad = (
            grad_out[lo:lo + step].astype(jnp.float32)
            + rstd[lo:lo + step] * (scaled - normed_c * mean_term)
        ).astype(jnp.bfloat16)
        inputs_grad.append(from_behind(input_grad, "pipe", -1))
        gain_part = gain_part + jnp.sum(row_total * normed_c, axis=0)
        if c == 0:
            _, h_own = lax.optimization_barrier((input_grad, hidden))
            pair = lax.dot_general(
                h_own, cols_own, (((0,), (0,)), ((), ())), preferred_element_type=jnp.float32
            ) + lax.dot_general(
                hidden_partner, cols_partner, (((0,), (0,)), ((), ())),
                preferred_element_type=jnp.float32,
            )
            own_g = me // 2
            total = lax.dynamic_slice_in_dim(pair, own_g * kv_block, kv_block, axis=1)
            for d in range(1, groups):
                dest_g = (own_g + d) % groups
                out = lax.dynamic_slice_in_dim(pair, dest_g * kv_block, kv_block, axis=1)
                total = total + shifted(out.astype(jnp.bfloat16), "dp", 2 * d).astype(jnp.float32)
            weight_total = total.astype(jnp.bfloat16)
        if c + 1 < CHUNKS:
            _, block = lax.optimization_barrier((pair, piece[lo + step:lo + 2 * step]))

    upstream = jnp.concatenate(inputs_grad, axis=0)
    gain_total = lax.psum(gain_part, "dp")
    return (upstream[None, None], weight_total[None], gain_total[None])


def solution(mesh):
    in_specs = (
        P("dp", "pipe", None, "tensor"),
        P("dp", "pipe", None, "tensor"),
        P("dp", "pipe", None, "tensor"),
        P("pipe", "tensor"),
        P("pipe", "tensor", None),
    )
    out_specs = (P("dp", "pipe", None, "tensor"), P("pipe", "tensor", "dp"), P("pipe", "tensor"))
    return jax.shard_map(
        on_device, mesh=mesh, in_specs=in_specs, out_specs=out_specs, check_vma=False
    )
```

time: 166 us -> 174 us (1.048)
  between operations: 0.86 us -> 14.2 us
  starting transfers between devices: 12 us -> 4.23 us
  matrix products: 28 us -> 20.6 us
  local copies, waits for them, and re-layouts: 4.62 us -> 7.93 us
  waiting for transfers between devices: 28.8 us -> 31.4 us
  other arithmetic: 18.5 us -> 20.8 us
  blocking collectives: 72.7 us -> 74.7 us
    psum x1, blocking collectives: 10.9 us -> 42.3 us  [on_device(): gain_total = lax.psum(gain_part, 'dp')]
    all_gather x0 -> x1, waiting for transfers between devices: none -> 30.7 us  [on_device(): piece = lax.all_gather(grad_kv, 'tensor', axis=1, tiled=True)]
    ppermute x2, waiting for transfers between devices: 28.8 us -> 0.01 us  [from_behind(): return lax.ppermute(block, axis, route)]
    psum x1, blocking collectives: 33.4 us -> 13.7 us  [on_device(): lax.psum(jnp.sum(values * values, axis=1, keepdims=True), 'tensor')]
    psum x2, blocking collectives: 28.4 us -> 18.7 us  [on_device(): lax.psum(jnp.sum(scaled * normed_c, axis=1, keepdims=True), 'tensor')]
    ppermute x5 -> x1, starting transfers between devices: 9.28 us -> 1.44 us  [shifted(): return lax.ppermute(block, axis, [(i, (i + shift) % n) for i in range(n)])]
    dot_general x2, matrix products: 14.5 us -> 9.92 us  [on_device(): lax.dot_general(block, weight, (((1,), (1,)), ((), ())), preferred_elemen...]
    broadcast_in_dim x1 -> x2, other arithmetic: 3.11 us -> 7.65 us  [on_device(): return (upstream[None, None], weight_total[None], gain_total[None])]
  transfers between devices with their start and end apart: 10 -> 6, of which waited for: 2 -> 1; matrix products, arithmetic and copies ran while one was open for 28% -> 25% of each run, Pallas kernels for 0% -> 0%
where the time goes in v4:
time: 174 us
  blocking collectives  74.7 us (43%)
  waiting for transfers between devices  31.4 us (18%)
  other arithmetic  20.8 us (12%)
  matrix products  20.6 us (12%)
  between operations  14.2 us (8%)
  local copies, waits for them, and re-layouts  7.93 us (5%)
  starting transfers between devices  4.23 us (2%)
    psum x1, blocking collectives, on_device(): gain_total = lax.psum(gain_part, 'dp')  42.3 us
    all_gather x1, waiting for transfers between devices, on_device(): piece = lax.all_gather(grad_kv, 'tensor', axis=1, tiled=True)  30.7 us
    psum x2, blocking collectives, on_device(): lax.psum(jnp.sum(scaled * normed_c, axis=1, keepdims=True), 'tensor')  18.7 us
    psum x1, blocking collectives, on_device(): lax.psum(jnp.sum(values * values, axis=1, keepdims=True), 'tensor')  13.7 us
    dot_general x2, matrix products, on_device(): lax.dot_general(block, weight, (((1,), (1,)), ((), ())), preferred_elemen...  9.92 us
    broadcast_in_dim x2, other arithmetic, on_device(): return (upstream[None, None], weight_total[None], gain_total[None])  7.65 us
    dot_general x1, matrix products, on_device(): lax.dot_general(hidden_partner, cols_partner, (((0,), (0,)), ((), ())), p...  6.44 us
    convert_element_type x2, other arithmetic, on_device(): input_grad = (grad_out[lo:lo + step].astype(jnp.float32) + rstd[lo:lo + s...  5.95 us
  transfers between devices with their start and end apart: 6, of which 1 were waited for; matrix products, arithmetic and copies ran while one was open for 25% of the time, Pallas kernels for 0%

profile of v4, /device:TPU:0, one launch (start us, length us, event | category | flops | bytes accessed | tf_op | source)
XLA Modules:
  0.0 173.8 jit_solution(16684890164002811753)
XLA Ops:
  7.2 0.7 all-gather.3.cloned.1.call-update
  7.9 0.7 mul.143
  8.6 2.1 %fusion.4 = f32[512]{0:T(512)S(1)} fusion(bf16[1,1,512,2048]{3,2,1,0:T(8,128)(2,1)} %param.5), kind=kLoop, calls=%fused_computation.6 | loop fusion | flops 3145216 | bytes 2099200 | tf_op jit(solution)/shard_map/reduce_sum | solution.py:41
  10.7 13.7 %psum.28 = f32[512,1]{0,1:T(1,128)S(1)} all-reduce(f32[512,1]{0,1:T(1,128)S(1)} %bitcast.61), channel_id=1, replica_groups=mesh['dp'=4,'pipe'=2,'tensor'=4] {'tensor'}, use_global_device_ids=true, to_apply=%region_1.2 | all-reduce | flops 512 | bytes 4096 | tf_op jit(solution)/shard_map/psum | solution.py:41
  24.4 3.3 %multiply_convert_fusion = (bf16[512,2048]{1,0:T(8,128)(2,1)}, f32[512,2048]{1,0:T(8,128)}) fusion(f32[2048]{0:T(1024)S(1)} %bitcast.54, f32[512]{0:T(512)S(1)} %bitcast.60, bf16[1,1,512,2048]{3,2,1,0:T(8,128)(2,1)S(1)} %copy-done.3), kind=kLoop, calls=%fused_computation.9 | loop fusion | flops 4194304 | bytes 8398848 | tf_op jit(solution)/shard_map/convert_element_type | solution.py:44
  27.6 30.7 %all-gather.3.cloned.1.call-done = bf16[1,1,512,2048]{3,2,1,0:T(8,128)(2,1)} async-done(((bf16[1,1,512,512]{3,2,1,0:T(8,128)(2,1)}), bf16[1,1,512,2048]{3,2,1,0:T(8,128)(2,1)}) %all-gather.3.cloned.1.call-update) | async-done | bytes 2097168 | tf_op jit(solution)/shard_map/all_gather | solution.py:47
  58.3 2.8 %dynamic-slice_bitcast_fusion.1 = (bf16[512,512]{1,0:T(8,128)(2,1)S(1)}, bf16[512,512]{1,0:T(8,128)(2,1)S(1)}, bf16[512,512]{1,0:T(8,128)(2,1)}, bf16[512,512]{1,0:T(8,128)(2,1)}) fusion(bf16[1,1,512,2048]{3,2,1,0:T(8,128)(2,1)} %all-gather.3.cloned.1.call-done, s32[]{:T(128)S(6)} %select_n.36, s32[]{:T(128)S(6)} %select_n.37, s32[]{:T(128)S(6)} %select_n.35, ...), kind=kLoop, calls=%fused_computation.29 | loop fusion | bytes 4194320 | tf_op jit(solution)/shard_map/dynamic_slice | solution.py:51
  61.1 1.2 pad_maximum_fusion
  62.3 0.8 copy-done.4
  63.1 7.3 %multiply_reduce_fusion.1 = (f32[2048]{0:T(1024)S(1)}, f32[256]{0:T(256)S(1)}, f32[256,2048]{1,0:T(8,128)}) fusion(f32[512,2048]{1,0:T(8,128)S(1)} %copy-done, f32[2048]{0:T(1024)S(1)} %bitcast.55, bf16[1,2048,2048]{2,1,0:T(8,128)(2,1)} %param.9, bf16[1,1,512,2048]{3,2,1,0:T(8,128)(2,1)S(1)} %copy-done.4), kind=kOutput, calls=%fused_computation.18 | convolution fusion | flops 2150102784 | bytes 13648896 | tf_op jit(solution)/shard_map/dot_general | solution.py:65
  70.4 9.4 %psum.29 = f32[256,1]{0,1:T(1,128)S(1)} all-reduce(f32[256,1]{0,1:T(1,128)S(1)} %bitcast.67), channel_id=1, replica_groups=mesh['dp'=4,'pipe'=2,'tensor'=4] {'tensor'}, use_global_device_ids=true, to_apply=%region_3.4 | all-reduce | flops 256 | bytes 2048 | tf_op jit(solution)/shard_map/psum | solution.py:70
  79.8 4.1 %fusion.7 = bf16[256,2048]{1,0:T(8,128)(2,1)} fusion(f32[256,2048]{1,0:T(8,128)} %get-tuple-element.19, f32[512,2048]{1,0:T(8,128)} %get-tuple-element.12, f32[256]{0:T(256)S(1)} %bitcast.63, f32[2048]{0:T(1024)S(1)} %bitcast.56, f32[256]{0:T(256)S(1)} %bitcast.65, bf16[1,1,512,2048]{3,2,1,0:T(8,128)(2,1)} %param.6), kind=kLoop, calls=%fused_computation.16 | loop fusion | flops 3670016 | bytes 6301696 | tf_op jit(solution)/shard_map/convert_element_type | solution.py:74
  84.0 1.5 collective-permute-start
  85.5 4.2 %fusion.8 = f32[2048,1024]{1,0:T(8,128)S(1)} fusion(bf16[512,2048]{1,0:T(8,128)(2,1)} %get-tuple-element.5, bf16[512,512]{1,0:T(8,128)(2,1)S(1)} %copy-done.6, bf16[512,512]{1,0:T(8,128)(2,1)S(1)} %copy-done.7), kind=kOutput, calls=%fused_computation.23 | convolution fusion | flops 2149580800 | bytes 11534336 | tf_op jit(solution)/shard_map/dot_general | solution.py:79
  89.8 6.4 %convolution_add_fusion = f32[2048,1024]{1,0:T(8,128)} fusion(f32[2048,1024]{1,0:T(8,128)S(1)} %fusion.8, bf16[512,2048]{1,0:T(8,128)(2,1)S(1)} %collective-permute-done.1, bf16[512,1024]{1,0:T(8,128)(2,1)S(1)} %collective-permute-done.2), kind=kOutput, calls=%fused_computation.10 | convolution fusion | flops 2149580800 | bytes 19922944 | tf_op jit(solution)/shard_map/dot_general | solution.py:81
  96.5 2.7 %multiply_reduce_fusion = (f32[2048]{0:T(1024)S(1)}, f32[256]{0:T(256)S(1)}, f32[256,2048]{1,0:T(8,128)S(1)}) fusion(f32[512,2048]{1,0:T(8,128)S(1)} %copy-done.1, f32[2048]{0:T(1024)S(1)} %bitcast.57, bf16[256,2048]{1,0:T(8,128)(2,1)S(1)} %slice_bitcast_fusion, bf16[1,2048,2048]{2,1,0:T(8,128)(2,1)S(1)} %bitcast.69), kind=kOutput, calls=%fused_computation.17 | convolution fusion | flops 2150102784 | bytes 13648896 | tf_op jit(solution)/shard_map/dot_general | solution.py:65
  99.2 9.3 %psum.30 = f32[256,1]{0,1:T(1,128)S(1)} all-reduce(f32[256,1]{0,1:T(1,128)S(1)} %bitcast.66), channel_id=1, replica_groups=mesh['dp'=4,'pipe'=2,'tensor'=4] {'tensor'}, use_global_device_ids=true, to_apply=%region_5.6 | all-reduce | flops 256 | bytes 2048 | tf_op jit(solution)/shard_map/psum | solution.py:70
  108.4 3.9 %dynamic-slice_convert_fusion = bf16[2048,512]{1,0:T(8,128)(2,1)} fusion(f32[2048,1024]{1,0:T(8,128)} %convolution_add_fusion, s32[]{:T(128)S(6)} %select_n.41), kind=kLoop, calls=%fused_computation.8 | loop fusion | bytes 4194308 | tf_op jit(solution)/shard_map/convert_element_type | solution.py:90
  112.4 1.4 collective-permute-start.4
  113.8 1.8 %fusion.6 = bf16[256,2048]{1,0:T(8,128)(2,1)S(1)} fusion(f32[256,2048]{1,0:T(8,128)S(1)} %get-tuple-element.20, f32[512,2048]{1,0:T(8,128)S(1)} %copy-done.2, f32[256]{0:T(256)S(1)} %bitcast.62, f32[256]{0:T(256)S(1)} %bitcast.64, bf16[1,1,512,2048]{3,2,1,0:T(8,128)(2,1)} %param.6, f32[2048]{0:T(1024)S(1)} %bitcast.58), kind=kLoop, calls=%fused_computation.14 | loop fusion | flops 3670016 | bytes 6301696 | tf_op jit(solution)/shard_map/convert_element_type | solution.py:74
  115.6 1.3 collective-permute-start.3
  117.0 42.3 %psum.31 = f32[1,2048]{1,0:T(1,128)} all-reduce(f32[1,2048]{1,0:T(1,128)S(1)} %bitcast.59), channel_id=1, replica_groups=mesh['dp'=4,'pipe'=2,'tensor'=4] {'dp'}, use_global_device_ids=true, to_apply=%region_8.9 | all-reduce | flops 2048 | bytes 16384 | tf_op jit(solution)/shard_map/psum | solution.py:96
  159.3 2.8 %maximum_bitcast_fusion = bf16[1,1,512,2048]{3,2,1,0:T(8,128)(2,1)} fusion(bf16[256,2048]{1,0:T(8,128)(2,1)S(1)} %collective-permute-done.3, bf16[256,2048]{1,0:T(8,128)(2,1)} %collective-permute-done), kind=kLoop, calls=%fused_computation.12 | loop fusion | flops 4194304 | bytes 4194304 | tf_op jit(solution)/shard_map/broadcast_in_dim | solution.py:97
  162.1 4.9 %fusion.5 = bf16[1,2048,512]{2,1,0:T(8,128)(2,1)} fusion(bf16[2048,512]{1,0:T(8,128)(2,1)} %collective-permute-done.4, f32[2048,1024]{1,0:T(8,128)} %convolution_add_fusion, s32[]{:T(128)S(6)} %select_n.39), kind=kLoop, calls=%fused_computation.11 | loop fusion | flops 3145728 | bytes 8388612 | tf_op jit(solution)/shard_map/broadcast_in_dim | solution.py:97
  (34 shorter events, 0.4 us)
Async XLA Ops:
  7.2 17.2 %copy-start.3 = (bf16[1,1,512,2048]{3,2,1,0:T(8,128)(2,1)S(1)}, bf16[1,1,512,2048]{3,2,1,0:T(8,128)(2,1)}, u32[]{:S(2)}) copy-start(bf16[1,1,512,2048]{3,2,1,0:T(8,128)(2,1)} %param.5) | copy-start | bytes 6291460
  7.2 51.1 %all-gather.3.cloned.1.call-start = ((), (), s32[]{:S(2)}) async-start(), calls=%async_computation | async-start | bytes 2621440 | tf_op jit(solution)/shard_map/all_gather | solution.py:47
  27.6 62.2 %collective-permute-start.1 = (bf16[512,2048]{1,0:T(8,128)(2,1)}, bf16[512,2048]{1,0:T(8,128)(2,1)S(1)}, u32[]{:S(2)}, u32[]{:S(2)}) collective-permute-start(bf16[512,2048]{1,0:T(8,128)(2,1)} %get-tuple-element.5), channel_id=1, source_target_pairs={{0,8},{8,0},{16,24},{24,16},{1,9},{9,1},{17,25},{25,17},{2,10},{10... | collective-permute-start | bytes 6291464 | tf_op jit(solution)/shard_map/ppermute | solution.py:23
  58.3 4.0 %copy-start = (f32[512,2048]{1,0:T(8,128)S(1)}, f32[512,2048]{1,0:T(8,128)}, u32[]{:S(2)}) copy-start(f32[512,2048]{1,0:T(8,128)} %get-tuple-element.12) | copy-start | bytes 12582916
  61.1 2.0 %copy-start.4 = (bf16[1,1,512,2048]{3,2,1,0:T(8,128)(2,1)S(1)}, bf16[1,1,512,2048]{3,2,1,0:T(8,128)(2,1)}, u32[]{:S(2)}) copy-start(bf16[1,1,512,2048]{3,2,1,0:T(8,128)(2,1)} %all-gather.3.cloned.1.call-done) | copy-start | bytes 6291460
  62.3 27.6 %collective-permute-start.2 = (bf16[512,1024]{1,0:T(8,128)(2,1)}, bf16[512,1024]{1,0:T(8,128)(2,1)S(1)}, u32[]{:S(2)}, u32[]{:S(2)}) collective-permute-start(bf16[512,1024]{1,0:T(8,128)(2,1)} %pad_maximum_fusion), channel_id=1, source_target_pairs={{0,8},{8,0},{16,24},{24,16},{1,9},{9,1},{17,25},{25,17},{2,10},{10... | collective-permute-start | bytes 3145736 | tf_op jit(solution)/shard_map/ppermute | solution.py:23
  79.8 5.6 %copy-start.6 = (bf16[512,512]{1,0:T(8,128)(2,1)S(1)}, bf16[512,512]{1,0:T(8,128)(2,1)}, u32[]{:S(2)}) copy-start(bf16[512,512]{1,0:T(8,128)(2,1)} %get-tuple-element.15) | copy-start | bytes 1572868
  79.8 5.6 %copy-start.7 = (bf16[512,512]{1,0:T(8,128)(2,1)S(1)}, bf16[512,512]{1,0:T(8,128)(2,1)}, u32[]{:S(2)}) copy-start(bf16[512,512]{1,0:T(8,128)(2,1)} %get-tuple-element.16) | copy-start | bytes 1572868
  84.0 75.3 %collective-permute-start = (bf16[256,2048]{1,0:T(8,128)(2,1)}, bf16[256,2048]{1,0:T(8,128)(2,1)}, u32[]{:S(2)}, u32[]{:S(2)}) collective-permute-start(bf16[256,2048]{1,0:T(8,128)(2,1)} %fusion.7), channel_id=1, source_target_pairs={{4,0},{5,1},{6,2},{7,3},{12,8},{13,9},{14,10},{15,11},{20,16},{21,... | collective-permute-start | bytes 3145736 | tf_op jit(solution)/shard_map/ppermute | solution.py:13
  85.4 4.2 %copy-start.5 = (bf16[1,1,512,2048]{3,2,1,0:T(8,128)(2,1)S(1)}, bf16[1,1,512,2048]{3,2,1,0:T(8,128)(2,1)}, u32[]{:S(2)}) copy-start(bf16[1,1,512,2048]{3,2,1,0:T(8,128)(2,1)} %all-gather.3.cloned.1.call-done) | copy-start | bytes 6291460
  89.7 6.6 %slice-start = ((s8[8388608]{0:T(1024)(128)(4,1)}), s8[4194304]{0:T(1024)(128)(4,1)S(1)}, s32[]{:S(2)}) async-start(s8[8388608]{0:T(1024)(128)(4,1)} %bitcast.68), calls=%async_computation.1 | async-start | bytes 8388608
  89.8 6.5 %copy-start.1 = (f32[512,2048]{1,0:T(8,128)S(1)}, f32[512,2048]{1,0:T(8,128)}, u32[]{:S(2)}) copy-start(f32[512,2048]{1,0:T(8,128)} %get-tuple-element.12) | copy-start | bytes 12582916
  89.8 6.7 %slice-start.1 = ((s8[8388608]{0:T(1024)(128)(4,1)}), s8[4194304]{0:T(1024)(128)(4,1)S(1)}, s32[]{:S(2)}) async-start(s8[8388608]{0:T(1024)(128)(4,1)} %bitcast.68), calls=%async_computation.2 | async-start | bytes 8388608
  108.4 5.4 %copy-start.2 = (f32[512,2048]{1,0:T(8,128)S(1)}, f32[512,2048]{1,0:T(8,128)}, u32[]{:S(2)}) copy-start(f32[512,2048]{1,0:T(8,128)} %get-tuple-element.12) | copy-start | bytes 12582916
  112.4 49.7 %collective-permute-start.4 = (bf16[2048,512]{1,0:T(8,128)(2,1)}, bf16[2048,512]{1,0:T(8,128)(2,1)}, u32[]{:S(2)}, u32[]{:S(2)}) collective-permute-start(bf16[2048,512]{1,0:T(8,128)(2,1)} %dynamic-slice_convert_fusion), channel_id=1, source_target_pairs={{0,16},{8,24},{16,0},{24,8},{1,17},{9,25},{17,1},{25,9},{2,18},{10... | collective-permute-start | bytes 6291464 | tf_op jit(solution)/shard_map/ppermute | solution.py:18
  115.6 43.6 %collective-permute-start.3 = (bf16[256,2048]{1,0:T(8,128)(2,1)S(1)}, bf16[256,2048]{1,0:T(8,128)(2,1)S(1)}, u32[]{:S(2)}, u32[]{:S(2)}) collective-permute-start(bf16[256,2048]{1,0:T(8,128)(2,1)S(1)} %fusion.6), channel_id=1, source_target_pairs={{4,0},{5,1},{6,2},{7,3},{12,8},{13,9},{14,10},{15,11},{20,16},{21,... | collective-permute-start | bytes 3145736 | tf_op jit(solution)/shard_map/ppermute | solution.py:13
Sparse Core Ops, SparseCore 0:
  9.6 48.6 all-gather.2

commit v5 on v4

--- a/solution.py
+++ b/solution.py
@@ -56,21 +56,35 @@
     cols_own = cols_of(parity)
 
     step = seq // CHUNKS
-    inputs_grad = []
-    gain_part = jnp.zeros((d_local,), jnp.float32)
+
+    def row_sums(part):
+        wide = jnp.broadcast_to(part[:, None], (part.shape[0], 128))
+        return lax.psum(wide, "tensor")[:, :1]
+
+    rows_total, means = [], []
     block = piece[:step]
-    weight_total = None
     for c in range(CHUNKS):
         lo = c * step
         row_total = lax.dot_general(
             block, weight, (((1,), (1,)), ((), ())), preferred_element_type=jnp.float32
         )
+        scaled = gain_f * row_total
+        means.append(row_sums(jnp.sum(scaled * normed[lo:lo + step], axis=1)) / d_model)
+        rows_total.append(row_total)
+        if c + 1 < CHUNKS:
+            _, block = lax.optimization_barrier((row_total, piece[lo + step:lo + 2 * step]))
+
+    inputs_grad = []
+    gain_part = jnp.zeros((d_local,), jnp.float32)
+    weight_total = None
+    for c in range(CHUNKS):
+        lo = c * step
+        row_total = rows_total[c]
         normed_c = normed[lo:lo + step]
         scaled = gain_f * row_total
-        mean_term = lax.psum(jnp.sum(scaled * normed_c, axis=1, keepdims=True), "tensor") / d_model
         input_grad = (
             grad_out[lo:lo + step].astype(jnp.float32)
-            + rstd[lo:lo + step] * (scaled - normed_c * mean_term)
+            + rstd[lo:lo + step] * (scaled - normed_c * means[c])
         ).astype(jnp.bfloat16)
         inputs_grad.append(from_behind(input_grad, "pipe", -1))
         gain_part = gain_part + jnp.sum(row_total * normed_c, axis=0)
@@ -84,16 +98,19 @@
             )
             own_g = me // 2
             total = lax.dynamic_slice_in_dim(pair, own_g * kv_block, kv_block, axis=1)
+            outs = []
             for d in range(1, groups):
                 dest_g = (own_g + d) % groups
                 out = lax.dynamic_slice_in_dim(pair, dest_g * kv_block, kv_block, axis=1)
-                total = total + shifted(out.astype(jnp.bfloat16), "dp", 2 * d).astype(jnp.float32)
+                outs.append(out.astype(jnp.bfloat16))
+            for d, out in enumerate(outs, start=1):
+                total = total + shifted(out, "dp", 2 * d).astype(jnp.float32)
             weight_total = total.astype(jnp.bfloat16)
-        if c + 1 < CHUNKS:
-            _, block = lax.optimization_barrier((pair, piece[lo + step:lo + 2 * step]))
+            if c + 1 < CHUNKS:
+                _, rows_total = lax.optimization_barrier((outs, rows_total))
 
     upstream = jnp.concatenate(inputs_grad, axis=0)
-    gain_total = lax.psum(gain_part, "dp")
+    gain_total = lax.psum(jnp.broadcast_to(gain_part[None], (8, d_local)), "dp")[0]
     return (upstream[None, None], weight_total[None], gain_total[None])
 
 

time: 174 us -> 189 us (1.086)
  waiting for transfers between devices: 31.4 us -> 103 us
  blocking collectives: 74.7 us -> 13.7 us
  local copies, waits for them, and re-layouts: 7.93 us -> 11 us
    psum x0 -> x2, waiting for transfers between devices: none -> 63.8 us  [the longest x1 33.5 us: on_device(): lax.psum(jnp.broadcast_to(gain_part[None], (8, d_local)), 'dp')[0]]
    psum x3 -> x0, blocking collectives: 61 us -> none  [the longest x1 42.3 us: on_device(): gain_total = lax.psum(gain_part, 'dp')]
    ppermute x2, waiting for transfers between devices: 0.01 us -> 7.78 us  [from_behind(): return lax.ppermute(block, axis, route)]
    dot_general x2, matrix products: 9.92 us -> 14.4 us  [on_device(): lax.dot_general(block, weight, (((1,), (1,)), ((), ())), preferred_elemen...]
    dot_general x1, matrix products: 6.44 us -> 2.53 us  [on_device(): lax.dot_general(hidden_partner, cols_partner, (((0,), (0,)), ((), ())), p...]
    convert_element_type x1, local copies, waits for them, and re-layouts: 3.94 us -> 0.32 us  [on_device(): outs.append(out.astype(jnp.bfloat16))]
    slice x2 -> x3, local copies, waits for them, and re-layouts: 0.1 us -> 2.74 us  [the longest x1 1.44 us: on_device(): lax.psum(jnp.broadcast_to(gain_part[None], (8, d_local)), 'dp')[0]]
    unnamed x20 -> x18, local copies, waits for them, and re-layouts: 1.1 us -> 3.27 us
  transfers between devices with their start and end apart: 6 -> 8, of which waited for: 1 -> 4; matrix products, arithmetic and copies ran while one was open for 25% -> 23% of each run, Pallas kernels for 0% -> 0%
where the time goes in v5:
time: 189 us; the launch traced here: 188 us
  waiting for transfers between devices  103 us (54%)
  other arithmetic  21.5 us (11%)
  matrix products  21 us (11%)
  between operations  13.9 us (7%)
  blocking collectives  13.7 us (7%)
  local copies, waits for them, and re-layouts  11 us (6%)
  starting transfers between devices  4.39 us (2%)
    psum x1, waiting for transfers between devices, on_device(): lax.psum(jnp.broadcast_to(gain_part[None], (8, d_local)), 'dp')[0]  33.5 us
    all_gather x1, waiting for transfers between devices, on_device(): piece = lax.all_gather(grad_kv, 'tensor', axis=1, tiled=True)  30.6 us
    psum x1, waiting for transfers between devices, row_sums(): return lax.psum(wide, 'tensor')[:, :1]  30.3 us
    dot_general x2, matrix products, on_device(): lax.dot_general(block, weight, (((1,), (1,)), ((), ())), preferred_elemen...  14.4 us
    psum x1, blocking collectives, on_device(): lax.psum(jnp.sum(values * values, axis=1, keepdims=True), 'tensor')  13.7 us
    ppermute x2, waiting for transfers between devices, from_behind(): return lax.ppermute(block, axis, route)  7.78 us
    broadcast_in_dim x2, other arithmetic, on_device(): return (upstream[None, None], weight_total[None], gain_total[None])  7.6 us
    convert_element_type x1, other arithmetic, on_device(): input_grad = (grad_out[lo:lo + step].astype(jnp.float32) + rstd[lo:lo + s...  4.16 us
  transfers between devices with their start and end apart: 8, of which 4 were waited for; matrix products, arithmetic and copies ran while one was open for 23% of the time, Pallas kernels for 0%

profile of v5, /device:TPU:0, one launch (start us, length us, event | category | flops | bytes accessed | tf_op | source)
XLA Modules:
  0.0 188.3 jit_solution(596161378911331771)
XLA Ops:
  8.7 2.1 %fusion.4 = f32[512]{0:T(512)S(1)} fusion(bf16[1,1,512,2048]{3,2,1,0:T(8,128)(2,1)} %param.5), kind=kLoop, calls=%fused_computation.6 | loop fusion | flops 3145216 | bytes 2099200 | tf_op jit(solution)/shard_map/reduce_sum | solution.py:41
  10.7 13.7 %psum.28 = f32[512,1]{0,1:T(1,128)S(1)} all-reduce(f32[512,1]{0,1:T(1,128)S(1)} %bitcast.52), channel_id=1, replica_groups=mesh['dp'=4,'pipe'=2,'tensor'=4] {'tensor'}, use_global_device_ids=true, to_apply=%region_1.2 | all-reduce | flops 512 | bytes 4096 | tf_op jit(solution)/shard_map/psum | solution.py:41
  24.4 3.3 %multiply_convert_fusion = (bf16[512,2048]{1,0:T(8,128)(2,1)}, f32[512,2048]{1,0:T(8,128)}) fusion(f32[2048]{0:T(1024)S(1)} %bitcast.47, f32[512]{0:T(512)S(1)} %bitcast.51, bf16[1,1,512,2048]{3,2,1,0:T(8,128)(2,1)S(1)} %copy-done.3), kind=kLoop, calls=%fused_computation.9 | loop fusion | flops 4194304 | bytes 8398848 | tf_op jit(solution)/shard_map/convert_element_type | solution.py:44
  27.7 30.6 %all-gather.3.cloned.1.call-done = bf16[1,1,512,2048]{3,2,1,0:T(8,128)(2,1)} async-done(((bf16[1,1,512,512]{3,2,1,0:T(8,128)(2,1)}), bf16[1,1,512,2048]{3,2,1,0:T(8,128)(2,1)}) %all-gather.3.cloned.1.call-update) | async-done | bytes 2097168 | tf_op jit(solution)/shard_map/all_gather | solution.py:47
  58.3 1.3 slice_bitcast_fusion
  59.6 6.2 %fusion.2 = f32[256,2048]{1,0:T(8,128)S(1)} fusion(bf16[1,2048,2048]{2,1,0:T(8,128)(2,1)} %param.9, bf16[1,1,512,2048]{3,2,1,0:T(8,128)(2,1)} %all-gather.3.cloned.1.call-done), kind=kOutput, calls=%fused_computation.2 | convolution fusion | flops 2147483648 | bytes 11534336 | tf_op jit(solution)/shard_map/dot_general | solution.py:68
  65.8 8.2 %multiply_reduce_fusion.1 = (f32[2048]{0:T(1024)S(1)}, f32[256]{0:T(256)S(1)}, f32[256]{0:T(256)S(1)}, f32[256,2048]{1,0:T(8,128)}) fusion(f32[256,2048]{1,0:T(8,128)S(1)} %fusion.2, f32[512,2048]{1,0:T(8,128)S(1)} %copy-done.1, f32[2048]{0:T(1024)S(1)} %bitcast.48, bf16[256,2048]{1,0:T(8,128)(2,1)S(1)} %slice_bitcast_fusion, bf16[1,2048,2048]{2,1,0:T(8,128)(2,1)} %param.9), kind=kOutput, calls=%fused_computation.18 | convolution fusion | flops 2151675392 | bytes 17844224 | tf_op jit(solution)/shard_map/dot_general | solution.py:68
  75.6 2.7 %dynamic-slice_bitcast_fusion.1 = (bf16[512,512]{1,0:T(8,128)(2,1)S(1)}, bf16[512,512]{1,0:T(8,128)(2,1)S(1)}, bf16[512,512]{1,0:T(8,128)(2,1)}, bf16[512,512]{1,0:T(8,128)(2,1)}) fusion(bf16[1,1,512,2048]{3,2,1,0:T(8,128)(2,1)} %all-gather.3.cloned.1.call-done, s32[]{:T(128)S(6)} %select_n.36, s32[]{:T(128)S(6)} %select_n.37, s32[]{:T(128)S(6)} %select_n.35, ...), kind=kLoop, calls=%fused_computation.29 | loop fusion | bytes 4194320 | tf_op jit(solution)/shard_map/dynamic_slice | solution.py:51
  78.3 1.2 pad_maximum_fusion
  79.4 30.3 %all-reduce.6.cloned.1.call-done = (f32[256,128]{0,1:T(8,128)}, f32[256,128]{0,1:T(8,128)}) async-done(((f32[256,128]{0,1:T(8,128)}, f32[256,128]{0,1:T(8,128)}), (f32[256,128]{0,1:T(8,128)}, f32[256,128]{0,1:T(8,128)})) %all-reduce.6.cloned.1.call-update) | async-done | bytes 262160 | tf_op jit(solution)/shard_map/psum | solution.py:62
  109.7 0.7 slice_multiply_fusion
  110.5 4.2 %fusion.7 = bf16[256,2048]{1,0:T(8,128)(2,1)} fusion(f32[256,2048]{1,0:T(8,128)} %copy-done.4, f32[512,2048]{1,0:T(8,128)} %get-tuple-element.17, f32[256]{0:T(256)S(1)} %bitcast.56, f32[2048]{0:T(1024)S(1)} %bitcast.49, f32[256]{0:T(256)S(1)} %bitcast.54, bf16[1,1,512,2048]{3,2,1,0:T(8,128)(2,1)} %param.6), kind=kLoop, calls=%fused_computation.16 | loop fusion | flops 3670016 | bytes 6301696 | tf_op jit(solution)/shard_map/convert_element_type | solution.py:88
  114.6 4.0 %fusion.8 = f32[2048,1024]{1,0:T(8,128)S(1)} fusion(bf16[512,2048]{1,0:T(8,128)(2,1)} %get-tuple-element.6, bf16[512,512]{1,0:T(8,128)(2,1)S(1)} %copy-done.7, bf16[512,512]{1,0:T(8,128)(2,1)S(1)} %copy-done.8), kind=kOutput, calls=%fused_computation.23 | convolution fusion | flops 2149580800 | bytes 11534336 | tf_op jit(solution)/shard_map/dot_general | solution.py:93
  118.7 2.5 %convolution_add_fusion = f32[2048,1024]{1,0:T(8,128)S(1)} fusion(f32[2048,1024]{1,0:T(8,128)S(1)} %fusion.8, bf16[512,2048]{1,0:T(8,128)(2,1)S(1)} %collective-permute-done.1, bf16[512,1024]{1,0:T(8,128)(2,1)S(1)} %collective-permute-done.2), kind=kOutput, calls=%fused_computation.10 | convolution fusion | flops 2149580800 | bytes 19922944 | tf_op jit(solution)/shard_map/dot_general | solution.py:95
  121.3 3.2 %copy-done = f32[2048,1024]{1,0:T(8,128)} copy-done((f32[2048,1024]{1,0:T(8,128)}, f32[2048,1024]{1,0:T(8,128)S(1)}, u32[]{:S(2)}) %copy-start) | copy-done | bytes 8388632
  124.8 1.5 collective-permute-start.4
  126.3 1.3 collective-permute-start
  127.7 1.8 multiply_reduce_fusion
  129.5 1.3 collective-permute-start.3
  131.5 33.5 %all-reduce.4.cloned.1.call-done = f32[8,2048]{1,0:T(8,128)} async-done(((f32[8,2048]{1,0:T(8,128)}), f32[8,2048]{1,0:T(8,128)}) %all-reduce.4.cloned.1.call-update) | async-done | bytes 65552 | tf_op jit(solution)/shard_map/psum | solution.py:113
  165.0 1.4 slice.58
  166.4 7.8 %collective-permute-done.3 = bf16[256,2048]{1,0:T(8,128)(2,1)} collective-permute-done((bf16[256,2048]{1,0:T(8,128)(2,1)}, bf16[256,2048]{1,0:T(8,128)(2,1)}, u32[]{:S(2)}, u32[]{:S(2)}) %collective-permute-start.3) | collective-permute-done | bytes 1048608 | tf_op jit(solution)/shard_map/ppermute | solution.py:13
  174.2 2.7 %maximum_bitcast_fusion = bf16[1,1,512,2048]{3,2,1,0:T(8,128)(2,1)} fusion(bf16[256,2048]{1,0:T(8,128)(2,1)} %collective-permute-done.3, bf16[256,2048]{1,0:T(8,128)(2,1)S(1)} %collective-permute-done), kind=kLoop, calls=%fused_computation.12 | loop fusion | flops 4194304 | bytes 4194304 | tf_op jit(solution)/shard_map/broadcast_in_dim | solution.py:114
  176.9 4.9 %fusion.5 = bf16[1,2048,512]{2,1,0:T(8,128)(2,1)} fusion(bf16[2048,512]{1,0:T(8,128)(2,1)} %collective-permute-done.4, f32[2048,1024]{1,0:T(8,128)} %copy-done, s32[]{:T(128)S(6)} %select_n.41), kind=kLoop, calls=%fused_computation.11 | loop fusion | flops 3145728 | bytes 8388612 | tf_op jit(solution)/shard_map/broadcast_in_dim | solution.py:114
  (37 shorter events, 4.1 us)
Async XLA Ops:
  7.2 17.3 %copy-start.3 = (bf16[1,1,512,2048]{3,2,1,0:T(8,128)(2,1)S(1)}, bf16[1,1,512,2048]{3,2,1,0:T(8,128)(2,1)}, u32[]{:S(2)}) copy-start(bf16[1,1,512,2048]{3,2,1,0:T(8,128)(2,1)} %param.5) | copy-start | bytes 6291460
  7.2 51.1 %all-gather.3.cloned.1.call-start = ((), (), s32[]{:S(2)}) async-start(), calls=%async_computation.1 | async-start | bytes 2621440 | tf_op jit(solution)/shard_map/all_gather | solution.py:47
  7.9 101.8 %all-reduce.6.cloned.1.call-start = ((), (), s32[]{:S(2)}) async-start(), calls=%async_computation.2 | async-start | bytes 524288 | tf_op jit(solution)/shard_map/psum | solution.py:62
  27.7 91.0 %collective-permute-start.1 = (bf16[512,2048]{1,0:T(8,128)(2,1)}, bf16[512,2048]{1,0:T(8,128)(2,1)S(1)}, u32[]{:S(2)}, u32[]{:S(2)}) collective-permute-start(bf16[512,2048]{1,0:T(8,128)(2,1)} %get-tuple-element.6), channel_id=1, source_target_pairs={{0,8},{8,0},{16,24},{24,16},{1,9},{9,1},{17,25},{25,17},{2,10},{10... | collective-permute-start | bytes 6291464 | tf_op jit(solution)/shard_map/ppermute | solution.py:23
  59.6 6.2 %copy-start.1 = (f32[512,2048]{1,0:T(8,128)S(1)}, f32[512,2048]{1,0:T(8,128)}, u32[]{:S(2)}) copy-start(f32[512,2048]{1,0:T(8,128)} %get-tuple-element.17) | copy-start | bytes 12582916
  65.8 8.2 %copy-start.4 = (f32[256,2048]{1,0:T(8,128)}, f32[256,2048]{1,0:T(8,128)S(1)}, u32[]{:S(2)}) copy-start(f32[256,2048]{1,0:T(8,128)S(1)} %fusion.2) | copy-start | bytes 6291460
  75.4 89.6 %all-reduce.4.cloned.1.call-start = ((), (), s32[]{:S(2)}) async-start(), calls=%async_computation | async-start | bytes 131072 | tf_op jit(solution)/shard_map/psum | solution.py:113
  79.4 39.3 %collective-permute-start.2 = (bf16[512,1024]{1,0:T(8,128)(2,1)}, bf16[512,1024]{1,0:T(8,128)(2,1)S(1)}, u32[]{:S(2)}, u32[]{:S(2)}) collective-permute-start(bf16[512,1024]{1,0:T(8,128)(2,1)} %pad_maximum_fusion), channel_id=1, source_target_pairs={{0,8},{8,0},{16,24},{24,16},{1,9},{9,1},{17,25},{25,17},{2,10},{10... | collective-permute-start | bytes 3145736 | tf_op jit(solution)/shard_map/ppermute | solution.py:23
  110.5 4.2 %copy-start.7 = (bf16[512,512]{1,0:T(8,128)(2,1)S(1)}, bf16[512,512]{1,0:T(8,128)(2,1)}, u32[]{:S(2)}) copy-start(bf16[512,512]{1,0:T(8,128)(2,1)} %get-tuple-element.20) | copy-start | bytes 1572868
  110.5 4.2 %copy-start.8 = (bf16[512,512]{1,0:T(8,128)(2,1)S(1)}, bf16[512,512]{1,0:T(8,128)(2,1)}, u32[]{:S(2)}) copy-start(bf16[512,512]{1,0:T(8,128)(2,1)} %get-tuple-element.21) | copy-start | bytes 1572868
  118.7 8.9 %copy-start.5 = (f32[256,2048]{1,0:T(8,128)S(1)}, f32[256,2048]{1,0:T(8,128)}, u32[]{:S(2)}) copy-start(f32[256,2048]{1,0:T(8,128)} %get-tuple-element.8) | copy-start | bytes 6291460
  118.7 8.9 %copy-start.6 = (bf16[1,1,512,2048]{3,2,1,0:T(8,128)(2,1)S(1)}, bf16[1,1,512,2048]{3,2,1,0:T(8,128)(2,1)}, u32[]{:S(2)}) copy-start(bf16[1,1,512,2048]{3,2,1,0:T(8,128)(2,1)} %param.6) | copy-start | bytes 6291460
  121.2 3.2 %copy-start = (f32[2048,1024]{1,0:T(8,128)}, f32[2048,1024]{1,0:T(8,128)S(1)}, u32[]{:S(2)}) copy-start(f32[2048,1024]{1,0:T(8,128)S(1)} %convolution_add_fusion) | copy-start | bytes 25165828
  124.5 3.2 %copy-start.2 = (f32[512,2048]{1,0:T(8,128)S(1)}, f32[512,2048]{1,0:T(8,128)}, u32[]{:S(2)}) copy-start(f32[512,2048]{1,0:T(8,128)} %get-tuple-element.17) | copy-start | bytes 12582916
  124.8 52.1 %collective-permute-start.4 = (bf16[2048,512]{1,0:T(8,128)(2,1)S(1)}, bf16[2048,512]{1,0:T(8,128)(2,1)}, u32[]{:S(2)}, u32[]{:S(2)}) collective-permute-start(bf16[2048,512]{1,0:T(8,128)(2,1)S(1)} %dynamic-slice_convert_fusion), channel_id=1, source_target_pairs={{0,16},{8,24},{16,0},{24,8},{1,17},{9,25},{17,1},{25,9},{2,18},{10... | collective-permute-start | bytes 6291464 | tf_op jit(solution)/shard_map/ppermute | solution.py:18
  126.3 40.1 %collective-permute-start = (bf16[256,2048]{1,0:T(8,128)(2,1)}, bf16[256,2048]{1,0:T(8,128)(2,1)S(1)}, u32[]{:S(2)}, u32[]{:S(2)}) collective-permute-start(bf16[256,2048]{1,0:T(8,128)(2,1)} %fusion.7), channel_id=1, source_target_pairs={{4,0},{5,1},{6,2},{7,3},{12,8},{13,9},{14,10},{15,11},{20,16},{21,... | collective-permute-start | bytes 3145736 | tf_op jit(solution)/shard_map/ppermute | solution.py:13
  129.5 44.7 %collective-permute-start.3 = (bf16[256,2048]{1,0:T(8,128)(2,1)}, bf16[256,2048]{1,0:T(8,128)(2,1)}, u32[]{:S(2)}, u32[]{:S(2)}) collective-permute-start(bf16[256,2048]{1,0:T(8,128)(2,1)} %get-tuple-element.15), channel_id=1, source_target_pairs={{4,0},{5,1},{6,2},{7,3},{12,8},{13,9},{14,10},{15,11},{20,16},{21,... | collective-permute-start | bytes 3145736 | tf_op jit(solution)/shard_map/ppermute | solution.py:13
Sparse Core Ops, SparseCore 0:
  9.6 48.6 all-gather.2
  75.5 34.2 all-reduce.5
  131.6 33.3 all-reduce.3

commit v6 on v4

--- a/solution.py
+++ b/solution.py
@@ -84,16 +84,26 @@
             )
             own_g = me // 2
             total = lax.dynamic_slice_in_dim(pair, own_g * kv_block, kv_block, axis=1)
+            outs = []
             for d in range(1, groups):
                 dest_g = (own_g + d) % groups
                 out = lax.dynamic_slice_in_dim(pair, dest_g * kv_block, kv_block, axis=1)
-                total = total + shifted(out.astype(jnp.bfloat16), "dp", 2 * d).astype(jnp.float32)
+                outs.append(out.astype(jnp.bfloat16))
+            for d, out in enumerate(outs, start=1):
+                total = total + shifted(out, "dp", 2 * d).astype(jnp.float32)
             weight_total = total.astype(jnp.bfloat16)
         if c + 1 < CHUNKS:
-            _, block = lax.optimization_barrier((pair, piece[lo + step:lo + 2 * step]))
+            _, block = lax.optimization_barrier(((input_grad, outs), piece[lo + step:lo + 2 * step]))
 
     upstream = jnp.concatenate(inputs_grad, axis=0)
-    gain_total = lax.psum(gain_part, "dp")
+    pair_gain = gain_part + to_partner(gain_part)
+    own_g = me // 2
+    stacked = jnp.zeros((groups, d_local), jnp.float32)
+    stacked = lax.dynamic_update_slice_in_dim(stacked, pair_gain[None], own_g, axis=0)
+    for d in range(1, groups):
+        got = shifted(pair_gain, "dp", 2 * d)
+        stacked = lax.dynamic_update_slice_in_dim(stacked, got[None], (own_g - d) % groups, axis=0)
+    gain_total = jnp.sum(stacked, axis=0)
     return (upstream[None, None], weight_total[None], gain_total[None])
 
 

time: 174 us -> 159 us (0.914)
  blocking collectives: 74.7 us -> 32.3 us
  waiting for transfers between devices: 31.4 us -> 58.7 us
  matrix products: 20.6 us -> 16.7 us
    psum x1 -> x0, blocking collectives: 42.3 us -> none  [on_device(): gain_total = lax.psum(gain_part, 'dp')]
    ppermute x1 -> x2, waiting for transfers between devices: 0.01 us -> 26.2 us  [shifted(): return lax.ppermute(block, axis, [(i, (i + shift) % n) for i in range(n)])]
    dot_general x1, matrix products: 6.44 us -> 2.62 us  [on_device(): lax.dot_general(hidden_partner, cols_partner, (((0,), (0,)), ((), ())), p...]
    unnamed x20, local copies, waits for them, and re-layouts: 1.1 us -> 4.08 us
    convert_element_type x1, local copies, waits for them, and re-layouts: 3.94 us -> 1.65 us  [on_device(): outs.append(out.astype(jnp.bfloat16))]
  transfers between devices with their start and end apart: 6 -> 8, of which waited for: 1 -> 3; matrix products, arithmetic and copies ran while one was open for 25% -> 24% of each run, Pallas kernels for 0% -> 0%
where the time goes in v6:
time: 159 us; the launch traced here: 158 us
  waiting for transfers between devices  58.7 us (37%)
  blocking collectives  32.3 us (20%)
  other arithmetic  22.1 us (14%)
  matrix products  16.7 us (11%)
  between operations  14.2 us (9%)
  local copies, waits for them, and re-layouts  8.76 us (6%)
  starting transfers between devices  5.6 us (4%)
    all_gather x1, waiting for transfers between devices, on_device(): piece = lax.all_gather(grad_kv, 'tensor', axis=1, tiled=True)  30.7 us
    ppermute x2, waiting for transfers between devices, shifted(): return lax.ppermute(block, axis, [(i, (i + shift) % n) for i in range(n)])  26.2 us
    psum x2, blocking collectives, on_device(): lax.psum(jnp.sum(scaled * normed_c, axis=1, keepdims=True), 'tensor')  18.7 us
    psum x1, blocking collectives, on_device(): lax.psum(jnp.sum(values * values, axis=1, keepdims=True), 'tensor')  13.7 us
    dot_general x2, matrix products, on_device(): lax.dot_general(block, weight, (((1,), (1,)), ((), ())), preferred_elemen...  9.92 us
    broadcast_in_dim x2, other arithmetic, on_device(): return (upstream[None, None], weight_total[None], gain_total[None])  7.58 us
    convert_element_type x2, other arithmetic, on_device(): input_grad = (grad_out[lo:lo + step].astype(jnp.float32) + rstd[lo:lo + s...  6.6 us
    dot_general x1, matrix products, on_device(): lax.dot_general(h_own, cols_own, (((0,), (0,)), ((), ())), preferred_elem...  4.19 us
  transfers between devices with their start and end apart: 8, of which 3 were waited for; matrix products, arithmetic and copies ran while one was open for 24% of the time, Pallas kernels for 0%

profile of v6, /device:TPU:0, one launch (start us, length us, event | category | flops | bytes accessed | tf_op | source)
XLA Modules:
  0.0 158.4 jit_solution(11253865823974235258)
XLA Ops:
  8.6 2.1 %fusion.4 = f32[512]{0:T(512)S(1)} fusion(bf16[1,1,512,2048]{3,2,1,0:T(8,128)(2,1)} %param.5), kind=kLoop, calls=%fused_computation.6 | loop fusion | flops 3145216 | bytes 2099200 | tf_op jit(solution)/shard_map/reduce_sum | solution.py:41
  10.7 13.7 %psum.21 = f32[512,1]{0,1:T(1,128)S(1)} all-reduce(f32[512,1]{0,1:T(1,128)S(1)} %bitcast.63), channel_id=1, replica_groups=mesh['dp'=4,'pipe'=2,'tensor'=4] {'tensor'}, use_global_device_ids=true, to_apply=%region_1.2 | all-reduce | flops 512 | bytes 4096 | tf_op jit(solution)/shard_map/psum | solution.py:41
  24.4 3.3 %multiply_convert_fusion = (bf16[512,2048]{1,0:T(8,128)(2,1)}, f32[512,2048]{1,0:T(8,128)}) fusion(f32[2048]{0:T(1024)S(1)} %bitcast.56, f32[512]{0:T(512)S(1)} %bitcast.62, bf16[1,1,512,2048]{3,2,1,0:T(8,128)(2,1)S(1)} %copy-done.3), kind=kLoop, calls=%fused_computation.9 | loop fusion | flops 4194304 | bytes 8398848 | tf_op jit(solution)/shard_map/convert_element_type | solution.py:44
  27.6 30.7 %all-gather.3.cloned.1.call-done = bf16[1,1,512,2048]{3,2,1,0:T(8,128)(2,1)} async-done(((bf16[1,1,512,512]{3,2,1,0:T(8,128)(2,1)}), bf16[1,1,512,2048]{3,2,1,0:T(8,128)(2,1)}) %all-gather.3.cloned.1.call-update) | async-done | bytes 2097168 | tf_op jit(solution)/shard_map/all_gather | solution.py:47
  58.3 2.8 %dynamic-slice_bitcast_fusion.1 = (bf16[512,512]{1,0:T(8,128)(2,1)S(1)}, bf16[512,512]{1,0:T(8,128)(2,1)S(1)}, bf16[512,512]{1,0:T(8,128)(2,1)}, bf16[512,512]{1,0:T(8,128)(2,1)}) fusion(bf16[1,1,512,2048]{3,2,1,0:T(8,128)(2,1)} %all-gather.3.cloned.1.call-done, s32[]{:T(128)S(6)} %select_n.47, s32[]{:T(128)S(6)} %select_n.48, s32[]{:T(128)S(6)} %select_n.46, ...), kind=kLoop, calls=%fused_computation.29 | loop fusion | bytes 4194320 | tf_op jit(solution)/shard_map/dynamic_slice | solution.py:51
  61.1 1.2 pad_maximum_fusion
  63.1 7.3 %multiply_reduce_fusion.1 = (f32[2048]{0:T(1024)S(1)}, f32[256]{0:T(256)S(1)}, f32[256,2048]{1,0:T(8,128)}) fusion(f32[512,2048]{1,0:T(8,128)S(1)} %copy-done.1, f32[2048]{0:T(1024)S(1)} %bitcast.57, bf16[1,2048,2048]{2,1,0:T(8,128)(2,1)} %param.9, bf16[1,1,512,2048]{3,2,1,0:T(8,128)(2,1)S(1)} %copy-done.4), kind=kOutput, calls=%fused_computation.18 | convolution fusion | flops 2150102784 | bytes 13648896 | tf_op jit(solution)/shard_map/dot_general | solution.py:65
  70.4 9.4 %psum.22 = f32[256,1]{0,1:T(1,128)S(1)} all-reduce(f32[256,1]{0,1:T(1,128)S(1)} %bitcast.71), channel_id=1, replica_groups=mesh['dp'=4,'pipe'=2,'tensor'=4] {'tensor'}, use_global_device_ids=true, to_apply=%region_3.4 | all-reduce | flops 256 | bytes 2048 | tf_op jit(solution)/shard_map/psum | solution.py:70
  79.8 4.2 %fusion.7 = bf16[256,2048]{1,0:T(8,128)(2,1)} fusion(f32[256,2048]{1,0:T(8,128)} %get-tuple-element.19, f32[512,2048]{1,0:T(8,128)} %get-tuple-element.12, f32[256]{0:T(256)S(1)} %bitcast.67, f32[2048]{0:T(1024)S(1)} %bitcast.58, f32[256]{0:T(256)S(1)} %bitcast.69, bf16[1,1,512,2048]{3,2,1,0:T(8,128)(2,1)} %param.6), kind=kLoop, calls=%fused_computation.16 | loop fusion | flops 3670016 | bytes 6301696 | tf_op jit(solution)/shard_map/convert_element_type | solution.py:74
  84.0 1.5 collective-permute-start
  85.5 4.2 %fusion.8 = f32[2048,1024]{1,0:T(8,128)S(1)} fusion(bf16[512,2048]{1,0:T(8,128)(2,1)} %get-tuple-element.5, bf16[512,512]{1,0:T(8,128)(2,1)S(1)} %copy-done.6, bf16[512,512]{1,0:T(8,128)(2,1)S(1)} %copy-done.7), kind=kOutput, calls=%fused_computation.23 | convolution fusion | flops 2149580800 | bytes 11534336 | tf_op jit(solution)/shard_map/dot_general | solution.py:79
  89.8 2.6 %convolution_add_fusion = f32[2048,1024]{1,0:T(8,128)S(1)} fusion(f32[2048,1024]{1,0:T(8,128)S(1)} %fusion.8, bf16[512,2048]{1,0:T(8,128)(2,1)S(1)} %collective-permute-done.1, bf16[512,1024]{1,0:T(8,128)(2,1)S(1)} %collective-permute-done.2), kind=kOutput, calls=%fused_computation.10 | convolution fusion | flops 2149580800 | bytes 19922944 | tf_op jit(solution)/shard_map/dot_general | solution.py:81
  92.5 3.2 %copy-done = f32[2048,1024]{1,0:T(8,128)} copy-done((f32[2048,1024]{1,0:T(8,128)}, f32[2048,1024]{1,0:T(8,128)S(1)}, u32[]{:S(2)}) %copy-start) | copy-done | bytes 8388632
  95.7 1.6 %dynamic-slice_convert_fusion = bf16[2048,512]{1,0:T(8,128)(2,1)} fusion(f32[2048,1024]{1,0:T(8,128)S(1)} %convolution_add_fusion, s32[]{:T(128)S(6)} %select_n.51), kind=kLoop, calls=%fused_computation.8 | loop fusion | bytes 4194308 | tf_op jit(solution)/shard_map/convert_element_type | solution.py:91
  97.3 1.5 collective-permute-start.4
  98.8 2.7 %multiply_reduce_fusion = (f32[2048]{0:T(1024)S(1)}, f32[256]{0:T(256)S(1)}, f32[256,2048]{1,0:T(8,128)S(1)}) fusion(f32[512,2048]{1,0:T(8,128)S(1)} %copy-done.2, f32[2048]{0:T(1024)S(1)} %bitcast.59, bf16[256,2048]{1,0:T(8,128)(2,1)S(1)} %slice_bitcast_fusion, bf16[1,2048,2048]{2,1,0:T(8,128)(2,1)S(1)} %bitcast.73), kind=kOutput, calls=%fused_computation.17 | convolution fusion | flops 2150102784 | bytes 13648896 | tf_op jit(solution)/shard_map/dot_general | solution.py:65
  101.5 9.3 %psum.23 = f32[256,1]{0,1:T(1,128)S(1)} all-reduce(f32[256,1]{0,1:T(1,128)S(1)} %bitcast.70), channel_id=1, replica_groups=mesh['dp'=4,'pipe'=2,'tensor'=4] {'tensor'}, use_global_device_ids=true, to_apply=%region_5.6 | all-reduce | flops 256 | bytes 2048 | tf_op jit(solution)/shard_map/psum | solution.py:70
  110.7 2.4 %fusion.6 = bf16[256,2048]{1,0:T(8,128)(2,1)S(1)} fusion(f32[256,2048]{1,0:T(8,128)S(1)} %get-tuple-element.20, f32[512,2048]{1,0:T(8,128)} %get-tuple-element.12, f32[256]{0:T(256)S(1)} %bitcast.66, f32[256]{0:T(256)S(1)} %bitcast.68, bf16[1,1,512,2048]{3,2,1,0:T(8,128)(2,1)} %param.6, f32[2048]{0:T(1024)S(1)} %bitcast.60), kind=kLoop, calls=%fused_computation.14 | loop fusion | flops 3670016 | bytes 6301696 | tf_op jit(solution)/shard_map/convert_element_type | solution.py:74
  113.2 1.3 collective-permute-start.3
  114.6 1.2 collective-permute-done.5
  115.7 1.3 collective-permute-start.6
  117.1 26.2 %collective-permute-done.6 = f32[2048]{0:T(1024)S(1)} collective-permute-done((f32[2048]{0:T(1024)S(1)}, f32[2048]{0:T(1024)S(1)}, u32[]{:S(2)}, u32[]{:S(2)}) %collective-permute-start.6) | collective-permute-done | bytes 8224 | tf_op jit(solution)/shard_map/ppermute | solution.py:18
  144.0 2.7 %maximum_bitcast_fusion = bf16[1,1,512,2048]{3,2,1,0:T(8,128)(2,1)} fusion(bf16[256,2048]{1,0:T(8,128)(2,1)S(1)} %collective-permute-done.3, bf16[256,2048]{1,0:T(8,128)(2,1)} %collective-permute-done), kind=kLoop, calls=%fused_computation.12 | loop fusion | flops 4194304 | bytes 4194304 | tf_op jit(solution)/shard_map/broadcast_in_dim | solution.py:107
  146.7 4.9 %fusion.5 = bf16[1,2048,512]{2,1,0:T(8,128)(2,1)} fusion(bf16[2048,512]{1,0:T(8,128)(2,1)} %collective-permute-done.4, f32[2048,1024]{1,0:T(8,128)} %copy-done, s32[]{:T(128)S(6)} %select_n.52), kind=kLoop, calls=%fused_computation.11 | loop fusion | flops 3145728 | bytes 8388612 | tf_op jit(solution)/shard_map/broadcast_in_dim | solution.py:107
  (42 shorter events, 3.3 us)
Async XLA Ops:
  7.2 17.2 %copy-start.3 = (bf16[1,1,512,2048]{3,2,1,0:T(8,128)(2,1)S(1)}, bf16[1,1,512,2048]{3,2,1,0:T(8,128)(2,1)}, u32[]{:S(2)}) copy-start(bf16[1,1,512,2048]{3,2,1,0:T(8,128)(2,1)} %param.5) | copy-start | bytes 6291460
  7.2 51.1 %all-gather.3.cloned.1.call-start = ((), (), s32[]{:S(2)}) async-start(), calls=%async_computation | async-start | bytes 2621440 | tf_op jit(solution)/shard_map/all_gather | solution.py:47
  27.6 62.2 %collective-permute-start.1 = (bf16[512,2048]{1,0:T(8,128)(2,1)}, bf16[512,2048]{1,0:T(8,128)(2,1)S(1)}, u32[]{:S(2)}, u32[]{:S(2)}) collective-permute-start(bf16[512,2048]{1,0:T(8,128)(2,1)} %get-tuple-element.5), channel_id=1, source_target_pairs={{0,8},{8,0},{16,24},{24,16},{1,9},{9,1},{17,25},{25,17},{2,10},{10... | collective-permute-start | bytes 6291464 | tf_op jit(solution)/shard_map/ppermute | solution.py:23
  58.3 4.0 %copy-start.1 = (f32[512,2048]{1,0:T(8,128)S(1)}, f32[512,2048]{1,0:T(8,128)}, u32[]{:S(2)}) copy-start(f32[512,2048]{1,0:T(8,128)} %get-tuple-element.12) | copy-start | bytes 12582916
  61.1 2.0 %copy-start.4 = (bf16[1,1,512,2048]{3,2,1,0:T(8,128)(2,1)S(1)}, bf16[1,1,512,2048]{3,2,1,0:T(8,128)(2,1)}, u32[]{:S(2)}) copy-start(bf16[1,1,512,2048]{3,2,1,0:T(8,128)(2,1)} %all-gather.3.cloned.1.call-done) | copy-start | bytes 6291460
  62.3 27.5 %collective-permute-start.2 = (bf16[512,1024]{1,0:T(8,128)(2,1)}, bf16[512,1024]{1,0:T(8,128)(2,1)S(1)}, u32[]{:S(2)}, u32[]{:S(2)}) collective-permute-start(bf16[512,1024]{1,0:T(8,128)(2,1)} %pad_maximum_fusion), channel_id=1, source_target_pairs={{0,8},{8,0},{16,24},{24,16},{1,9},{9,1},{17,25},{25,17},{2,10},{10... | collective-permute-start | bytes 3145736 | tf_op jit(solution)/shard_map/ppermute | solution.py:23
  79.8 5.6 %copy-start.6 = (bf16[512,512]{1,0:T(8,128)(2,1)S(1)}, bf16[512,512]{1,0:T(8,128)(2,1)}, u32[]{:S(2)}) copy-start(bf16[512,512]{1,0:T(8,128)(2,1)} %get-tuple-element.15) | copy-start | bytes 1572868
  79.8 5.6 %copy-start.7 = (bf16[512,512]{1,0:T(8,128)(2,1)S(1)}, bf16[512,512]{1,0:T(8,128)(2,1)}, u32[]{:S(2)}) copy-start(bf16[512,512]{1,0:T(8,128)(2,1)} %get-tuple-element.16) | copy-start | bytes 1572868
  84.0 60.0 %collective-permute-start = (bf16[256,2048]{1,0:T(8,128)(2,1)}, bf16[256,2048]{1,0:T(8,128)(2,1)}, u32[]{:S(2)}, u32[]{:S(2)}) collective-permute-start(bf16[256,2048]{1,0:T(8,128)(2,1)} %fusion.7), channel_id=1, source_target_pairs={{4,0},{5,1},{6,2},{7,3},{12,8},{13,9},{14,10},{15,11},{20,16},{21,... | collective-permute-start | bytes 3145736 | tf_op jit(solution)/shard_map/ppermute | solution.py:13
  85.4 4.2 %copy-start.5 = (bf16[1,1,512,2048]{3,2,1,0:T(8,128)(2,1)S(1)}, bf16[1,1,512,2048]{3,2,1,0:T(8,128)(2,1)}, u32[]{:S(2)}) copy-start(bf16[1,1,512,2048]{3,2,1,0:T(8,128)(2,1)} %all-gather.3.cloned.1.call-done) | copy-start | bytes 6291460
  89.7 9.1 %slice-start = ((s8[8388608]{0:T(1024)(128)(4,1)}), s8[4194304]{0:T(1024)(128)(4,1)S(1)}, s32[]{:S(2)}) async-start(s8[8388608]{0:T(1024)(128)(4,1)} %bitcast.72), calls=%async_computation.1 | async-start | bytes 8388608
  89.8 9.0 %slice-start.1 = ((s8[8388608]{0:T(1024)(128)(4,1)}), s8[4194304]{0:T(1024)(128)(4,1)S(1)}, s32[]{:S(2)}) async-start(s8[8388608]{0:T(1024)(128)(4,1)} %bitcast.72), calls=%async_computation.2 | async-start | bytes 8388608
  92.5 3.2 %copy-start = (f32[2048,1024]{1,0:T(8,128)}, f32[2048,1024]{1,0:T(8,128)S(1)}, u32[]{:S(2)}) copy-start(f32[2048,1024]{1,0:T(8,128)S(1)} %convolution_add_fusion) | copy-start | bytes 25165828
  95.7 3.1 %copy-start.2 = (f32[512,2048]{1,0:T(8,128)S(1)}, f32[512,2048]{1,0:T(8,128)}, u32[]{:S(2)}) copy-start(f32[512,2048]{1,0:T(8,128)} %get-tuple-element.12) | copy-start | bytes 12582916
  97.3 49.4 %collective-permute-start.4 = (bf16[2048,512]{1,0:T(8,128)(2,1)}, bf16[2048,512]{1,0:T(8,128)(2,1)}, u32[]{:S(2)}, u32[]{:S(2)}) collective-permute-start(bf16[2048,512]{1,0:T(8,128)(2,1)} %dynamic-slice_convert_fusion), channel_id=1, source_target_pairs={{0,16},{8,24},{16,0},{24,8},{1,17},{9,25},{17,1},{25,9},{2,18},{10... | collective-permute-start | bytes 6291464 | tf_op jit(solution)/shard_map/ppermute | solution.py:18
  113.2 30.8 %collective-permute-start.3 = (bf16[256,2048]{1,0:T(8,128)(2,1)S(1)}, bf16[256,2048]{1,0:T(8,128)(2,1)S(1)}, u32[]{:S(2)}, u32[]{:S(2)}) collective-permute-start(bf16[256,2048]{1,0:T(8,128)(2,1)S(1)} %fusion.6), channel_id=1, source_target_pairs={{4,0},{5,1},{6,2},{7,3},{12,8},{13,9},{14,10},{15,11},{20,16},{21,... | collective-permute-start | bytes 3145736 | tf_op jit(solution)/shard_map/ppermute | solution.py:13
  114.5 1.2 collective-permute-start.5
  115.7 27.5 %collective-permute-start.6 = (f32[2048]{0:T(1024)S(1)}, f32[2048]{0:T(1024)S(1)}, u32[]{:S(2)}, u32[]{:S(2)}) collective-permute-start(f32[2048]{0:T(1024)S(1)} %add.94), channel_id=1, source_target_pairs={{0,16},{8,24},{16,0},{24,8},{1,17},{9,25},{17,1},{25,9},{2,18},{10... | collective-permute-start | bytes 24584 | tf_op jit(solution)/shard_map/ppermute | solution.py:18
Sparse Core Ops, SparseCore 0:
  9.6 48.6 all-gather.2

commit v7 on v6

--- a/solution.py
+++ b/solution.py
@@ -44,7 +44,12 @@
     hidden = (normed * gain_f).astype(jnp.bfloat16)
     hidden_partner = to_partner(hidden)
 
-    piece = lax.all_gather(grad_kv, "tensor", axis=1, tiled=True)
+    step = seq // CHUNKS
+    pieces = [
+        lax.all_gather(grad_kv[c * step:(c + 1) * step], "tensor", axis=1, tiled=True)
+        for c in range(CHUNKS)
+    ]
+    piece = jnp.concatenate(pieces, axis=0)
 
     def cols_of(p):
         return jnp.concatenate(
@@ -52,13 +57,10 @@
             axis=1,
         )
 
-    cols_partner = to_partner(cols_of(1 - parity))
-    cols_own = cols_of(parity)
 
-    step = seq // CHUNKS
     inputs_grad = []
     gain_part = jnp.zeros((d_local,), jnp.float32)
-    block = piece[:step]
+    block = pieces[0]
     weight_total = None
     for c in range(CHUNKS):
         lo = c * step
@@ -75,7 +77,9 @@
         inputs_grad.append(from_behind(input_grad, "pipe", -1))
         gain_part = gain_part + jnp.sum(row_total * normed_c, axis=0)
         if c == 0:
-            _, h_own = lax.optimization_barrier((input_grad, hidden))
+            _, (h_own, piece) = lax.optimization_barrier((input_grad, (hidden, piece)))
+            cols_partner = to_partner(cols_of(1 - parity))
+            cols_own = cols_of(parity)
             pair = lax.dot_general(
                 h_own, cols_own, (((0,), (0,)), ((), ())), preferred_element_type=jnp.float32
             ) + lax.dot_general(
@@ -93,7 +97,7 @@
                 total = total + shifted(out, "dp", 2 * d).astype(jnp.float32)
             weight_total = total.astype(jnp.bfloat16)
         if c + 1 < CHUNKS:
-            _, block = lax.optimization_barrier(((input_grad, outs), piece[lo + step:lo + 2 * step]))
+            _, block = lax.optimization_barrier(((input_grad, outs), pieces[c + 1]))
 
     upstream = jnp.concatenate(inputs_grad, axis=0)
     pair_gain = gain_part + to_partner(gain_part)

time: 159 us -> 156 us (0.981)
  waiting for transfers between devices: 58.7 us -> 51.5 us
  blocking collectives: 32.3 us -> 34.2 us
    all_gather x1 -> x2, waiting for transfers between devices: 30.7 us -> 21.9 us  [on_device(): lax.all_gather(grad_kv[c * step:(c + 1) * step], 'tensor', axis=1, tiled=...]
    psum x2, blocking collectives: 18.7 us -> 20.6 us  [on_device(): lax.psum(jnp.sum(scaled * normed_c, axis=1, keepdims=True), 'tensor')]
    slice x1, local copies, waits for them, and re-layouts: 0.1 us -> 1.99 us  [on_device(): grad_kv[c * step:(c + 1) * step]]
    unnamed x20 -> x16, local copies, waits for them, and re-layouts: 4.08 us -> 4.18 us
  transfers between devices with their start and end apart: 8 -> 9, of which waited for: 3 -> 4; matrix products, arithmetic and copies ran while one was open for 24% -> 25% of each run, Pallas kernels for 0% -> 0%
where the time goes in v7:
time: 156 us; the launch traced here: 155 us
  waiting for transfers between devices  51.5 us (33%)
  blocking collectives  34.2 us (22%)
  other arithmetic  22.8 us (15%)
  matrix products  17.9 us (11%)
  between operations  14.2 us (9%)
  local copies, waits for them, and re-layouts  9.23 us (6%)
  starting transfers between devices  5.64 us (4%)
    ppermute x2, waiting for transfers between devices, shifted(): return lax.ppermute(block, axis, [(i, (i + shift) % n) for i in range(n)])  27.7 us
    all_gather x2, waiting for transfers between devices, on_device(): lax.all_gather(grad_kv[c * step:(c + 1) * step], 'tensor', axis=1, tiled=...  21.9 us
    psum x2, blocking collectives, on_device(): lax.psum(jnp.sum(scaled * normed_c, axis=1, keepdims=True), 'tensor')  20.6 us
    psum x1, blocking collectives, on_device(): lax.psum(jnp.sum(values * values, axis=1, keepdims=True), 'tensor')  13.5 us
    dot_general x2, matrix products, on_device(): lax.dot_general(block, weight, (((1,), (1,)), ((), ())), preferred_elemen...  10.9 us
    broadcast_in_dim x2, other arithmetic, on_device(): return (upstream[None, None], weight_total[None], gain_total[None])  7.58 us
    convert_element_type x2, other arithmetic, on_device(): input_grad = (grad_out[lo:lo + step].astype(jnp.float32) + rstd[lo:lo + s...  5.92 us
    dot_general x1, matrix products, on_device(): lax.dot_general(h_own, cols_own, (((0,), (0,)), ((), ())), preferred_elem...  4.38 us
  transfers between devices with their start and end apart: 9, of which 4 were waited for; matrix products, arithmetic and copies ran while one was open for 25% of the time, Pallas kernels for 0%

profile of v7, /device:TPU:0, one launch (start us, length us, event | category | flops | bytes accessed | tf_op | source)
XLA Modules:
  0.0 155.5 jit_solution(6335171428496985431)
XLA Ops:
  7.2 2.0 %fusion.14 = (bf16[1,1,256,512]{3,2,1,0:T(8,128)(2,1)}, bf16[1,1,256,512]{3,2,1,0:T(8,128)(2,1)}) fusion(bf16[1,1,512,512]{3,2,1,0:T(8,128)(2,1)} %param.7), kind=kLoop, calls=%fused_computation.36 | loop fusion | bytes 1048576 | tf_op jit(solution)/shard_map/slice | solution.py:49
  10.7 2.1 %fusion.4 = f32[512]{0:T(512)S(1)} fusion(bf16[1,1,512,2048]{3,2,1,0:T(8,128)(2,1)} %param.5), kind=kLoop, calls=%fused_computation.6 | loop fusion | flops 3145216 | bytes 2099200 | tf_op jit(solution)/shard_map/reduce_sum | solution.py:41
  12.8 13.5 %psum.21 = f32[512,1]{0,1:T(1,128)S(1)} all-reduce(f32[512,1]{0,1:T(1,128)S(1)} %bitcast.57), channel_id=1, replica_groups=mesh['dp'=4,'pipe'=2,'tensor'=4] {'tensor'}, use_global_device_ids=true, to_apply=%region_1.2 | all-reduce | flops 512 | bytes 4096 | tf_op jit(solution)/shard_map/psum | solution.py:41
  26.3 3.3 %multiply_convert_fusion = (bf16[512,2048]{1,0:T(8,128)(2,1)}, f32[512,2048]{1,0:T(8,128)}) fusion(f32[2048]{0:T(1024)S(1)} %bitcast.50, f32[512]{0:T(512)S(1)} %bitcast.56, bf16[1,1,512,2048]{3,2,1,0:T(8,128)(2,1)S(1)} %copy-done.3), kind=kLoop, calls=%fused_computation.9 | loop fusion | flops 4194304 | bytes 8398848 | tf_op jit(solution)/shard_map/convert_element_type | solution.py:44
  29.6 11.3 %all-gather.5.cloned.1.call-done = bf16[1,1,256,2048]{3,2,1,0:T(8,128)(2,1)} async-done(((bf16[1,1,256,512]{3,2,1,0:T(8,128)(2,1)}), bf16[1,1,256,2048]{3,2,1,0:T(8,128)(2,1)}) %all-gather.5.cloned.1.call-update) | async-done | bytes 1048592 | tf_op jit(solution)/shard_map/all_gather | solution.py:49
  40.9 8.2 %multiply_reduce_fusion.1 = (f32[2048]{0:T(1024)S(1)}, f32[256]{0:T(256)S(1)}, f32[256,2048]{1,0:T(8,128)}) fusion(f32[512,2048]{1,0:T(8,128)} %get-tuple-element.14, f32[2048]{0:T(1024)S(1)} %bitcast.51, bf16[1,2048,2048]{2,1,0:T(8,128)(2,1)} %param.9, bf16[1,1,256,2048]{3,2,1,0:T(8,128)(2,1)} %all-gather.5.cloned.1.call-done), kind=kOutput, calls=%fused_computation.19 | convolution fusion | flops 2150102784 | bytes 13648896 | tf_op jit(solution)/shard_map/dot_general | solution.py:67
  49.1 10.4 %psum.22 = f32[256,1]{0,1:T(1,128)S(1)} all-reduce(f32[256,1]{0,1:T(1,128)S(1)} %bitcast.65), channel_id=1, replica_groups=mesh['dp'=4,'pipe'=2,'tensor'=4] {'tensor'}, use_global_device_ids=true, to_apply=%region_3.4 | all-reduce | flops 256 | bytes 2048 | tf_op jit(solution)/shard_map/psum | solution.py:72
  59.5 10.6 %all-gather.7.cloned.1.call-done = bf16[1,1,256,2048]{3,2,1,0:T(8,128)(2,1)} async-done(((bf16[1,1,256,512]{3,2,1,0:T(8,128)(2,1)}), bf16[1,1,256,2048]{3,2,1,0:T(8,128)(2,1)}) %all-gather.7.cloned.1.call-update) | async-done | bytes 1048592 | tf_op jit(solution)/shard_map/all_gather | solution.py:49
  70.2 1.6 %pad_maximum_fusion = bf16[512,2048]{1,0:T(8,128)(2,1)S(1)} fusion(bf16[256,2048]{1,0:T(8,128)(2,1)} %bitcast.47, bf16[256,2048]{1,0:T(8,128)(2,1)S(1)} %bitcast.49), kind=kLoop, calls=%fused_computation.12 | loop fusion | flops 4194304 | bytes 4194304 | tf_op jit(solution)/shard_map/concatenate | solution.py:52
  72.7 3.5 %fusion.7 = bf16[256,2048]{1,0:T(8,128)(2,1)} fusion(f32[256,2048]{1,0:T(8,128)} %get-tuple-element.23, f32[512,2048]{1,0:T(8,128)S(1)} %copy-done.1, f32[256]{0:T(256)S(1)} %bitcast.61, f32[2048]{0:T(1024)S(1)} %bitcast.52, f32[256]{0:T(256)S(1)} %bitcast.63, bf16[1,1,512,2048]{3,2,1,0:T(8,128)(2,1)} %param.6), kind=kLoop, calls=%fused_computation.17 | loop fusion | flops 3670016 | bytes 6301696 | tf_op jit(solution)/shard_map/convert_element_type | solution.py:76
  76.1 1.3 constant_dynamic-slice_fusion.1
  78.5 1.5 collective-permute-start
  80.0 4.4 %fusion.8 = f32[2048,1024]{1,0:T(8,128)S(1)} fusion(bf16[512,2048]{1,0:T(8,128)(2,1)} %get-tuple-element.6, bf16[512,512]{1,0:T(8,128)(2,1)} %get-tuple-element.17, bf16[512,512]{1,0:T(8,128)(2,1)} %get-tuple-element.18), kind=kOutput, calls=%fused_computation.22 | convolution fusion | flops 2149580800 | bytes 11534336 | tf_op jit(solution)/shard_map/dot_general | solution.py:83
  84.4 2.6 %convolution_add_fusion = f32[2048,1024]{1,0:T(8,128)S(1)} fusion(f32[2048,1024]{1,0:T(8,128)S(1)} %fusion.8, bf16[512,2048]{1,0:T(8,128)(2,1)S(1)} %collective-permute-done.1, bf16[512,1024]{1,0:T(8,128)(2,1)S(1)} %collective-permute-done.2), kind=kOutput, calls=%fused_computation.10 | convolution fusion | flops 2149580800 | bytes 19922944 | tf_op jit(solution)/shard_map/dot_general | solution.py:85
  87.1 3.2 %copy-done = f32[2048,1024]{1,0:T(8,128)} copy-done((f32[2048,1024]{1,0:T(8,128)}, f32[2048,1024]{1,0:T(8,128)S(1)}, u32[]{:S(2)}) %copy-start) | copy-done | bytes 8388632
  90.3 1.6 %dynamic-slice_convert_fusion = bf16[2048,512]{1,0:T(8,128)(2,1)} fusion(f32[2048,1024]{1,0:T(8,128)S(1)} %convolution_add_fusion, s32[]{:T(128)S(6)} %select_n.51), kind=kLoop, calls=%fused_computation.8 | loop fusion | bytes 4194308 | tf_op jit(solution)/shard_map/convert_element_type | solution.py:95
  91.9 1.5 collective-permute-start.4
  93.4 2.7 %multiply_reduce_fusion = (f32[2048]{0:T(1024)S(1)}, f32[256]{0:T(256)S(1)}, f32[256,2048]{1,0:T(8,128)S(1)}) fusion(f32[512,2048]{1,0:T(8,128)S(1)} %copy-done.2, f32[2048]{0:T(1024)S(1)} %bitcast.53, bf16[256,2048]{1,0:T(8,128)(2,1)S(1)} %bitcast.48, bf16[1,2048,2048]{2,1,0:T(8,128)(2,1)S(1)} %bitcast.67), kind=kOutput, calls=%fused_computation.18 | convolution fusion | flops 2150102784 | bytes 13648896 | tf_op jit(solution)/shard_map/dot_general | solution.py:67
  96.1 10.3 %psum.23 = f32[256,1]{0,1:T(1,128)S(1)} all-reduce(f32[256,1]{0,1:T(1,128)S(1)} %bitcast.64), channel_id=1, replica_groups=mesh['dp'=4,'pipe'=2,'tensor'=4] {'tensor'}, use_global_device_ids=true, to_apply=%region_5.6 | all-reduce | flops 256 | bytes 2048 | tf_op jit(solution)/shard_map/psum | solution.py:72
  106.3 2.4 %fusion.6 = bf16[256,2048]{1,0:T(8,128)(2,1)S(1)} fusion(f32[256,2048]{1,0:T(8,128)S(1)} %get-tuple-element.24, f32[512,2048]{1,0:T(8,128)} %get-tuple-element.14, f32[256]{0:T(256)S(1)} %bitcast.60, f32[256]{0:T(256)S(1)} %bitcast.62, bf16[1,1,512,2048]{3,2,1,0:T(8,128)(2,1)} %param.6, f32[2048]{0:T(1024)S(1)} %bitcast.54), kind=kLoop, calls=%fused_computation.15 | loop fusion | flops 3670016 | bytes 6301696 | tf_op jit(solution)/shard_map/convert_element_type | solution.py:76
  108.8 1.3 collective-permute-start.3
  112.7 27.7 %collective-permute-done.6 = f32[2048]{0:T(1024)S(1)} collective-permute-done((f32[2048]{0:T(1024)S(1)}, f32[2048]{0:T(1024)S(1)}, u32[]{:S(2)}, u32[]{:S(2)}) %collective-permute-start.6) | collective-permute-done | bytes 8224 | tf_op jit(solution)/shard_map/ppermute | solution.py:18
  141.1 2.7 %maximum_bitcast_fusion = bf16[1,1,512,2048]{3,2,1,0:T(8,128)(2,1)} fusion(bf16[256,2048]{1,0:T(8,128)(2,1)S(1)} %collective-permute-done.3, bf16[256,2048]{1,0:T(8,128)(2,1)} %collective-permute-done), kind=kLoop, calls=%fused_computation.13 | loop fusion | flops 4194304 | bytes 4194304 | tf_op jit(solution)/shard_map/broadcast_in_dim | solution.py:111
  143.8 4.9 %fusion.5 = bf16[1,2048,512]{2,1,0:T(8,128)(2,1)} fusion(bf16[2048,512]{1,0:T(8,128)(2,1)} %collective-permute-done.4, f32[2048,1024]{1,0:T(8,128)} %copy-done, s32[]{:T(128)S(6)} %select_n.52), kind=kLoop, calls=%fused_computation.11 | loop fusion | flops 3145728 | bytes 8388612 | tf_op jit(solution)/shard_map/broadcast_in_dim | solution.py:111
  (42 shorter events, 6.9 us)
Async XLA Ops:
  7.2 19.2 %copy-start.3 = (bf16[1,1,512,2048]{3,2,1,0:T(8,128)(2,1)S(1)}, bf16[1,1,512,2048]{3,2,1,0:T(8,128)(2,1)}, u32[]{:S(2)}) copy-start(bf16[1,1,512,2048]{3,2,1,0:T(8,128)(2,1)} %param.5) | copy-start | bytes 6291460
  7.2 33.7 %all-gather.5.cloned.1.call-start = ((), (), s32[]{:S(2)}) async-start(), calls=%async_computation | async-start | bytes 1310720 | tf_op jit(solution)/shard_map/all_gather | solution.py:49
  9.2 60.9 %all-gather.7.cloned.1.call-start = ((), (), s32[]{:S(2)}) async-start(), calls=%async_computation.1 | async-start | bytes 1310720 | tf_op jit(solution)/shard_map/all_gather | solution.py:49
  29.6 54.8 %collective-permute-start.1 = (bf16[512,2048]{1,0:T(8,128)(2,1)}, bf16[512,2048]{1,0:T(8,128)(2,1)S(1)}, u32[]{:S(2)}, u32[]{:S(2)}) collective-permute-start(bf16[512,2048]{1,0:T(8,128)(2,1)} %get-tuple-element.6), channel_id=1, source_target_pairs={{0,8},{8,0},{16,24},{24,16},{1,9},{9,1},{17,25},{25,17},{2,10},{10... | collective-permute-start | bytes 6291464 | tf_op jit(solution)/shard_map/ppermute | solution.py:23
  40.9 29.3 %copy-start.5 = (bf16[1,1,256,2048]{3,2,1,0:T(8,128)(2,1)S(1)}, bf16[1,1,256,2048]{3,2,1,0:T(8,128)(2,1)}, u32[]{:S(2)}) copy-start(bf16[1,1,256,2048]{3,2,1,0:T(8,128)(2,1)} %all-gather.5.cloned.1.call-done) | copy-start | bytes 3145732
  70.2 2.5 %copy-start.1 = (f32[512,2048]{1,0:T(8,128)S(1)}, f32[512,2048]{1,0:T(8,128)}, u32[]{:S(2)}) copy-start(f32[512,2048]{1,0:T(8,128)} %get-tuple-element.14) | copy-start | bytes 12582916
  78.5 5.9 %collective-permute-start.2 = (bf16[512,1024]{1,0:T(8,128)(2,1)}, bf16[512,1024]{1,0:T(8,128)(2,1)S(1)}, u32[]{:S(2)}, u32[]{:S(2)}) collective-permute-start(bf16[512,1024]{1,0:T(8,128)(2,1)} %pad_maximum_fusion.1), channel_id=1, source_target_pairs={{0,8},{8,0},{16,24},{24,16},{1,9},{9,1},{17,25},{25,17},{2,10},{10... | collective-permute-start | bytes 3145736 | tf_op jit(solution)/shard_map/ppermute | solution.py:23
  78.5 62.6 %collective-permute-start = (bf16[256,2048]{1,0:T(8,128)(2,1)}, bf16[256,2048]{1,0:T(8,128)(2,1)}, u32[]{:S(2)}, u32[]{:S(2)}) collective-permute-start(bf16[256,2048]{1,0:T(8,128)(2,1)} %fusion.7), channel_id=1, source_target_pairs={{4,0},{5,1},{6,2},{7,3},{12,8},{13,9},{14,10},{15,11},{20,16},{21,... | collective-permute-start | bytes 3145736 | tf_op jit(solution)/shard_map/ppermute | solution.py:13
  80.0 13.4 %slice-start = ((s8[8388608]{0:T(1024)(128)(4,1)}), s8[4194304]{0:T(1024)(128)(4,1)S(1)}, s32[]{:S(2)}) async-start(s8[8388608]{0:T(1024)(128)(4,1)} %bitcast.66), calls=%async_computation.2 | async-start | bytes 8388608
  84.4 9.0 %slice-start.1 = ((s8[8388608]{0:T(1024)(128)(4,1)}), s8[4194304]{0:T(1024)(128)(4,1)S(1)}, s32[]{:S(2)}) async-start(s8[8388608]{0:T(1024)(128)(4,1)} %bitcast.66), calls=%async_computation.3 | async-start | bytes 8388608
  84.4 9.0 %copy-start.4 = (bf16[1,1,256,2048]{3,2,1,0:T(8,128)(2,1)S(1)}, bf16[1,1,256,2048]{3,2,1,0:T(8,128)(2,1)}, u32[]{:S(2)}) copy-start(bf16[1,1,256,2048]{3,2,1,0:T(8,128)(2,1)} %all-gather.7.cloned.1.call-done) | copy-start | bytes 3145732
  87.0 3.2 %copy-start = (f32[2048,1024]{1,0:T(8,128)}, f32[2048,1024]{1,0:T(8,128)S(1)}, u32[]{:S(2)}) copy-start(f32[2048,1024]{1,0:T(8,128)S(1)} %convolution_add_fusion) | copy-start | bytes 25165828
  90.3 3.1 %copy-start.2 = (f32[512,2048]{1,0:T(8,128)S(1)}, f32[512,2048]{1,0:T(8,128)}, u32[]{:S(2)}) copy-start(f32[512,2048]{1,0:T(8,128)} %get-tuple-element.14) | copy-start | bytes 12582916
  91.9 51.9 %collective-permute-start.4 = (bf16[2048,512]{1,0:T(8,128)(2,1)}, bf16[2048,512]{1,0:T(8,128)(2,1)}, u32[]{:S(2)}, u32[]{:S(2)}) collective-permute-start(bf16[2048,512]{1,0:T(8,128)(2,1)} %dynamic-slice_convert_fusion), channel_id=1, source_target_pairs={{0,16},{8,24},{16,0},{24,8},{1,17},{9,25},{17,1},{25,9},{2,18},{10... | collective-permute-start | bytes 6291464 | tf_op jit(solution)/shard_map/ppermute | solution.py:18
  108.8 32.3 %collective-permute-start.3 = (bf16[256,2048]{1,0:T(8,128)(2,1)S(1)}, bf16[256,2048]{1,0:T(8,128)(2,1)S(1)}, u32[]{:S(2)}, u32[]{:S(2)}) collective-permute-start(bf16[256,2048]{1,0:T(8,128)(2,1)S(1)} %fusion.6), channel_id=1, source_target_pairs={{4,0},{5,1},{6,2},{7,3},{12,8},{13,9},{14,10},{15,11},{20,16},{21,... | collective-permute-start | bytes 3145736 | tf_op jit(solution)/shard_map/ppermute | solution.py:13
  110.1 1.2 collective-permute-start.5
  111.4 29.0 %collective-permute-start.6 = (f32[2048]{0:T(1024)S(1)}, f32[2048]{0:T(1024)S(1)}, u32[]{:S(2)}, u32[]{:S(2)}) collective-permute-start(f32[2048]{0:T(1024)S(1)} %add.94), channel_id=1, source_target_pairs={{0,16},{8,24},{16,0},{24,8},{1,17},{9,25},{17,1},{25,9},{2,18},{10... | collective-permute-start | bytes 24584 | tf_op jit(solution)/shard_map/ppermute | solution.py:18
Sparse Core Ops, SparseCore 0:
  10.2 30.6 all-gather.4
  42.5 27.6 all-gather.6

commit v8 on v7

--- a/solution.py
+++ b/solution.py
@@ -23,6 +23,18 @@
     return lax.ppermute(block, "dp", [(i, i ^ 1) for i in range(n)])
 
 
+def gather_columns(block):
+    n = lax.axis_size("tensor")
+    me = lax.axis_index("tensor")
+    rows, width = block.shape
+    full = jnp.zeros((rows, width * n), block.dtype)
+    full = lax.dynamic_update_slice(full, block, (0, me * width))
+    for d in range(1, n):
+        got = shifted(block, "tensor", d)
+        full = lax.dynamic_update_slice(full, got, (0, ((me - d) % n) * width))
+    return full
+
+
 def on_device(layer_input, output_grad, kv_grad, norm_gain, kv_weight):
     rows = layer_input[0, 0]
     grad_out = output_grad[0, 0]
@@ -45,16 +57,18 @@
     hidden_partner = to_partner(hidden)
 
     step = seq // CHUNKS
-    pieces = [
-        lax.all_gather(grad_kv[c * step:(c + 1) * step], "tensor", axis=1, tiled=True)
-        for c in range(CHUNKS)
-    ]
-    piece = jnp.concatenate(pieces, axis=0)
+    pieces = [gather_columns(grad_kv[c * step:(c + 1) * step]) for c in range(CHUNKS)]
 
-    def cols_of(p):
+    def cols_of(parts, p):
         return jnp.concatenate(
-            [lax.dynamic_slice_in_dim(piece, (2 * g + p) * kv_block, kv_block, axis=1) for g in range(groups)],
-            axis=1,
+            [
+                jnp.concatenate(
+                    [lax.dynamic_slice_in_dim(q, (2 * g + p) * kv_block, kv_block, axis=1) for g in range(groups)],
+                    axis=1,
+                )
+                for q in parts
+            ],
+            axis=0,
         )
 
 
@@ -77,9 +91,9 @@
         inputs_grad.append(from_behind(input_grad, "pipe", -1))
         gain_part = gain_part + jnp.sum(row_total * normed_c, axis=0)
         if c == 0:
-            _, (h_own, piece) = lax.optimization_barrier((input_grad, (hidden, piece)))
-            cols_partner = to_partner(cols_of(1 - parity))
-            cols_own = cols_of(parity)
+            _, (h_own, parts) = lax.optimization_barrier((input_grad, (hidden, pieces)))
+            cols_partner = to_partner(cols_of(parts, 1 - parity))
+            cols_own = cols_of(parts, parity)
             pair = lax.dot_general(
                 h_own, cols_own, (((0,), (0,)), ((), ())), preferred_element_type=jnp.float32
             ) + lax.dot_general(

time: 156 us -> 161 us (1.032)
  waiting for transfers between devices: 51.5 us -> 31.1 us
  starting transfers between devices: 5.64 us -> 25.5 us
  between operations: 14.2 us -> 0.99 us
  blocking collectives: 34.2 us -> 45.5 us
  local copies, waits for them, and re-layouts: 9.23 us -> 16.2 us
    all_gather x2 -> x0, waiting for transfers between devices: 21.9 us -> none  [on_device(): lax.all_gather(grad_kv[c * step:(c + 1) * step], 'tensor', axis=1, tiled=...]
    ppermute x2 -> x8, starting transfers between devices: 2.73 us -> 22.5 us  [shifted(): return lax.ppermute(block, axis, [(i, (i + shift) % n) for i in range(n)])]
    psum x1, blocking collectives: 13.5 us -> 26.8 us  [on_device(): lax.psum(jnp.sum(values * values, axis=1, keepdims=True), 'tensor')]
    dynamic_update_slice x0 -> x8, local copies, waits for them, and re-layouts: none -> 7.04 us  [the longest x6 6.99 us: gather_columns(): full = lax.dynamic_update_slice(full, got, (0, (me - d) % n * width))]
    psum x2, blocking collectives: 20.6 us -> 18.7 us  [on_device(): lax.psum(jnp.sum(scaled * normed_c, axis=1, keepdims=True), 'tensor')]
    dot_general x1, matrix products: 2.62 us -> 4.43 us  [on_device(): lax.dot_general(hidden_partner, cols_partner, (((0,), (0,)), ((), ())), p...]
    dot_general x1, matrix products: 4.38 us -> 2.58 us  [on_device(): lax.dot_general(h_own, cols_own, (((0,), (0,)), ((), ())), preferred_elem...]
    ppermute x2 -> x8, waiting for transfers between devices: 27.7 us -> 28.5 us  [shifted(): return lax.ppermute(block, axis, [(i, (i + shift) % n) for i in range(n)])]
  transfers between devices with their start and end apart: 9 -> 13, of which waited for: 4 -> 3; matrix products, arithmetic and copies ran while one was open for 25% -> 29% of each run, Pallas kernels for 0% -> 0%
where the time goes in v8:
time: 161 us; the launch traced here: 160 us
  blocking collectives  45.5 us (28%)
  waiting for transfers between devices  31.1 us (19%)
  starting transfers between devices  25.5 us (16%)
  other arithmetic  23 us (14%)
  matrix products  17.8 us (11%)
  local copies, waits for them, and re-layouts  16.2 us (10%)
    ppermute x8, waiting for transfers between devices, shifted(): return lax.ppermute(block, axis, [(i, (i + shift) % n) for i in range(n)])  28.5 us
    psum x1, blocking collectives, on_device(): lax.psum(jnp.sum(values * values, axis=1, keepdims=True), 'tensor')  26.8 us
    ppermute x8, starting transfers between devices, shifted(): return lax.ppermute(block, axis, [(i, (i + shift) % n) for i in range(n)])  22.5 us
    psum x2, blocking collectives, on_device(): lax.psum(jnp.sum(scaled * normed_c, axis=1, keepdims=True), 'tensor')  18.7 us
    dot_general x2, matrix products, on_device(): lax.dot_general(block, weight, (((1,), (1,)), ((), ())), preferred_elemen...  10.8 us
    broadcast_in_dim x2, other arithmetic, on_device(): return (upstream[None, None], weight_total[None], gain_total[None])  7.65 us
    dynamic_update_slice x6, local copies, waits for them, and re-layouts, gather_columns(): full = lax.dynamic_update_slice(full, got, (0, (me - d) % n * width))  6.99 us
    convert_element_type x2, other arithmetic, on_device(): input_grad = (grad_out[lo:lo + step].astype(jnp.float32) + rstd[lo:lo + s...  6.61 us
  transfers between devices with their start and end apart: 13, of which 3 were waited for; matrix products, arithmetic and copies ran while one was open for 29% of the time, Pallas kernels for 0%

profile of v8, /device:TPU:0, one launch (start us, length us, event | category | flops | bytes accessed | tf_op | source)
XLA Modules:
  0.0 160.1 jit_solution(17791181859018277458)
XLA Ops:
  0.6 1.9 %slice_bitcast_fusion = (bf16[256,512]{1,0:T(8,128)(2,1)}, bf16[256,512]{1,0:T(8,128)(2,1)}) fusion(bf16[1,1,512,512]{3,2,1,0:T(8,128)(2,1)} %param.7), kind=kLoop, calls=%fused_computation.29 | loop fusion | bytes 1048576 | tf_op jit(solution)/shard_map/slice | solution.py:60
  2.6 3.0 %collective-permute-start = (bf16[256,512]{1,0:T(8,128)(2,1)}, bf16[256,512]{1,0:T(8,128)(2,1)}, u32[]{:S(2)}, u32[]{:S(2)}) collective-permute-start(bf16[256,512]{1,0:T(8,128)(2,1)} %get-tuple-element.26), channel_id=1, source_target_pairs={{0,1},{1,2},{2,3},{3,0},{4,5},{5,6},{6,7},{7,4},{8,9},{9,10},{10,1... | collective-permute-start | bytes 786440 | tf_op jit(solution)/shard_map/ppermute | solution.py:18
  5.6 2.6 %collective-permute-start.1 = (bf16[256,512]{1,0:T(8,128)(2,1)}, bf16[256,512]{1,0:T(8,128)(2,1)}, u32[]{:S(2)}, u32[]{:S(2)}) collective-permute-start(bf16[256,512]{1,0:T(8,128)(2,1)} %get-tuple-element.26), channel_id=1, source_target_pairs={{0,2},{1,3},{2,0},{3,1},{4,6},{5,7},{6,4},{7,5},{8,10},{9,11},{10,... | collective-permute-start | bytes 786440 | tf_op jit(solution)/shard_map/ppermute | solution.py:18
  11.2 2.1 %fusion.4 = f32[512]{0:T(512)S(1)} fusion(bf16[1,1,512,2048]{3,2,1,0:T(8,128)(2,1)} %param.5), kind=kLoop, calls=%fused_computation.6 | loop fusion | flops 3145216 | bytes 2099200 | tf_op jit(solution)/shard_map/reduce_sum | solution.py:53
  13.3 26.8 %psum.21 = f32[512,1]{0,1:T(1,128)S(1)} all-reduce(f32[512,1]{0,1:T(1,128)S(1)} %bitcast.57), channel_id=1, replica_groups=mesh['dp'=4,'pipe'=2,'tensor'=4] {'tensor'}, use_global_device_ids=true, to_apply=%region_1.2 | all-reduce | flops 512 | bytes 4096 | tf_op jit(solution)/shard_map/psum | solution.py:53
  41.3 4.2 %multiply_convert_fusion = (bf16[512,2048]{1,0:T(8,128)(2,1)S(1)}, f32[512,2048]{1,0:T(8,128)}) fusion(f32[2048]{0:T(1024)S(1)} %bitcast.50, f32[512]{0:T(512)S(1)} %bitcast.56, bf16[1,1,512,2048]{3,2,1,0:T(8,128)(2,1)} %param.5), kind=kLoop, calls=%fused_computation.9 | loop fusion | flops 4194304 | bytes 8398848 | tf_op jit(solution)/shard_map/convert_element_type | solution.py:56
  45.7 11.8 %collective-permute-start.6 = (bf16[256,512]{1,0:T(8,128)(2,1)}, bf16[256,512]{1,0:T(8,128)(2,1)}, u32[]{:S(2)}, u32[]{:S(2)}) collective-permute-start(bf16[256,512]{1,0:T(8,128)(2,1)} %get-tuple-element.25), channel_id=1, source_target_pairs={{0,3},{1,0},{2,1},{3,2},{4,7},{5,4},{6,5},{7,6},{8,11},{9,8},{10,9... | collective-permute-start | bytes 786440 | tf_op jit(solution)/shard_map/ppermute | solution.py:18
  57.5 1.7 %constant_dynamic-update-slice_fusion.6 = bf16[256,2048]{1,0:T(8,128)(2,1)} fusion(bf16[256,2048]{1,0:T(8,128)(2,1)} %copy-done.2, bf16[256,512]{1,0:T(8,128)(2,1)} %collective-permute-done, s32[]{:T(128)S(6)} %select_n.84), kind=kLoop, calls=%fused_computation.45 | loop fusion | bytes 524292 | tf_op jit(solution)/shard_map/dynamic_update_slice | solution.py:34
  59.2 1.7 %constant_dynamic-update-slice_fusion.5 = bf16[256,2048]{1,0:T(8,128)(2,1)} fusion(bf16[256,2048]{1,0:T(8,128)(2,1)} %constant_dynamic-update-slice_fusion.6, bf16[256,512]{1,0:T(8,128)(2,1)} %collective-permute-done.1, s32[]{:T(128)S(6)} %select_n.86), kind=kLoop, calls=%fused_computation.44 | loop fusion | bytes 524292 | tf_op jit(solution)/shard_map/dynamic_update_slice | solution.py:34
  60.8 1.7 %constant_dynamic-update-slice_fusion.4 = bf16[256,2048]{1,0:T(8,128)(2,1)} fusion(bf16[256,2048]{1,0:T(8,128)(2,1)} %constant_dynamic-update-slice_fusion.5, bf16[256,512]{1,0:T(8,128)(2,1)} %collective-permute-done.2, s32[]{:T(128)S(6)} %select_n.88), kind=kLoop, calls=%fused_computation.43 | loop fusion | bytes 524292 | tf_op jit(solution)/shard_map/dynamic_update_slice | solution.py:34
  62.5 8.2 %multiply_reduce_fusion.1 = (f32[2048]{0:T(1024)S(1)}, f32[256]{0:T(256)S(1)}, f32[256,2048]{1,0:T(8,128)}) fusion(f32[512,2048]{1,0:T(8,128)} %get-tuple-element.16, f32[2048]{0:T(1024)S(1)} %bitcast.51, bf16[256,2048]{1,0:T(8,128)(2,1)} %constant_dynamic-update-slice_fusion.4, bf16[1,2048,2048]{2,1,0:T(8,128)(2,1)} %param.9), kind=kOutput, calls=%fused_computation.18 | convolution fusion | flops 2150102784 | bytes 13648896 | tf_op jit(solution)/shard_map/dot_general | solution.py:81
  70.7 9.7 %psum.22 = f32[256,1]{0,1:T(1,128)S(1)} all-reduce(f32[256,1]{0,1:T(1,128)S(1)} %bitcast.65), channel_id=1, replica_groups=mesh['dp'=4,'pipe'=2,'tensor'=4] {'tensor'}, use_global_device_ids=true, to_apply=%region_3.4 | all-reduce | flops 256 | bytes 2048 | tf_op jit(solution)/shard_map/psum | solution.py:86
  82.4 4.2 %fusion.7 = bf16[256,2048]{1,0:T(8,128)(2,1)} fusion(f32[256,2048]{1,0:T(8,128)} %get-tuple-element.29, f32[512,2048]{1,0:T(8,128)} %get-tuple-element.16, f32[256]{0:T(256)S(1)} %bitcast.60, f32[2048]{0:T(1024)S(1)} %bitcast.52, f32[256]{0:T(256)S(1)} %bitcast.63, bf16[1,1,512,2048]{3,2,1,0:T(8,128)(2,1)} %param.6), kind=kLoop, calls=%fused_computation.16 | loop fusion | flops 3670016 | bytes 6301696 | tf_op jit(solution)/shard_map/convert_element_type | solution.py:90
  88.7 1.6 %collective-permute-start.3 = (bf16[256,2048]{1,0:T(8,128)(2,1)}, bf16[256,2048]{1,0:T(8,128)(2,1)}, u32[]{:S(2)}, u32[]{:S(2)}) collective-permute-start(bf16[256,2048]{1,0:T(8,128)(2,1)} %fusion.7), channel_id=1, source_target_pairs={{4,0},{5,1},{6,2},{7,3},{12,8},{13,9},{14,10},{15,11},{20,16},{21,... | collective-permute-start | bytes 3145736 | tf_op jit(solution)/shard_map/ppermute | solution.py:13
  91.7 4.4 %fusion.17 = f32[2048,1024]{1,0:T(8,128)S(1)} fusion(bf16[512,2048]{1,0:T(8,128)(2,1)} %collective-permute-done.7, bf16[512,1024]{1,0:T(8,128)(2,1)} %collective-permute-done.8), kind=kOutput, calls=%fused_computation.52 | convolution fusion | flops 2147483648 | bytes 11534336 | tf_op jit(solution)/shard_map/dot_general | solution.py:99
  96.2 2.6 %convolution_add_fusion = f32[2048,1024]{1,0:T(8,128)S(1)} fusion(f32[2048,1024]{1,0:T(8,128)S(1)} %fusion.17, bf16[512,2048]{1,0:T(8,128)(2,1)S(1)} %get-tuple-element.7, bf16[256,512]{1,0:T(8,128)(2,1)S(1)} %copy-done.6, bf16[256,512]{1,0:T(8,128)(2,1)S(1)} %get-tuple-element.21, bf16[256,512]{1,0:T(8,128)(2,1)S(1)} %copy-done.7, ...), kind=kOutput, calls=%fused_computation.10 | convolution fusion | flops 2153775104 | bytes 19922944 | tf_op jit(solution)/shard_map/dot_general | solution.py:97
  98.8 3.2 %copy-done = f32[2048,1024]{1,0:T(8,128)} copy-done((f32[2048,1024]{1,0:T(8,128)}, f32[2048,1024]{1,0:T(8,128)S(1)}, u32[]{:S(2)}) %copy-start) | copy-done | bytes 8388632
  102.0 1.6 %dynamic-slice_convert_fusion = bf16[2048,512]{1,0:T(8,128)(2,1)} fusion(f32[2048,1024]{1,0:T(8,128)S(1)} %convolution_add_fusion, s32[]{:T(128)S(6)} %select_n.96), kind=kLoop, calls=%fused_computation.8 | loop fusion | bytes 4194308 | tf_op jit(solution)/shard_map/convert_element_type | solution.py:109
  105.1 2.7 %multiply_reduce_fusion = (f32[2048]{0:T(1024)S(1)}, f32[256]{0:T(256)S(1)}, f32[256,2048]{1,0:T(8,128)S(1)}) fusion(f32[512,2048]{1,0:T(8,128)S(1)} %copy-done.1, f32[2048]{0:T(1024)S(1)} %bitcast.53, bf16[256,2048]{1,0:T(8,128)(2,1)S(1)} %constant_dynamic-update-slice_fusion, bf16[1,2048,2048]{2,1,0:T(8,128)(2,1)S(1)} %bitcast.67), kind=kOutput, calls=%fused_computation.17 | convolution fusion | flops 2150102784 | bytes 13648896 | tf_op jit(solution)/shard_map/dot_general | solution.py:81
  107.8 9.0 %psum.23 = f32[256,1]{0,1:T(1,128)S(1)} all-reduce(f32[256,1]{0,1:T(1,128)S(1)} %bitcast.64), channel_id=1, replica_groups=mesh['dp'=4,'pipe'=2,'tensor'=4] {'tensor'}, use_global_device_ids=true, to_apply=%region_5.6 | all-reduce | flops 256 | bytes 2048 | tf_op jit(solution)/shard_map/psum | solution.py:86
  116.8 2.4 %fusion.6 = bf16[256,2048]{1,0:T(8,128)(2,1)S(1)} fusion(f32[256,2048]{1,0:T(8,128)S(1)} %get-tuple-element.30, f32[512,2048]{1,0:T(8,128)} %get-tuple-element.16, f32[256]{0:T(256)S(1)} %bitcast.61, f32[256]{0:T(256)S(1)} %bitcast.62, bf16[1,1,512,2048]{3,2,1,0:T(8,128)(2,1)} %param.6, f32[2048]{0:T(1024)S(1)} %bitcast.54), kind=kLoop, calls=%fused_computation.14 | loop fusion | flops 3670016 | bytes 6301696 | tf_op jit(solution)/shard_map/convert_element_type | solution.py:90
  123.2 28.5 %collective-permute-done.12 = f32[2048]{0:T(1024)S(1)} collective-permute-done((f32[2048]{0:T(1024)S(1)}, f32[2048]{0:T(1024)S(1)}, u32[]{:S(2)}, u32[]{:S(2)}) %collective-permute-start.12) | collective-permute-done | bytes 8224 | tf_op jit(solution)/shard_map/ppermute | solution.py:18
  152.4 2.8 %maximum_bitcast_fusion = bf16[1,1,512,2048]{3,2,1,0:T(8,128)(2,1)} fusion(bf16[256,2048]{1,0:T(8,128)(2,1)S(1)} %collective-permute-done.9, bf16[256,2048]{1,0:T(8,128)(2,1)} %collective-permute-done.3), kind=kLoop, calls=%fused_computation.12 | loop fusion | flops 4194304 | bytes 4194304 | tf_op jit(solution)/shard_map/broadcast_in_dim | solution.py:125
  155.2 4.9 %fusion.5 = bf16[1,2048,512]{2,1,0:T(8,128)(2,1)} fusion(bf16[2048,512]{1,0:T(8,128)(2,1)} %collective-permute-done.10, f32[2048,1024]{1,0:T(8,128)} %copy-done, s32[]{:T(128)S(6)} %select_n.97), kind=kLoop, calls=%fused_computation.11 | loop fusion | flops 3145728 | bytes 8388612 | tf_op jit(solution)/shard_map/broadcast_in_dim | solution.py:125
  (63 shorter events, 15.9 us)
Async XLA Ops:
  0.6 39.6 %copy-start.4 = (bf16[1,1,512,512]{3,2,1,0:T(8,128)(2,1)S(1)}, bf16[1,1,512,512]{3,2,1,0:T(8,128)(2,1)}, u32[]{:S(2)}) copy-start(bf16[1,1,512,512]{3,2,1,0:T(8,128)(2,1)} %param.7) | copy-start | bytes 1572868
  2.6 43.2 %collective-permute-start = (bf16[256,512]{1,0:T(8,128)(2,1)}, bf16[256,512]{1,0:T(8,128)(2,1)}, u32[]{:S(2)}, u32[]{:S(2)}) collective-permute-start(bf16[256,512]{1,0:T(8,128)(2,1)} %get-tuple-element.26), channel_id=1, source_target_pairs={{0,1},{1,2},{2,3},{3,0},{4,5},{5,6},{6,7},{7,4},{8,9},{9,10},{10,1... | collective-permute-start | bytes 786440 | tf_op jit(solution)/shard_map/ppermute | solution.py:18
  5.6 53.6 %collective-permute-start.1 = (bf16[256,512]{1,0:T(8,128)(2,1)}, bf16[256,512]{1,0:T(8,128)(2,1)}, u32[]{:S(2)}, u32[]{:S(2)}) collective-permute-start(bf16[256,512]{1,0:T(8,128)(2,1)} %get-tuple-element.26), channel_id=1, source_target_pairs={{0,2},{1,3},{2,0},{3,1},{4,6},{5,7},{6,4},{7,5},{8,10},{9,11},{10,... | collective-permute-start | bytes 786440 | tf_op jit(solution)/shard_map/ppermute | solution.py:18
  8.2 52.7 %collective-permute-start.2 = (bf16[256,512]{1,0:T(8,128)(2,1)}, bf16[256,512]{1,0:T(8,128)(2,1)}, u32[]{:S(2)}, u32[]{:S(2)}) collective-permute-start(bf16[256,512]{1,0:T(8,128)(2,1)} %get-tuple-element.26), channel_id=1, source_target_pairs={{0,3},{1,0},{2,1},{3,2},{4,7},{5,4},{6,5},{7,6},{8,11},{9,8},{10,9... | collective-permute-start | bytes 786440 | tf_op jit(solution)/shard_map/ppermute | solution.py:18
  9.5 70.9 %collective-permute-start.4 = (bf16[256,512]{1,0:T(8,128)(2,1)}, bf16[256,512]{1,0:T(8,128)(2,1)}, u32[]{:S(2)}, u32[]{:S(2)}) collective-permute-start(bf16[256,512]{1,0:T(8,128)(2,1)} %get-tuple-element.25), channel_id=1, source_target_pairs={{0,1},{1,2},{2,3},{3,0},{4,5},{5,6},{6,7},{7,4},{8,9},{9,10},{10,1... | collective-permute-start | bytes 786440 | tf_op jit(solution)/shard_map/ppermute | solution.py:18
  10.2 71.2 %collective-permute-start.5 = (bf16[256,512]{1,0:T(8,128)(2,1)}, bf16[256,512]{1,0:T(8,128)(2,1)S(1)}, u32[]{:S(2)}, u32[]{:S(2)}) collective-permute-start(bf16[256,512]{1,0:T(8,128)(2,1)} %get-tuple-element.25), channel_id=1, source_target_pairs={{0,2},{1,3},{2,0},{3,1},{4,6},{5,7},{6,4},{7,5},{8,10},{9,11},{10,... | collective-permute-start | bytes 786440 | tf_op jit(solution)/shard_map/ppermute | solution.py:18
  40.3 1.0 copy-start.2
  41.3 4.3 %copy-start.5 = (bf16[1,1,512,512]{3,2,1,0:T(8,128)(2,1)S(1)}, bf16[1,1,512,512]{3,2,1,0:T(8,128)(2,1)}, u32[]{:S(2)}) copy-start(bf16[1,1,512,512]{3,2,1,0:T(8,128)(2,1)} %param.7) | copy-start | bytes 1572868
  45.7 35.7 %collective-permute-start.6 = (bf16[256,512]{1,0:T(8,128)(2,1)}, bf16[256,512]{1,0:T(8,128)(2,1)}, u32[]{:S(2)}, u32[]{:S(2)}) collective-permute-start(bf16[256,512]{1,0:T(8,128)(2,1)} %get-tuple-element.25), channel_id=1, source_target_pairs={{0,3},{1,0},{2,1},{3,2},{4,7},{5,4},{6,5},{7,6},{8,11},{9,8},{10,9... | collective-permute-start | bytes 786440 | tf_op jit(solution)/shard_map/ppermute | solution.py:18
  59.2 32.5 %collective-permute-start.7 = (bf16[512,2048]{1,0:T(8,128)(2,1)S(1)}, bf16[512,2048]{1,0:T(8,128)(2,1)}, u32[]{:S(2)}, u32[]{:S(2)}) collective-permute-start(bf16[512,2048]{1,0:T(8,128)(2,1)S(1)} %get-tuple-element.7), channel_id=1, source_target_pairs={{0,8},{8,0},{16,24},{24,16},{1,9},{9,1},{17,25},{25,17},{2,10},{10... | collective-permute-start | bytes 6291464 | tf_op jit(solution)/shard_map/ppermute | solution.py:23
  82.4 4.2 %copy-start.3 = (bf16[256,2048]{1,0:T(8,128)(2,1)S(1)}, bf16[256,2048]{1,0:T(8,128)(2,1)}, u32[]{:S(2)}) copy-start(bf16[256,2048]{1,0:T(8,128)(2,1)} %constant_dynamic-update-slice_fusion.4) | copy-start | bytes 3145732
  88.7 3.0 %collective-permute-start.8 = (bf16[512,1024]{1,0:T(8,128)(2,1)}, bf16[512,1024]{1,0:T(8,128)(2,1)}, u32[]{:S(2)}, u32[]{:S(2)}) collective-permute-start(bf16[512,1024]{1,0:T(8,128)(2,1)} %maximum_maximum_fusion), channel_id=1, source_target_pairs={{0,8},{8,0},{16,24},{24,16},{1,9},{9,1},{17,25},{25,17},{2,10},{10... | collective-permute-start | bytes 3145736 | tf_op jit(solution)/shard_map/ppermute | solution.py:23
  88.7 7.4 %copy-start.6 = (bf16[256,512]{1,0:T(8,128)(2,1)S(1)}, bf16[256,512]{1,0:T(8,128)(2,1)}, u32[]{:S(2)}) copy-start(bf16[256,512]{1,0:T(8,128)(2,1)} %get-tuple-element.24) | copy-start | bytes 786436
  88.7 7.4 %copy-start.7 = (bf16[256,512]{1,0:T(8,128)(2,1)S(1)}, bf16[256,512]{1,0:T(8,128)(2,1)}, u32[]{:S(2)}) copy-start(bf16[256,512]{1,0:T(8,128)(2,1)} %get-tuple-element.31) | copy-start | bytes 786436
  88.7 7.5 %copy-start.8 = (bf16[256,512]{1,0:T(8,128)(2,1)S(1)}, bf16[256,512]{1,0:T(8,128)(2,1)}, u32[]{:S(2)}) copy-start(bf16[256,512]{1,0:T(8,128)(2,1)} %get-tuple-element.34) | copy-start | bytes 786436
  88.7 63.7 %collective-permute-start.3 = (bf16[256,2048]{1,0:T(8,128)(2,1)}, bf16[256,2048]{1,0:T(8,128)(2,1)}, u32[]{:S(2)}, u32[]{:S(2)}) collective-permute-start(bf16[256,2048]{1,0:T(8,128)(2,1)} %fusion.7), channel_id=1, source_target_pairs={{4,0},{5,1},{6,2},{7,3},{12,8},{13,9},{14,10},{15,11},{20,16},{21,... | collective-permute-start | bytes 3145736 | tf_op jit(solution)/shard_map/ppermute | solution.py:13
  91.7 13.4 %slice-start = ((s8[8388608]{0:T(1024)(128)(4,1)}), s8[4194304]{0:T(1024)(128)(4,1)S(1)}, s32[]{:S(2)}) async-start(s8[8388608]{0:T(1024)(128)(4,1)} %bitcast.66), calls=%async_computation | async-start | bytes 8388608
  96.2 9.0 %slice-start.1 = ((s8[8388608]{0:T(1024)(128)(4,1)}), s8[4194304]{0:T(1024)(128)(4,1)S(1)}, s32[]{:S(2)}) async-start(s8[8388608]{0:T(1024)(128)(4,1)} %bitcast.66), calls=%async_computation.1 | async-start | bytes 8388608
  98.8 3.2 %copy-start = (f32[2048,1024]{1,0:T(8,128)}, f32[2048,1024]{1,0:T(8,128)S(1)}, u32[]{:S(2)}) copy-start(f32[2048,1024]{1,0:T(8,128)S(1)} %convolution_add_fusion) | copy-start | bytes 25165828
  102.0 3.1 %copy-start.1 = (f32[512,2048]{1,0:T(8,128)S(1)}, f32[512,2048]{1,0:T(8,128)}, u32[]{:S(2)}) copy-start(f32[512,2048]{1,0:T(8,128)} %get-tuple-element.16) | copy-start | bytes 12582916
  103.6 51.6 %collective-permute-start.10 = (bf16[2048,512]{1,0:T(8,128)(2,1)}, bf16[2048,512]{1,0:T(8,128)(2,1)}, u32[]{:S(2)}, u32[]{:S(2)}) collective-permute-start(bf16[2048,512]{1,0:T(8,128)(2,1)} %dynamic-slice_convert_fusion), channel_id=1, source_target_pairs={{0,16},{8,24},{16,0},{24,8},{1,17},{9,25},{17,1},{25,9},{2,18},{10... | collective-permute-start | bytes 6291464 | tf_op jit(solution)/shard_map/ppermute | solution.py:18
  119.3 33.1 %collective-permute-start.9 = (bf16[256,2048]{1,0:T(8,128)(2,1)S(1)}, bf16[256,2048]{1,0:T(8,128)(2,1)S(1)}, u32[]{:S(2)}, u32[]{:S(2)}) collective-permute-start(bf16[256,2048]{1,0:T(8,128)(2,1)S(1)} %fusion.6), channel_id=1, source_target_pairs={{4,0},{5,1},{6,2},{7,3},{12,8},{13,9},{14,10},{15,11},{20,16},{21,... | collective-permute-start | bytes 3145736 | tf_op jit(solution)/shard_map/ppermute | solution.py:13
  120.6 1.2 collective-permute-start.11
  121.8 29.9 %collective-permute-start.12 = (f32[2048]{0:T(1024)S(1)}, f32[2048]{0:T(1024)S(1)}, u32[]{:S(2)}, u32[]{:S(2)}) collective-permute-start(f32[2048]{0:T(1024)S(1)} %add.138), channel_id=1, source_target_pairs={{0,16},{8,24},{16,0},{24,8},{1,17},{9,25},{17,1},{25,9},{2,18},{10... | collective-permute-start | bytes 24584 | tf_op jit(solution)/shard_map/ppermute | solution.py:18

commit v9 on v6

--- a/solution.py
+++ b/solution.py
@@ -4,7 +4,7 @@
 from jax.sharding import PartitionSpec as P
 
 EPS = 1e-05
-CHUNKS = 2
+CHUNKS = 1
 
 
 def from_behind(block, axis, distance):

time: 159 us -> 165 us (1.038)
  waiting for transfers between devices: 58.7 us -> 78.5 us
  blocking collectives: 32.3 us -> 23.3 us
  other arithmetic: 22.1 us -> 15 us
  matrix products: 16.7 us -> 20.3 us
  starting transfers between devices: 5.6 us -> 3.83 us
    ppermute x2, waiting for transfers between devices: 26.2 us -> 42.7 us  [shifted(): return lax.ppermute(block, axis, [(i, (i + shift) % n) for i in range(n)])]
    psum x2 -> x1, blocking collectives: 18.7 us -> 9.6 us  [on_device(): lax.psum(jnp.sum(scaled * normed_c, axis=1, keepdims=True), 'tensor')]
    all_gather x1, waiting for transfers between devices: 30.7 us -> 33.9 us  [on_device(): piece = lax.all_gather(grad_kv, 'tensor', axis=1, tiled=True)]
    convert_element_type x1 -> x0, other arithmetic: 3.25 us -> none  [on_device(): hidden = (normed * gain_f).astype(jnp.bfloat16)]
    broadcast_in_dim x2 -> x1, other arithmetic: 7.58 us -> 4.86 us  [on_device(): return (upstream[None, None], weight_total[None], gain_total[None])]
    dot_general x2 -> x1, matrix products: 9.92 us -> 12.1 us  [on_device(): lax.dot_general(block, weight, (((1,), (1,)), ((), ())), preferred_elemen...]
    convert_element_type x2 -> x1, other arithmetic: 6.6 us -> 5.59 us  [on_device(): input_grad = (grad_out[lo:lo + step].astype(jnp.float32) + rstd[lo:lo + s...]
    unnamed x20 -> x9, local copies, waits for them, and re-layouts: 4.08 us -> 4.54 us
  transfers between devices with their start and end apart: 8 -> 7, of which waited for: 3 -> 3; matrix products, arithmetic and copies ran while one was open for 24% -> 14% of each run, Pallas kernels for 0% -> 0%
where the time goes in v9:
time: 165 us; the launch traced here: 164 us
  waiting for transfers between devices  78.5 us (48%)
  blocking collectives  23.3 us (14%)
  matrix products  20.3 us (12%)
  other arithmetic  15 us (9%)
  between operations  14.2 us (9%)
  local copies, waits for them, and re-layouts  9.21 us (6%)
  starting transfers between devices  3.83 us (2%)
    ppermute x2, waiting for transfers between devices, shifted(): return lax.ppermute(block, axis, [(i, (i + shift) % n) for i in range(n)])  42.7 us
    all_gather x1, waiting for transfers between devices, on_device(): piece = lax.all_gather(grad_kv, 'tensor', axis=1, tiled=True)  33.9 us
    psum x1, blocking collectives, on_device(): lax.psum(jnp.sum(values * values, axis=1, keepdims=True), 'tensor')  13.7 us
    dot_general x1, matrix products, on_device(): lax.dot_general(block, weight, (((1,), (1,)), ((), ())), preferred_elemen...  12.1 us
    psum x1, blocking collectives, on_device(): lax.psum(jnp.sum(scaled * normed_c, axis=1, keepdims=True), 'tensor')  9.6 us
    convert_element_type x1, other arithmetic, on_device(): input_grad = (grad_out[lo:lo + step].astype(jnp.float32) + rstd[lo:lo + s...  5.59 us
    broadcast_in_dim x1, other arithmetic, on_device(): return (upstream[None, None], weight_total[None], gain_total[None])  4.86 us
    unnamed x9, local copies, waits for them, and re-layouts  4.54 us
  transfers between devices with their start and end apart: 7, of which 3 were waited for; matrix products, arithmetic and copies ran while one was open for 14% of the time, Pallas kernels for 0%

profile of v9, /device:TPU:0, one launch (start us, length us, event | category | flops | bytes accessed | tf_op | source)
XLA Modules:
  0.0 164.2 jit_solution(8157118735292519295)
XLA Ops:
  7.2 0.7 all-gather.3.cloned.1.call-update
  7.9 0.7 mul.93
  8.6 2.1 %fusion.13 = f32[512]{0:T(512)S(1)} fusion(bf16[1,1,512,2048]{3,2,1,0:T(8,128)(2,1)} %param.5), kind=kLoop, calls=%fused_computation.15 | loop fusion | flops 3145216 | bytes 2099200 | tf_op jit(solution)/shard_map/reduce_sum | solution.py:41
  10.7 13.7 %psum.14 = f32[512,1]{0,1:T(1,128)S(1)} all-reduce(f32[512,1]{0,1:T(1,128)S(1)} %bitcast.46), channel_id=1, replica_groups=mesh['dp'=4,'pipe'=2,'tensor'=4] {'tensor'}, use_global_device_ids=true, to_apply=%region_1.2 | all-reduce | flops 512 | bytes 4096 | tf_op jit(solution)/shard_map/psum | solution.py:41
  24.4 33.9 %all-gather.3.cloned.1.call-done = bf16[1,1,512,2048]{3,2,1,0:T(8,128)(2,1)} async-done(((bf16[1,1,512,512]{3,2,1,0:T(8,128)(2,1)}), bf16[1,1,512,2048]{3,2,1,0:T(8,128)(2,1)}) %all-gather.3.cloned.1.call-update) | async-done | bytes 2097168 | tf_op jit(solution)/shard_map/all_gather | solution.py:47
  58.3 12.1 %fusion.12 = (f32[2048]{0:T(1024)S(1)}, f32[512]{0:T(512)S(1)}, bf16[512,2048]{1,0:T(8,128)(2,1)}, f32[512,2048]{1,0:T(8,128)}) fusion(bf16[1,1,512,2048]{3,2,1,0:T(8,128)(2,1)} %param.5, f32[512]{0:T(512)S(1)} %bitcast.49, f32[2048]{0:T(1024)S(1)} %bitcast.44, bf16[1,2048,2048]{2,1,0:T(8,128)(2,1)} %param.9, ...), kind=kOutput, calls=%fused_computation.14 | convolution fusion | flops 4304401920 | bytes 18894848 | tf_op jit(solution)/shard_map/dot_general | solution.py:65
  70.5 2.9 %dynamic-slice_bitcast_fusion.1 = (bf16[512,512]{1,0:T(8,128)(2,1)S(1)}, bf16[512,512]{1,0:T(8,128)(2,1)S(1)}, bf16[512,512]{1,0:T(8,128)(2,1)}, bf16[512,512]{1,0:T(8,128)(2,1)}) fusion(bf16[1,1,512,2048]{3,2,1,0:T(8,128)(2,1)} %all-gather.3.cloned.1.call-done, s32[]{:T(128)S(6)} %select_n.47, s32[]{:T(128)S(6)} %select_n.48, s32[]{:T(128)S(6)} %select_n.46, ...), kind=kLoop, calls=%fused_computation.27 | loop fusion | bytes 4194320 | tf_op jit(solution)/shard_map/dynamic_slice | solution.py:51
  73.4 1.1 pad_maximum_fusion
  74.5 0.3 collective-permute-start.2
  74.8 9.6 %psum.15 = f32[512,1]{0,1:T(1,128)S(1)} all-reduce(f32[512,1]{0,1:T(1,128)S(1)} %bitcast.52), channel_id=1, replica_groups=mesh['dp'=4,'pipe'=2,'tensor'=4] {'tensor'}, use_global_device_ids=true, to_apply=%region_3.4 | all-reduce | flops 512 | bytes 4096 | tf_op jit(solution)/shard_map/psum | solution.py:70
  84.4 5.6 %fusion.10 = bf16[512,2048]{1,0:T(8,128)(2,1)} fusion(f32[512,2048]{1,0:T(8,128)} %get-tuple-element.12, bf16[1,1,512,2048]{3,2,1,0:T(8,128)(2,1)} %param.6, bf16[1,1,512,2048]{3,2,1,0:T(8,128)(2,1)S(1)} %copy-done.1, f32[512]{0:T(512)S(1)} %bitcast.51, f32[2048]{0:T(1024)S(1)} %bitcast.45, f32[512]{0:T(512)S(1)} %bitcast.50), kind=kLoop, calls=%fused_computation.12 | loop fusion | flops 9437184 | bytes 10498048 | tf_op jit(solution)/shard_map/convert_element_type | solution.py:74
  90.0 1.5 collective-permute-start
  91.5 4.0 %fusion.16 = f32[2048,1024]{1,0:T(8,128)S(1)} fusion(bf16[512,2048]{1,0:T(8,128)(2,1)} %get-tuple-element.4, bf16[512,512]{1,0:T(8,128)(2,1)S(1)} %copy-done.2, bf16[512,512]{1,0:T(8,128)(2,1)S(1)} %copy-done.3), kind=kOutput, calls=%fused_computation.21 | convolution fusion | flops 2149580800 | bytes 11534336 | tf_op jit(solution)/shard_map/dot_general | solution.py:79
  95.6 4.1 %convolution_add_fusion = f32[2048,1024]{1,0:T(8,128)S(1)} fusion(f32[2048,1024]{1,0:T(8,128)S(1)} %fusion.16, bf16[512,2048]{1,0:T(8,128)(2,1)} %collective-permute-done.1, bf16[512,1024]{1,0:T(8,128)(2,1)S(1)} %collective-permute-done.2), kind=kOutput, calls=%fused_computation.18 | convolution fusion | flops 2149580800 | bytes 19922944 | tf_op jit(solution)/shard_map/dot_general | solution.py:81
  99.7 3.2 %copy-done = f32[2048,1024]{1,0:T(8,128)} copy-done((f32[2048,1024]{1,0:T(8,128)}, f32[2048,1024]{1,0:T(8,128)S(1)}, u32[]{:S(2)}) %copy-start) | copy-done | bytes 8388632
  102.9 1.6 %dynamic-slice_convert_fusion = bf16[2048,512]{1,0:T(8,128)(2,1)} fusion(f32[2048,1024]{1,0:T(8,128)S(1)} %convolution_add_fusion, s32[]{:T(128)S(6)} %select_n.52), kind=kLoop, calls=%fused_computation.17 | loop fusion | bytes 4194308 | tf_op jit(solution)/shard_map/convert_element_type | solution.py:91
  104.5 1.5 collective-permute-start.3
  106.0 1.2 collective-permute-done.4
  107.2 0.6 collective-permute-start.5
  107.7 0.1 dynamic_update_slice.6
  107.8 42.7 %collective-permute-done.5 = f32[2048]{0:T(1024)S(1)} collective-permute-done((f32[2048]{0:T(1024)S(1)}, f32[2048]{0:T(1024)S(1)}, u32[]{:S(2)}, u32[]{:S(2)}) %collective-permute-start.5) | collective-permute-done | bytes 8224 | tf_op jit(solution)/shard_map/ppermute | solution.py:18
  150.5 0.6 reduce_sum.39
  151.2 4.9 %fusion.14 = bf16[1,2048,512]{2,1,0:T(8,128)(2,1)} fusion(bf16[2048,512]{1,0:T(8,128)(2,1)} %collective-permute-done.3, f32[2048,1024]{1,0:T(8,128)} %copy-done, s32[]{:T(128)S(6)} %select_n.50), kind=kLoop, calls=%fused_computation.19 | loop fusion | flops 3145728 | bytes 8388612 | tf_op jit(solution)/shard_map/broadcast_in_dim | solution.py:107
  156.0 1.3 copy.11
  (19 shorter events, 0.2 us)
Async XLA Ops:
  7.2 51.1 %all-gather.3.cloned.1.call-start = ((), (), s32[]{:S(2)}) async-start(), calls=%async_computation | async-start | bytes 2621440 | tf_op jit(solution)/shard_map/all_gather | solution.py:47
  70.4 14.0 %copy-start.1 = (bf16[1,1,512,2048]{3,2,1,0:T(8,128)(2,1)S(1)}, bf16[1,1,512,2048]{3,2,1,0:T(8,128)(2,1)}, u32[]{:S(2)}) copy-start(bf16[1,1,512,2048]{3,2,1,0:T(8,128)(2,1)} %param.5) | copy-start | bytes 6291460
  70.4 25.1 %collective-permute-start.1 = (bf16[512,2048]{1,0:T(8,128)(2,1)}, bf16[512,2048]{1,0:T(8,128)(2,1)}, u32[]{:S(2)}, u32[]{:S(2)}) collective-permute-start(bf16[512,2048]{1,0:T(8,128)(2,1)} %get-tuple-element.4), channel_id=1, source_target_pairs={{0,8},{8,0},{16,24},{24,16},{1,9},{9,1},{17,25},{25,17},{2,10},{10... | collective-permute-start | bytes 6291464 | tf_op jit(solution)/shard_map/ppermute | solution.py:23
  74.5 21.1 %collective-permute-start.2 = (bf16[512,1024]{1,0:T(8,128)(2,1)}, bf16[512,1024]{1,0:T(8,128)(2,1)S(1)}, u32[]{:S(2)}, u32[]{:S(2)}) collective-permute-start(bf16[512,1024]{1,0:T(8,128)(2,1)} %pad_maximum_fusion), channel_id=1, source_target_pairs={{0,8},{8,0},{16,24},{24,16},{1,9},{9,1},{17,25},{25,17},{2,10},{10... | collective-permute-start | bytes 3145736 | tf_op jit(solution)/shard_map/ppermute | solution.py:23
  84.4 7.1 %copy-start.2 = (bf16[512,512]{1,0:T(8,128)(2,1)S(1)}, bf16[512,512]{1,0:T(8,128)(2,1)}, u32[]{:S(2)}) copy-start(bf16[512,512]{1,0:T(8,128)(2,1)} %get-tuple-element.10) | copy-start | bytes 1572868
  84.4 7.1 %copy-start.3 = (bf16[512,512]{1,0:T(8,128)(2,1)S(1)}, bf16[512,512]{1,0:T(8,128)(2,1)}, u32[]{:S(2)}) copy-start(bf16[512,512]{1,0:T(8,128)(2,1)} %get-tuple-element.11) | copy-start | bytes 1572868
  90.0 61.2 %collective-permute-start = (bf16[512,2048]{1,0:T(8,128)(2,1)}, bf16[512,2048]{1,0:T(8,128)(2,1)S(1)}, u32[]{:S(2)}, u32[]{:S(2)}) collective-permute-start(bf16[512,2048]{1,0:T(8,128)(2,1)} %fusion.10), channel_id=1, source_target_pairs={{4,0},{5,1},{6,2},{7,3},{12,8},{13,9},{14,10},{15,11},{20,16},{21,... | collective-permute-start | bytes 6291464 | tf_op jit(solution)/shard_map/ppermute | solution.py:13
  99.6 3.2 %copy-start = (f32[2048,1024]{1,0:T(8,128)}, f32[2048,1024]{1,0:T(8,128)S(1)}, u32[]{:S(2)}) copy-start(f32[2048,1024]{1,0:T(8,128)S(1)} %convolution_add_fusion) | copy-start | bytes 25165828
  104.5 46.7 %collective-permute-start.3 = (bf16[2048,512]{1,0:T(8,128)(2,1)}, bf16[2048,512]{1,0:T(8,128)(2,1)}, u32[]{:S(2)}, u32[]{:S(2)}) collective-permute-start(bf16[2048,512]{1,0:T(8,128)(2,1)} %dynamic-slice_convert_fusion), channel_id=1, source_target_pairs={{0,16},{8,24},{16,0},{24,8},{1,17},{9,25},{17,1},{25,9},{2,18},{10... | collective-permute-start | bytes 6291464 | tf_op jit(solution)/shard_map/ppermute | solution.py:18
  106.0 1.2 collective-permute-start.4
  107.2 43.3 %collective-permute-start.5 = (f32[2048]{0:T(1024)S(1)}, f32[2048]{0:T(1024)S(1)}, u32[]{:S(2)}, u32[]{:S(2)}) collective-permute-start(f32[2048]{0:T(1024)S(1)} %add.84), channel_id=1, source_target_pairs={{0,16},{8,24},{16,0},{24,8},{1,17},{9,25},{17,1},{25,9},{2,18},{10... | collective-permute-start | bytes 24584 | tf_op jit(solution)/shard_map/ppermute | solution.py:18
Sparse Core Ops, SparseCore 0:
  9.6 48.6 all-gather.2

commit v10 on v0

--- a/solution.py
+++ b/solution.py
@@ -12,6 +12,23 @@
     return lax.ppermute(block, axis, route)
 
 
+def line_gather(block, axis):
+    n = lax.axis_size(axis)
+    me = lax.axis_index(axis)
+    rows, width = block.shape
+    right = [(i, i + 1) for i in range(n - 1)]
+    left = [(i + 1, i) for i in range(n - 1)]
+    full = jnp.zeros((rows, (3 * n - 2) * width), block.dtype)
+    full = lax.dynamic_update_slice(full, block, (0, (me + n - 1) * width))
+    from_left, from_right = block, block
+    for k in range(1, n):
+        from_left = lax.ppermute(from_left, axis, right)
+        from_right = lax.ppermute(from_right, axis, left)
+        full = lax.dynamic_update_slice(full, from_left, (0, (me - k + n - 1) * width))
+        full = lax.dynamic_update_slice(full, from_right, (0, (me + k + n - 1) * width))
+    return full[:, (n - 1) * width:(2 * n - 1) * width]
+
+
 def on_device(layer_input, output_grad, kv_grad, norm_gain, kv_weight):
     rows = layer_input[0, 0]
     grad_out = output_grad[0, 0]
@@ -24,7 +41,7 @@
     rstd = lax.rsqrt(total_squares / D + 1e-05)
     normed = values * rstd
     hidden = (normed * gain_f).astype(jnp.bfloat16)
-    piece = lax.all_gather(grad_kv, "tensor", axis=1, tiled=True)
+    piece = line_gather(grad_kv, "tensor")
     row_total = lax.dot_general(
         piece, weight, (((1,), (1,)), ((), ())), preferred_element_type=jnp.float32
     )

time: 153 us -> 155 us (1.013)
  waiting for transfers between devices: 74.5 us -> 48.9 us
  starting transfers between devices: 1.36 us -> 20.5 us
  local copies, waits for them, and re-layouts: 2.89 us -> 13.6 us
  matrix products: 21.9 us -> 19.8 us
    all_gather x1 -> x0, waiting for transfers between devices: 33.9 us -> none  [on_device(): piece = lax.all_gather(grad_kv, 'tensor', axis=1, tiled=True)]
    ppermute x0 -> x6, starting transfers between devices: none -> 19.1 us  [the longest x3 15.3 us: line_gather(): from_left = lax.ppermute(from_left, axis, right)]
    ppermute x0 -> x6, waiting for transfers between devices: none -> 12.5 us  [the longest x3 9.47 us: line_gather(): from_left = lax.ppermute(from_left, axis, right)]
    dynamic_update_slice x0 -> x7, local copies, waits for them, and re-layouts: none -> 9.28 us  [the longest x3 4.75 us: line_gather(): lax.dynamic_update_slice(full, from_left, (0, (me - k + n - 1) * width))]
    ppermute x1, waiting for transfers between devices: 39.9 us -> 34.3 us  [from_behind(): return lax.ppermute(block, axis, route)]
    broadcast_in_dim x0 -> x1, local copies, waits for them, and re-layouts: none -> 3.02 us  [line_gather(): full = jnp.zeros((rows, (3 * n - 2) * width), block.dtype)]
    reduce_scatter x1, waiting for transfers between devices: 0.01 us -> 2.09 us  [on_device(): lax.psum_scatter(wgrad.astype(jnp.bfloat16), 'dp', scatter_dimension=1, t...]
    dot_general x1, matrix products: 10.1 us -> 8.53 us  [on_device(): lax.dot_general(hidden, piece, (((0,), (0,)), ((), ())), preferred_elemen...]
  transfers between devices with their start and end apart: 3 -> 8, of which waited for: 2 -> 5; matrix products, arithmetic and copies ran while one was open for 13% -> 20% of each run, Pallas kernels for 0% -> 0%
where the time goes in v10:
time: 155 us
  waiting for transfers between devices  48.9 us (32%)
  blocking collectives  29.7 us (19%)
  starting transfers between devices  20.5 us (13%)
  matrix products  19.8 us (13%)
  between operations  14.1 us (9%)
  local copies, waits for them, and re-layouts  13.6 us (9%)
  other arithmetic  8.24 us (5%)
    ppermute x1, waiting for transfers between devices, from_behind(): return lax.ppermute(block, axis, route)  34.3 us
    ppermute x3, starting transfers between devices, line_gather(): from_left = lax.ppermute(from_left, axis, right)  15.3 us
    psum x1, blocking collectives, on_device(): total_squares = lax.psum(local_squares, 'tensor')  14 us
    dot_general x1, matrix products, on_device(): lax.dot_general(piece, weight, (((1,), (1,)), ((), ())), preferred_elemen...  11.2 us
    ppermute x3, waiting for transfers between devices, line_gather(): from_left = lax.ppermute(from_left, axis, right)  9.47 us
    psum x1, blocking collectives, on_device(): mean_term = lax.psum(local_dot, 'tensor') / D  8.61 us
    dot_general x1, matrix products, on_device(): lax.dot_general(hidden, piece, (((0,), (0,)), ((), ())), preferred_elemen...  8.53 us
    psum x1, blocking collectives, on_device(): gain_total = lax.psum(gain_part, 'dp')  7.03 us
  transfers between devices with their start and end apart: 8, of which 5 were waited for; matrix products, arithmetic and copies ran while one was open for 20% of the time, Pallas kernels for 0%

profile of v10, /device:TPU:0, one launch (start us, length us, event | category | flops | bytes accessed | tf_op | source)
XLA Modules:
  0.0 154.8 jit_solution(9143256078066941247)
XLA Ops:
  7.2 5.9 %collective-permute-start = (bf16[512,512]{1,0:T(8,128)(2,1)}, bf16[512,512]{1,0:T(8,128)(2,1)}, u32[]{:S(2)}, u32[]{:S(2)}) collective-permute-start(bf16[512,512]{1,0:T(8,128)(2,1)} %bitcast.29), channel_id=1, source_target_pairs={{0,1},{1,2},{2,3},{4,5},{5,6},{6,7},{8,9},{9,10},{10,11},{12,13},{... | collective-permute-start | bytes 1572872 | tf_op jit(solution)/shard_map/ppermute | solution.py:25
  13.1 1.3 collective-permute-start.1
  14.4 9.4 %collective-permute-done = bf16[512,512]{1,0:T(8,128)(2,1)} collective-permute-done((bf16[512,512]{1,0:T(8,128)(2,1)}, bf16[512,512]{1,0:T(8,128)(2,1)}, u32[]{:S(2)}, u32[]{:S(2)}) %collective-permute-start) | collective-permute-done | bytes 524320 | tf_op jit(solution)/shard_map/ppermute | solution.py:25
  23.8 5.2 %collective-permute-start.2 = (bf16[512,512]{1,0:T(8,128)(2,1)}, bf16[512,512]{1,0:T(8,128)(2,1)}, u32[]{:S(2)}, u32[]{:S(2)}) collective-permute-start(bf16[512,512]{1,0:T(8,128)(2,1)} %collective-permute-done), channel_id=1, source_target_pairs={{0,1},{1,2},{2,3},{4,5},{5,6},{6,7},{8,9},{9,10},{10,11},{12,13},{... | collective-permute-start | bytes 1572872 | tf_op jit(solution)/shard_map/ppermute | solution.py:25
  29.0 1.3 collective-permute-start.3
  30.2 2.1 %fusion.13 = f32[512]{0:T(512)S(1)} fusion(bf16[1,1,512,2048]{3,2,1,0:T(8,128)(2,1)} %param.5), kind=kLoop, calls=%fused_computation.16 | loop fusion | flops 3145216 | bytes 2099200 | tf_op jit(solution)/shard_map/reduce_sum | solution.py:39
  32.3 14.0 %psum.21 = f32[512,1]{0,1:T(1,128)S(1)} all-reduce(f32[512,1]{0,1:T(1,128)S(1)} %bitcast.34), channel_id=1, replica_groups=mesh['dp'=4,'pipe'=2,'tensor'=4] {'tensor'}, use_global_device_ids=true, to_apply=%region_1.0 | all-reduce | flops 512 | bytes 4096 | tf_op jit(solution)/shard_map/psum | solution.py:40
  46.3 3.0 %broadcast_in_dim.21 = bf16[512,5120]{1,0:T(8,128)(2,1)} broadcast(bf16[]{:T(256)} %constant.42.clone.1), dimensions={} | broadcast | bytes 5242882 | tf_op jit(solution)/shard_map/broadcast_in_dim | solution.py:21
  50.2 4.2 %collective-permute-start.4 = (bf16[512,512]{1,0:T(8,128)(2,1)}, bf16[512,512]{1,0:T(8,128)(2,1)S(1)}, u32[]{:S(2)}, u32[]{:S(2)}) collective-permute-start(bf16[512,512]{1,0:T(8,128)(2,1)} %collective-permute-done.2), channel_id=1, source_target_pairs={{0,1},{1,2},{2,3},{4,5},{5,6},{6,7},{8,9},{9,10},{10,11},{12,13},{... | collective-permute-start | bytes 1572872 | tf_op jit(solution)/shard_map/ppermute | solution.py:25
  54.5 1.3 collective-permute-start.5
  55.8 1.9 %constant_dynamic-update-slice_fusion.5 = bf16[512,5120]{1,0:T(8,128)(2,1)} fusion(bf16[512,5120]{1,0:T(8,128)(2,1)} %constant_dynamic-update-slice_fusion.6, bf16[512,512]{1,0:T(8,128)(2,1)} %collective-permute-done, s32[]{:T(128)S(6)} %select_n.22), kind=kLoop, calls=%fused_computation.28 | loop fusion | bytes 1048580 | tf_op jit(solution)/shard_map/dynamic_update_slice | solution.py:27
  57.7 1.9 %constant_dynamic-update-slice_fusion.4 = bf16[512,5120]{1,0:T(8,128)(2,1)} fusion(bf16[512,5120]{1,0:T(8,128)(2,1)} %constant_dynamic-update-slice_fusion.5, bf16[512,512]{1,0:T(8,128)(2,1)} %collective-permute-done.1, s32[]{:T(128)S(6)} %select_n.23), kind=kLoop, calls=%fused_computation.27 | loop fusion | bytes 1048580 | tf_op jit(solution)/shard_map/dynamic_update_slice | solution.py:28
  59.6 2.0 %constant_dynamic-update-slice_fusion.3 = bf16[512,5120]{1,0:T(8,128)(2,1)} fusion(bf16[512,5120]{1,0:T(8,128)(2,1)} %constant_dynamic-update-slice_fusion.4, bf16[512,512]{1,0:T(8,128)(2,1)} %collective-permute-done.2, s32[]{:T(128)S(6)} %select_n.24), kind=kLoop, calls=%fused_computation.26 | loop fusion | bytes 1048580 | tf_op jit(solution)/shard_map/dynamic_update_slice | solution.py:27
  63.5 3.0 %collective-permute-done.5 = bf16[512,512]{1,0:T(8,128)(2,1)S(1)} collective-permute-done((bf16[512,512]{1,0:T(8,128)(2,1)S(1)}, bf16[512,512]{1,0:T(8,128)(2,1)S(1)}, u32[]{:S(2)}, u32[]{:S(2)}) %collective-permute-start.5) | collective-permute-done | bytes 524320 | tf_op jit(solution)/shard_map/ppermute | solution.py:26
  66.5 0.9 constant_dynamic-update-slice_fusion
  67.4 8.5 %convolution_convert_fusion = bf16[2048,2048]{1,0:T(8,128)(2,1)} fusion(bf16[1,1,512,2048]{3,2,1,0:T(8,128)(2,1)S(1)} %copy-done, f32[2048]{0:T(1024)S(1)} %bitcast.31, f32[512]{0:T(512)S(1)} %bitcast.36, bf16[512,5120]{1,0:T(8,128)(2,1)} %constant_dynamic-update-slice_fusion), kind=kOutput, calls=%fused_computation.2 | convolution fusion | flops 4303355904 | bytes 12593152 | tf_op jit(solution)/shard_map/dot_general | solution.py:48
  75.9 11.2 %fusion.12 = (f32[2048]{0:T(1024)S(1)}, f32[512]{0:T(512)S(1)}, f32[512,2048]{1,0:T(8,128)}) fusion(bf16[1,1,512,2048]{3,2,1,0:T(8,128)(2,1)S(1)} %copy-done, f32[512]{0:T(512)S(1)} %bitcast.37, f32[2048]{0:T(1024)S(1)} %bitcast.32, bf16[1,2048,2048]{2,1,0:T(8,128)(2,1)} %param.9, bf16[512,5120]{1,0:T(8,128)(2,1)} %constant_dynamic-update-slice_fusion), kind=kOutput, calls=%fused_computation.15 | convolution fusion | flops 4302304768 | bytes 16797696 | tf_op jit(solution)/shard_map/dot_general | solution.py:45
  87.2 8.6 %psum.22 = f32[512,1]{0,1:T(1,128)S(1)} all-reduce(f32[512,1]{0,1:T(1,128)S(1)} %bitcast.40), channel_id=1, replica_groups=mesh['dp'=4,'pipe'=2,'tensor'=4] {'tensor'}, use_global_device_ids=true, to_apply=%region_3.0 | all-reduce | flops 512 | bytes 4096 | tf_op jit(solution)/shard_map/psum | solution.py:55
  95.8 6.1 %fusion.10 = bf16[512,2048]{1,0:T(8,128)(2,1)} fusion(f32[512,2048]{1,0:T(8,128)} %get-tuple-element.5, bf16[1,1,512,2048]{3,2,1,0:T(8,128)(2,1)} %param.6, bf16[1,1,512,2048]{3,2,1,0:T(8,128)(2,1)S(1)} %copy-done, f32[512]{0:T(512)S(1)} %bitcast.39, f32[2048]{0:T(1024)S(1)} %bitcast.33, f32[512]{0:T(512)S(1)} %bitcast.38), kind=kLoop, calls=%fused_computation.13 | loop fusion | flops 9437184 | bytes 10498048 | tf_op jit(solution)/shard_map/convert_element_type | solution.py:56
  101.9 1.3 collective-permute-start.6
  103.2 7.0 %psum.23 = f32[1,2048]{1,0:T(1,128)} all-reduce(f32[1,2048]{1,0:T(1,128)S(1)} %bitcast.35), channel_id=1, replica_groups=mesh['dp'=4,'pipe'=2,'tensor'=4] {'dp'}, use_global_device_ids=true, to_apply=%region_6.0 | all-reduce | flops 2048 | bytes 16384 | tf_op jit(solution)/shard_map/psum | solution.py:61
  110.2 34.3 %collective-permute-done.6 = bf16[512,2048]{1,0:T(8,128)(2,1)S(1)} collective-permute-done((bf16[512,2048]{1,0:T(8,128)(2,1)}, bf16[512,2048]{1,0:T(8,128)(2,1)S(1)}, u32[]{:S(2)}, u32[]{:S(2)}) %collective-permute-start.6) | collective-permute-done | bytes 2097184 | tf_op jit(solution)/shard_map/ppermute | solution.py:12
  144.5 2.1 %reduce-scatter.2.cloned.1.call-done = bf16[2048,512]{1,0:T(8,128)(2,1)} async-done(((bf16[2048,2048]{1,0:T(8,128)(2,1)}), bf16[2048,512]{1,0:T(8,128)(2,1)}) %reduce-scatter.2.cloned.1.call-update) | async-done | bytes 2097168 | tf_op jit(solution)/shard_map/reduce_scatter | solution.py:62
  146.6 1.3 copy.16
  (18 shorter events, 2.8 us)
Async XLA Ops:
  7.2 42.2 %copy-start.1 = (bf16[1,1,512,512]{3,2,1,0:T(8,128)(2,1)S(1)}, bf16[1,1,512,512]{3,2,1,0:T(8,128)(2,1)}, u32[]{:S(2)}) copy-start(bf16[1,1,512,512]{3,2,1,0:T(8,128)(2,1)} %param.7) | copy-start | bytes 1572868
  7.2 139.4 %reduce-scatter.2.cloned.1.call-start = ((), (), s32[]{:S(2)}) async-start(), calls=%async_computation.1 | async-start | bytes 10485760 | tf_op jit(solution)/shard_map/reduce_scatter | solution.py:62
  7.2 47.3 %copy-start.2 = (bf16[1,2048]{1,0:T(2,128)(2,1)S(1)}, bf16[1,2048]{1,0:T(2,128)(2,1)}, u32[]{:S(2)}) copy-start(bf16[1,2048]{1,0:T(2,128)(2,1)} %param.8) | copy-start | bytes 12292
  7.2 16.5 %collective-permute-start = (bf16[512,512]{1,0:T(8,128)(2,1)}, bf16[512,512]{1,0:T(8,128)(2,1)}, u32[]{:S(2)}, u32[]{:S(2)}) collective-permute-start(bf16[512,512]{1,0:T(8,128)(2,1)} %bitcast.29), channel_id=1, source_target_pairs={{0,1},{1,2},{2,3},{4,5},{5,6},{6,7},{8,9},{9,10},{10,11},{12,13},{... | collective-permute-start | bytes 1572872 | tf_op jit(solution)/shard_map/ppermute | solution.py:25
  13.1 15.8 %collective-permute-start.1 = (bf16[512,512]{1,0:T(8,128)(2,1)}, bf16[512,512]{1,0:T(8,128)(2,1)}, u32[]{:S(2)}, u32[]{:S(2)}) collective-permute-start(bf16[512,512]{1,0:T(8,128)(2,1)} %bitcast.30), channel_id=1, source_target_pairs={{1,0},{2,1},{3,2},{5,4},{6,5},{7,6},{9,8},{10,9},{11,10},{13,12},{... | collective-permute-start | bytes 1572872 | tf_op jit(solution)/shard_map/ppermute | solution.py:26
  23.8 26.4 %collective-permute-start.2 = (bf16[512,512]{1,0:T(8,128)(2,1)}, bf16[512,512]{1,0:T(8,128)(2,1)}, u32[]{:S(2)}, u32[]{:S(2)}) collective-permute-start(bf16[512,512]{1,0:T(8,128)(2,1)} %collective-permute-done), channel_id=1, source_target_pairs={{0,1},{1,2},{2,3},{4,5},{5,6},{6,7},{8,9},{9,10},{10,11},{12,13},{... | collective-permute-start | bytes 1572872 | tf_op jit(solution)/shard_map/ppermute | solution.py:25
  29.0 25.6 %collective-permute-start.3 = (bf16[512,512]{1,0:T(8,128)(2,1)}, bf16[512,512]{1,0:T(8,128)(2,1)S(1)}, u32[]{:S(2)}, u32[]{:S(2)}) collective-permute-start(bf16[512,512]{1,0:T(8,128)(2,1)} %collective-permute-done.1), channel_id=1, source_target_pairs={{1,0},{2,1},{3,2},{5,4},{6,5},{7,6},{9,8},{10,9},{11,10},{13,12},{... | collective-permute-start | bytes 1572872 | tf_op jit(solution)/shard_map/ppermute | solution.py:26
  49.4 18.0 %copy-start = (bf16[1,1,512,2048]{3,2,1,0:T(8,128)(2,1)S(1)}, bf16[1,1,512,2048]{3,2,1,0:T(8,128)(2,1)}, u32[]{:S(2)}) copy-start(bf16[1,1,512,2048]{3,2,1,0:T(8,128)(2,1)} %param.5) | copy-start | bytes 6291460
  50.2 12.4 %collective-permute-start.4 = (bf16[512,512]{1,0:T(8,128)(2,1)}, bf16[512,512]{1,0:T(8,128)(2,1)S(1)}, u32[]{:S(2)}, u32[]{:S(2)}) collective-permute-start(bf16[512,512]{1,0:T(8,128)(2,1)} %collective-permute-done.2), channel_id=1, source_target_pairs={{0,1},{1,2},{2,3},{4,5},{5,6},{6,7},{8,9},{9,10},{10,11},{12,13},{... | collective-permute-start | bytes 1572872 | tf_op jit(solution)/shard_map/ppermute | solution.py:25
  54.5 12.0 %collective-permute-start.5 = (bf16[512,512]{1,0:T(8,128)(2,1)S(1)}, bf16[512,512]{1,0:T(8,128)(2,1)S(1)}, u32[]{:S(2)}, u32[]{:S(2)}) collective-permute-start(bf16[512,512]{1,0:T(8,128)(2,1)S(1)} %collective-permute-done.3), channel_id=1, source_target_pairs={{1,0},{2,1},{3,2},{5,4},{6,5},{7,6},{9,8},{10,9},{11,10},{13,12},{... | collective-permute-start | bytes 1572872 | tf_op jit(solution)/shard_map/ppermute | solution.py:26
  101.9 42.6 %collective-permute-start.6 = (bf16[512,2048]{1,0:T(8,128)(2,1)}, bf16[512,2048]{1,0:T(8,128)(2,1)S(1)}, u32[]{:S(2)}, u32[]{:S(2)}) collective-permute-start(bf16[512,2048]{1,0:T(8,128)(2,1)} %fusion.10), channel_id=1, source_target_pairs={{4,0},{5,1},{6,2},{7,3},{12,8},{13,9},{14,10},{15,11},{20,16},{21,... | collective-permute-start | bytes 6291464 | tf_op jit(solution)/shard_map/ppermute | solution.py:12
Sparse Core Ops, SparseCore 0:
  76.0 70.5 reduce-scatter.1

commit v11 on v8

--- a/solution.py
+++ b/solution.py
@@ -23,18 +23,6 @@
     return lax.ppermute(block, "dp", [(i, i ^ 1) for i in range(n)])
 
 
-def gather_columns(block):
-    n = lax.axis_size("tensor")
-    me = lax.axis_index("tensor")
-    rows, width = block.shape
-    full = jnp.zeros((rows, width * n), block.dtype)
-    full = lax.dynamic_update_slice(full, block, (0, me * width))
-    for d in range(1, n):
-        got = shifted(block, "tensor", d)
-        full = lax.dynamic_update_slice(full, got, (0, ((me - d) % n) * width))
-    return full
-
-
 def on_device(layer_input, output_grad, kv_grad, norm_gain, kv_weight):
     rows = layer_input[0, 0]
     grad_out = output_grad[0, 0]
@@ -57,7 +45,10 @@
     hidden_partner = to_partner(hidden)
 
     step = seq // CHUNKS
-    pieces = [gather_columns(grad_kv[c * step:(c + 1) * step]) for c in range(CHUNKS)]
+    pieces = [
+        lax.all_gather(grad_kv[c * step:(c + 1) * step], "tensor", axis=1, tiled=True)
+        for c in range(CHUNKS)
+    ]
 
     def cols_of(parts, p):
         return jnp.concatenate(

time: 161 us -> 151 us (0.938)
  starting transfers between devices: 25.5 us -> 5.65 us
  waiting for transfers between devices: 31.1 us -> 47.2 us
  between operations: 0.99 us -> 14.2 us
  blocking collectives: 45.5 us -> 34.3 us
  local copies, waits for them, and re-layouts: 16.2 us -> 9.21 us
    ppermute x8 -> x2, starting transfers between devices: 22.5 us -> 2.74 us  [shifted(): return lax.ppermute(block, axis, [(i, (i + shift) % n) for i in range(n)])]
    all_gather x0 -> x2, waiting for transfers between devices: none -> 18.4 us  [on_device(): lax.all_gather(grad_kv[c * step:(c + 1) * step], 'tensor', axis=1, tiled=...]
    psum x1, blocking collectives: 26.8 us -> 13.5 us  [on_device(): lax.psum(jnp.sum(values * values, axis=1, keepdims=True), 'tensor')]
    dynamic_update_slice x8 -> x0, local copies, waits for them, and re-layouts: 7.04 us -> none  [the longest x6 6.99 us: gather_columns(): full = lax.dynamic_update_slice(full, got, (0, (me - d) % n * width))]
    psum x2, blocking collectives: 18.7 us -> 20.8 us  [on_device(): lax.psum(jnp.sum(scaled * normed_c, axis=1, keepdims=True), 'tensor')]
    dot_general x1, matrix products: 4.43 us -> 2.62 us  [on_device(): lax.dot_general(hidden_partner, cols_partner, (((0,), (0,)), ((), ())), p...]
    dot_general x1, matrix products: 2.58 us -> 4.32 us  [on_device(): lax.dot_general(h_own, cols_own, (((0,), (0,)), ((), ())), preferred_elem...]
    unnamed x22 -> x14, local copies, waits for them, and re-layouts: 4.23 us -> 3.24 us
  transfers between devices with their start and end apart: 13 -> 9, of which waited for: 3 -> 4; matrix products, arithmetic and copies ran while one was open for 29% -> 26% of each run, Pallas kernels for 0% -> 0%
where the time goes in v11:
time: 151 us; the launch traced here: 150 us
  waiting for transfers between devices  47.2 us (31%)
  blocking collectives  34.3 us (23%)
  other arithmetic  22 us (15%)
  matrix products  17.8 us (12%)
  between operations  14.2 us (9%)
  local copies, waits for them, and re-layouts  9.21 us (6%)
  starting transfers between devices  5.65 us (4%)
    ppermute x2, waiting for transfers between devices, shifted(): return lax.ppermute(block, axis, [(i, (i + shift) % n) for i in range(n)])  27.6 us
    psum x2, blocking collectives, on_device(): lax.psum(jnp.sum(scaled * normed_c, axis=1, keepdims=True), 'tensor')  20.8 us
    all_gather x2, waiting for transfers between devices, on_device(): lax.all_gather(grad_kv[c * step:(c + 1) * step], 'tensor', axis=1, tiled=...  18.4 us
    psum x1, blocking collectives, on_device(): lax.psum(jnp.sum(values * values, axis=1, keepdims=True), 'tensor')  13.5 us
    dot_general x2, matrix products, on_device(): lax.dot_general(block, weight, (((1,), (1,)), ((), ())), preferred_elemen...  10.8 us
    broadcast_in_dim x2, other arithmetic, on_device(): return (upstream[None, None], weight_total[None], gain_total[None])  7.58 us
    convert_element_type x2, other arithmetic, on_device(): input_grad = (grad_out[lo:lo + step].astype(jnp.float32) + rstd[lo:lo + s...  6.63 us
    dot_general x1, matrix products, on_device(): lax.dot_general(h_own, cols_own, (((0,), (0,)), ((), ())), preferred_elem...  4.32 us
  transfers between devices with their start and end apart: 9, of which 4 were waited for; matrix products, arithmetic and copies ran while one was open for 26% of the time, Pallas kernels for 0%

profile of v11, /device:TPU:0, one launch (start us, length us, event | category | flops | bytes accessed | tf_op | source)
XLA Modules:
  0.0 150.3 jit_solution(12542372915906435291)
XLA Ops:
  7.2 2.0 %fusion.18 = (bf16[1,1,256,512]{3,2,1,0:T(8,128)(2,1)}, bf16[1,1,256,512]{3,2,1,0:T(8,128)(2,1)}) fusion(bf16[1,1,512,512]{3,2,1,0:T(8,128)(2,1)} %param.7), kind=kLoop, calls=%fused_computation.43 | loop fusion | bytes 1048576 | tf_op jit(solution)/shard_map/slice | solution.py:49
  10.0 2.1 %fusion.4 = f32[512]{0:T(512)S(1)} fusion(bf16[1,1,512,2048]{3,2,1,0:T(8,128)(2,1)} %param.5), kind=kLoop, calls=%fused_computation.6 | loop fusion | flops 3145216 | bytes 2099200 | tf_op jit(solution)/shard_map/reduce_sum | solution.py:41
  12.1 13.5 %psum.21 = f32[512,1]{0,1:T(1,128)S(1)} all-reduce(f32[512,1]{0,1:T(1,128)S(1)} %bitcast.57), channel_id=1, replica_groups=mesh['dp'=4,'pipe'=2,'tensor'=4] {'tensor'}, use_global_device_ids=true, to_apply=%region_1.2 | all-reduce | flops 512 | bytes 4096 | tf_op jit(solution)/shard_map/psum | solution.py:41
  25.6 3.3 %multiply_convert_fusion = (bf16[512,2048]{1,0:T(8,128)(2,1)}, f32[512,2048]{1,0:T(8,128)}) fusion(f32[2048]{0:T(1024)S(1)} %bitcast.50, f32[512]{0:T(512)S(1)} %bitcast.56, bf16[1,1,512,2048]{3,2,1,0:T(8,128)(2,1)S(1)} %copy-done.2), kind=kLoop, calls=%fused_computation.9 | loop fusion | flops 4194304 | bytes 8398848 | tf_op jit(solution)/shard_map/convert_element_type | solution.py:44
  28.9 11.9 %all-gather.5.cloned.1.call-done = bf16[1,1,256,2048]{3,2,1,0:T(8,128)(2,1)} async-done(((bf16[1,1,256,512]{3,2,1,0:T(8,128)(2,1)}), bf16[1,1,256,2048]{3,2,1,0:T(8,128)(2,1)}) %all-gather.5.cloned.1.call-update) | async-done | bytes 1048592 | tf_op jit(solution)/shard_map/all_gather | solution.py:49
  40.9 8.2 %multiply_reduce_fusion.1 = (f32[2048]{0:T(1024)S(1)}, f32[256]{0:T(256)S(1)}, f32[256,2048]{1,0:T(8,128)}) fusion(f32[512,2048]{1,0:T(8,128)} %get-tuple-element.16, f32[2048]{0:T(1024)S(1)} %bitcast.51, bf16[1,2048,2048]{2,1,0:T(8,128)(2,1)} %param.9, bf16[1,1,256,2048]{3,2,1,0:T(8,128)(2,1)} %all-gather.5.cloned.1.call-done), kind=kOutput, calls=%fused_computation.18 | convolution fusion | flops 2150102784 | bytes 13648896 | tf_op jit(solution)/shard_map/dot_general | solution.py:72
  49.0 10.5 %psum.22 = f32[256,1]{0,1:T(1,128)S(1)} all-reduce(f32[256,1]{0,1:T(1,128)S(1)} %bitcast.65), channel_id=1, replica_groups=mesh['dp'=4,'pipe'=2,'tensor'=4] {'tensor'}, use_global_device_ids=true, to_apply=%region_3.4 | all-reduce | flops 256 | bytes 2048 | tf_op jit(solution)/shard_map/psum | solution.py:77
  59.5 4.2 %fusion.7 = bf16[256,2048]{1,0:T(8,128)(2,1)} fusion(f32[256,2048]{1,0:T(8,128)} %get-tuple-element.29, f32[512,2048]{1,0:T(8,128)} %get-tuple-element.16, f32[256]{0:T(256)S(1)} %bitcast.61, f32[2048]{0:T(1024)S(1)} %bitcast.52, f32[256]{0:T(256)S(1)} %bitcast.63, bf16[1,1,512,2048]{3,2,1,0:T(8,128)(2,1)} %param.6), kind=kLoop, calls=%fused_computation.16 | loop fusion | flops 3670016 | bytes 6301696 | tf_op jit(solution)/shard_map/convert_element_type | solution.py:81
  63.7 6.4 %all-gather.7.cloned.1.call-done = bf16[1,1,256,2048]{3,2,1,0:T(8,128)(2,1)} async-done(((bf16[1,1,256,512]{3,2,1,0:T(8,128)(2,1)}), bf16[1,1,256,2048]{3,2,1,0:T(8,128)(2,1)}) %all-gather.7.cloned.1.call-update) | async-done | bytes 1048592 | tf_op jit(solution)/shard_map/all_gather | solution.py:49
  70.1 2.2 %constant_dynamic-slice_fusion.1 = (bf16[256,512]{1,0:T(8,128)(2,1)S(1)}, bf16[256,512]{1,0:T(8,128)(2,1)S(1)}, bf16[256,512]{1,0:T(8,128)(2,1)S(1)}, bf16[256,5...) fusion(bf16[256,2048]{1,0:T(8,128)(2,1)} %bitcast.47, ...), kind=kLoop, calls=%fused_computation.31 | loop fusion | bytes 4194320 | tf_op jit(solution)/shard_map/dynamic_slice | solution.py:57
  73.4 1.5 collective-permute-start
  74.9 4.3 %fusion.8 = f32[2048,1024]{1,0:T(8,128)S(1)} fusion(bf16[512,2048]{1,0:T(8,128)(2,1)} %get-tuple-element.7, bf16[256,512]{1,0:T(8,128)(2,1)S(1)} %get-tuple-element.23, bf16[256,512]{1,0:T(8,128)(2,1)} %get-tuple-element.24, bf16[256,512]{1,0:T(8,128)(2,1)} %get-tuple-element.32, bf16[256,512]{1,0:T(8,128)(2,1)} %get-tuple-element.31), kind=kOutput, calls=%fused_computation.21 | convolution fusion | flops 2151677952 | bytes 11534336 | tf_op jit(solution)/shard_map/dot_general | solution.py:88
  79.3 2.6 %convolution_add_fusion = f32[2048,1024]{1,0:T(8,128)S(1)} fusion(f32[2048,1024]{1,0:T(8,128)S(1)} %fusion.8, bf16[512,2048]{1,0:T(8,128)(2,1)S(1)} %collective-permute-done.1, bf16[512,1024]{1,0:T(8,128)(2,1)S(1)} %collective-permute-done.2), kind=kOutput, calls=%fused_computation.10 | convolution fusion | flops 2149580800 | bytes 19922944 | tf_op jit(solution)/shard_map/dot_general | solution.py:90
  81.9 3.2 %copy-done = f32[2048,1024]{1,0:T(8,128)} copy-done((f32[2048,1024]{1,0:T(8,128)}, f32[2048,1024]{1,0:T(8,128)S(1)}, u32[]{:S(2)}) %copy-start) | copy-done | bytes 8388632
  85.1 1.6 %dynamic-slice_convert_fusion = bf16[2048,512]{1,0:T(8,128)(2,1)} fusion(f32[2048,1024]{1,0:T(8,128)S(1)} %convolution_add_fusion, s32[]{:T(128)S(6)} %select_n.55), kind=kLoop, calls=%fused_computation.8 | loop fusion | bytes 4194308 | tf_op jit(solution)/shard_map/convert_element_type | solution.py:100
  86.8 1.5 collective-permute-start.4
  88.3 2.7 %multiply_reduce_fusion = (f32[2048]{0:T(1024)S(1)}, f32[256]{0:T(256)S(1)}, f32[256,2048]{1,0:T(8,128)S(1)}) fusion(f32[512,2048]{1,0:T(8,128)S(1)} %copy-done.1, f32[2048]{0:T(1024)S(1)} %bitcast.53, bf16[256,2048]{1,0:T(8,128)(2,1)S(1)} %bitcast.48, bf16[1,2048,2048]{2,1,0:T(8,128)(2,1)S(1)} %bitcast.67), kind=kOutput, calls=%fused_computation.17 | convolution fusion | flops 2150102784 | bytes 13648896 | tf_op jit(solution)/shard_map/dot_general | solution.py:72
  90.9 10.3 %psum.23 = f32[256,1]{0,1:T(1,128)S(1)} all-reduce(f32[256,1]{0,1:T(1,128)S(1)} %bitcast.64), channel_id=1, replica_groups=mesh['dp'=4,'pipe'=2,'tensor'=4] {'tensor'}, use_global_device_ids=true, to_apply=%region_5.6 | all-reduce | flops 256 | bytes 2048 | tf_op jit(solution)/shard_map/psum | solution.py:77
  101.2 2.4 %fusion.6 = bf16[256,2048]{1,0:T(8,128)(2,1)S(1)} fusion(f32[256,2048]{1,0:T(8,128)S(1)} %get-tuple-element.30, f32[512,2048]{1,0:T(8,128)} %get-tuple-element.16, f32[256]{0:T(256)S(1)} %bitcast.60, f32[256]{0:T(256)S(1)} %bitcast.62, bf16[1,1,512,2048]{3,2,1,0:T(8,128)(2,1)} %param.6, f32[2048]{0:T(1024)S(1)} %bitcast.54), kind=kLoop, calls=%fused_computation.14 | loop fusion | flops 3670016 | bytes 6301696 | tf_op jit(solution)/shard_map/convert_element_type | solution.py:81
  103.7 1.3 collective-permute-start.3
  106.2 1.3 collective-permute-start.6
  107.6 27.6 %collective-permute-done.6 = f32[2048]{0:T(1024)S(1)} collective-permute-done((f32[2048]{0:T(1024)S(1)}, f32[2048]{0:T(1024)S(1)}, u32[]{:S(2)}, u32[]{:S(2)}) %collective-permute-start.6) | collective-permute-done | bytes 8224 | tf_op jit(solution)/shard_map/ppermute | solution.py:18
  135.9 2.7 %maximum_bitcast_fusion = bf16[1,1,512,2048]{3,2,1,0:T(8,128)(2,1)} fusion(bf16[256,2048]{1,0:T(8,128)(2,1)S(1)} %collective-permute-done.3, bf16[256,2048]{1,0:T(8,128)(2,1)} %collective-permute-done), kind=kLoop, calls=%fused_computation.12 | loop fusion | flops 4194304 | bytes 4194304 | tf_op jit(solution)/shard_map/broadcast_in_dim | solution.py:116
  138.6 4.9 %fusion.5 = bf16[1,2048,512]{2,1,0:T(8,128)(2,1)} fusion(bf16[2048,512]{1,0:T(8,128)(2,1)} %collective-permute-done.4, f32[2048,1024]{1,0:T(8,128)} %copy-done, s32[]{:T(128)S(6)} %select_n.56), kind=kLoop, calls=%fused_computation.11 | loop fusion | flops 3145728 | bytes 8388612 | tf_op jit(solution)/shard_map/broadcast_in_dim | solution.py:116
  (39 shorter events, 4.0 us)
Async XLA Ops:
  7.2 18.4 %copy-start.2 = (bf16[1,1,512,2048]{3,2,1,0:T(8,128)(2,1)S(1)}, bf16[1,1,512,2048]{3,2,1,0:T(8,128)(2,1)}, u32[]{:S(2)}) copy-start(bf16[1,1,512,2048]{3,2,1,0:T(8,128)(2,1)} %param.5) | copy-start | bytes 6291460
  7.2 33.7 %all-gather.5.cloned.1.call-start = ((), (), s32[]{:S(2)}) async-start(), calls=%async_computation | async-start | bytes 1310720 | tf_op jit(solution)/shard_map/all_gather | solution.py:49
  9.2 60.9 %all-gather.7.cloned.1.call-start = ((), (), s32[]{:S(2)}) async-start(), calls=%async_computation.1 | async-start | bytes 1310720 | tf_op jit(solution)/shard_map/all_gather | solution.py:49
  28.9 50.4 %collective-permute-start.1 = (bf16[512,2048]{1,0:T(8,128)(2,1)}, bf16[512,2048]{1,0:T(8,128)(2,1)S(1)}, u32[]{:S(2)}, u32[]{:S(2)}) collective-permute-start(bf16[512,2048]{1,0:T(8,128)(2,1)} %get-tuple-element.7), channel_id=1, source_target_pairs={{0,8},{8,0},{16,24},{24,16},{1,9},{9,1},{17,25},{25,17},{2,10},{10... | collective-permute-start | bytes 6291464 | tf_op jit(solution)/shard_map/ppermute | solution.py:23
  59.5 10.6 %copy-start.4 = (bf16[1,1,256,2048]{3,2,1,0:T(8,128)(2,1)S(1)}, bf16[1,1,256,2048]{3,2,1,0:T(8,128)(2,1)}, u32[]{:S(2)}) copy-start(bf16[1,1,256,2048]{3,2,1,0:T(8,128)(2,1)} %all-gather.5.cloned.1.call-done) | copy-start | bytes 3145732
  73.4 5.8 %collective-permute-start.2 = (bf16[512,1024]{1,0:T(8,128)(2,1)}, bf16[512,1024]{1,0:T(8,128)(2,1)S(1)}, u32[]{:S(2)}, u32[]{:S(2)}) collective-permute-start(bf16[512,1024]{1,0:T(8,128)(2,1)} %maximum_maximum_fusion), channel_id=1, source_target_pairs={{0,8},{8,0},{16,24},{24,16},{1,9},{9,1},{17,25},{25,17},{2,10},{10... | collective-permute-start | bytes 3145736 | tf_op jit(solution)/shard_map/ppermute | solution.py:23
  73.4 62.5 %collective-permute-start = (bf16[256,2048]{1,0:T(8,128)(2,1)}, bf16[256,2048]{1,0:T(8,128)(2,1)}, u32[]{:S(2)}, u32[]{:S(2)}) collective-permute-start(bf16[256,2048]{1,0:T(8,128)(2,1)} %fusion.7), channel_id=1, source_target_pairs={{4,0},{5,1},{6,2},{7,3},{12,8},{13,9},{14,10},{15,11},{20,16},{21,... | collective-permute-start | bytes 3145736 | tf_op jit(solution)/shard_map/ppermute | solution.py:13
  74.9 13.3 %slice-start = ((s8[8388608]{0:T(1024)(128)(4,1)}), s8[4194304]{0:T(1024)(128)(4,1)S(1)}, s32[]{:S(2)}) async-start(s8[8388608]{0:T(1024)(128)(4,1)} %bitcast.66), calls=%async_computation.2 | async-start | bytes 8388608
  79.2 9.0 %slice-start.1 = ((s8[8388608]{0:T(1024)(128)(4,1)}), s8[4194304]{0:T(1024)(128)(4,1)S(1)}, s32[]{:S(2)}) async-start(s8[8388608]{0:T(1024)(128)(4,1)} %bitcast.66), calls=%async_computation.3 | async-start | bytes 8388608
  79.3 9.0 %copy-start.3 = (bf16[1,1,256,2048]{3,2,1,0:T(8,128)(2,1)S(1)}, bf16[1,1,256,2048]{3,2,1,0:T(8,128)(2,1)}, u32[]{:S(2)}) copy-start(bf16[1,1,256,2048]{3,2,1,0:T(8,128)(2,1)} %all-gather.7.cloned.1.call-done) | copy-start | bytes 3145732
  81.9 3.2 %copy-start = (f32[2048,1024]{1,0:T(8,128)}, f32[2048,1024]{1,0:T(8,128)S(1)}, u32[]{:S(2)}) copy-start(f32[2048,1024]{1,0:T(8,128)S(1)} %convolution_add_fusion) | copy-start | bytes 25165828
  85.1 3.1 %copy-start.1 = (f32[512,2048]{1,0:T(8,128)S(1)}, f32[512,2048]{1,0:T(8,128)}, u32[]{:S(2)}) copy-start(f32[512,2048]{1,0:T(8,128)} %get-tuple-element.16) | copy-start | bytes 12582916
  86.8 51.9 %collective-permute-start.4 = (bf16[2048,512]{1,0:T(8,128)(2,1)}, bf16[2048,512]{1,0:T(8,128)(2,1)}, u32[]{:S(2)}, u32[]{:S(2)}) collective-permute-start(bf16[2048,512]{1,0:T(8,128)(2,1)} %dynamic-slice_convert_fusion), channel_id=1, source_target_pairs={{0,16},{8,24},{16,0},{24,8},{1,17},{9,25},{17,1},{25,9},{2,18},{10... | collective-permute-start | bytes 6291464 | tf_op jit(solution)/shard_map/ppermute | solution.py:18
  103.7 32.3 %collective-permute-start.3 = (bf16[256,2048]{1,0:T(8,128)(2,1)S(1)}, bf16[256,2048]{1,0:T(8,128)(2,1)S(1)}, u32[]{:S(2)}, u32[]{:S(2)}) collective-permute-start(bf16[256,2048]{1,0:T(8,128)(2,1)S(1)} %fusion.6), channel_id=1, source_target_pairs={{4,0},{5,1},{6,2},{7,3},{12,8},{13,9},{14,10},{15,11},{20,16},{21,... | collective-permute-start | bytes 3145736 | tf_op jit(solution)/shard_map/ppermute | solution.py:13
  105.0 1.2 collective-permute-start.5
  106.2 29.0 %collective-permute-start.6 = (f32[2048]{0:T(1024)S(1)}, f32[2048]{0:T(1024)S(1)}, u32[]{:S(2)}, u32[]{:S(2)}) collective-permute-start(f32[2048]{0:T(1024)S(1)} %add.100), channel_id=1, source_target_pairs={{0,16},{8,24},{16,0},{24,8},{1,17},{9,25},{17,1},{25,9},{2,18},{10... | collective-permute-start | bytes 24584 | tf_op jit(solution)/shard_map/ppermute | solution.py:18
Sparse Core Ops, SparseCore 0:
  10.2 30.6 all-gather.4
  42.4 27.6 all-gather.6

commit v12 on v11

--- a/solution.py
+++ b/solution.py
@@ -85,21 +85,24 @@
             _, (h_own, parts) = lax.optimization_barrier((input_grad, (hidden, pieces)))
             cols_partner = to_partner(cols_of(parts, 1 - parity))
             cols_own = cols_of(parts, parity)
-            pair = lax.dot_general(
-                h_own, cols_own, (((0,), (0,)), ((), ())), preferred_element_type=jnp.float32
-            ) + lax.dot_general(
-                hidden_partner, cols_partner, (((0,), (0,)), ((), ())),
-                preferred_element_type=jnp.float32,
-            )
             own_g = me // 2
-            total = lax.dynamic_slice_in_dim(pair, own_g * kv_block, kv_block, axis=1)
-            outs = []
-            for d in range(1, groups):
-                dest_g = (own_g + d) % groups
-                out = lax.dynamic_slice_in_dim(pair, dest_g * kv_block, kv_block, axis=1)
-                outs.append(out.astype(jnp.bfloat16))
-            for d, out in enumerate(outs, start=1):
-                total = total + shifted(out, "dp", 2 * d).astype(jnp.float32)
+
+            def pair_block(g):
+                own_cols = lax.dynamic_slice_in_dim(cols_own, g * kv_block, kv_block, axis=1)
+                partner_cols = lax.dynamic_slice_in_dim(cols_partner, g * kv_block, kv_block, axis=1)
+                return lax.dot_general(
+                    h_own, own_cols, (((0,), (0,)), ((), ())), preferred_element_type=jnp.float32
+                ) + lax.dot_general(
+                    hidden_partner, partner_cols, (((0,), (0,)), ((), ())),
+                    preferred_element_type=jnp.float32,
+                )
+
+            outs = [pair_block((own_g + d) % groups).astype(jnp.bfloat16) for d in range(1, groups)]
+            received = [shifted(out, "dp", 2 * d) for d, out in enumerate(outs, start=1)]
+            _, h_own = lax.optimization_barrier((outs, h_own))
+            total = pair_block(own_g)
+            for got in received:
+                total = total + got.astype(jnp.float32)
             weight_total = total.astype(jnp.bfloat16)
         if c + 1 < CHUNKS:
             _, block = lax.optimization_barrier(((input_grad, outs), pieces[c + 1]))

time: 151 us -> 148 us (0.980)
  matrix products: 17.8 us -> 26.3 us
  waiting for transfers between devices: 47.2 us -> 41.6 us
  local copies, waits for them, and re-layouts: 9.21 us -> 4.18 us
    dot_general x2 -> x4, matrix products: 6.94 us -> 14.2 us  [the longest x2 9.71 us: pair_block(): lax.dot_general(hidden_partner, partner_cols, (((0,), (0,)), ((), ())), p...]
    ppermute x2, waiting for transfers between devices: 27.6 us -> 22.2 us  [shifted(): return lax.ppermute(block, axis, [(i, (i + shift) % n) for i in range(n)])]
    broadcast_in_dim x2 -> x1, other arithmetic: 7.58 us -> 3.26 us  [on_device(): return (upstream[None, None], weight_total[None], gain_total[None])]
    unnamed x14 -> x12, local copies, waits for them, and re-layouts: 3.24 us -> 0.03 us
    convert_element_type x1 -> x0, local copies, waits for them, and re-layouts: 1.65 us -> none  [on_device(): outs.append(out.astype(jnp.bfloat16))]
    convert_element_type x2, other arithmetic: 6.63 us -> 8.21 us  [on_device(): input_grad = (grad_out[lo:lo + step].astype(jnp.float32) + rstd[lo:lo + s...]
  transfers between devices with their start and end apart: 9 -> 9, of which waited for: 4 -> 4; matrix products, arithmetic and copies ran while one was open for 26% -> 31% of each run, Pallas kernels for 0% -> 0%
where the time goes in v12:
time: 148 us; the launch traced here: 147 us
  waiting for transfers between devices  41.6 us (28%)
  blocking collectives  34.3 us (23%)
  matrix products  26.3 us (18%)
  other arithmetic  21.3 us (14%)
  between operations  14.2 us (10%)
  starting transfers between devices  4.93 us (3%)
  local copies, waits for them, and re-layouts  4.18 us (3%)
    ppermute x2, waiting for transfers between devices, shifted(): return lax.ppermute(block, axis, [(i, (i + shift) % n) for i in range(n)])  22.2 us
    psum x2, blocking collectives, on_device(): lax.psum(jnp.sum(scaled * normed_c, axis=1, keepdims=True), 'tensor')  20.7 us
    all_gather x2, waiting for transfers between devices, on_device(): lax.all_gather(grad_kv[c * step:(c + 1) * step], 'tensor', axis=1, tiled=...  18.2 us
    psum x1, blocking collectives, on_device(): lax.psum(jnp.sum(values * values, axis=1, keepdims=True), 'tensor')  13.6 us
    dot_general x2, matrix products, on_device(): lax.dot_general(block, weight, (((1,), (1,)), ((), ())), preferred_elemen...  12.1 us
    dot_general x2, matrix products, pair_block(): lax.dot_general(hidden_partner, partner_cols, (((0,), (0,)), ((), ())), p...  9.71 us
    convert_element_type x2, other arithmetic, on_device(): input_grad = (grad_out[lo:lo + step].astype(jnp.float32) + rstd[lo:lo + s...  8.21 us
    dot_general x2, matrix products, pair_block(): lax.dot_general(h_own, own_cols, (((0,), (0,)), ((), ())), preferred_elem...  4.53 us
  transfers between devices with their start and end apart: 9, of which 4 were waited for; matrix products, arithmetic and copies ran while one was open for 31% of the time, Pallas kernels for 0%

profile of v12, /device:TPU:0, one launch (start us, length us, event | category | flops | bytes accessed | tf_op | source)
XLA Modules:
  0.0 146.8 jit_solution(15634298870874612941)
XLA Ops:
  7.2 1.9 %fusion.19 = (bf16[1,1,256,512]{3,2,1,0:T(8,128)(2,1)}, bf16[1,1,256,512]{3,2,1,0:T(8,128)(2,1)}) fusion(bf16[1,1,512,512]{3,2,1,0:T(8,128)(2,1)} %param.7), kind=kLoop, calls=%fused_computation.44 | loop fusion | bytes 1048576 | tf_op jit(solution)/shard_map/slice | solution.py:49
  9.8 2.1 %fusion.4 = f32[512]{0:T(512)S(1)} fusion(bf16[1,1,512,2048]{3,2,1,0:T(8,128)(2,1)} %param.5), kind=kLoop, calls=%fused_computation.6 | loop fusion | flops 3145216 | bytes 2099200 | tf_op jit(solution)/shard_map/reduce_sum | solution.py:41
  11.9 13.6 %psum.21 = f32[512,1]{0,1:T(1,128)S(1)} all-reduce(f32[512,1]{0,1:T(1,128)S(1)} %bitcast.58), channel_id=1, replica_groups=mesh['dp'=4,'pipe'=2,'tensor'=4] {'tensor'}, use_global_device_ids=true, to_apply=%region_1.2 | all-reduce | flops 512 | bytes 4096 | tf_op jit(solution)/shard_map/psum | solution.py:41
  25.5 4.1 %multiply_convert_fusion = (bf16[512,2048]{1,0:T(8,128)(2,1)S(1)}, f32[512,2048]{1,0:T(8,128)}) fusion(f32[2048]{0:T(1024)S(1)} %bitcast.51, f32[512]{0:T(512)S(1)} %bitcast.57, bf16[1,1,512,2048]{3,2,1,0:T(8,128)(2,1)} %param.5), kind=kLoop, calls=%fused_computation.9 | loop fusion | flops 4194304 | bytes 8398848 | tf_op jit(solution)/shard_map/convert_element_type | solution.py:44
  29.6 11.2 %all-gather.5.cloned.1.call-done = bf16[1,1,256,2048]{3,2,1,0:T(8,128)(2,1)} async-done(((bf16[1,1,256,512]{3,2,1,0:T(8,128)(2,1)}), bf16[1,1,256,2048]{3,2,1,0:T(8,128)(2,1)}) %all-gather.5.cloned.1.call-update) | async-done | bytes 1048592 | tf_op jit(solution)/shard_map/all_gather | solution.py:49
  40.8 8.2 %multiply_reduce_fusion.1 = (f32[2048]{0:T(1024)S(1)}, f32[256]{0:T(256)S(1)}, f32[256,2048]{1,0:T(8,128)}) fusion(f32[512,2048]{1,0:T(8,128)} %get-tuple-element.18, f32[2048]{0:T(1024)S(1)} %bitcast.52, bf16[1,2048,2048]{2,1,0:T(8,128)(2,1)} %param.9, bf16[1,1,256,2048]{3,2,1,0:T(8,128)(2,1)} %all-gather.5.cloned.1.call-done), kind=kOutput, calls=%fused_computation.17 | convolution fusion | flops 2150102784 | bytes 13648896 | tf_op jit(solution)/shard_map/dot_general | solution.py:72
  49.0 10.5 %psum.22 = f32[256,1]{0,1:T(1,128)S(1)} all-reduce(f32[256,1]{0,1:T(1,128)S(1)} %bitcast.66), channel_id=1, replica_groups=mesh['dp'=4,'pipe'=2,'tensor'=4] {'tensor'}, use_global_device_ids=true, to_apply=%region_3.4 | all-reduce | flops 256 | bytes 2048 | tf_op jit(solution)/shard_map/psum | solution.py:77
  59.5 4.2 %fusion.7 = bf16[256,2048]{1,0:T(8,128)(2,1)} fusion(f32[256,2048]{1,0:T(8,128)} %get-tuple-element.31, f32[512,2048]{1,0:T(8,128)} %get-tuple-element.18, f32[256]{0:T(256)S(1)} %bitcast.62, f32[2048]{0:T(1024)S(1)} %bitcast.53, f32[256]{0:T(256)S(1)} %bitcast.64, bf16[1,1,512,2048]{3,2,1,0:T(8,128)(2,1)} %param.6), kind=kLoop, calls=%fused_computation.15 | loop fusion | flops 3670016 | bytes 6301696 | tf_op jit(solution)/shard_map/convert_element_type | solution.py:81
  63.7 7.0 %all-gather.7.cloned.1.call-done = bf16[1,1,256,2048]{3,2,1,0:T(8,128)(2,1)} async-done(((bf16[1,1,256,512]{3,2,1,0:T(8,128)(2,1)}), bf16[1,1,256,2048]{3,2,1,0:T(8,128)(2,1)}) %all-gather.7.cloned.1.call-update) | async-done | bytes 1048592 | tf_op jit(solution)/shard_map/all_gather | solution.py:49
  70.7 2.2 %constant_dynamic-slice_fusion.1 = (bf16[256,512]{1,0:T(8,128)(2,1)S(1)}, bf16[256,512]{1,0:T(8,128)(2,1)S(1)}, bf16[256,512]{1,0:T(8,128)(2,1)S(1)}, bf16[256,5...) fusion(bf16[256,2048]{1,0:T(8,128)(2,1)} %bitcast.48, ...), kind=kLoop, calls=%fused_computation.32 | loop fusion | bytes 4194320 | tf_op jit(solution)/shard_map/dynamic_slice | solution.py:57
  74.0 1.3 collective-permute-start
  75.3 1.2 maximum_maximum_fusion
  76.5 1.3 fusion.12
  77.9 4.6 %add_convert_fusion.1 = bf16[2048,512]{1,0:T(8,128)(2,1)} fusion(f32[2048,512]{1,0:T(8,128)S(1)} %fusion.12, bf16[512,2048]{1,0:T(8,128)(2,1)} %collective-permute-done.1, bf16[512,1024]{1,0:T(8,128)(2,1)} %collective-permute-done.2, s32[]{:T(128)S(6)} %select_n.55), kind=kOutput, calls=%fused_computation.8 | convolution fusion | flops 1075838976 | bytes 8912900 | tf_op jit(solution)/shard_map/dot_general | solution.py:95
  82.5 1.5 collective-permute-start.4
  84.0 3.9 %multiply_reduce_fusion = (f32[2048]{0:T(1024)S(1)}, f32[256]{0:T(256)S(1)}, f32[256,2048]{1,0:T(8,128)}) fusion(f32[512,2048]{1,0:T(8,128)S(1)} %copy-done.1, f32[2048]{0:T(1024)S(1)} %bitcast.54, bf16[256,2048]{1,0:T(8,128)(2,1)S(1)} %bitcast.49, bf16[1,2048,2048]{2,1,0:T(8,128)(2,1)S(1)} %bitcast.68), kind=kOutput, calls=%fused_computation.16 | convolution fusion | flops 2150102784 | bytes 13648896 | tf_op jit(solution)/shard_map/dot_general | solution.py:72
  87.9 10.2 %psum.23 = f32[256,1]{0,1:T(1,128)S(1)} all-reduce(f32[256,1]{0,1:T(1,128)S(1)} %bitcast.65), channel_id=1, replica_groups=mesh['dp'=4,'pipe'=2,'tensor'=4] {'tensor'}, use_global_device_ids=true, to_apply=%region_5.6 | all-reduce | flops 256 | bytes 2048 | tf_op jit(solution)/shard_map/psum | solution.py:77
  98.1 4.0 %fusion.6 = bf16[256,2048]{1,0:T(8,128)(2,1)} fusion(f32[256,2048]{1,0:T(8,128)} %get-tuple-element.32, f32[512,2048]{1,0:T(8,128)} %get-tuple-element.18, f32[256]{0:T(256)S(1)} %bitcast.61, f32[256]{0:T(256)S(1)} %bitcast.63, bf16[1,1,512,2048]{3,2,1,0:T(8,128)(2,1)} %param.6, f32[2048]{0:T(1024)S(1)} %bitcast.55), kind=kLoop, calls=%fused_computation.13 | loop fusion | flops 3670016 | bytes 6301696 | tf_op jit(solution)/shard_map/convert_element_type | solution.py:81
  102.1 1.5 collective-permute-start.3
  103.7 1.1 collective-permute-done.5
  105.4 3.2 %fusion.9 = f32[2048,512]{1,0:T(8,128)} fusion(bf16[512,2048]{1,0:T(8,128)(2,1)S(1)} %get-tuple-element.12, bf16[512,1024]{1,0:T(8,128)(2,1)S(1)} %maximum_maximum_fusion, s32[]{:T(128)S(6)} %select_n.58), kind=kOutput, calls=%fused_computation.23 | convolution fusion | flops 1073741824 | bytes 6815748 | tf_op jit(solution)/shard_map/dot_general | solution.py:93
  108.7 22.2 %collective-permute-done.6 = f32[2048]{0:T(1024)S(1)} collective-permute-done((f32[2048]{0:T(1024)S(1)}, f32[2048]{0:T(1024)S(1)}, u32[]{:S(2)}, u32[]{:S(2)}) %collective-permute-start.6) | collective-permute-done | bytes 8224 | tf_op jit(solution)/shard_map/ppermute | solution.py:18
  131.6 3.3 %maximum_bitcast_fusion = bf16[1,1,512,2048]{3,2,1,0:T(8,128)(2,1)} fusion(bf16[256,2048]{1,0:T(8,128)(2,1)} %collective-permute-done.3, bf16[256,2048]{1,0:T(8,128)(2,1)} %collective-permute-done), kind=kLoop, calls=%fused_computation.11 | loop fusion | flops 4194304 | bytes 4194304 | tf_op jit(solution)/shard_map/broadcast_in_dim | solution.py:119
  134.9 5.1 %fusion.5 = bf16[1,2048,512]{2,1,0:T(8,128)(2,1)} fusion(bf16[2048,512]{1,0:T(8,128)(2,1)} %collective-permute-done.4, f32[2048,512]{1,0:T(8,128)S(1)} %copy-done, bf16[512,2048]{1,0:T(8,128)(2,1)} %collective-permute-done.1, bf16[512,1024]{1,0:T(8,128)(2,1)} %collective-permute-done.2, s32[]{:T(128)S(6)} %select_n.58), kind=kOutput, calls=%fused_computation.10 | convolution fusion | flops 1077936128 | bytes 11010052 | tf_op jit(solution)/shard_map/dot_general | solution.py:95
  (38 shorter events, 3.4 us)
Async XLA Ops:
  7.2 33.7 %all-gather.5.cloned.1.call-start = ((), (), s32[]{:S(2)}) async-start(), calls=%async_computation | async-start | bytes 1310720 | tf_op jit(solution)/shard_map/all_gather | solution.py:49
  9.1 61.6 %all-gather.7.cloned.1.call-start = ((), (), s32[]{:S(2)}) async-start(), calls=%async_computation.1 | async-start | bytes 1310720 | tf_op jit(solution)/shard_map/all_gather | solution.py:49
  29.6 48.3 %collective-permute-start.1 = (bf16[512,2048]{1,0:T(8,128)(2,1)S(1)}, bf16[512,2048]{1,0:T(8,128)(2,1)}, u32[]{:S(2)}, u32[]{:S(2)}) collective-permute-start(bf16[512,2048]{1,0:T(8,128)(2,1)S(1)} %get-tuple-element.12), channel_id=1, source_target_pairs={{0,8},{8,0},{16,24},{24,16},{1,9},{9,1},{17,25},{25,17},{2,10},{10... | collective-permute-start | bytes 6291464 | tf_op jit(solution)/shard_map/ppermute | solution.py:23
  59.5 11.2 %copy-start.3 = (bf16[1,1,256,2048]{3,2,1,0:T(8,128)(2,1)S(1)}, bf16[1,1,256,2048]{3,2,1,0:T(8,128)(2,1)}, u32[]{:S(2)}) copy-start(bf16[1,1,256,2048]{3,2,1,0:T(8,128)(2,1)} %all-gather.5.cloned.1.call-done) | copy-start | bytes 3145732
  74.0 3.9 %collective-permute-start.2 = (bf16[512,1024]{1,0:T(8,128)(2,1)}, bf16[512,1024]{1,0:T(8,128)(2,1)}, u32[]{:S(2)}, u32[]{:S(2)}) collective-permute-start(bf16[512,1024]{1,0:T(8,128)(2,1)} %maximum_maximum_fusion.1), channel_id=1, source_target_pairs={{0,8},{8,0},{16,24},{24,16},{1,9},{9,1},{17,25},{25,17},{2,10},{10... | collective-permute-start | bytes 3145736 | tf_op jit(solution)/shard_map/ppermute | solution.py:23
  74.0 57.6 %collective-permute-start = (bf16[256,2048]{1,0:T(8,128)(2,1)}, bf16[256,2048]{1,0:T(8,128)(2,1)}, u32[]{:S(2)}, u32[]{:S(2)}) collective-permute-start(bf16[256,2048]{1,0:T(8,128)(2,1)} %fusion.7), channel_id=1, source_target_pairs={{4,0},{5,1},{6,2},{7,3},{12,8},{13,9},{14,10},{15,11},{20,16},{21,... | collective-permute-start | bytes 3145736 | tf_op jit(solution)/shard_map/ppermute | solution.py:13
  76.5 7.4 %slice-start = ((s8[8388608]{0:T(1024)(128)(4,1)}), s8[4194304]{0:T(1024)(128)(4,1)S(1)}, s32[]{:S(2)}) async-start(s8[8388608]{0:T(1024)(128)(4,1)} %bitcast.67), calls=%async_computation.2 | async-start | bytes 8388608
  77.8 6.1 %copy-start.1 = (f32[512,2048]{1,0:T(8,128)S(1)}, f32[512,2048]{1,0:T(8,128)}, u32[]{:S(2)}) copy-start(f32[512,2048]{1,0:T(8,128)} %get-tuple-element.18) | copy-start | bytes 12582916
  77.8 6.1 %copy-start.2 = (bf16[1,1,256,2048]{3,2,1,0:T(8,128)(2,1)S(1)}, bf16[1,1,256,2048]{3,2,1,0:T(8,128)(2,1)}, u32[]{:S(2)}) copy-start(bf16[1,1,256,2048]{3,2,1,0:T(8,128)(2,1)} %all-gather.7.cloned.1.call-done) | copy-start | bytes 3145732
  77.8 6.1 %slice-start.1 = ((s8[8388608]{0:T(1024)(128)(4,1)}), s8[4194304]{0:T(1024)(128)(4,1)S(1)}, s32[]{:S(2)}) async-start(s8[8388608]{0:T(1024)(128)(4,1)} %bitcast.67), calls=%async_computation.3 | async-start | bytes 8388608
  82.5 52.4 %collective-permute-start.4 = (bf16[2048,512]{1,0:T(8,128)(2,1)}, bf16[2048,512]{1,0:T(8,128)(2,1)}, u32[]{:S(2)}, u32[]{:S(2)}) collective-permute-start(bf16[2048,512]{1,0:T(8,128)(2,1)} %add_convert_fusion.1), channel_id=1, source_target_pairs={{0,16},{8,24},{16,0},{24,8},{1,17},{9,25},{17,1},{25,9},{2,18},{10... | collective-permute-start | bytes 6291464 | tf_op jit(solution)/shard_map/ppermute | solution.py:18
  102.1 29.5 %collective-permute-start.3 = (bf16[256,2048]{1,0:T(8,128)(2,1)}, bf16[256,2048]{1,0:T(8,128)(2,1)}, u32[]{:S(2)}, u32[]{:S(2)}) collective-permute-start(bf16[256,2048]{1,0:T(8,128)(2,1)} %fusion.6), channel_id=1, source_target_pairs={{4,0},{5,1},{6,2},{7,3},{12,8},{13,9},{14,10},{15,11},{20,16},{21,... | collective-permute-start | bytes 3145736 | tf_op jit(solution)/shard_map/ppermute | solution.py:13
  103.6 1.2 collective-permute-start.5
  104.8 26.1 %collective-permute-start.6 = (f32[2048]{0:T(1024)S(1)}, f32[2048]{0:T(1024)S(1)}, u32[]{:S(2)}, u32[]{:S(2)}) collective-permute-start(f32[2048]{0:T(1024)S(1)} %add.106), channel_id=1, source_target_pairs={{0,16},{8,24},{16,0},{24,8},{1,17},{9,25},{17,1},{25,9},{2,18},{10... | collective-permute-start | bytes 24584 | tf_op jit(solution)/shard_map/ppermute | solution.py:18
  131.6 3.3 %copy-start = (f32[2048,512]{1,0:T(8,128)S(1)}, f32[2048,512]{1,0:T(8,128)}, u32[]{:S(2)}) copy-start(f32[2048,512]{1,0:T(8,128)} %fusion.9) | copy-start | bytes 12582916
Sparse Core Ops, SparseCore 0:
  10.1 30.6 all-gather.4
  43.0 27.6 all-gather.6

commit v13 on v7

--- a/solution.py
+++ b/solution.py
@@ -49,14 +49,29 @@
         lax.all_gather(grad_kv[c * step:(c + 1) * step], "tensor", axis=1, tiled=True)
         for c in range(CHUNKS)
     ]
-    piece = jnp.concatenate(pieces, axis=0)
 
-    def cols_of(p):
+    def cols_of(q, p):
         return jnp.concatenate(
-            [lax.dynamic_slice_in_dim(piece, (2 * g + p) * kv_block, kv_block, axis=1) for g in range(groups)],
+            [lax.dynamic_slice_in_dim(q, (2 * g + p) * kv_block, kv_block, axis=1) for g in range(groups)],
             axis=1,
         )
 
+    def tn(a, b):
+        return lax.dot_general(a, b, (((0,), (0,)), ((), ())), preferred_element_type=jnp.float32)
+
+    own_g = me // 2
+    dests = [(own_g + d) % groups for d in range(1, groups)]
+
+    def pair_blocks(h_own, h_partner, q):
+        own_cols = cols_of(q, parity)
+        partner_cols = to_partner(cols_of(q, 1 - parity))
+
+        def block_of(g):
+            oc = lax.dynamic_slice_in_dim(own_cols, g * kv_block, kv_block, axis=1)
+            pc = lax.dynamic_slice_in_dim(partner_cols, g * kv_block, kv_block, axis=1)
+            return tn(h_own, oc) + tn(h_partner, pc)
+
+        return block_of
 
     inputs_grad = []
     gain_part = jnp.zeros((d_local,), jnp.float32)
@@ -77,27 +92,27 @@
         inputs_grad.append(from_behind(input_grad, "pipe", -1))
         gain_part = gain_part + jnp.sum(row_total * normed_c, axis=0)
         if c == 0:
-            _, (h_own, piece) = lax.optimization_barrier((input_grad, (hidden, piece)))
-            cols_partner = to_partner(cols_of(1 - parity))
-            cols_own = cols_of(parity)
-            pair = lax.dot_general(
-                h_own, cols_own, (((0,), (0,)), ((), ())), preferred_element_type=jnp.float32
-            ) + lax.dot_general(
-                hidden_partner, cols_partner, (((0,), (0,)), ((), ())),
-                preferred_element_type=jnp.float32,
-            )
-            own_g = me // 2
-            total = lax.dynamic_slice_in_dim(pair, own_g * kv_block, kv_block, axis=1)
+            _, (h, hp, parts) = lax.optimization_barrier((input_grad, (hidden, hidden_partner, pieces)))
+            chunk_blocks = [
+                pair_blocks(h[k * step:(k + 1) * step], hp[k * step:(k + 1) * step], parts[k])
+                for k in range(CHUNKS)
+            ]
             outs = []
-            for d in range(1, groups):
-                dest_g = (own_g + d) % groups
-                out = lax.dynamic_slice_in_dim(pair, dest_g * kv_block, kv_block, axis=1)
-                outs.append(out.astype(jnp.bfloat16))
-            for d, out in enumerate(outs, start=1):
-                total = total + shifted(out, "dp", 2 * d).astype(jnp.float32)
+            for g in dests:
+                acc = chunk_blocks[0](g)
+                for k in range(1, CHUNKS):
+                    acc = acc + chunk_blocks[k](g)
+                outs.append(acc.astype(jnp.bfloat16))
+            received = [shifted(out, "dp", 2 * d) for d, out in enumerate(outs, start=1)]
+            _, first = lax.optimization_barrier((outs, chunk_blocks[0](own_g)))
+            total = first
+            for k in range(1, CHUNKS):
+                total = total + chunk_blocks[k](own_g)
+            for got in received:
+                total = total + got.astype(jnp.float32)
             weight_total = total.astype(jnp.bfloat16)
         if c + 1 < CHUNKS:
-            _, block = lax.optimization_barrier(((input_grad, outs), pieces[c + 1]))
+            _, block = lax.optimization_barrier(((input_grad, outs), parts[c + 1]))
 
     upstream = jnp.concatenate(inputs_grad, axis=0)
     pair_gain = gain_part + to_partner(gain_part)

time: 156 us -> 146 us (0.936)
  waiting for transfers between devices: 51.5 us -> 35.7 us
  matrix products: 17.9 us -> 32.9 us
  local copies, waits for them, and re-layouts: 9.23 us -> 3.76 us
  other arithmetic: 22.8 us -> 18.3 us
    dot_general x2 -> x8, matrix products: 7 us -> 20.8 us  [tn(): lax.dot_general(a, b, (((0,), (0,)), ((), ())), preferred_element_type=jn...]
    ppermute x2, waiting for transfers between devices: 27.7 us -> 17.9 us  [shifted(): return lax.ppermute(block, axis, [(i, (i + shift) % n) for i in range(n)])]
    broadcast_in_dim x2 -> x1, other arithmetic: 7.58 us -> 3.26 us  [on_device(): return (upstream[None, None], weight_total[None], gain_total[None])]
    all_gather x2, waiting for transfers between devices: 21.9 us -> 17.7 us  [on_device(): lax.all_gather(grad_kv[c * step:(c + 1) * step], 'tensor', axis=1, tiled=...]
    unnamed x16 -> x20, local copies, waits for them, and re-layouts: 4.18 us -> 0.17 us
    concatenate x2, other arithmetic: 2.66 us -> 0.12 us  [cols_of(): jnp.concatenate([lax.dynamic_slice_in_dim(q, (2 * g + p) * kv_block, kv_b...]
    convert_element_type x2, other arithmetic: 5.92 us -> 8.2 us  [on_device(): input_grad = (grad_out[lo:lo + step].astype(jnp.float32) + rstd[lo:lo + s...]
    convert_element_type x1 -> x0, local copies, waits for them, and re-layouts: 1.65 us -> none  [on_device(): outs.append(out.astype(jnp.bfloat16))]
  transfers between devices with their start and end apart: 9 -> 10, of which waited for: 4 -> 3; matrix products, arithmetic and copies ran while one was open for 25% -> 32% of each run, Pallas kernels for 0% -> 0%
where the time goes in v13:
time: 146 us; the launch traced here: 145 us
  waiting for transfers between devices  35.7 us (24%)
  blocking collectives  34.2 us (23%)
  matrix products  32.9 us (23%)
  other arithmetic  18.3 us (13%)
  between operations  14.3 us (10%)
  starting transfers between devices  6.08 us (4%)
  local copies, waits for them, and re-layouts  3.76 us (3%)
    dot_general x8, matrix products, tn(): lax.dot_general(a, b, (((0,), (0,)), ((), ())), preferred_element_type=jn...  20.8 us
    psum x2, blocking collectives, on_device(): lax.psum(jnp.sum(scaled * normed_c, axis=1, keepdims=True), 'tensor')  20.7 us
    ppermute x2, waiting for transfers between devices, shifted(): return lax.ppermute(block, axis, [(i, (i + shift) % n) for i in range(n)])  17.9 us
    all_gather x2, waiting for transfers between devices, on_device(): lax.all_gather(grad_kv[c * step:(c + 1) * step], 'tensor', axis=1, tiled=...  17.7 us
    psum x1, blocking collectives, on_device(): lax.psum(jnp.sum(values * values, axis=1, keepdims=True), 'tensor')  13.5 us
    dot_general x2, matrix products, on_device(): lax.dot_general(block, weight, (((1,), (1,)), ((), ())), preferred_elemen...  12.1 us
    convert_element_type x2, other arithmetic, on_device(): input_grad = (grad_out[lo:lo + step].astype(jnp.float32) + rstd[lo:lo + s...  8.2 us
    convert_element_type x1, other arithmetic, on_device(): hidden = (normed * gain_f).astype(jnp.bfloat16)  3.29 us
  transfers between devices with their start and end apart: 10, of which 3 were waited for; matrix products, arithmetic and copies ran while one was open for 32% of the time, Pallas kernels for 0%

profile of v13, /device:TPU:0, one launch (start us, length us, event | category | flops | bytes accessed | tf_op | source)
XLA Modules:
  0.0 145.2 jit_solution(9623613785982596993)
XLA Ops:
  7.2 2.0 %fusion.46 = (bf16[1,1,256,512]{3,2,1,0:T(8,128)(2,1)}, bf16[1,1,256,512]{3,2,1,0:T(8,128)(2,1)}) fusion(bf16[1,1,512,512]{3,2,1,0:T(8,128)(2,1)} %param.7), kind=kLoop, calls=%fused_computation.76 | loop fusion | bytes 1048576 | tf_op jit(solution)/shard_map/slice | solution.py:49
  10.0 2.1 %fusion.4 = f32[512]{0:T(512)S(1)} fusion(bf16[1,1,512,2048]{3,2,1,0:T(8,128)(2,1)} %param.5), kind=kLoop, calls=%fused_computation.6 | loop fusion | flops 3145216 | bytes 2099200 | tf_op jit(solution)/shard_map/reduce_sum | solution.py:41
  12.1 13.5 %psum.21 = f32[512,1]{0,1:T(1,128)S(1)} all-reduce(f32[512,1]{0,1:T(1,128)S(1)} %bitcast.54), channel_id=1, replica_groups=mesh['dp'=4,'pipe'=2,'tensor'=4] {'tensor'}, use_global_device_ids=true, to_apply=%region_1.2 | all-reduce | flops 512 | bytes 4096 | tf_op jit(solution)/shard_map/psum | solution.py:41
  25.6 3.3 %multiply_convert_fusion = (bf16[512,2048]{1,0:T(8,128)(2,1)}, f32[512,2048]{1,0:T(8,128)}) fusion(f32[2048]{0:T(1024)S(1)} %bitcast.47, f32[512]{0:T(512)S(1)} %bitcast.53, bf16[1,1,512,2048]{3,2,1,0:T(8,128)(2,1)S(1)} %copy-done.2), kind=kLoop, calls=%fused_computation.9 | loop fusion | flops 4194304 | bytes 8398848 | tf_op jit(solution)/shard_map/convert_element_type | solution.py:44
  29.0 11.8 %all-gather.5.cloned.1.call-done = bf16[1,1,256,2048]{3,2,1,0:T(8,128)(2,1)} async-done(((bf16[1,1,256,512]{3,2,1,0:T(8,128)(2,1)}), bf16[1,1,256,2048]{3,2,1,0:T(8,128)(2,1)}) %all-gather.5.cloned.1.call-update) | async-done | bytes 1048592 | tf_op jit(solution)/shard_map/all_gather | solution.py:49
  40.9 8.2 %multiply_reduce_fusion.1 = (f32[2048]{0:T(1024)S(1)}, f32[256]{0:T(256)S(1)}, f32[256,2048]{1,0:T(8,128)}) fusion(f32[512,2048]{1,0:T(8,128)} %get-tuple-element.20, f32[2048]{0:T(1024)S(1)} %bitcast.48, bf16[1,2048,2048]{2,1,0:T(8,128)(2,1)} %param.9, bf16[1,1,256,2048]{3,2,1,0:T(8,128)(2,1)} %all-gather.5.cloned.1.call-done), kind=kOutput, calls=%fused_computation.18 | convolution fusion | flops 2150102784 | bytes 13648896 | tf_op jit(solution)/shard_map/dot_general | solution.py:82
  49.0 10.5 %psum.22 = f32[256,1]{0,1:T(1,128)S(1)} all-reduce(f32[256,1]{0,1:T(1,128)S(1)} %bitcast.62), channel_id=1, replica_groups=mesh['dp'=4,'pipe'=2,'tensor'=4] {'tensor'}, use_global_device_ids=true, to_apply=%region_3.4 | all-reduce | flops 256 | bytes 2048 | tf_op jit(solution)/shard_map/psum | solution.py:87
  59.5 4.1 %fusion.7 = bf16[256,2048]{1,0:T(8,128)(2,1)} fusion(f32[256,2048]{1,0:T(8,128)} %get-tuple-element.33, f32[512,2048]{1,0:T(8,128)} %get-tuple-element.20, f32[256]{0:T(256)S(1)} %bitcast.58, f32[2048]{0:T(1024)S(1)} %bitcast.49, f32[256]{0:T(256)S(1)} %bitcast.60, bf16[1,1,512,2048]{3,2,1,0:T(8,128)(2,1)} %param.6), kind=kLoop, calls=%fused_computation.16 | loop fusion | flops 3670016 | bytes 6301696 | tf_op jit(solution)/shard_map/convert_element_type | solution.py:91
  63.6 1.3 collective-permute-start
  64.9 5.8 %all-gather.7.cloned.1.call-done = bf16[1,1,256,2048]{3,2,1,0:T(8,128)(2,1)} async-done(((bf16[1,1,256,512]{3,2,1,0:T(8,128)(2,1)}), bf16[1,1,256,2048]{3,2,1,0:T(8,128)(2,1)}) %all-gather.7.cloned.1.call-update) | async-done | bytes 1048592 | tf_op jit(solution)/shard_map/all_gather | solution.py:49
  70.7 1.4 constant_dynamic-slice_fusion.5
  73.0 2.0 %fusion.19 = f32[2048,512]{1,0:T(8,128)S(1)} fusion(bf16[512,2048]{1,0:T(8,128)(2,1)} %get-tuple-element.9, s32[]{:T(128)S(6)} %select_n.59, bf16[256,512]{1,0:T(8,128)(2,1)S(1)} %get-tuple-element.28, bf16[256,512]{1,0:T(8,128)(2,1)S(1)} %get-tuple-element.27), kind=kOutput, calls=%fused_computation.32 | convolution fusion | flops 537395200 | bytes 5767172 | tf_op jit(solution)/shard_map/dot_general | solution.py:60
  76.6 4.1 %add_convert_fusion.1 = bf16[2048,512]{1,0:T(8,128)(2,1)} fusion(f32[2048,512]{1,0:T(8,128)S(1)} %fusion.10, f32[2048,512]{1,0:T(8,128)S(1)} %fusion.19, f32[2048,512]{1,0:T(8,128)S(1)} %fusion.16, bf16[512,2048]{1,0:T(8,128)(2,1)} %get-tuple-element.9, s32[]{:T(128)S(6)} %select_n.59, bf16[256,512]{1,0:T(8,128)(2,1)S(1)} %get-tuple-element.24, ...), kind=kOutput, calls=%fused_computation.8 | convolution fusion | flops 541589504 | bytes 16252932 | tf_op jit(solution)/shard_map/dot_general | solution.py:60
  80.7 1.5 %collective-permute-start.5 = (bf16[2048,512]{1,0:T(8,128)(2,1)}, bf16[2048,512]{1,0:T(8,128)(2,1)}, u32[]{:S(2)}, u32[]{:S(2)}) collective-permute-start(bf16[2048,512]{1,0:T(8,128)(2,1)} %add_convert_fusion.1), channel_id=1, source_target_pairs={{0,16},{8,24},{16,0},{24,8},{1,17},{9,25},{17,1},{25,9},{2,18},{10... | collective-permute-start | bytes 6291464 | tf_op jit(solution)/shard_map/ppermute | solution.py:18
  82.2 4.0 %multiply_reduce_fusion = (f32[2048]{0:T(1024)S(1)}, f32[256]{0:T(256)S(1)}, f32[256,2048]{1,0:T(8,128)}) fusion(f32[512,2048]{1,0:T(8,128)S(1)} %copy-done.1, f32[2048]{0:T(1024)S(1)} %bitcast.50, bf16[256,2048]{1,0:T(8,128)(2,1)S(1)} %bitcast.45, bf16[1,2048,2048]{2,1,0:T(8,128)(2,1)S(1)} %bitcast.64), kind=kOutput, calls=%fused_computation.17 | convolution fusion | flops 2150102784 | bytes 13648896 | tf_op jit(solution)/shard_map/dot_general | solution.py:82
  86.2 10.2 %psum.23 = f32[256,1]{0,1:T(1,128)S(1)} all-reduce(f32[256,1]{0,1:T(1,128)S(1)} %bitcast.61), channel_id=1, replica_groups=mesh['dp'=4,'pipe'=2,'tensor'=4] {'tensor'}, use_global_device_ids=true, to_apply=%region_5.6 | all-reduce | flops 256 | bytes 2048 | tf_op jit(solution)/shard_map/psum | solution.py:87
  96.4 4.1 %fusion.6 = bf16[256,2048]{1,0:T(8,128)(2,1)} fusion(f32[256,2048]{1,0:T(8,128)} %get-tuple-element.34, f32[512,2048]{1,0:T(8,128)} %get-tuple-element.20, f32[256]{0:T(256)S(1)} %bitcast.57, f32[256]{0:T(256)S(1)} %bitcast.59, bf16[1,1,512,2048]{3,2,1,0:T(8,128)(2,1)} %param.6, f32[2048]{0:T(1024)S(1)} %bitcast.51), kind=kLoop, calls=%fused_computation.14 | loop fusion | flops 3670016 | bytes 6301696 | tf_op jit(solution)/shard_map/convert_element_type | solution.py:91
  100.5 1.5 %collective-permute-start.4 = (bf16[256,2048]{1,0:T(8,128)(2,1)}, bf16[256,2048]{1,0:T(8,128)(2,1)}, u32[]{:S(2)}, u32[]{:S(2)}) collective-permute-start(bf16[256,2048]{1,0:T(8,128)(2,1)} %fusion.6), channel_id=1, source_target_pairs={{4,0},{5,1},{6,2},{7,3},{12,8},{13,9},{14,10},{15,11},{20,16},{21,... | collective-permute-start | bytes 3145736 | tf_op jit(solution)/shard_map/ppermute | solution.py:13
  102.7 4.1 %convolution_add_fusion = f32[2048,512]{1,0:T(8,128)} fusion(f32[2048,512]{1,0:T(8,128)S(1)} %fusion.14, bf16[512,2048]{1,0:T(8,128)(2,1)} %get-tuple-element.9, s32[]{:T(128)S(6)} %select_n.62, bf16[256,512]{1,0:T(8,128)(2,1)S(1)} %get-tuple-element.28, bf16[256,512]{1,0:T(8,128)(2,1)S(1)} %get-tuple-element.27), kind=kOutput, calls=%fused_computation.10 | convolution fusion | flops 538443776 | bytes 9961476 | tf_op jit(solution)/shard_map/dot_general | solution.py:60
  106.8 1.2 collective-permute-start.7
  108.0 2.7 %fusion.8 = f32[2048,512]{1,0:T(8,128)} fusion(bf16[512,2048]{1,0:T(8,128)(2,1)S(1)} %collective-permute-done.1, bf16[256,1024]{1,0:T(8,128)(2,1)S(1)} %copy-done.5, s32[]{:T(128)S(6)} %select_n.62), kind=kOutput, calls=%fused_computation.21 | convolution fusion | flops 536870912 | bytes 5505028 | tf_op jit(solution)/shard_map/dot_general | solution.py:60
  110.8 17.9 %collective-permute-done.7 = f32[2048]{0:T(1024)S(1)} collective-permute-done((f32[2048]{0:T(1024)S(1)}, f32[2048]{0:T(1024)S(1)}, u32[]{:S(2)}, u32[]{:S(2)}) %collective-permute-start.7) | collective-permute-done | bytes 8224 | tf_op jit(solution)/shard_map/ppermute | solution.py:18
  129.4 3.3 %maximum_bitcast_fusion = bf16[1,1,512,2048]{3,2,1,0:T(8,128)(2,1)} fusion(bf16[256,2048]{1,0:T(8,128)(2,1)} %collective-permute-done.4, bf16[256,2048]{1,0:T(8,128)(2,1)} %collective-permute-done), kind=kLoop, calls=%fused_computation.12 | loop fusion | flops 4194304 | bytes 4194304 | tf_op jit(solution)/shard_map/broadcast_in_dim | solution.py:126
  132.7 5.7 %fusion.5 = bf16[1,2048,512]{2,1,0:T(8,128)(2,1)} fusion(bf16[2048,512]{1,0:T(8,128)(2,1)} %collective-permute-done.5, f32[2048,512]{1,0:T(8,128)} %convolution_add_fusion, f32[2048,512]{1,0:T(8,128)S(1)} %copy-done, bf16[512,2048]{1,0:T(8,128)(2,1)} %get-tuple-element.9, s32[]{:T(128)S(6)} %select_n.62, bf16[256,512]{1,0:T(8,128)(2,1)S(1)} %get-tuple-element.24, ...), kind=kOutput, calls=%fused_computation.11 | convolution fusion | flops 542638080 | bytes 14155780 | tf_op jit(solution)/shard_map/dot_general | solution.py:60
  (53 shorter events, 4.9 us)
Async XLA Ops:
  7.2 18.4 %copy-start.2 = (bf16[1,1,512,2048]{3,2,1,0:T(8,128)(2,1)S(1)}, bf16[1,1,512,2048]{3,2,1,0:T(8,128)(2,1)}, u32[]{:S(2)}) copy-start(bf16[1,1,512,2048]{3,2,1,0:T(8,128)(2,1)} %param.5) | copy-start | bytes 6291460
  7.2 33.7 %all-gather.5.cloned.1.call-start = ((), (), s32[]{:S(2)}) async-start(), calls=%async_computation | async-start | bytes 1310720 | tf_op jit(solution)/shard_map/all_gather | solution.py:49
  9.2 61.5 %all-gather.7.cloned.1.call-start = ((), (), s32[]{:S(2)}) async-start(), calls=%async_computation.1 | async-start | bytes 1310720 | tf_op jit(solution)/shard_map/all_gather | solution.py:49
  28.9 41.8 %collective-permute-start.1 = (bf16[512,2048]{1,0:T(8,128)(2,1)}, bf16[512,2048]{1,0:T(8,128)(2,1)S(1)}, u32[]{:S(2)}, u32[]{:S(2)}) collective-permute-start(bf16[512,2048]{1,0:T(8,128)(2,1)} %get-tuple-element.9), channel_id=1, source_target_pairs={{0,8},{8,0},{16,24},{24,16},{1,9},{9,1},{17,25},{25,17},{2,10},{10... | collective-permute-start | bytes 6291464 | tf_op jit(solution)/shard_map/ppermute | solution.py:23
  63.6 65.8 %collective-permute-start = (bf16[256,2048]{1,0:T(8,128)(2,1)}, bf16[256,2048]{1,0:T(8,128)(2,1)}, u32[]{:S(2)}, u32[]{:S(2)}) collective-permute-start(bf16[256,2048]{1,0:T(8,128)(2,1)} %fusion.7), channel_id=1, source_target_pairs={{4,0},{5,1},{6,2},{7,3},{12,8},{13,9},{14,10},{15,11},{20,16},{21,... | collective-permute-start | bytes 3145736 | tf_op jit(solution)/shard_map/ppermute | solution.py:13
  70.7 1.5 %copy-start.3 = (bf16[1,1,256,2048]{3,2,1,0:T(8,128)(2,1)S(1)}, bf16[1,1,256,2048]{3,2,1,0:T(8,128)(2,1)}, u32[]{:S(2)}) copy-start(bf16[1,1,256,2048]{3,2,1,0:T(8,128)(2,1)} %all-gather.7.cloned.1.call-done) | copy-start | bytes 3145732
  72.2 2.8 %collective-permute-start.2 = (bf16[256,1024]{1,0:T(8,128)(2,1)S(1)}, bf16[256,1024]{1,0:T(8,128)(2,1)S(1)}, u32[]{:S(2)}, u32[]{:S(2)}) collective-permute-start(bf16[256,1024]{1,0:T(8,128)(2,1)S(1)} %pad_maximum_fusion), channel_id=1, source_target_pairs={{0,8},{8,0},{16,24},{24,16},{1,9},{9,1},{17,25},{25,17},{2,10},{10... | collective-permute-start | bytes 1572872 | tf_op jit(solution)/shard_map/ppermute | solution.py:23
  72.5 3.4 %collective-permute-start.3 = (bf16[256,1024]{1,0:T(8,128)(2,1)S(1)}, bf16[256,1024]{1,0:T(8,128)(2,1)S(1)}, u32[]{:S(2)}, u32[]{:S(2)}) collective-permute-start(bf16[256,1024]{1,0:T(8,128)(2,1)S(1)} %pad_maximum_fusion.1), channel_id=1, source_target_pairs={{0,8},{8,0},{16,24},{24,16},{1,9},{9,1},{17,25},{25,17},{2,10},{10... | collective-permute-start | bytes 1572872 | tf_op jit(solution)/shard_map/ppermute | solution.py:23
  75.0 0.8 copy-start.6
  75.8 0.8 copy-start.4
  75.8 6.4 %slice-start = ((s8[8388608]{0:T(1024)(128)(4,1)}), s8[4194304]{0:T(1024)(128)(4,1)S(1)}, s32[]{:S(2)}) async-start(s8[8388608]{0:T(1024)(128)(4,1)} %bitcast.63), calls=%async_computation.2 | async-start | bytes 8388608
  76.6 5.6 %copy-start.1 = (f32[512,2048]{1,0:T(8,128)S(1)}, f32[512,2048]{1,0:T(8,128)}, u32[]{:S(2)}) copy-start(f32[512,2048]{1,0:T(8,128)} %get-tuple-element.20) | copy-start | bytes 12582916
  76.6 5.6 %slice-start.1 = ((s8[8388608]{0:T(1024)(128)(4,1)}), s8[4194304]{0:T(1024)(128)(4,1)S(1)}, s32[]{:S(2)}) async-start(s8[8388608]{0:T(1024)(128)(4,1)} %bitcast.63), calls=%async_computation.3 | async-start | bytes 8388608
  80.7 52.0 %collective-permute-start.5 = (bf16[2048,512]{1,0:T(8,128)(2,1)}, bf16[2048,512]{1,0:T(8,128)(2,1)}, u32[]{:S(2)}, u32[]{:S(2)}) collective-permute-start(bf16[2048,512]{1,0:T(8,128)(2,1)} %add_convert_fusion.1), channel_id=1, source_target_pairs={{0,16},{8,24},{16,0},{24,8},{1,17},{9,25},{17,1},{25,9},{2,18},{10... | collective-permute-start | bytes 6291464 | tf_op jit(solution)/shard_map/ppermute | solution.py:18
  86.2 20.6 %collective-permute-start.6 = (f32[2048]{0:T(1024)S(1)}, f32[2048]{0:T(1024)S(1)}, u32[]{:S(2)}, u32[]{:S(2)}) collective-permute-start(f32[2048]{0:T(1024)S(1)} %add.125), channel_id=1, source_target_pairs={{0,8},{8,0},{16,24},{24,16},{1,9},{9,1},{17,25},{25,17},{2,10},{10... | collective-permute-start | bytes 24584 | tf_op jit(solution)/shard_map/ppermute | solution.py:23
  96.4 5.6 %copy-start.7 = (bf16[256,1024]{1,0:T(8,128)(2,1)S(1)}, bf16[256,1024]{1,0:T(8,128)(2,1)}, u32[]{:S(2)}) copy-start(bf16[256,1024]{1,0:T(8,128)(2,1)} %copy-done.6) | copy-start | bytes 1572868
  100.5 28.9 %collective-permute-start.4 = (bf16[256,2048]{1,0:T(8,128)(2,1)}, bf16[256,2048]{1,0:T(8,128)(2,1)}, u32[]{:S(2)}, u32[]{:S(2)}) collective-permute-start(bf16[256,2048]{1,0:T(8,128)(2,1)} %fusion.6), channel_id=1, source_target_pairs={{4,0},{5,1},{6,2},{7,3},{12,8},{13,9},{14,10},{15,11},{20,16},{21,... | collective-permute-start | bytes 3145736 | tf_op jit(solution)/shard_map/ppermute | solution.py:13
  102.7 5.3 %copy-start.5 = (bf16[256,1024]{1,0:T(8,128)(2,1)S(1)}, bf16[256,1024]{1,0:T(8,128)(2,1)}, u32[]{:S(2)}) copy-start(bf16[256,1024]{1,0:T(8,128)(2,1)} %copy-done.4) | copy-start | bytes 1572868
  106.8 21.9 %collective-permute-start.7 = (f32[2048]{0:T(1024)S(1)}, f32[2048]{0:T(1024)S(1)}, u32[]{:S(2)}, u32[]{:S(2)}) collective-permute-start(f32[2048]{0:T(1024)S(1)} %add.126), channel_id=1, source_target_pairs={{0,16},{8,24},{16,0},{24,8},{1,17},{9,25},{17,1},{25,9},{2,18},{10... | collective-permute-start | bytes 24584 | tf_op jit(solution)/shard_map/ppermute | solution.py:18
  129.4 3.3 %copy-start = (f32[2048,512]{1,0:T(8,128)S(1)}, f32[2048,512]{1,0:T(8,128)}, u32[]{:S(2)}) copy-start(f32[2048,512]{1,0:T(8,128)} %fusion.8) | copy-start | bytes 12582916
Sparse Core Ops, SparseCore 0:
  10.2 30.6 all-gather.4
  43.0 27.6 all-gather.6

commit v14 on v13

--- a/solution.py
+++ b/solution.py
@@ -66,10 +66,10 @@
         own_cols = cols_of(q, parity)
         partner_cols = to_partner(cols_of(q, 1 - parity))
 
-        def block_of(g):
+        def block_of(g, rows):
             oc = lax.dynamic_slice_in_dim(own_cols, g * kv_block, kv_block, axis=1)
             pc = lax.dynamic_slice_in_dim(partner_cols, g * kv_block, kv_block, axis=1)
-            return tn(h_own, oc) + tn(h_partner, pc)
+            return tn(h_own[:, rows], oc) + tn(h_partner[:, rows], pc)
 
         return block_of
 
@@ -97,20 +97,28 @@
                 pair_blocks(h[k * step:(k + 1) * step], hp[k * step:(k + 1) * step], parts[k])
                 for k in range(CHUNKS)
             ]
-            outs = []
-            for g in dests:
-                acc = chunk_blocks[0](g)
+            halves = [slice(0, d_local // 2), slice(d_local // 2, d_local)]
+            outs, received = [], []
+            for rows_half in halves:
+                for d, g in enumerate(dests, start=1):
+                    acc = chunk_blocks[0](g, rows_half)
+                    for k in range(1, CHUNKS):
+                        acc = acc + chunk_blocks[k](g, rows_half)
+                    out = acc.astype(jnp.bfloat16)
+                    outs.append(out)
+                    received.append(shifted(out, "dp", 2 * d))
+            _, h_first = lax.optimization_barrier((outs, [chunk_blocks[0](own_g, r) for r in halves]))
+            pieces_out = []
+            n_dest = len(dests)
+            for i_half, rows_half in enumerate(halves):
+                total = h_first[i_half]
                 for k in range(1, CHUNKS):
-                    acc = acc + chunk_blocks[k](g)
-                outs.append(acc.astype(jnp.bfloat16))
-            received = [shifted(out, "dp", 2 * d) for d, out in enumerate(outs, start=1)]
-            _, first = lax.optimization_barrier((outs, chunk_blocks[0](own_g)))
-            total = first
-            for k in range(1, CHUNKS):
-                total = total + chunk_blocks[k](own_g)
-            for got in received:
-                total = total + got.astype(jnp.float32)
-            weight_total = total.astype(jnp.bfloat16)
+                    total = total + chunk_blocks[k](own_g, rows_half)
+                for got in received[i_half * n_dest:(i_half + 1) * n_dest]:
+                    total = total + got.astype(jnp.float32)
+                pieces_out.append(total.astype(jnp.bfloat16))
+            total = jnp.concatenate(pieces_out, axis=0)
+            weight_total = total
         if c + 1 < CHUNKS:
             _, block = lax.optimization_barrier(((input_grad, outs), parts[c + 1]))
 

time: 146 us -> 147 us (level)
  waiting for transfers between devices: 35.7 us -> 24.4 us
  matrix products: 32.9 us -> 40.2 us
  other arithmetic: 18.3 us -> 20.5 us
  local copies, waits for them, and re-layouts: 3.76 us -> 5.55 us
    ppermute x2 -> x3, waiting for transfers between devices: 17.9 us -> 7.4 us  [shifted(): return lax.ppermute(block, axis, [(i, (i + shift) % n) for i in range(n)])]
    dot_general x8 -> x16, matrix products: 20.8 us -> 28.2 us  [tn(): lax.dot_general(a, b, (((0,), (0,)), ((), ())), preferred_element_type=jn...]
    broadcast_in_dim x1 -> x2, other arithmetic: 3.26 us -> 4.57 us  [on_device(): return (upstream[None, None], weight_total[None], gain_total[None])]
    ppermute x2 -> x3, starting transfers between devices: 2.66 us -> 3.19 us  [shifted(): return lax.ppermute(block, axis, [(i, (i + shift) % n) for i in range(n)])]
  transfers between devices with their start and end apart: 10 -> 11, of which waited for: 3 -> 3; matrix products, arithmetic and copies ran while one was open for 32% -> 41% of each run, Pallas kernels for 0% -> 0%
where the time goes in v14:
time: 147 us; the launch traced here: 146 us
  matrix products  40.2 us (27%)
  blocking collectives  34.4 us (23%)
  waiting for transfers between devices  24.4 us (17%)
  other arithmetic  20.5 us (14%)
  between operations  14.4 us (10%)
  starting transfers between devices  6.46 us (4%)
  local copies, waits for them, and re-layouts  5.55 us (4%)
    dot_general x16, matrix products, tn(): lax.dot_general(a, b, (((0,), (0,)), ((), ())), preferred_element_type=jn...  28.2 us
    psum x2, blocking collectives, on_device(): lax.psum(jnp.sum(scaled * normed_c, axis=1, keepdims=True), 'tensor')  20.9 us
    all_gather x2, waiting for transfers between devices, on_device(): lax.all_gather(grad_kv[c * step:(c + 1) * step], 'tensor', axis=1, tiled=...  17 us
    psum x1, blocking collectives, on_device(): lax.psum(jnp.sum(values * values, axis=1, keepdims=True), 'tensor')  13.6 us
    dot_general x2, matrix products, on_device(): lax.dot_general(block, weight, (((1,), (1,)), ((), ())), preferred_elemen...  12.1 us
    convert_element_type x2, other arithmetic, on_device(): input_grad = (grad_out[lo:lo + step].astype(jnp.float32) + rstd[lo:lo + s...  8.28 us
    ppermute x3, waiting for transfers between devices, shifted(): return lax.ppermute(block, axis, [(i, (i + shift) % n) for i in range(n)])  7.4 us
    broadcast_in_dim x2, other arithmetic, on_device(): return (upstream[None, None], weight_total[None], gain_total[None])  4.57 us
  transfers between devices with their start and end apart: 11, of which 3 were waited for; matrix products, arithmetic and copies ran while one was open for 41% of the time, Pallas kernels for 0%

profile of v14, /device:TPU:0, one launch (start us, length us, event | category | flops | bytes accessed | tf_op | source)
XLA Modules:
  0.0 145.9 jit_solution(6109455450230777045)
XLA Ops:
  7.2 1.9 %fusion.62 = (bf16[1,1,256,512]{3,2,1,0:T(8,128)(2,1)}, bf16[1,1,256,512]{3,2,1,0:T(8,128)(2,1)}) fusion(bf16[1,1,512,512]{3,2,1,0:T(8,128)(2,1)} %param.7), kind=kLoop, calls=%fused_computation.92 | loop fusion | bytes 1048576 | tf_op jit(solution)/shard_map/slice | solution.py:49
  9.8 2.1 %fusion.4 = f32[512]{0:T(512)S(1)} fusion(bf16[1,1,512,2048]{3,2,1,0:T(8,128)(2,1)} %param.5), kind=kLoop, calls=%fused_computation.6 | loop fusion | flops 3145216 | bytes 2099200 | tf_op jit(solution)/shard_map/reduce_sum | solution.py:41
  11.9 13.6 %psum.21 = f32[512,1]{0,1:T(1,128)S(1)} all-reduce(f32[512,1]{0,1:T(1,128)S(1)} %bitcast.54), channel_id=1, replica_groups=mesh['dp'=4,'pipe'=2,'tensor'=4] {'tensor'}, use_global_device_ids=true, to_apply=%region_1.2 | all-reduce | flops 512 | bytes 4096 | tf_op jit(solution)/shard_map/psum | solution.py:41
  25.5 4.1 %multiply_convert_fusion = (bf16[512,2048]{1,0:T(8,128)(2,1)S(1)}, f32[512,2048]{1,0:T(8,128)}) fusion(f32[2048]{0:T(1024)S(1)} %bitcast.47, f32[512]{0:T(512)S(1)} %bitcast.53, bf16[1,1,512,2048]{3,2,1,0:T(8,128)(2,1)} %param.5), kind=kLoop, calls=%fused_computation.7 | loop fusion | flops 4194304 | bytes 8398848 | tf_op jit(solution)/shard_map/convert_element_type | solution.py:44
  29.7 11.1 %all-gather.5.cloned.1.call-done = bf16[1,1,256,2048]{3,2,1,0:T(8,128)(2,1)} async-done(((bf16[1,1,256,512]{3,2,1,0:T(8,128)(2,1)}), bf16[1,1,256,2048]{3,2,1,0:T(8,128)(2,1)}) %all-gather.5.cloned.1.call-update) | async-done | bytes 1048592 | tf_op jit(solution)/shard_map/all_gather | solution.py:49
  40.8 8.2 %multiply_reduce_fusion.1 = (f32[2048]{0:T(1024)S(1)}, f32[256]{0:T(256)S(1)}, f32[256,2048]{1,0:T(8,128)}) fusion(f32[512,2048]{1,0:T(8,128)} %get-tuple-element.22, f32[2048]{0:T(1024)S(1)} %bitcast.48, bf16[1,2048,2048]{2,1,0:T(8,128)(2,1)} %param.9, bf16[1,1,256,2048]{3,2,1,0:T(8,128)(2,1)} %all-gather.5.cloned.1.call-done), kind=kOutput, calls=%fused_computation.15 | convolution fusion | flops 2150102784 | bytes 13648896 | tf_op jit(solution)/shard_map/dot_general | solution.py:82
  49.0 10.5 %psum.22 = f32[256,1]{0,1:T(1,128)S(1)} all-reduce(f32[256,1]{0,1:T(1,128)S(1)} %bitcast.62), channel_id=1, replica_groups=mesh['dp'=4,'pipe'=2,'tensor'=4] {'tensor'}, use_global_device_ids=true, to_apply=%region_3.4 | all-reduce | flops 256 | bytes 2048 | tf_op jit(solution)/shard_map/psum | solution.py:87
  59.5 4.1 %fusion.6 = bf16[256,2048]{1,0:T(8,128)(2,1)} fusion(f32[256,2048]{1,0:T(8,128)} %get-tuple-element.35, f32[512,2048]{1,0:T(8,128)} %get-tuple-element.22, f32[256]{0:T(256)S(1)} %bitcast.58, f32[2048]{0:T(1024)S(1)} %bitcast.49, f32[256]{0:T(256)S(1)} %bitcast.60, bf16[1,1,512,2048]{3,2,1,0:T(8,128)(2,1)} %param.6), kind=kLoop, calls=%fused_computation.13 | loop fusion | flops 3670016 | bytes 6301696 | tf_op jit(solution)/shard_map/convert_element_type | solution.py:91
  64.9 5.8 %all-gather.7.cloned.1.call-done = bf16[1,1,256,2048]{3,2,1,0:T(8,128)(2,1)} async-done(((bf16[1,1,256,512]{3,2,1,0:T(8,128)(2,1)}), bf16[1,1,256,2048]{3,2,1,0:T(8,128)(2,1)}) %all-gather.7.cloned.1.call-update) | async-done | bytes 1048592 | tf_op jit(solution)/shard_map/all_gather | solution.py:49
  75.1 1.7 %fusion.9 = f32[1024,512]{1,0:T(8,128)S(1)} fusion(bf16[512,2048]{1,0:T(8,128)(2,1)} %collective-permute-done.1, bf16[256,1024]{1,0:T(8,128)(2,1)S(1)} %collective-permute-done.3, s32[]{:T(128)S(6)} %select_n.67), kind=kOutput, calls=%fused_computation.36 | convolution fusion | flops 268435456 | bytes 2883588 | tf_op jit(solution)/shard_map/dot_general | solution.py:60
  76.9 1.7 %fusion.15 = f32[1024,512]{1,0:T(8,128)S(1)} fusion(bf16[512,2048]{1,0:T(8,128)(2,1)} %collective-permute-done.1, bf16[256,1024]{1,0:T(8,128)(2,1)S(1)} %collective-permute-done.2, s32[]{:T(128)S(6)} %select_n.67), kind=kOutput, calls=%fused_computation.42 | convolution fusion | flops 268435456 | bytes 2883588 | tf_op jit(solution)/shard_map/dot_general | solution.py:60
  78.6 1.6 %add_convert_fusion.2 = bf16[1024,512]{1,0:T(8,128)(2,1)} fusion(f32[1024,512]{1,0:T(8,128)S(1)} %fusion.9, f32[1024,512]{1,0:T(8,128)S(1)} %fusion.18, f32[1024,512]{1,0:T(8,128)S(1)} %fusion.15, bf16[512,2048]{1,0:T(8,128)(2,1)S(1)} %get-tuple-element.10, s32[]{:T(128)S(6)} %select_n.67, bf16[256,512]{1,0:T(8,128)(2,1)S(1)} %get-tuple-element.26, ...), kind=kOutput, calls=%fused_computation.19 | convolution fusion | flops 271056896 | bytes 8388612 | tf_op jit(solution)/shard_map/dot_general | solution.py:60
  84.7 1.6 %add_convert_fusion.3 = bf16[1024,512]{1,0:T(8,128)(2,1)} fusion(f32[1024,512]{1,0:T(8,128)S(1)} %fusion.22, f32[1024,512]{1,0:T(8,128)S(1)} %fusion.31, f32[1024,512]{1,0:T(8,128)S(1)} %fusion.28, bf16[512,2048]{1,0:T(8,128)(2,1)S(1)} %get-tuple-element.10, s32[]{:T(128)S(6)} %select_n.67, bf16[256,512]{1,0:T(8,128)(2,1)S(1)} %get-tuple-element.26, ...), kind=kOutput, calls=%fused_computation.20 | convolution fusion | flops 271056896 | bytes 8388612 | tf_op jit(solution)/shard_map/dot_general | solution.py:60
  87.6 3.9 %multiply_reduce_fusion = (f32[2048]{0:T(1024)S(1)}, f32[256]{0:T(256)S(1)}, f32[256,2048]{1,0:T(8,128)}) fusion(f32[512,2048]{1,0:T(8,128)S(1)} %copy-done, f32[2048]{0:T(1024)S(1)} %bitcast.50, bf16[256,2048]{1,0:T(8,128)(2,1)S(1)} %bitcast.45, bf16[1,2048,2048]{2,1,0:T(8,128)(2,1)S(1)} %bitcast.64), kind=kOutput, calls=%fused_computation.14 | convolution fusion | flops 2150102784 | bytes 13648896 | tf_op jit(solution)/shard_map/dot_general | solution.py:82
  91.5 10.4 %psum.23 = f32[256,1]{0,1:T(1,128)S(1)} all-reduce(f32[256,1]{0,1:T(1,128)S(1)} %bitcast.61), channel_id=1, replica_groups=mesh['dp'=4,'pipe'=2,'tensor'=4] {'tensor'}, use_global_device_ids=true, to_apply=%region_5.6 | all-reduce | flops 256 | bytes 2048 | tf_op jit(solution)/shard_map/psum | solution.py:87
  101.8 4.2 %fusion.5 = bf16[256,2048]{1,0:T(8,128)(2,1)} fusion(f32[256,2048]{1,0:T(8,128)} %get-tuple-element.36, f32[512,2048]{1,0:T(8,128)} %get-tuple-element.22, f32[256]{0:T(256)S(1)} %bitcast.57, f32[256]{0:T(256)S(1)} %bitcast.59, bf16[1,1,512,2048]{3,2,1,0:T(8,128)(2,1)} %param.6, f32[2048]{0:T(1024)S(1)} %bitcast.51), kind=kLoop, calls=%fused_computation.11 | loop fusion | flops 3670016 | bytes 6301696 | tf_op jit(solution)/shard_map/convert_element_type | solution.py:91
  108.8 1.9 %convolution_add_fusion.1 = f32[1024,512]{1,0:T(8,128)} fusion(f32[1024,512]{1,0:T(8,128)S(1)} %fusion.26, bf16[512,2048]{1,0:T(8,128)(2,1)S(1)} %get-tuple-element.10, s32[]{:T(128)S(6)} %select_n.70, bf16[256,512]{1,0:T(8,128)(2,1)S(1)} %get-tuple-element.30, bf16[256,512]{1,0:T(8,128)(2,1)S(1)} %get-tuple-element.29), kind=kOutput, calls=%fused_computation.23 | convolution fusion | flops 269484032 | bytes 5242884 | tf_op jit(solution)/shard_map/dot_general | solution.py:60
  112.2 1.9 %convolution_add_fusion = f32[1024,512]{1,0:T(8,128)} fusion(f32[1024,512]{1,0:T(8,128)S(1)} %fusion.13, bf16[512,2048]{1,0:T(8,128)(2,1)S(1)} %get-tuple-element.10, s32[]{:T(128)S(6)} %select_n.70, bf16[256,512]{1,0:T(8,128)(2,1)S(1)} %get-tuple-element.30, bf16[256,512]{1,0:T(8,128)(2,1)S(1)} %get-tuple-element.29), kind=kOutput, calls=%fused_computation.22 | convolution fusion | flops 269484032 | bytes 5242884 | tf_op jit(solution)/shard_map/dot_general | solution.py:60
  114.1 2.8 %fusion.7 = f32[1024,512]{1,0:T(8,128)} fusion(bf16[512,2048]{1,0:T(8,128)(2,1)} %collective-permute-done.1, bf16[256,1024]{1,0:T(8,128)(2,1)S(1)} %copy-done.4, s32[]{:T(128)S(6)} %select_n.70), kind=kOutput, calls=%fused_computation.34 | convolution fusion | flops 268435456 | bytes 2883588 | tf_op jit(solution)/shard_map/dot_general | solution.py:60
  117.9 2.8 %fusion.20 = f32[1024,512]{1,0:T(8,128)} fusion(bf16[512,2048]{1,0:T(8,128)(2,1)} %collective-permute-done.1, bf16[256,1024]{1,0:T(8,128)(2,1)S(1)} %copy-done.4, s32[]{:T(128)S(6)} %select_n.70), kind=kOutput, calls=%fused_computation.47 | convolution fusion | flops 268435456 | bytes 2883588 | tf_op jit(solution)/shard_map/dot_general | solution.py:60
  120.8 7.4 %collective-permute-done.8 = f32[2048]{0:T(1024)S(1)} collective-permute-done((f32[2048]{0:T(1024)S(1)}, f32[2048]{0:T(1024)S(1)}, u32[]{:S(2)}, u32[]{:S(2)}) %collective-permute-start.8) | collective-permute-done | bytes 8224 | tf_op jit(solution)/shard_map/ppermute | solution.py:18
  128.9 3.2 %add_convert_fusion = bf16[1024,512]{1,0:T(8,128)(2,1)S(1)} fusion(bf16[1024,512]{1,0:T(8,128)(2,1)} %collective-permute-done.6, f32[1024,512]{1,0:T(8,128)} %convolution_add_fusion, f32[1024,512]{1,0:T(8,128)} %fusion.7, bf16[512,2048]{1,0:T(8,128)(2,1)S(1)} %get-tuple-element.10, s32[]{:T(128)S(6)} %select_n.70, ...), kind=kOutput, calls=%fused_computation.16 | convolution fusion | flops 271581184 | bytes 7340036 | tf_op jit(solution)/shard_map/dot_general | solution.py:60
  132.6 1.8 %add_convert_fusion.1 = bf16[1024,512]{1,0:T(8,128)(2,1)S(1)} fusion(bf16[1024,512]{1,0:T(8,128)(2,1)} %collective-permute-done.5, f32[1024,512]{1,0:T(8,128)S(1)} %copy-done.1, f32[1024,512]{1,0:T(8,128)S(1)} %copy-done.2, bf16[512,2048]{1,0:T(8,128)(2,1)S(1)} %get-tuple-element.10, s32[]{:T(128)S(6)} %select_n.70, ...), kind=kOutput, calls=%fused_computation.17 | convolution fusion | flops 271581184 | bytes 7340036 | tf_op jit(solution)/shard_map/dot_general | solution.py:60
  135.9 3.1 %maximum_bitcast_fusion = bf16[1,1,512,2048]{3,2,1,0:T(8,128)(2,1)} fusion(bf16[256,2048]{1,0:T(8,128)(2,1)} %collective-permute-done.4, bf16[256,2048]{1,0:T(8,128)(2,1)} %collective-permute-done), kind=kLoop, calls=%fused_computation.8 | loop fusion | flops 4194304 | bytes 4194304 | tf_op jit(solution)/shard_map/broadcast_in_dim | solution.py:134
  (64 shorter events, 20.3 us)
Async XLA Ops:
  7.2 33.7 %all-gather.5.cloned.1.call-start = ((), (), s32[]{:S(2)}) async-start(), calls=%async_computation | async-start | bytes 1310720 | tf_op jit(solution)/shard_map/all_gather | solution.py:49
  9.1 61.6 %all-gather.7.cloned.1.call-start = ((), (), s32[]{:S(2)}) async-start(), calls=%async_computation.1 | async-start | bytes 1310720 | tf_op jit(solution)/shard_map/all_gather | solution.py:49
  29.6 41.1 %collective-permute-start.1 = (bf16[512,2048]{1,0:T(8,128)(2,1)S(1)}, bf16[512,2048]{1,0:T(8,128)(2,1)}, u32[]{:S(2)}, u32[]{:S(2)}) collective-permute-start(bf16[512,2048]{1,0:T(8,128)(2,1)S(1)} %get-tuple-element.10), channel_id=1, source_target_pairs={{0,8},{8,0},{16,24},{24,16},{1,9},{9,1},{17,25},{25,17},{2,10},{10... | collective-permute-start | bytes 6291464 | tf_op jit(solution)/shard_map/ppermute | solution.py:23
  63.6 72.3 %collective-permute-start = (bf16[256,2048]{1,0:T(8,128)(2,1)}, bf16[256,2048]{1,0:T(8,128)(2,1)}, u32[]{:S(2)}, u32[]{:S(2)}) collective-permute-start(bf16[256,2048]{1,0:T(8,128)(2,1)} %fusion.6), channel_id=1, source_target_pairs={{4,0},{5,1},{6,2},{7,3},{12,8},{13,9},{14,10},{15,11},{20,16},{21,... | collective-permute-start | bytes 3145736 | tf_op jit(solution)/shard_map/ppermute | solution.py:13
  72.1 3.1 %collective-permute-start.3 = (bf16[256,1024]{1,0:T(8,128)(2,1)S(1)}, bf16[256,1024]{1,0:T(8,128)(2,1)S(1)}, u32[]{:S(2)}, u32[]{:S(2)}) collective-permute-start(bf16[256,1024]{1,0:T(8,128)(2,1)S(1)} %pad_maximum_fusion.1), channel_id=1, source_target_pairs={{0,8},{8,0},{16,24},{24,16},{1,9},{9,1},{17,25},{25,17},{2,10},{10... | collective-permute-start | bytes 1572872 | tf_op jit(solution)/shard_map/ppermute | solution.py:23
  73.5 3.3 %collective-permute-start.2 = (bf16[256,1024]{1,0:T(8,128)(2,1)S(1)}, bf16[256,1024]{1,0:T(8,128)(2,1)S(1)}, u32[]{:S(2)}, u32[]{:S(2)}) collective-permute-start(bf16[256,1024]{1,0:T(8,128)(2,1)S(1)} %pad_maximum_fusion), channel_id=1, source_target_pairs={{0,8},{8,0},{16,24},{24,16},{1,9},{9,1},{17,25},{25,17},{2,10},{10... | collective-permute-start | bytes 1572872 | tf_op jit(solution)/shard_map/ppermute | solution.py:23
  75.1 6.5 %copy-start.3 = (bf16[256,1024]{1,0:T(8,128)(2,1)}, bf16[256,1024]{1,0:T(8,128)(2,1)S(1)}, u32[]{:S(2)}) copy-start(bf16[256,1024]{1,0:T(8,128)(2,1)S(1)} %collective-permute-done.3) | copy-start | bytes 1572868
  76.9 6.3 %copy-start.5 = (bf16[256,1024]{1,0:T(8,128)(2,1)}, bf16[256,1024]{1,0:T(8,128)(2,1)S(1)}, u32[]{:S(2)}) copy-start(bf16[256,1024]{1,0:T(8,128)(2,1)S(1)} %collective-permute-done.2) | copy-start | bytes 1572868
  76.9 10.3 %slice-start = ((s8[8388608]{0:T(1024)(128)(4,1)}), s8[4194304]{0:T(1024)(128)(4,1)S(1)}, s32[]{:S(2)}) async-start(s8[8388608]{0:T(1024)(128)(4,1)} %bitcast.63), calls=%async_computation.2 | async-start | bytes 8388608
  80.2 6.9 %slice-start.1 = ((s8[8388608]{0:T(1024)(128)(4,1)}), s8[4194304]{0:T(1024)(128)(4,1)S(1)}, s32[]{:S(2)}) async-start(s8[8388608]{0:T(1024)(128)(4,1)} %bitcast.63), calls=%async_computation.3 | async-start | bytes 8388608
  80.2 48.7 %collective-permute-start.6 = (bf16[1024,512]{1,0:T(8,128)(2,1)}, bf16[1024,512]{1,0:T(8,128)(2,1)}, u32[]{:S(2)}, u32[]{:S(2)}) collective-permute-start(bf16[1024,512]{1,0:T(8,128)(2,1)} %add_convert_fusion.2), channel_id=1, source_target_pairs={{0,16},{8,24},{16,0},{24,8},{1,17},{9,25},{17,1},{25,9},{2,18},{10... | collective-permute-start | bytes 3145736 | tf_op jit(solution)/shard_map/ppermute | solution.py:18
  84.7 2.6 %copy-start = (f32[512,2048]{1,0:T(8,128)S(1)}, f32[512,2048]{1,0:T(8,128)}, u32[]{:S(2)}) copy-start(f32[512,2048]{1,0:T(8,128)} %get-tuple-element.22) | copy-start | bytes 12582916
  84.7 2.9 %copy-start.7 = (bf16[1,1,256,2048]{3,2,1,0:T(8,128)(2,1)S(1)}, bf16[1,1,256,2048]{3,2,1,0:T(8,128)(2,1)}, u32[]{:S(2)}) copy-start(bf16[1,1,256,2048]{3,2,1,0:T(8,128)(2,1)} %all-gather.7.cloned.1.call-done) | copy-start | bytes 3145732
  86.3 45.8 %collective-permute-start.5 = (bf16[1024,512]{1,0:T(8,128)(2,1)}, bf16[1024,512]{1,0:T(8,128)(2,1)}, u32[]{:S(2)}, u32[]{:S(2)}) collective-permute-start(bf16[1024,512]{1,0:T(8,128)(2,1)} %add_convert_fusion.3), channel_id=1, source_target_pairs={{0,16},{8,24},{16,0},{24,8},{1,17},{9,25},{17,1},{25,9},{2,18},{10... | collective-permute-start | bytes 3145736 | tf_op jit(solution)/shard_map/ppermute | solution.py:18
  101.8 5.5 %copy-start.6 = (bf16[256,1024]{1,0:T(8,128)(2,1)S(1)}, bf16[256,1024]{1,0:T(8,128)(2,1)}, u32[]{:S(2)}) copy-start(bf16[256,1024]{1,0:T(8,128)(2,1)} %copy-done.5) | copy-start | bytes 1572868
  106.0 29.9 %collective-permute-start.4 = (bf16[256,2048]{1,0:T(8,128)(2,1)}, bf16[256,2048]{1,0:T(8,128)(2,1)}, u32[]{:S(2)}, u32[]{:S(2)}) collective-permute-start(bf16[256,2048]{1,0:T(8,128)(2,1)} %fusion.5), channel_id=1, source_target_pairs={{4,0},{5,1},{6,2},{7,3},{12,8},{13,9},{14,10},{15,11},{20,16},{21,... | collective-permute-start | bytes 3145736 | tf_op jit(solution)/shard_map/ppermute | solution.py:13
  112.2 1.9 %copy-start.4 = (bf16[256,1024]{1,0:T(8,128)(2,1)S(1)}, bf16[256,1024]{1,0:T(8,128)(2,1)}, u32[]{:S(2)}) copy-start(bf16[256,1024]{1,0:T(8,128)(2,1)} %copy-done.3) | copy-start | bytes 1572868
  114.1 2.9 %collective-permute-start.7 = (f32[2048]{0:T(1024)S(1)}, f32[2048]{0:T(1024)S(1)}, u32[]{:S(2)}, u32[]{:S(2)}) collective-permute-start(f32[2048]{0:T(1024)S(1)} %add.161), channel_id=1, source_target_pairs={{0,8},{8,0},{16,24},{24,16},{1,9},{9,1},{17,25},{25,17},{2,10},{10... | collective-permute-start | bytes 24584 | tf_op jit(solution)/shard_map/ppermute | solution.py:23
  117.0 11.2 %collective-permute-start.8 = (f32[2048]{0:T(1024)S(1)}, f32[2048]{0:T(1024)S(1)}, u32[]{:S(2)}, u32[]{:S(2)}) collective-permute-start(f32[2048]{0:T(1024)S(1)} %add.162), channel_id=1, source_target_pairs={{0,16},{8,24},{16,0},{24,8},{1,17},{9,25},{17,1},{25,9},{2,18},{10... | collective-permute-start | bytes 24584 | tf_op jit(solution)/shard_map/ppermute | solution.py:18
  128.8 3.3 %copy-start.1 = (f32[1024,512]{1,0:T(8,128)S(1)}, f32[1024,512]{1,0:T(8,128)}, u32[]{:S(2)}) copy-start(f32[1024,512]{1,0:T(8,128)} %convolution_add_fusion.1) | copy-start | bytes 6291460
  128.9 3.8 %copy-start.2 = (f32[1024,512]{1,0:T(8,128)S(1)}, f32[1024,512]{1,0:T(8,128)}, u32[]{:S(2)}) copy-start(f32[1024,512]{1,0:T(8,128)} %fusion.20) | copy-start | bytes 6291460
Sparse Core Ops, SparseCore 0:
  10.1 30.6 all-gather.4
  43.0 27.6 all-gather.6

commit v15 on v13

--- a/solution.py
+++ b/solution.py
@@ -23,6 +23,18 @@
     return lax.ppermute(block, "dp", [(i, i ^ 1) for i in range(n)])
 
 
+def gather_columns(block):
+    n = lax.axis_size("tensor")
+    me = lax.axis_index("tensor")
+    rows, width = block.shape
+    full = jnp.zeros((rows, width * n), block.dtype)
+    full = lax.dynamic_update_slice(full, block, (0, me * width))
+    for d in range(1, n):
+        got = shifted(block, "tensor", d)
+        full = lax.dynamic_update_slice(full, got, (0, ((me - d) % n) * width))
+    return full
+
+
 def on_device(layer_input, output_grad, kv_grad, norm_gain, kv_weight):
     rows = layer_input[0, 0]
     grad_out = output_grad[0, 0]
@@ -45,9 +57,8 @@
     hidden_partner = to_partner(hidden)
 
     step = seq // CHUNKS
-    pieces = [
-        lax.all_gather(grad_kv[c * step:(c + 1) * step], "tensor", axis=1, tiled=True)
-        for c in range(CHUNKS)
+    pieces = [lax.all_gather(grad_kv[:step], "tensor", axis=1, tiled=True)] + [
+        gather_columns(grad_kv[c * step:(c + 1) * step]) for c in range(1, CHUNKS)
     ]
 
     def cols_of(q, p):

time: 146 us -> 160 us (1.096)
  blocking collectives: 34.2 us -> 54.7 us
  waiting for transfers between devices: 35.7 us -> 20.2 us
  starting transfers between devices: 6.08 us -> 13 us
  local copies, waits for them, and re-layouts: 3.76 us -> 5.57 us
    all_gather x2 -> x1, waiting for transfers between devices: 17.7 us -> 1.72 us  [on_device(): lax.all_gather(grad_kv[:step], 'tensor', axis=1, tiled=True)]
    psum x1, blocking collectives: 13.5 us -> 25 us  [on_device(): lax.psum(jnp.sum(values * values, axis=1, keepdims=True), 'tensor')]
    psum x2, blocking collectives: 20.7 us -> 29.7 us  [on_device(): lax.psum(jnp.sum(scaled * normed_c, axis=1, keepdims=True), 'tensor')]
    ppermute x2 -> x5, starting transfers between devices: 2.66 us -> 9.65 us  [shifted(): return lax.ppermute(block, axis, [(i, (i + shift) % n) for i in range(n)])]
    dynamic_update_slice x0 -> x4, local copies, waits for them, and re-layouts: none -> 2.96 us  [the longest x3 1.98 us: gather_columns(): full = lax.dynamic_update_slice(full, got, (0, (me - d) % n * width))]
    ppermute x2 -> x5, waiting for transfers between devices: 17.9 us -> 18.4 us  [shifted(): return lax.ppermute(block, axis, [(i, (i + shift) % n) for i in range(n)])]
  transfers between devices with their start and end apart: 10 -> 12, of which waited for: 3 -> 2; matrix products, arithmetic and copies ran while one was open for 32% -> 31% of each run, Pallas kernels for 0% -> 0%
where the time goes in v15:
time: 160 us; the launch traced here: 159 us
  blocking collectives  54.7 us (34%)
  matrix products  33 us (21%)
  waiting for transfers between devices  20.2 us (13%)
  other arithmetic  17.6 us (11%)
  between operations  14.5 us (9%)
  starting transfers between devices  13 us (8%)
  local copies, waits for them, and re-layouts  5.57 us (3%)
    psum x2, blocking collectives, on_device(): lax.psum(jnp.sum(scaled * normed_c, axis=1, keepdims=True), 'tensor')  29.7 us
    psum x1, blocking collectives, on_device(): lax.psum(jnp.sum(values * values, axis=1, keepdims=True), 'tensor')  25 us
    dot_general x8, matrix products, tn(): lax.dot_general(a, b, (((0,), (0,)), ((), ())), preferred_element_type=jn...  20.8 us
    ppermute x5, waiting for transfers between devices, shifted(): return lax.ppermute(block, axis, [(i, (i + shift) % n) for i in range(n)])  18.4 us
    dot_general x2, matrix products, on_device(): lax.dot_general(block, weight, (((1,), (1,)), ((), ())), preferred_elemen...  12.2 us
    ppermute x5, starting transfers between devices, shifted(): return lax.ppermute(block, axis, [(i, (i + shift) % n) for i in range(n)])  9.65 us
    convert_element_type x2, other arithmetic, on_device(): input_grad = (grad_out[lo:lo + step].astype(jnp.float32) + rstd[lo:lo + s...  8.25 us
    convert_element_type x1, other arithmetic, on_device(): hidden = (normed * gain_f).astype(jnp.bfloat16)  3.28 us
  transfers between devices with their start and end apart: 12, of which 2 were waited for; matrix products, arithmetic and copies ran while one was open for 31% of the time, Pallas kernels for 0%

profile of v15, /device:TPU:0, one launch (start us, length us, event | category | flops | bytes accessed | tf_op | source)
XLA Modules:
  0.0 158.6 jit_solution(9052933746683067687)
XLA Ops:
  7.2 2.0 %slice_bitcast_fusion = (bf16[256,512]{1,0:T(8,128)(2,1)}, bf16[1,1,256,512]{3,2,1,0:T(8,128)(2,1)}) fusion(bf16[1,1,512,512]{3,2,1,0:T(8,128)(2,1)} %param.7), kind=kLoop, calls=%fused_computation.52 | loop fusion | bytes 1048576 | tf_op jit(solution)/shard_map/slice | solution.py:61
  9.2 3.0 %collective-permute-start.2 = (bf16[256,512]{1,0:T(8,128)(2,1)}, bf16[256,512]{1,0:T(8,128)(2,1)}, u32[]{:S(2)}, u32[]{:S(2)}) collective-permute-start(bf16[256,512]{1,0:T(8,128)(2,1)} %get-tuple-element.29), channel_id=1, source_target_pairs={{0,1},{1,2},{2,3},{3,0},{4,5},{5,6},{6,7},{7,4},{8,9},{9,10},{10,1... | collective-permute-start | bytes 786440 | tf_op jit(solution)/shard_map/ppermute | solution.py:18
  12.2 2.6 %collective-permute-start.3 = (bf16[256,512]{1,0:T(8,128)(2,1)}, bf16[256,512]{1,0:T(8,128)(2,1)}, u32[]{:S(2)}, u32[]{:S(2)}) collective-permute-start(bf16[256,512]{1,0:T(8,128)(2,1)} %get-tuple-element.29), channel_id=1, source_target_pairs={{0,2},{1,3},{2,0},{3,1},{4,6},{5,7},{6,4},{7,5},{8,10},{9,11},{10,... | collective-permute-start | bytes 786440 | tf_op jit(solution)/shard_map/ppermute | solution.py:18
  14.8 1.3 collective-permute-start.4
  16.2 2.1 %fusion.4 = f32[512]{0:T(512)S(1)} fusion(bf16[1,1,512,2048]{3,2,1,0:T(8,128)(2,1)} %param.5), kind=kLoop, calls=%fused_computation.6 | loop fusion | flops 3145216 | bytes 2099200 | tf_op jit(solution)/shard_map/reduce_sum | solution.py:53
  18.3 25.0 %psum.21 = f32[512,1]{0,1:T(1,128)S(1)} all-reduce(f32[512,1]{0,1:T(1,128)S(1)} %bitcast.55), channel_id=1, replica_groups=mesh['dp'=4,'pipe'=2,'tensor'=4] {'tensor'}, use_global_device_ids=true, to_apply=%region_1.2 | all-reduce | flops 512 | bytes 4096 | tf_op jit(solution)/shard_map/psum | solution.py:53
  43.3 3.3 %multiply_convert_fusion = (bf16[512,2048]{1,0:T(8,128)(2,1)}, f32[512,2048]{1,0:T(8,128)}) fusion(f32[2048]{0:T(1024)S(1)} %bitcast.48, f32[512]{0:T(512)S(1)} %bitcast.54, bf16[1,1,512,2048]{3,2,1,0:T(8,128)(2,1)S(1)} %copy-done.2), kind=kLoop, calls=%fused_computation.9 | loop fusion | flops 4194304 | bytes 8398848 | tf_op jit(solution)/shard_map/convert_element_type | solution.py:56
  49.9 1.7 %all-gather.3.cloned.1.call-done = bf16[1,1,256,2048]{3,2,1,0:T(8,128)(2,1)} async-done(((bf16[1,1,256,512]{3,2,1,0:T(8,128)(2,1)}), bf16[1,1,256,2048]{3,2,1,0:T(8,128)(2,1)}) %all-gather.3.cloned.1.call-update) | async-done | bytes 1048592 | tf_op jit(solution)/shard_map/all_gather | solution.py:60
  51.6 8.2 %multiply_reduce_fusion.1 = (f32[2048]{0:T(1024)S(1)}, f32[256]{0:T(256)S(1)}, f32[256,2048]{1,0:T(8,128)}) fusion(f32[512,2048]{1,0:T(8,128)} %get-tuple-element.20, f32[2048]{0:T(1024)S(1)} %bitcast.49, bf16[1,2048,2048]{2,1,0:T(8,128)(2,1)} %param.9, bf16[1,1,256,2048]{3,2,1,0:T(8,128)(2,1)} %all-gather.3.cloned.1.call-done), kind=kOutput, calls=%fused_computation.18 | convolution fusion | flops 2150102784 | bytes 13648896 | tf_op jit(solution)/shard_map/dot_general | solution.py:93
  59.8 20.1 %psum.22 = f32[256,1]{0,1:T(1,128)S(1)} all-reduce(f32[256,1]{0,1:T(1,128)S(1)} %bitcast.63), channel_id=1, replica_groups=mesh['dp'=4,'pipe'=2,'tensor'=4] {'tensor'}, use_global_device_ids=true, to_apply=%region_3.4 | all-reduce | flops 256 | bytes 2048 | tf_op jit(solution)/shard_map/psum | solution.py:98
  79.9 4.1 %fusion.7 = bf16[256,2048]{1,0:T(8,128)(2,1)} fusion(f32[256,2048]{1,0:T(8,128)} %get-tuple-element.33, f32[512,2048]{1,0:T(8,128)} %get-tuple-element.20, f32[256]{0:T(256)S(1)} %bitcast.59, f32[2048]{0:T(1024)S(1)} %bitcast.50, f32[256]{0:T(256)S(1)} %bitcast.61, bf16[1,1,512,2048]{3,2,1,0:T(8,128)(2,1)} %param.6), kind=kLoop, calls=%fused_computation.16 | loop fusion | flops 3670016 | bytes 6301696 | tf_op jit(solution)/shard_map/convert_element_type | solution.py:102
  84.1 1.3 collective-permute-start
  86.4 2.0 %fusion.19 = f32[2048,512]{1,0:T(8,128)S(1)} fusion(bf16[512,2048]{1,0:T(8,128)(2,1)} %get-tuple-element.9, s32[]{:T(128)S(6)} %select_n.90, bf16[256,512]{1,0:T(8,128)(2,1)S(1)} %get-tuple-element.28, bf16[256,512]{1,0:T(8,128)(2,1)S(1)} %get-tuple-element.27), kind=kOutput, calls=%fused_computation.32 | convolution fusion | flops 537395200 | bytes 5767172 | tf_op jit(solution)/shard_map/dot_general | solution.py:71
  90.0 4.1 %add_convert_fusion.1 = bf16[2048,512]{1,0:T(8,128)(2,1)} fusion(f32[2048,512]{1,0:T(8,128)S(1)} %fusion.10, f32[2048,512]{1,0:T(8,128)S(1)} %fusion.19, f32[2048,512]{1,0:T(8,128)S(1)} %fusion.16, bf16[512,2048]{1,0:T(8,128)(2,1)} %get-tuple-element.9, s32[]{:T(128)S(6)} %select_n.90, bf16[256,512]{1,0:T(8,128)(2,1)S(1)} %get-tuple-element.24, ...), kind=kOutput, calls=%fused_computation.8 | convolution fusion | flops 541589504 | bytes 16252932 | tf_op jit(solution)/shard_map/dot_general | solution.py:71
  94.1 1.5 collective-permute-start.8
  95.7 4.1 %multiply_reduce_fusion = (f32[2048]{0:T(1024)S(1)}, f32[256]{0:T(256)S(1)}, f32[256,2048]{1,0:T(8,128)}) fusion(f32[512,2048]{1,0:T(8,128)S(1)} %copy-done.1, f32[2048]{0:T(1024)S(1)} %bitcast.51, bf16[256,2048]{1,0:T(8,128)(2,1)S(1)} %constant_dynamic-update-slice_fusion, bf16[1,2048,2048]{2,1,0:T(8,128)(2,1)S(1)} %bitcast.65), kind=kOutput, calls=%fused_computation.17 | convolution fusion | flops 2150102784 | bytes 13648896 | tf_op jit(solution)/shard_map/dot_general | solution.py:93
  99.8 9.6 %psum.23 = f32[256,1]{0,1:T(1,128)S(1)} all-reduce(f32[256,1]{0,1:T(1,128)S(1)} %bitcast.62), channel_id=1, replica_groups=mesh['dp'=4,'pipe'=2,'tensor'=4] {'tensor'}, use_global_device_ids=true, to_apply=%region_5.6 | all-reduce | flops 256 | bytes 2048 | tf_op jit(solution)/shard_map/psum | solution.py:98
  109.3 4.1 %fusion.6 = bf16[256,2048]{1,0:T(8,128)(2,1)} fusion(f32[256,2048]{1,0:T(8,128)} %get-tuple-element.34, f32[512,2048]{1,0:T(8,128)} %get-tuple-element.20, f32[256]{0:T(256)S(1)} %bitcast.58, f32[256]{0:T(256)S(1)} %bitcast.60, bf16[1,1,512,2048]{3,2,1,0:T(8,128)(2,1)} %param.6, f32[2048]{0:T(1024)S(1)} %bitcast.52), kind=kLoop, calls=%fused_computation.14 | loop fusion | flops 3670016 | bytes 6301696 | tf_op jit(solution)/shard_map/convert_element_type | solution.py:102
  113.4 1.4 collective-permute-start.7
  115.6 4.1 %convolution_add_fusion = f32[2048,512]{1,0:T(8,128)} fusion(f32[2048,512]{1,0:T(8,128)S(1)} %fusion.14, bf16[512,2048]{1,0:T(8,128)(2,1)} %get-tuple-element.9, s32[]{:T(128)S(6)} %select_n.93, bf16[256,512]{1,0:T(8,128)(2,1)S(1)} %copy-done.8, bf16[256,512]{1,0:T(8,128)(2,1)S(1)} %copy-done.6), kind=kOutput, calls=%fused_computation.10 | convolution fusion | flops 538443776 | bytes 9961476 | tf_op jit(solution)/shard_map/dot_general | solution.py:71
  120.9 2.7 %fusion.8 = f32[2048,512]{1,0:T(8,128)} fusion(bf16[512,2048]{1,0:T(8,128)(2,1)S(1)} %collective-permute-done.1, bf16[256,1024]{1,0:T(8,128)(2,1)S(1)} %copy-done.11, s32[]{:T(128)S(6)} %select_n.93), kind=kOutput, calls=%fused_computation.21 | convolution fusion | flops 536870912 | bytes 5505028 | tf_op jit(solution)/shard_map/dot_general | solution.py:71
  123.7 18.4 %collective-permute-done.10 = f32[2048]{0:T(1024)S(1)} collective-permute-done((f32[2048]{0:T(1024)S(1)}, f32[2048]{0:T(1024)S(1)}, u32[]{:S(2)}, u32[]{:S(2)}) %collective-permute-start.10) | collective-permute-done | bytes 8224 | tf_op jit(solution)/shard_map/ppermute | solution.py:18
  142.8 3.3 %maximum_bitcast_fusion = bf16[1,1,512,2048]{3,2,1,0:T(8,128)(2,1)} fusion(bf16[256,2048]{1,0:T(8,128)(2,1)} %collective-permute-done.7, bf16[256,2048]{1,0:T(8,128)(2,1)} %collective-permute-done), kind=kLoop, calls=%fused_computation.12 | loop fusion | flops 4194304 | bytes 4194304 | tf_op jit(solution)/shard_map/broadcast_in_dim | solution.py:137
  146.1 5.7 %fusion.5 = bf16[1,2048,512]{2,1,0:T(8,128)(2,1)} fusion(bf16[2048,512]{1,0:T(8,128)(2,1)} %collective-permute-done.8, f32[2048,512]{1,0:T(8,128)} %convolution_add_fusion, f32[2048,512]{1,0:T(8,128)S(1)} %copy-done, bf16[512,2048]{1,0:T(8,128)(2,1)} %get-tuple-element.9, s32[]{:T(128)S(6)} %select_n.93, bf16[256,512]{1,0:T(8,128)(2,1)S(1)} %copy-done.4, ...), kind=kOutput, calls=%fused_computation.11 | convolution fusion | flops 542638080 | bytes 14155780 | tf_op jit(solution)/shard_map/dot_general | solution.py:71
  (75 shorter events, 8.4 us)
Async XLA Ops:
  7.2 36.2 %copy-start.2 = (bf16[1,1,512,2048]{3,2,1,0:T(8,128)(2,1)S(1)}, bf16[1,1,512,2048]{3,2,1,0:T(8,128)(2,1)}, u32[]{:S(2)}) copy-start(bf16[1,1,512,2048]{3,2,1,0:T(8,128)(2,1)} %param.5) | copy-start | bytes 6291460
  7.2 36.1 %copy-start.14 = (bf16[1,2048]{1,0:T(2,128)(2,1)S(1)}, bf16[1,2048]{1,0:T(2,128)(2,1)}, u32[]{:S(2)}) copy-start(bf16[1,2048]{1,0:T(2,128)(2,1)} %param.8) | copy-start | bytes 12292
  7.2 44.5 %all-gather.3.cloned.1.call-start = ((), (), s32[]{:S(2)}) async-start(), calls=%async_computation | async-start | bytes 1310720 | tf_op jit(solution)/shard_map/all_gather | solution.py:60
  9.2 38.7 %collective-permute-start.2 = (bf16[256,512]{1,0:T(8,128)(2,1)}, bf16[256,512]{1,0:T(8,128)(2,1)}, u32[]{:S(2)}, u32[]{:S(2)}) collective-permute-start(bf16[256,512]{1,0:T(8,128)(2,1)} %get-tuple-element.29), channel_id=1, source_target_pairs={{0,1},{1,2},{2,3},{3,0},{4,5},{5,6},{6,7},{7,4},{8,9},{9,10},{10,1... | collective-permute-start | bytes 786440 | tf_op jit(solution)/shard_map/ppermute | solution.py:18
  12.2 36.6 %collective-permute-start.3 = (bf16[256,512]{1,0:T(8,128)(2,1)}, bf16[256,512]{1,0:T(8,128)(2,1)}, u32[]{:S(2)}, u32[]{:S(2)}) collective-permute-start(bf16[256,512]{1,0:T(8,128)(2,1)} %get-tuple-element.29), channel_id=1, source_target_pairs={{0,2},{1,3},{2,0},{3,1},{4,6},{5,7},{6,4},{7,5},{8,10},{9,11},{10,... | collective-permute-start | bytes 786440 | tf_op jit(solution)/shard_map/ppermute | solution.py:18
  14.8 35.0 %collective-permute-start.4 = (bf16[256,512]{1,0:T(8,128)(2,1)}, bf16[256,512]{1,0:T(8,128)(2,1)S(1)}, u32[]{:S(2)}, u32[]{:S(2)}) collective-permute-start(bf16[256,512]{1,0:T(8,128)(2,1)} %get-tuple-element.29), channel_id=1, source_target_pairs={{0,3},{1,0},{2,1},{3,2},{4,7},{5,4},{6,5},{7,6},{8,11},{9,8},{10,9... | collective-permute-start | bytes 786440 | tf_op jit(solution)/shard_map/ppermute | solution.py:18
  46.6 38.7 %collective-permute-start.1 = (bf16[512,2048]{1,0:T(8,128)(2,1)}, bf16[512,2048]{1,0:T(8,128)(2,1)S(1)}, u32[]{:S(2)}, u32[]{:S(2)}) collective-permute-start(bf16[512,2048]{1,0:T(8,128)(2,1)} %get-tuple-element.9), channel_id=1, source_target_pairs={{0,8},{8,0},{16,24},{24,16},{1,9},{9,1},{17,25},{25,17},{2,10},{10... | collective-permute-start | bytes 6291464 | tf_op jit(solution)/shard_map/ppermute | solution.py:23
  79.9 5.5 %copy-start.9 = (bf16[1,1,256,2048]{3,2,1,0:T(8,128)(2,1)S(1)}, bf16[1,1,256,2048]{3,2,1,0:T(8,128)(2,1)}, u32[]{:S(2)}) copy-start(bf16[1,1,256,2048]{3,2,1,0:T(8,128)(2,1)} %all-gather.3.cloned.1.call-done) | copy-start | bytes 3145732
  84.1 58.7 %collective-permute-start = (bf16[256,2048]{1,0:T(8,128)(2,1)}, bf16[256,2048]{1,0:T(8,128)(2,1)}, u32[]{:S(2)}, u32[]{:S(2)}) collective-permute-start(bf16[256,2048]{1,0:T(8,128)(2,1)} %fusion.7), channel_id=1, source_target_pairs={{4,0},{5,1},{6,2},{7,3},{12,8},{13,9},{14,10},{15,11},{20,16},{21,... | collective-permute-start | bytes 3145736 | tf_op jit(solution)/shard_map/ppermute | solution.py:13
  85.6 2.8 %collective-permute-start.5 = (bf16[256,1024]{1,0:T(8,128)(2,1)S(1)}, bf16[256,1024]{1,0:T(8,128)(2,1)S(1)}, u32[]{:S(2)}, u32[]{:S(2)}) collective-permute-start(bf16[256,1024]{1,0:T(8,128)(2,1)S(1)} %pad_maximum_fusion), channel_id=1, source_target_pairs={{0,8},{8,0},{16,24},{24,16},{1,9},{9,1},{17,25},{25,17},{2,10},{10... | collective-permute-start | bytes 1572872 | tf_op jit(solution)/shard_map/ppermute | solution.py:23
  85.8 4.2 %copy-start.3 = (bf16[256,512]{1,0:T(8,128)(2,1)}, bf16[256,512]{1,0:T(8,128)(2,1)S(1)}, u32[]{:S(2)}) copy-start(bf16[256,512]{1,0:T(8,128)(2,1)S(1)} %get-tuple-element.24) | copy-start | bytes 786436
  85.8 3.4 %collective-permute-start.6 = (bf16[256,1024]{1,0:T(8,128)(2,1)S(1)}, bf16[256,1024]{1,0:T(8,128)(2,1)S(1)}, u32[]{:S(2)}, u32[]{:S(2)}) collective-permute-start(bf16[256,1024]{1,0:T(8,128)(2,1)S(1)} %pad_maximum_fusion.1), channel_id=1, source_target_pairs={{0,8},{8,0},{16,24},{24,16},{1,9},{9,1},{17,25},{25,17},{2,10},{10... | collective-permute-start | bytes 1572872 | tf_op jit(solution)/shard_map/ppermute | solution.py:23
  89.2 6.4 %slice-start = ((s8[8388608]{0:T(1024)(128)(4,1)}), s8[4194304]{0:T(1024)(128)(4,1)S(1)}, s32[]{:S(2)}) async-start(s8[8388608]{0:T(1024)(128)(4,1)} %bitcast.64), calls=%async_computation.1 | async-start | bytes 8388608
  90.0 5.6 %copy-start.1 = (f32[512,2048]{1,0:T(8,128)S(1)}, f32[512,2048]{1,0:T(8,128)}, u32[]{:S(2)}) copy-start(f32[512,2048]{1,0:T(8,128)} %get-tuple-element.20) | copy-start | bytes 12582916
  90.0 5.6 %slice-start.1 = ((s8[8388608]{0:T(1024)(128)(4,1)}), s8[4194304]{0:T(1024)(128)(4,1)S(1)}, s32[]{:S(2)}) async-start(s8[8388608]{0:T(1024)(128)(4,1)} %bitcast.64), calls=%async_computation.2 | async-start | bytes 8388608
  94.1 51.9 %collective-permute-start.8 = (bf16[2048,512]{1,0:T(8,128)(2,1)}, bf16[2048,512]{1,0:T(8,128)(2,1)}, u32[]{:S(2)}, u32[]{:S(2)}) collective-permute-start(bf16[2048,512]{1,0:T(8,128)(2,1)} %add_convert_fusion.1), channel_id=1, source_target_pairs={{0,16},{8,24},{16,0},{24,8},{1,17},{9,25},{17,1},{25,9},{2,18},{10... | collective-permute-start | bytes 6291464 | tf_op jit(solution)/shard_map/ppermute | solution.py:18
  99.8 19.9 %collective-permute-start.9 = (f32[2048]{0:T(1024)S(1)}, f32[2048]{0:T(1024)S(1)}, u32[]{:S(2)}, u32[]{:S(2)}) collective-permute-start(f32[2048]{0:T(1024)S(1)} %add.156), channel_id=1, source_target_pairs={{0,8},{8,0},{16,24},{24,16},{1,9},{9,1},{17,25},{25,17},{2,10},{10... | collective-permute-start | bytes 24584 | tf_op jit(solution)/shard_map/ppermute | solution.py:23
  109.3 5.5 %copy-start.13 = (bf16[256,1024]{1,0:T(8,128)(2,1)S(1)}, bf16[256,1024]{1,0:T(8,128)(2,1)}, u32[]{:S(2)}) copy-start(bf16[256,1024]{1,0:T(8,128)(2,1)} %copy-done.12) | copy-start | bytes 1572868
  113.4 2.2 %copy-start.8 = (bf16[256,512]{1,0:T(8,128)(2,1)S(1)}, bf16[256,512]{1,0:T(8,128)(2,1)}, u32[]{:S(2)}) copy-start(bf16[256,512]{1,0:T(8,128)(2,1)} %copy-done.7) | copy-start | bytes 786436
  113.4 29.4 %collective-permute-start.7 = (bf16[256,2048]{1,0:T(8,128)(2,1)}, bf16[256,2048]{1,0:T(8,128)(2,1)}, u32[]{:S(2)}, u32[]{:S(2)}) collective-permute-start(bf16[256,2048]{1,0:T(8,128)(2,1)} %fusion.6), channel_id=1, source_target_pairs={{4,0},{5,1},{6,2},{7,3},{12,8},{13,9},{14,10},{15,11},{20,16},{21,... | collective-permute-start | bytes 3145736 | tf_op jit(solution)/shard_map/ppermute | solution.py:13
  115.6 5.2 %copy-start.11 = (bf16[256,1024]{1,0:T(8,128)(2,1)S(1)}, bf16[256,1024]{1,0:T(8,128)(2,1)}, u32[]{:S(2)}) copy-start(bf16[256,1024]{1,0:T(8,128)(2,1)} %copy-done.10) | copy-start | bytes 1572868
  119.7 22.4 %collective-permute-start.10 = (f32[2048]{0:T(1024)S(1)}, f32[2048]{0:T(1024)S(1)}, u32[]{:S(2)}, u32[]{:S(2)}) collective-permute-start(f32[2048]{0:T(1024)S(1)} %add.157), channel_id=1, source_target_pairs={{0,16},{8,24},{16,0},{24,8},{1,17},{9,25},{17,1},{25,9},{2,18},{10... | collective-permute-start | bytes 24584 | tf_op jit(solution)/shard_map/ppermute | solution.py:18
  120.9 25.2 %copy-start.4 = (bf16[256,512]{1,0:T(8,128)(2,1)S(1)}, bf16[256,512]{1,0:T(8,128)(2,1)}, u32[]{:S(2)}) copy-start(bf16[256,512]{1,0:T(8,128)(2,1)} %copy-done.3) | copy-start | bytes 786436
  142.8 3.3 %copy-start = (f32[2048,512]{1,0:T(8,128)S(1)}, f32[2048,512]{1,0:T(8,128)}, u32[]{:S(2)}) copy-start(f32[2048,512]{1,0:T(8,128)} %fusion.8) | copy-start | bytes 12582916
  (5 other events, 5.6 us)
Sparse Core Ops, SparseCore 0:
  16.3 35.2 all-gather.2

commit v16 on v13

--- a/solution.py
+++ b/solution.py
@@ -62,10 +62,7 @@
     own_g = me // 2
     dests = [(own_g + d) % groups for d in range(1, groups)]
 
-    def pair_blocks(h_own, h_partner, q):
-        own_cols = cols_of(q, parity)
-        partner_cols = to_partner(cols_of(q, 1 - parity))
-
+    def pair_blocks(h_own, h_partner, own_cols, partner_cols):
         def block_of(g):
             oc = lax.dynamic_slice_in_dim(own_cols, g * kv_block, kv_block, axis=1)
             pc = lax.dynamic_slice_in_dim(partner_cols, g * kv_block, kv_block, axis=1)
@@ -93,10 +90,16 @@
         gain_part = gain_part + jnp.sum(row_total * normed_c, axis=0)
         if c == 0:
             _, (h, hp, parts) = lax.optimization_barrier((input_grad, (hidden, hidden_partner, pieces)))
-            chunk_blocks = [
-                pair_blocks(h[k * step:(k + 1) * step], hp[k * step:(k + 1) * step], parts[k])
+            chunk_inputs = [
+                (
+                    h[k * step:(k + 1) * step],
+                    hp[k * step:(k + 1) * step],
+                    cols_of(parts[k], parity),
+                    to_partner(cols_of(parts[k], 1 - parity)),
+                )
                 for k in range(CHUNKS)
             ]
+            chunk_blocks = [pair_blocks(*inputs) for inputs in chunk_inputs]
             outs = []
             for g in dests:
                 acc = chunk_blocks[0](g)
@@ -104,10 +107,11 @@
                     acc = acc + chunk_blocks[k](g)
                 outs.append(acc.astype(jnp.bfloat16))
             received = [shifted(out, "dp", 2 * d) for d, out in enumerate(outs, start=1)]
-            _, first = lax.optimization_barrier((outs, chunk_blocks[0](own_g)))
-            total = first
+            _, later_inputs = lax.optimization_barrier((outs, chunk_inputs))
+            later_blocks = [pair_blocks(*inputs) for inputs in later_inputs]
+            total = later_blocks[0](own_g)
             for k in range(1, CHUNKS):
-                total = total + chunk_blocks[k](own_g)
+                total = total + later_blocks[k](own_g)
             for got in received:
                 total = total + got.astype(jnp.float32)
             weight_total = total.astype(jnp.bfloat16)

time: 146 us -> 152 us (1.041)
  local copies, waits for them, and re-layouts: 3.76 us -> 7.62 us
  waiting for transfers between devices: 35.7 us -> 33.6 us
  other arithmetic: 18.3 us -> 20.4 us
  matrix products: 32.9 us -> 34.6 us
    slice x0 -> x1, local copies, waits for them, and re-layouts: none -> 3.35 us  [on_device(): hp[k * step:(k + 1) * step]]
    unnamed x20 -> x30, local copies, waits for them, and re-layouts: 0.17 us -> 2.07 us
    dot_general x8, matrix products: 20.8 us -> 22.5 us  [tn(): lax.dot_general(a, b, (((0,), (0,)), ((), ())), preferred_element_type=jn...]
  transfers between devices with their start and end apart: 10 -> 10, of which waited for: 3 -> 3; matrix products, arithmetic and copies ran while one was open for 32% -> 34% of each run, Pallas kernels for 0% -> 0%
where the time goes in v16:
time: 152 us; the launch traced here: 151 us
  matrix products  34.6 us (23%)
  blocking collectives  34.4 us (23%)
  waiting for transfers between devices  33.6 us (22%)
  other arithmetic  20.4 us (13%)
  between operations  14.3 us (9%)
  local copies, waits for them, and re-layouts  7.62 us (5%)
  starting transfers between devices  6.36 us (4%)
    dot_general x8, matrix products, tn(): lax.dot_general(a, b, (((0,), (0,)), ((), ())), preferred_element_type=jn...  22.5 us
    psum x2, blocking collectives, on_device(): lax.psum(jnp.sum(scaled * normed_c, axis=1, keepdims=True), 'tensor')  20.9 us
    all_gather x2, waiting for transfers between devices, on_device(): lax.all_gather(grad_kv[c * step:(c + 1) * step], 'tensor', axis=1, tiled=...  16.9 us
    ppermute x2, waiting for transfers between devices, shifted(): return lax.ppermute(block, axis, [(i, (i + shift) % n) for i in range(n)])  16.7 us
    psum x1, blocking collectives, on_device(): lax.psum(jnp.sum(values * values, axis=1, keepdims=True), 'tensor')  13.6 us
    dot_general x2, matrix products, on_device(): lax.dot_general(block, weight, (((1,), (1,)), ((), ())), preferred_elemen...  12 us
    convert_element_type x2, other arithmetic, on_device(): input_grad = (grad_out[lo:lo + step].astype(jnp.float32) + rstd[lo:lo + s...  8.33 us
    convert_element_type x1, other arithmetic, on_device(): hidden = (normed * gain_f).astype(jnp.bfloat16)  4.09 us
  transfers between devices with their start and end apart: 10, of which 3 were waited for; matrix products, arithmetic and copies ran while one was open for 34% of the time, Pallas kernels for 0%

profile of v16, /device:TPU:0, one launch (start us, length us, event | category | flops | bytes accessed | tf_op | source)
XLA Modules:
  0.0 151.3 jit_solution(12750538764185925336)
XLA Ops:
  7.2 1.9 %fusion.41 = (bf16[1,1,256,512]{3,2,1,0:T(8,128)(2,1)}, bf16[1,1,256,512]{3,2,1,0:T(8,128)(2,1)}) fusion(bf16[1,1,512,512]{3,2,1,0:T(8,128)(2,1)} %param.7), kind=kLoop, calls=%fused_computation.70 | loop fusion | bytes 1048576 | tf_op jit(solution)/shard_map/slice | solution.py:49
  9.8 2.1 %fusion.4 = f32[512]{0:T(512)S(1)} fusion(bf16[1,1,512,2048]{3,2,1,0:T(8,128)(2,1)} %param.5), kind=kLoop, calls=%fused_computation.6 | loop fusion | flops 3145216 | bytes 2099200 | tf_op jit(solution)/shard_map/reduce_sum | solution.py:41
  11.9 13.6 %psum.21 = f32[512,1]{0,1:T(1,128)S(1)} all-reduce(f32[512,1]{0,1:T(1,128)S(1)} %bitcast.58), channel_id=1, replica_groups=mesh['dp'=4,'pipe'=2,'tensor'=4] {'tensor'}, use_global_device_ids=true, to_apply=%region_1.2 | all-reduce | flops 512 | bytes 4096 | tf_op jit(solution)/shard_map/psum | solution.py:41
  25.5 4.1 %multiply_convert_fusion = (bf16[512,2048]{1,0:T(8,128)(2,1)S(1)}, f32[512,2048]{1,0:T(8,128)}) fusion(f32[2048]{0:T(1024)S(1)} %bitcast.51, f32[512]{0:T(512)S(1)} %bitcast.57, bf16[1,1,512,2048]{3,2,1,0:T(8,128)(2,1)} %param.5), kind=kLoop, calls=%fused_computation.9 | loop fusion | flops 4194304 | bytes 8398848 | tf_op jit(solution)/shard_map/convert_element_type | solution.py:44
  29.7 11.1 %all-gather.5.cloned.1.call-done = bf16[1,1,256,2048]{3,2,1,0:T(8,128)(2,1)} async-done(((bf16[1,1,256,512]{3,2,1,0:T(8,128)(2,1)}), bf16[1,1,256,2048]{3,2,1,0:T(8,128)(2,1)}) %all-gather.5.cloned.1.call-update) | async-done | bytes 1048592 | tf_op jit(solution)/shard_map/all_gather | solution.py:49
  40.8 8.2 %multiply_reduce_fusion.1 = (f32[2048]{0:T(1024)S(1)}, f32[256]{0:T(256)S(1)}, f32[256,2048]{1,0:T(8,128)}) fusion(f32[512,2048]{1,0:T(8,128)} %get-tuple-element.34, f32[2048]{0:T(1024)S(1)} %bitcast.52, bf16[1,2048,2048]{2,1,0:T(8,128)(2,1)} %param.9, bf16[1,1,256,2048]{3,2,1,0:T(8,128)(2,1)} %all-gather.5.cloned.1.call-done), kind=kOutput, calls=%fused_computation.17 | convolution fusion | flops 2150102784 | bytes 13648896 | tf_op jit(solution)/shard_map/dot_general | solution.py:79
  49.0 10.5 %psum.22 = f32[256,1]{0,1:T(1,128)S(1)} all-reduce(f32[256,1]{0,1:T(1,128)S(1)} %bitcast.66), channel_id=1, replica_groups=mesh['dp'=4,'pipe'=2,'tensor'=4] {'tensor'}, use_global_device_ids=true, to_apply=%region_3.4 | all-reduce | flops 256 | bytes 2048 | tf_op jit(solution)/shard_map/psum | solution.py:84
  59.5 4.2 %fusion.7 = bf16[256,2048]{1,0:T(8,128)(2,1)} fusion(f32[256,2048]{1,0:T(8,128)} %get-tuple-element.51, f32[512,2048]{1,0:T(8,128)} %get-tuple-element.34, f32[256]{0:T(256)S(1)} %bitcast.62, f32[2048]{0:T(1024)S(1)} %bitcast.53, f32[256]{0:T(256)S(1)} %bitcast.64, bf16[1,1,512,2048]{3,2,1,0:T(8,128)(2,1)} %param.6), kind=kLoop, calls=%fused_computation.15 | loop fusion | flops 3670016 | bytes 6301696 | tf_op jit(solution)/shard_map/convert_element_type | solution.py:88
  65.0 5.8 %all-gather.7.cloned.1.call-done = bf16[1,1,256,2048]{3,2,1,0:T(8,128)(2,1)} async-done(((bf16[1,1,256,512]{3,2,1,0:T(8,128)(2,1)}), bf16[1,1,256,2048]{3,2,1,0:T(8,128)(2,1)}) %all-gather.7.cloned.1.call-update) | async-done | bytes 1048592 | tf_op jit(solution)/shard_map/all_gather | solution.py:49
  72.2 3.4 %fusion.39 = (bf16[256,2048]{1,0:T(8,128)(2,1)S(1)}, bf16[256,2048]{1,0:T(8,128)(2,1)}, bf16[256,2048]{1,0:T(8,128)(2,1)}, bf16[256,2048]{1,0:T(8,128)(2,1)}) fusion(bf16[512,2048]{1,0:T(8,128)(2,1)} %collective-permute-done.1, bf16[512,2048]{1,0:T(8,128)(2,1)S(1)} %get-tuple-element.16), kind=kLoop, calls=%fused_computation.68 | loop fusion | bytes 8388608 | tf_op jit(solution)/shard_map/slice | solution.py:96
  77.5 2.2 %fusion.22 = f32[2048,512]{1,0:T(8,128)S(1)} fusion(bf16[256,1024]{1,0:T(8,128)(2,1)S(1)} %collective-permute-done.2, s32[]{:T(128)S(6)} %select_n.59, bf16[512,2048]{1,0:T(8,128)(2,1)} %collective-permute-done.1), kind=kOutput, calls=%fused_computation.40 | convolution fusion | flops 536870912 | bytes 5505028 | tf_op jit(solution)/shard_map/dot_general | solution.py:60
  80.5 2.1 %fusion.20 = f32[2048,512]{1,0:T(8,128)S(1)} fusion(bf16[256,1024]{1,0:T(8,128)(2,1)S(1)} %collective-permute-done.3, s32[]{:T(128)S(6)} %select_n.59, bf16[512,2048]{1,0:T(8,128)(2,1)} %collective-permute-done.1), kind=kOutput, calls=%fused_computation.38 | convolution fusion | flops 536870912 | bytes 5505028 | tf_op jit(solution)/shard_map/dot_general | solution.py:60
  82.7 2.5 %add_convert_fusion.1 = bf16[2048,512]{1,0:T(8,128)(2,1)} fusion(f32[2048,512]{1,0:T(8,128)S(1)} %fusion.20, f32[2048,512]{1,0:T(8,128)S(1)} %fusion.11, f32[2048,512]{1,0:T(8,128)S(1)} %fusion.22, s32[]{:T(128)S(6)} %select_n.59, bf16[256,512]{1,0:T(8,128)(2,1)S(1)} %get-tuple-element.42, bf16[256,512]{1,0:T(8,128)(2,1)S(1)} %get-tuple-element.39, ...), kind=kOutput, calls=%fused_computation.8 | convolution fusion | flops 541589504 | bytes 16252932 | tf_op jit(solution)/shard_map/dot_general | solution.py:60
  85.2 1.5 collective-permute-start.5
  86.9 3.9 %multiply_reduce_fusion = (f32[2048]{0:T(1024)S(1)}, f32[256]{0:T(256)S(1)}, f32[256,2048]{1,0:T(8,128)}) fusion(f32[512,2048]{1,0:T(8,128)S(1)} %copy-done.1, f32[2048]{0:T(1024)S(1)} %bitcast.54, bf16[256,2048]{1,0:T(8,128)(2,1)S(1)} %bitcast.49, bf16[1,2048,2048]{2,1,0:T(8,128)(2,1)S(1)} %bitcast.68), kind=kOutput, calls=%fused_computation.16 | convolution fusion | flops 2150102784 | bytes 13648896 | tf_op jit(solution)/shard_map/dot_general | solution.py:79
  91.3 10.4 %psum.23 = f32[256,1]{0,1:T(1,128)S(1)} all-reduce(f32[256,1]{0,1:T(1,128)S(1)} %bitcast.65), channel_id=1, replica_groups=mesh['dp'=4,'pipe'=2,'tensor'=4] {'tensor'}, use_global_device_ids=true, to_apply=%region_5.6 | all-reduce | flops 256 | bytes 2048 | tf_op jit(solution)/shard_map/psum | solution.py:84
  101.7 4.2 %fusion.6 = bf16[256,2048]{1,0:T(8,128)(2,1)} fusion(f32[256,2048]{1,0:T(8,128)} %get-tuple-element.52, f32[512,2048]{1,0:T(8,128)} %get-tuple-element.34, f32[256]{0:T(256)S(1)} %bitcast.61, f32[256]{0:T(256)S(1)} %bitcast.63, bf16[1,1,512,2048]{3,2,1,0:T(8,128)(2,1)} %param.6, f32[2048]{0:T(1024)S(1)} %bitcast.55), kind=kLoop, calls=%fused_computation.13 | loop fusion | flops 3670016 | bytes 6301696 | tf_op jit(solution)/shard_map/convert_element_type | solution.py:88
  107.3 2.7 %fusion.16 = f32[2048,512]{1,0:T(8,128)} fusion(bf16[256,2048]{1,0:T(8,128)(2,1)S(1)} %copy-done.3, bf16[256,1024]{1,0:T(8,128)(2,1)S(1)} %copy-done.10, s32[]{:T(128)S(6)} %select_n.62), kind=kOutput, calls=%fused_computation.34 | convolution fusion | flops 536870912 | bytes 5505028 | tf_op jit(solution)/shard_map/dot_general | solution.py:60
  110.0 2.7 %fusion.18 = f32[2048,512]{1,0:T(8,128)} fusion(bf16[256,2048]{1,0:T(8,128)(2,1)S(1)} %copy-done.2, bf16[256,1024]{1,0:T(8,128)(2,1)S(1)} %copy-done.5, s32[]{:T(128)S(6)} %select_n.62), kind=kOutput, calls=%fused_computation.36 | convolution fusion | flops 536870912 | bytes 5505028 | tf_op jit(solution)/shard_map/dot_general | solution.py:60
  112.7 1.5 collective-permute-start.7
  114.2 2.7 %fusion.13 = f32[2048,512]{1,0:T(8,128)} fusion(bf16[256,2048]{1,0:T(8,128)(2,1)S(1)} %get-tuple-element.27, bf16[256,1024]{1,0:T(8,128)(2,1)S(1)} %copy-done.12, s32[]{:T(128)S(6)} %select_n.62), kind=kOutput, calls=%fused_computation.31 | convolution fusion | flops 536870912 | bytes 5505028 | tf_op jit(solution)/shard_map/dot_general | solution.py:60
  117.0 16.7 %collective-permute-done.7 = f32[2048]{0:T(1024)S(1)} collective-permute-done((f32[2048]{0:T(1024)S(1)}, f32[2048]{0:T(1024)S(1)}, u32[]{:S(2)}, u32[]{:S(2)}) %collective-permute-start.7) | collective-permute-done | bytes 8224 | tf_op jit(solution)/shard_map/ppermute | solution.py:18
  134.3 3.3 %maximum_bitcast_fusion = bf16[1,1,512,2048]{3,2,1,0:T(8,128)(2,1)} fusion(bf16[256,2048]{1,0:T(8,128)(2,1)} %collective-permute-done.4, bf16[256,2048]{1,0:T(8,128)(2,1)} %collective-permute-done), kind=kLoop, calls=%fused_computation.11 | loop fusion | flops 4194304 | bytes 4194304 | tf_op jit(solution)/shard_map/broadcast_in_dim | solution.py:130
  137.6 6.9 %fusion.5 = bf16[1,2048,512]{2,1,0:T(8,128)(2,1)} fusion(bf16[2048,512]{1,0:T(8,128)(2,1)} %collective-permute-done.5, f32[2048,512]{1,0:T(8,128)} %fusion.13, bf16[256,2048]{1,0:T(8,128)(2,1)S(1)} %copy-done.4, f32[2048,512]{1,0:T(8,128)} %fusion.18, f32[2048,512]{1,0:T(8,128)S(1)} %copy-done, bf16[256,1024]{1,0:T(8,128)(2,1)S(1)} %copy-done.6, ...), kind=kOutput, calls=%fused_computation.10 | convolution fusion | flops 543162368 | bytes 18087940 | tf_op jit(solution)/shard_map/dot_general | solution.py:60
  (65 shorter events, 9.3 us)
Async XLA Ops:
  7.2 33.7 %all-gather.5.cloned.1.call-start = ((), (), s32[]{:S(2)}) async-start(), calls=%async_computation | async-start | bytes 1310720 | tf_op jit(solution)/shard_map/all_gather | solution.py:49
  9.1 61.6 %all-gather.7.cloned.1.call-start = ((), (), s32[]{:S(2)}) async-start(), calls=%async_computation.1 | async-start | bytes 1310720 | tf_op jit(solution)/shard_map/all_gather | solution.py:49
  29.6 41.1 %collective-permute-start.1 = (bf16[512,2048]{1,0:T(8,128)(2,1)S(1)}, bf16[512,2048]{1,0:T(8,128)(2,1)}, u32[]{:S(2)}, u32[]{:S(2)}) collective-permute-start(bf16[512,2048]{1,0:T(8,128)(2,1)S(1)} %get-tuple-element.16), channel_id=1, source_target_pairs={{0,8},{8,0},{16,24},{24,16},{1,9},{9,1},{17,25},{25,17},{2,10},{10... | collective-permute-start | bytes 6291464 | tf_op jit(solution)/shard_map/ppermute | solution.py:23
  59.5 11.2 %copy-start.8 = (bf16[1,1,256,2048]{3,2,1,0:T(8,128)(2,1)S(1)}, bf16[1,1,256,2048]{3,2,1,0:T(8,128)(2,1)}, u32[]{:S(2)}) copy-start(bf16[1,1,256,2048]{3,2,1,0:T(8,128)(2,1)} %all-gather.5.cloned.1.call-done) | copy-start | bytes 3145732
  63.7 70.6 %collective-permute-start = (bf16[256,2048]{1,0:T(8,128)(2,1)}, bf16[256,2048]{1,0:T(8,128)(2,1)}, u32[]{:S(2)}, u32[]{:S(2)}) collective-permute-start(bf16[256,2048]{1,0:T(8,128)(2,1)} %fusion.7), channel_id=1, source_target_pairs={{4,0},{5,1},{6,2},{7,3},{12,8},{13,9},{14,10},{15,11},{20,16},{21,... | collective-permute-start | bytes 3145736 | tf_op jit(solution)/shard_map/ppermute | solution.py:13
  70.7 1.2 copy-start.7
  70.9 6.6 %collective-permute-start.2 = (bf16[256,1024]{1,0:T(8,128)(2,1)S(1)}, bf16[256,1024]{1,0:T(8,128)(2,1)S(1)}, u32[]{:S(2)}, u32[]{:S(2)}) collective-permute-start(bf16[256,1024]{1,0:T(8,128)(2,1)S(1)} %pad_maximum_fusion.2), channel_id=1, source_target_pairs={{0,8},{8,0},{16,24},{24,16},{1,9},{9,1},{17,25},{25,17},{2,10},{10... | collective-permute-start | bytes 1572872 | tf_op jit(solution)/shard_map/ppermute | solution.py:23
  72.1 7.6 %collective-permute-start.3 = (bf16[256,1024]{1,0:T(8,128)(2,1)S(1)}, bf16[256,1024]{1,0:T(8,128)(2,1)S(1)}, u32[]{:S(2)}, u32[]{:S(2)}) collective-permute-start(bf16[256,1024]{1,0:T(8,128)(2,1)S(1)} %pad_maximum_fusion.3), channel_id=1, source_target_pairs={{0,8},{8,0},{16,24},{24,16},{1,9},{9,1},{17,25},{25,17},{2,10},{10... | collective-permute-start | bytes 1572872 | tf_op jit(solution)/shard_map/ppermute | solution.py:23
  77.5 2.2 %copy-start.9 = (bf16[256,1024]{1,0:T(8,128)(2,1)}, bf16[256,1024]{1,0:T(8,128)(2,1)S(1)}, u32[]{:S(2)}) copy-start(bf16[256,1024]{1,0:T(8,128)(2,1)S(1)} %collective-permute-done.2) | copy-start | bytes 1572868
  80.5 6.1 %slice-start = ((s8[8388608]{0:T(1024)(128)(4,1)}), s8[4194304]{0:T(1024)(128)(4,1)S(1)}, s32[]{:S(2)}) async-start(s8[8388608]{0:T(1024)(128)(4,1)} %bitcast.67), calls=%async_computation.2 | async-start | bytes 8388608
  82.7 4.0 %copy-start.1 = (f32[512,2048]{1,0:T(8,128)S(1)}, f32[512,2048]{1,0:T(8,128)}, u32[]{:S(2)}) copy-start(f32[512,2048]{1,0:T(8,128)} %get-tuple-element.34) | copy-start | bytes 12582916
  82.7 4.2 %slice-start.1 = ((s8[8388608]{0:T(1024)(128)(4,1)}), s8[4194304]{0:T(1024)(128)(4,1)S(1)}, s32[]{:S(2)}) async-start(s8[8388608]{0:T(1024)(128)(4,1)} %bitcast.67), calls=%async_computation.3 | async-start | bytes 8388608
  85.2 52.4 %collective-permute-start.5 = (bf16[2048,512]{1,0:T(8,128)(2,1)}, bf16[2048,512]{1,0:T(8,128)(2,1)}, u32[]{:S(2)}, u32[]{:S(2)}) collective-permute-start(bf16[2048,512]{1,0:T(8,128)(2,1)} %add_convert_fusion.1), channel_id=1, source_target_pairs={{0,16},{8,24},{16,0},{24,8},{1,17},{9,25},{17,1},{25,9},{2,18},{10... | collective-permute-start | bytes 6291464 | tf_op jit(solution)/shard_map/ppermute | solution.py:18
  90.8 21.9 %collective-permute-start.6 = (f32[2048]{0:T(1024)S(1)}, f32[2048]{0:T(1024)S(1)}, u32[]{:S(2)}, u32[]{:S(2)}) collective-permute-start(f32[2048]{0:T(1024)S(1)} %add.125), channel_id=1, source_target_pairs={{0,8},{8,0},{16,24},{24,16},{1,9},{9,1},{17,25},{25,17},{2,10},{10... | collective-permute-start | bytes 24584 | tf_op jit(solution)/shard_map/ppermute | solution.py:23
  101.7 5.6 %copy-start.3 = (bf16[256,2048]{1,0:T(8,128)(2,1)S(1)}, bf16[256,2048]{1,0:T(8,128)(2,1)}, u32[]{:S(2)}) copy-start(bf16[256,2048]{1,0:T(8,128)(2,1)} %get-tuple-element.23) | copy-start | bytes 3145732
  101.7 5.6 %copy-start.10 = (bf16[256,1024]{1,0:T(8,128)(2,1)S(1)}, bf16[256,1024]{1,0:T(8,128)(2,1)}, u32[]{:S(2)}) copy-start(bf16[256,1024]{1,0:T(8,128)(2,1)} %copy-done.9) | copy-start | bytes 1572868
  105.8 4.1 %copy-start.2 = (bf16[256,2048]{1,0:T(8,128)(2,1)S(1)}, bf16[256,2048]{1,0:T(8,128)(2,1)}, u32[]{:S(2)}) copy-start(bf16[256,2048]{1,0:T(8,128)(2,1)} %get-tuple-element.21) | copy-start | bytes 3145732
  105.8 4.1 %copy-start.5 = (bf16[256,1024]{1,0:T(8,128)(2,1)S(1)}, bf16[256,1024]{1,0:T(8,128)(2,1)}, u32[]{:S(2)}) copy-start(bf16[256,1024]{1,0:T(8,128)(2,1)} %get-tuple-element.22) | copy-start | bytes 1572868
  105.8 28.5 %collective-permute-start.4 = (bf16[256,2048]{1,0:T(8,128)(2,1)}, bf16[256,2048]{1,0:T(8,128)(2,1)}, u32[]{:S(2)}, u32[]{:S(2)}) collective-permute-start(bf16[256,2048]{1,0:T(8,128)(2,1)} %fusion.6), channel_id=1, source_target_pairs={{4,0},{5,1},{6,2},{7,3},{12,8},{13,9},{14,10},{15,11},{20,16},{21,... | collective-permute-start | bytes 3145736 | tf_op jit(solution)/shard_map/ppermute | solution.py:13
  110.0 4.2 %copy-start.12 = (bf16[256,1024]{1,0:T(8,128)(2,1)S(1)}, bf16[256,1024]{1,0:T(8,128)(2,1)}, u32[]{:S(2)}) copy-start(bf16[256,1024]{1,0:T(8,128)(2,1)} %copy-done.11) | copy-start | bytes 1572868
  112.7 20.9 %collective-permute-start.7 = (f32[2048]{0:T(1024)S(1)}, f32[2048]{0:T(1024)S(1)}, u32[]{:S(2)}, u32[]{:S(2)}) collective-permute-start(f32[2048]{0:T(1024)S(1)} %add.126), channel_id=1, source_target_pairs={{0,16},{8,24},{16,0},{24,8},{1,17},{9,25},{17,1},{25,9},{2,18},{10... | collective-permute-start | bytes 24584 | tf_op jit(solution)/shard_map/ppermute | solution.py:18
  114.2 23.4 %copy-start.4 = (bf16[256,2048]{1,0:T(8,128)(2,1)S(1)}, bf16[256,2048]{1,0:T(8,128)(2,1)}, u32[]{:S(2)}) copy-start(bf16[256,2048]{1,0:T(8,128)(2,1)} %get-tuple-element.25) | copy-start | bytes 3145732
  114.2 23.4 %copy-start.6 = (bf16[256,1024]{1,0:T(8,128)(2,1)S(1)}, bf16[256,1024]{1,0:T(8,128)(2,1)}, u32[]{:S(2)}) copy-start(bf16[256,1024]{1,0:T(8,128)(2,1)} %get-tuple-element.26) | copy-start | bytes 1572868
  134.3 3.3 %copy-start = (f32[2048,512]{1,0:T(8,128)S(1)}, f32[2048,512]{1,0:T(8,128)}, u32[]{:S(2)}) copy-start(f32[2048,512]{1,0:T(8,128)} %fusion.16) | copy-start | bytes 12582916
  (1 other events, 0.8 us)
Sparse Core Ops, SparseCore 0:
  10.1 30.6 all-gather.4
  43.0 27.6 all-gather.6

commit v17 on v13

--- a/solution.py
+++ b/solution.py
@@ -92,14 +92,18 @@
         inputs_grad.append(from_behind(input_grad, "pipe", -1))
         gain_part = gain_part + jnp.sum(row_total * normed_c, axis=0)
         if c == 0:
-            _, (h, hp, parts) = lax.optimization_barrier((input_grad, (hidden, hidden_partner, pieces)))
-            chunk_blocks = [
+            _, (h, hp, first_part) = lax.optimization_barrier((input_grad, (hidden, hidden_partner, pieces[0])))
+            first_blocks = pair_blocks(h[:step], hp[:step], first_part)
+            first_sends = [first_blocks(g) for g in dests]
+            _, later = lax.optimization_barrier((first_sends, pieces[1:]))
+            parts = [first_part] + list(later)
+            chunk_blocks = [first_blocks] + [
                 pair_blocks(h[k * step:(k + 1) * step], hp[k * step:(k + 1) * step], parts[k])
-                for k in range(CHUNKS)
+                for k in range(1, CHUNKS)
             ]
             outs = []
-            for g in dests:
-                acc = chunk_blocks[0](g)
+            for i, g in enumerate(dests):
+                acc = first_sends[i]
                 for k in range(1, CHUNKS):
                     acc = acc + chunk_blocks[k](g)
                 outs.append(acc.astype(jnp.bfloat16))

time: 146 us -> 147 us (level)
  matrix products: 32.9 us -> 39.6 us
  waiting for transfers between devices: 35.7 us -> 30.2 us
  other arithmetic: 18.3 us -> 20 us
    all_gather x2, waiting for transfers between devices: 17.7 us -> 11.9 us  [on_device(): lax.all_gather(grad_kv[c * step:(c + 1) * step], 'tensor', axis=1, tiled=...]
    dot_general x8, matrix products: 20.8 us -> 24.1 us  [tn(): lax.dot_general(a, b, (((0,), (0,)), ((), ())), preferred_element_type=jn...]
    dot_general x2, matrix products: 12.1 us -> 15.4 us  [on_device(): lax.dot_general(block, weight, (((1,), (1,)), ((), ())), preferred_elemen...]
    ppermute x4, waiting for transfers between devices: 0.01 us -> 2.95 us  [to_partner(): return lax.ppermute(block, 'dp', [(i, i ^ 1) for i in range(n)])]
    ppermute x2, waiting for transfers between devices: 17.9 us -> 15.3 us  [shifted(): return lax.ppermute(block, axis, [(i, (i + shift) % n) for i in range(n)])]
    concatenate x2, other arithmetic: 0.12 us -> 1.73 us  [cols_of(): jnp.concatenate([lax.dynamic_slice_in_dim(q, (2 * g + p) * kv_block, kv_b...]
  transfers between devices with their start and end apart: 10 -> 10, of which waited for: 3 -> 4; matrix products, arithmetic and copies ran while one was open for 32% -> 36% of each run, Pallas kernels for 0% -> 0%
where the time goes in v17:
time: 147 us; the launch traced here: 146 us
  matrix products  39.6 us (27%)
  blocking collectives  33.4 us (23%)
  waiting for transfers between devices  30.2 us (21%)
  other arithmetic  20 us (14%)
  between operations  14.2 us (10%)
  starting transfers between devices  4.99 us (3%)
  local copies, waits for them, and re-layouts  4.01 us (3%)
    dot_general x8, matrix products, tn(): lax.dot_general(a, b, (((0,), (0,)), ((), ())), preferred_element_type=jn...  24.1 us
    psum x2, blocking collectives, on_device(): lax.psum(jnp.sum(scaled * normed_c, axis=1, keepdims=True), 'tensor')  19.9 us
    dot_general x2, matrix products, on_device(): lax.dot_general(block, weight, (((1,), (1,)), ((), ())), preferred_elemen...  15.4 us
    ppermute x2, waiting for transfers between devices, shifted(): return lax.ppermute(block, axis, [(i, (i + shift) % n) for i in range(n)])  15.3 us
    psum x1, blocking collectives, on_device(): lax.psum(jnp.sum(values * values, axis=1, keepdims=True), 'tensor')  13.5 us
    all_gather x2, waiting for transfers between devices, on_device(): lax.all_gather(grad_kv[c * step:(c + 1) * step], 'tensor', axis=1, tiled=...  11.9 us
    convert_element_type x2, other arithmetic, on_device(): input_grad = (grad_out[lo:lo + step].astype(jnp.float32) + rstd[lo:lo + s...  8.29 us
    convert_element_type x1, other arithmetic, on_device(): hidden = (normed * gain_f).astype(jnp.bfloat16)  3.31 us
  transfers between devices with their start and end apart: 10, of which 4 were waited for; matrix products, arithmetic and copies ran while one was open for 36% of the time, Pallas kernels for 0%

profile of v17, /device:TPU:0, one launch (start us, length us, event | category | flops | bytes accessed | tf_op | source)
XLA Modules:
  0.0 146.3 jit_solution(17011084304078713899)
XLA Ops:
  7.2 2.0 %fusion.45 = (bf16[1,1,256,512]{3,2,1,0:T(8,128)(2,1)}, bf16[1,1,256,512]{3,2,1,0:T(8,128)(2,1)}) fusion(bf16[1,1,512,512]{3,2,1,0:T(8,128)(2,1)} %param.7), kind=kLoop, calls=%fused_computation.76 | loop fusion | bytes 1048576 | tf_op jit(solution)/shard_map/slice | solution.py:49
  10.0 2.1 %fusion.4 = f32[512]{0:T(512)S(1)} fusion(bf16[1,1,512,2048]{3,2,1,0:T(8,128)(2,1)} %param.5), kind=kLoop, calls=%fused_computation.6 | loop fusion | flops 3145216 | bytes 2099200 | tf_op jit(solution)/shard_map/reduce_sum | solution.py:41
  12.1 13.5 %psum.21 = f32[512,1]{0,1:T(1,128)S(1)} all-reduce(f32[512,1]{0,1:T(1,128)S(1)} %bitcast.54), channel_id=1, replica_groups=mesh['dp'=4,'pipe'=2,'tensor'=4] {'tensor'}, use_global_device_ids=true, to_apply=%region_1.2 | all-reduce | flops 512 | bytes 4096 | tf_op jit(solution)/shard_map/psum | solution.py:41
  25.6 3.3 %multiply_convert_fusion = (bf16[512,2048]{1,0:T(8,128)(2,1)}, f32[512,2048]{1,0:T(8,128)}) fusion(f32[2048]{0:T(1024)S(1)} %bitcast.47, f32[512]{0:T(512)S(1)} %bitcast.53, bf16[1,1,512,2048]{3,2,1,0:T(8,128)(2,1)S(1)} %copy-done.3), kind=kLoop, calls=%fused_computation.9 | loop fusion | flops 4194304 | bytes 8398848 | tf_op jit(solution)/shard_map/convert_element_type | solution.py:44
  29.0 11.9 %all-gather.5.cloned.1.call-done = bf16[1,1,256,2048]{3,2,1,0:T(8,128)(2,1)} async-done(((bf16[1,1,256,512]{3,2,1,0:T(8,128)(2,1)}), bf16[1,1,256,2048]{3,2,1,0:T(8,128)(2,1)}) %all-gather.5.cloned.1.call-update) | async-done | bytes 1048592 | tf_op jit(solution)/shard_map/all_gather | solution.py:49
  40.9 8.2 %multiply_reduce_fusion.1 = (f32[2048]{0:T(1024)S(1)}, f32[256]{0:T(256)S(1)}, f32[256,2048]{1,0:T(8,128)}) fusion(f32[512,2048]{1,0:T(8,128)} %get-tuple-element.20, f32[2048]{0:T(1024)S(1)} %bitcast.48, bf16[1,2048,2048]{2,1,0:T(8,128)(2,1)} %param.9, bf16[1,1,256,2048]{3,2,1,0:T(8,128)(2,1)} %all-gather.5.cloned.1.call-done), kind=kOutput, calls=%fused_computation.19 | convolution fusion | flops 2150102784 | bytes 13648896 | tf_op jit(solution)/shard_map/dot_general | solution.py:82
  49.0 10.5 %psum.22 = f32[256,1]{0,1:T(1,128)S(1)} all-reduce(f32[256,1]{0,1:T(1,128)S(1)} %bitcast.62), channel_id=1, replica_groups=mesh['dp'=4,'pipe'=2,'tensor'=4] {'tensor'}, use_global_device_ids=true, to_apply=%region_3.4 | all-reduce | flops 256 | bytes 2048 | tf_op jit(solution)/shard_map/psum | solution.py:87
  59.5 4.2 %fusion.7 = bf16[256,2048]{1,0:T(8,128)(2,1)} fusion(f32[256,2048]{1,0:T(8,128)} %get-tuple-element.33, f32[512,2048]{1,0:T(8,128)} %get-tuple-element.20, f32[256]{0:T(256)S(1)} %bitcast.58, f32[2048]{0:T(1024)S(1)} %bitcast.49, f32[256]{0:T(256)S(1)} %bitcast.60, bf16[1,1,512,2048]{3,2,1,0:T(8,128)(2,1)} %param.6), kind=kLoop, calls=%fused_computation.17 | loop fusion | flops 3670016 | bytes 6301696 | tf_op jit(solution)/shard_map/convert_element_type | solution.py:91
  64.7 2.1 %collective-permute-done.2 = bf16[256,1024]{1,0:T(8,128)(2,1)S(1)} collective-permute-done((bf16[256,1024]{1,0:T(8,128)(2,1)}, bf16[256,1024]{1,0:T(8,128)(2,1)S(1)}, u32[]{:S(2)}, u32[]{:S(2)}) %collective-permute-start.2) | collective-permute-done | bytes 524320 | tf_op jit(solution)/shard_map/ppermute | solution.py:23
  67.6 4.0 %convolution_add_fusion.1 = f32[2048,512]{1,0:T(8,128)} fusion(f32[2048,512]{1,0:T(8,128)S(1)} %fusion.16, bf16[512,2048]{1,0:T(8,128)(2,1)} %get-tuple-element.9, s32[]{:T(128)S(6)} %select_n.59, bf16[256,512]{1,0:T(8,128)(2,1)S(1)} %get-tuple-element.28, bf16[256,512]{1,0:T(8,128)(2,1)S(1)} %get-tuple-element.25), kind=kOutput, calls=%fused_computation.11 | convolution fusion | flops 538443776 | bytes 9961476 | tf_op jit(solution)/shard_map/dot_general | solution.py:60
  71.6 1.3 constant_dynamic-slice_fusion.2
  73.9 1.3 collective-permute-start
  76.0 1.8 %fusion.10 = f32[2048,512]{1,0:T(8,128)S(1)} fusion(bf16[512,2048]{1,0:T(8,128)(2,1)S(1)} %collective-permute-done.1, bf16[256,1024]{1,0:T(8,128)(2,1)} %collective-permute-done.3, s32[]{:T(128)S(6)} %select_n.59), kind=kOutput, calls=%fused_computation.24 | convolution fusion | flops 536870912 | bytes 5505028 | tf_op jit(solution)/shard_map/dot_general | solution.py:60
  78.3 3.5 %add_convert_fusion.1 = bf16[2048,512]{1,0:T(8,128)(2,1)} fusion(f32[2048,512]{1,0:T(8,128)S(1)} %copy-done.2, f32[2048,512]{1,0:T(8,128)S(1)} %fusion.10, bf16[512,2048]{1,0:T(8,128)(2,1)} %get-tuple-element.9, s32[]{:T(128)S(6)} %select_n.59, bf16[256,512]{1,0:T(8,128)(2,1)S(1)} %get-tuple-element.24, bf16[256,512]{1,0:T(8,128)(2,1)S(1)} %get-tuple-element.21), kind=kOutput, calls=%fused_computation.8 | convolution fusion | flops 540540928 | bytes 12058628 | tf_op jit(solution)/shard_map/dot_general | solution.py:60
  81.8 1.4 collective-permute-start.5
  83.2 7.3 %multiply_reduce_fusion = (f32[2048]{0:T(1024)S(1)}, f32[256]{0:T(256)S(1)}, f32[256,2048]{1,0:T(8,128)}) fusion(f32[512,2048]{1,0:T(8,128)S(1)} %copy-done.1, f32[2048]{0:T(1024)S(1)} %bitcast.50, bf16[256,2048]{1,0:T(8,128)(2,1)S(1)} %bitcast.45, bf16[1,2048,2048]{2,1,0:T(8,128)(2,1)} %param.9), kind=kOutput, calls=%fused_computation.18 | convolution fusion | flops 2150102784 | bytes 13648896 | tf_op jit(solution)/shard_map/dot_general | solution.py:82
  90.5 9.4 %psum.23 = f32[256,1]{0,1:T(1,128)S(1)} all-reduce(f32[256,1]{0,1:T(1,128)S(1)} %bitcast.61), channel_id=1, replica_groups=mesh['dp'=4,'pipe'=2,'tensor'=4] {'tensor'}, use_global_device_ids=true, to_apply=%region_5.6 | all-reduce | flops 256 | bytes 2048 | tf_op jit(solution)/shard_map/psum | solution.py:87
  99.8 4.1 %fusion.6 = bf16[256,2048]{1,0:T(8,128)(2,1)} fusion(f32[256,2048]{1,0:T(8,128)} %get-tuple-element.34, f32[512,2048]{1,0:T(8,128)} %get-tuple-element.20, f32[256]{0:T(256)S(1)} %bitcast.57, f32[256]{0:T(256)S(1)} %bitcast.59, bf16[1,1,512,2048]{3,2,1,0:T(8,128)(2,1)} %param.6, f32[2048]{0:T(1024)S(1)} %bitcast.51), kind=kLoop, calls=%fused_computation.15 | loop fusion | flops 3670016 | bytes 6301696 | tf_op jit(solution)/shard_map/convert_element_type | solution.py:91
  103.9 1.5 collective-permute-start.4
  106.2 4.0 %convolution_add_fusion = f32[2048,512]{1,0:T(8,128)} fusion(f32[2048,512]{1,0:T(8,128)S(1)} %fusion.14, bf16[512,2048]{1,0:T(8,128)(2,1)} %get-tuple-element.9, s32[]{:T(128)S(6)} %select_n.62, bf16[256,512]{1,0:T(8,128)(2,1)S(1)} %get-tuple-element.28, bf16[256,512]{1,0:T(8,128)(2,1)S(1)} %get-tuple-element.25), kind=kOutput, calls=%fused_computation.10 | convolution fusion | flops 538443776 | bytes 9961476 | tf_op jit(solution)/shard_map/dot_general | solution.py:60
  110.8 3.7 %fusion.8 = f32[2048,512]{1,0:T(8,128)} fusion(bf16[512,2048]{1,0:T(8,128)(2,1)S(1)} %collective-permute-done.1, bf16[256,1024]{1,0:T(8,128)(2,1)} %collective-permute-done.3, s32[]{:T(128)S(6)} %select_n.62), kind=kOutput, calls=%fused_computation.22 | convolution fusion | flops 536870912 | bytes 5505028 | tf_op jit(solution)/shard_map/dot_general | solution.py:60
  114.6 15.3 %collective-permute-done.7 = f32[2048]{0:T(1024)S(1)} collective-permute-done((f32[2048]{0:T(1024)S(1)}, f32[2048]{0:T(1024)S(1)}, u32[]{:S(2)}, u32[]{:S(2)}) %collective-permute-start.7) | collective-permute-done | bytes 8224 | tf_op jit(solution)/shard_map/ppermute | solution.py:18
  130.6 3.3 %maximum_bitcast_fusion = bf16[1,1,512,2048]{3,2,1,0:T(8,128)(2,1)} fusion(bf16[256,2048]{1,0:T(8,128)(2,1)} %collective-permute-done.4, bf16[256,2048]{1,0:T(8,128)(2,1)} %collective-permute-done), kind=kLoop, calls=%fused_computation.13 | loop fusion | flops 4194304 | bytes 4194304 | tf_op jit(solution)/shard_map/broadcast_in_dim | solution.py:130
  133.9 5.6 %fusion.5 = bf16[1,2048,512]{2,1,0:T(8,128)(2,1)} fusion(bf16[2048,512]{1,0:T(8,128)(2,1)} %collective-permute-done.5, f32[2048,512]{1,0:T(8,128)} %convolution_add_fusion, f32[2048,512]{1,0:T(8,128)S(1)} %copy-done, bf16[512,2048]{1,0:T(8,128)(2,1)} %get-tuple-element.9, s32[]{:T(128)S(6)} %select_n.62, bf16[256,512]{1,0:T(8,128)(2,1)S(1)} %get-tuple-element.24, ...), kind=kOutput, calls=%fused_computation.12 | convolution fusion | flops 542638080 | bytes 14155780 | tf_op jit(solution)/shard_map/dot_general | solution.py:60
  (48 shorter events, 7.1 us)
Async XLA Ops:
  7.2 18.4 %copy-start.3 = (bf16[1,1,512,2048]{3,2,1,0:T(8,128)(2,1)S(1)}, bf16[1,1,512,2048]{3,2,1,0:T(8,128)(2,1)}, u32[]{:S(2)}) copy-start(bf16[1,1,512,2048]{3,2,1,0:T(8,128)(2,1)} %param.5) | copy-start | bytes 6291460
  7.2 33.7 %all-gather.5.cloned.1.call-start = ((), (), s32[]{:S(2)}) async-start(), calls=%async_computation | async-start | bytes 1310720 | tf_op jit(solution)/shard_map/all_gather | solution.py:49
  9.2 62.4 %all-gather.7.cloned.1.call-start = ((), (), s32[]{:S(2)}) async-start(), calls=%async_computation.1 | async-start | bytes 1310720 | tf_op jit(solution)/shard_map/all_gather | solution.py:49
  28.9 34.8 %collective-permute-start.1 = (bf16[512,2048]{1,0:T(8,128)(2,1)}, bf16[512,2048]{1,0:T(8,128)(2,1)S(1)}, u32[]{:S(2)}, u32[]{:S(2)}) collective-permute-start(bf16[512,2048]{1,0:T(8,128)(2,1)} %get-tuple-element.9), channel_id=1, source_target_pairs={{0,8},{8,0},{16,24},{24,16},{1,9},{9,1},{17,25},{25,17},{2,10},{10... | collective-permute-start | bytes 6291464 | tf_op jit(solution)/shard_map/ppermute | solution.py:23
  59.5 4.2 %copy-start.5 = (bf16[1,1,256,2048]{3,2,1,0:T(8,128)(2,1)S(1)}, bf16[1,1,256,2048]{3,2,1,0:T(8,128)(2,1)}, u32[]{:S(2)}) copy-start(bf16[1,1,256,2048]{3,2,1,0:T(8,128)(2,1)} %all-gather.5.cloned.1.call-done) | copy-start | bytes 3145732
  64.7 2.1 %collective-permute-start.2 = (bf16[256,1024]{1,0:T(8,128)(2,1)}, bf16[256,1024]{1,0:T(8,128)(2,1)S(1)}, u32[]{:S(2)}, u32[]{:S(2)}) collective-permute-start(bf16[256,1024]{1,0:T(8,128)(2,1)} %pad_maximum_fusion), channel_id=1, source_target_pairs={{0,8},{8,0},{16,24},{24,16},{1,9},{9,1},{17,25},{25,17},{2,10},{10... | collective-permute-start | bytes 1572872 | tf_op jit(solution)/shard_map/ppermute | solution.py:23
  66.8 0.8 copy-start.6
  73.8 2.3 %collective-permute-start.3 = (bf16[256,1024]{1,0:T(8,128)(2,1)}, bf16[256,1024]{1,0:T(8,128)(2,1)}, u32[]{:S(2)}, u32[]{:S(2)}) collective-permute-start(bf16[256,1024]{1,0:T(8,128)(2,1)} %pad_maximum_fusion.1), channel_id=1, source_target_pairs={{0,8},{8,0},{16,24},{24,16},{1,9},{9,1},{17,25},{25,17},{2,10},{10... | collective-permute-start | bytes 1572872 | tf_op jit(solution)/shard_map/ppermute | solution.py:23
  73.9 56.7 %collective-permute-start = (bf16[256,2048]{1,0:T(8,128)(2,1)}, bf16[256,2048]{1,0:T(8,128)(2,1)}, u32[]{:S(2)}, u32[]{:S(2)}) collective-permute-start(bf16[256,2048]{1,0:T(8,128)(2,1)} %fusion.7), channel_id=1, source_target_pairs={{4,0},{5,1},{6,2},{7,3},{12,8},{13,9},{14,10},{15,11},{20,16},{21,... | collective-permute-start | bytes 3145736 | tf_op jit(solution)/shard_map/ppermute | solution.py:13
  76.0 2.3 %copy-start.2 = (f32[2048,512]{1,0:T(8,128)S(1)}, f32[2048,512]{1,0:T(8,128)}, u32[]{:S(2)}) copy-start(f32[2048,512]{1,0:T(8,128)} %convolution_add_fusion.1) | copy-start | bytes 12582916
  78.3 4.9 %copy-start.1 = (f32[512,2048]{1,0:T(8,128)S(1)}, f32[512,2048]{1,0:T(8,128)}, u32[]{:S(2)}) copy-start(f32[512,2048]{1,0:T(8,128)} %get-tuple-element.20) | copy-start | bytes 12582916
  78.3 4.9 %copy-start.4 = (bf16[1,1,256,2048]{3,2,1,0:T(8,128)(2,1)S(1)}, bf16[1,1,256,2048]{3,2,1,0:T(8,128)(2,1)}, u32[]{:S(2)}) copy-start(bf16[1,1,256,2048]{3,2,1,0:T(8,128)(2,1)} %all-gather.7.cloned.1.call-done) | copy-start | bytes 3145732
  81.8 52.0 %collective-permute-start.5 = (bf16[2048,512]{1,0:T(8,128)(2,1)}, bf16[2048,512]{1,0:T(8,128)(2,1)}, u32[]{:S(2)}, u32[]{:S(2)}) collective-permute-start(bf16[2048,512]{1,0:T(8,128)(2,1)} %add_convert_fusion.1), channel_id=1, source_target_pairs={{0,16},{8,24},{16,0},{24,8},{1,17},{9,25},{17,1},{25,9},{2,18},{10... | collective-permute-start | bytes 6291464 | tf_op jit(solution)/shard_map/ppermute | solution.py:18
  99.8 5.6 %copy-start.7 = (bf16[256,1024]{1,0:T(8,128)(2,1)S(1)}, bf16[256,1024]{1,0:T(8,128)(2,1)}, u32[]{:S(2)}) copy-start(bf16[256,1024]{1,0:T(8,128)(2,1)} %copy-done.6) | copy-start | bytes 1572868
  103.9 26.7 %collective-permute-start.4 = (bf16[256,2048]{1,0:T(8,128)(2,1)}, bf16[256,2048]{1,0:T(8,128)(2,1)}, u32[]{:S(2)}, u32[]{:S(2)}) collective-permute-start(bf16[256,2048]{1,0:T(8,128)(2,1)} %fusion.6), channel_id=1, source_target_pairs={{4,0},{5,1},{6,2},{7,3},{12,8},{13,9},{14,10},{15,11},{20,16},{21,... | collective-permute-start | bytes 3145736 | tf_op jit(solution)/shard_map/ppermute | solution.py:13
  106.2 4.1 %collective-permute-start.6 = (f32[2048]{0:T(1024)S(1)}, f32[2048]{0:T(1024)S(1)}, u32[]{:S(2)}, u32[]{:S(2)}) collective-permute-start(f32[2048]{0:T(1024)S(1)} %add.125), channel_id=1, source_target_pairs={{0,8},{8,0},{16,24},{24,16},{1,9},{9,1},{17,25},{25,17},{2,10},{10... | collective-permute-start | bytes 24584 | tf_op jit(solution)/shard_map/ppermute | solution.py:23
  110.2 19.6 %collective-permute-start.7 = (f32[2048]{0:T(1024)S(1)}, f32[2048]{0:T(1024)S(1)}, u32[]{:S(2)}, u32[]{:S(2)}) collective-permute-start(f32[2048]{0:T(1024)S(1)} %add.126), channel_id=1, source_target_pairs={{0,16},{8,24},{16,0},{24,8},{1,17},{9,25},{17,1},{25,9},{2,18},{10... | collective-permute-start | bytes 24584 | tf_op jit(solution)/shard_map/ppermute | solution.py:18
  130.6 3.3 %copy-start = (f32[2048,512]{1,0:T(8,128)S(1)}, f32[2048,512]{1,0:T(8,128)}, u32[]{:S(2)}) copy-start(f32[2048,512]{1,0:T(8,128)} %fusion.8) | copy-start | bytes 12582916
Sparse Core Ops, SparseCore 0:
  10.2 30.6 all-gather.4
  43.0 27.6 all-gather.6

commit v18 on v13

--- a/solution.py
+++ b/solution.py
@@ -108,6 +108,7 @@
             total = first
             for k in range(1, CHUNKS):
                 total = total + chunk_blocks[k](own_g)
+            total = lax.optimization_barrier(total)
             for got in received:
                 total = total + got.astype(jnp.float32)
             weight_total = total.astype(jnp.bfloat16)

time: 146 us -> 143 us (0.979)
  matrix products: 32.9 us -> 27.4 us
  other arithmetic: 18.3 us -> 22 us
    dot_general x8, matrix products: 20.8 us -> 15.2 us  [tn(): lax.dot_general(a, b, (((0,), (0,)), ((), ())), preferred_element_type=jn...]
    broadcast_in_dim x1 -> x2, other arithmetic: 3.26 us -> 7.07 us  [on_device(): return (upstream[None, None], weight_total[None], gain_total[None])]
  transfers between devices with their start and end apart: 10 -> 10, of which waited for: 3 -> 3; matrix products, arithmetic and copies ran while one was open for 32% -> 33% of each run, Pallas kernels for 0% -> 0%
where the time goes in v18:
time: 143 us
  waiting for transfers between devices  34.9 us (24%)
  blocking collectives  34.3 us (24%)
  matrix products  27.4 us (19%)
  other arithmetic  22 us (15%)
  between operations  14.3 us (10%)
  starting transfers between devices  6.12 us (4%)
  local copies, waits for them, and re-layouts  3.78 us (3%)
    psum x2, blocking collectives, on_device(): lax.psum(jnp.sum(scaled * normed_c, axis=1, keepdims=True), 'tensor')  20.7 us
    ppermute x2, waiting for transfers between devices, shifted(): return lax.ppermute(block, axis, [(i, (i + shift) % n) for i in range(n)])  17.7 us
    all_gather x2, waiting for transfers between devices, on_device(): lax.all_gather(grad_kv[c * step:(c + 1) * step], 'tensor', axis=1, tiled=...  17.2 us
    dot_general x8, matrix products, tn(): lax.dot_general(a, b, (((0,), (0,)), ((), ())), preferred_element_type=jn...  15.2 us
    psum x1, blocking collectives, on_device(): lax.psum(jnp.sum(values * values, axis=1, keepdims=True), 'tensor')  13.5 us
    dot_general x2, matrix products, on_device(): lax.dot_general(block, weight, (((1,), (1,)), ((), ())), preferred_elemen...  12.1 us
    convert_element_type x2, other arithmetic, on_device(): input_grad = (grad_out[lo:lo + step].astype(jnp.float32) + rstd[lo:lo + s...  8.17 us
    broadcast_in_dim x2, other arithmetic, on_device(): return (upstream[None, None], weight_total[None], gain_total[None])  7.07 us
  transfers between devices with their start and end apart: 10, of which 3 were waited for; matrix products, arithmetic and copies ran while one was open for 33% of the time, Pallas kernels for 0%

profile of v18, /device:TPU:0, one launch (start us, length us, event | category | flops | bytes accessed | tf_op | source)
XLA Modules:
  0.0 142.8 jit_solution(2295276264203756256)
XLA Ops:
  7.2 2.0 %fusion.46 = (bf16[1,1,256,512]{3,2,1,0:T(8,128)(2,1)}, bf16[1,1,256,512]{3,2,1,0:T(8,128)(2,1)}) fusion(bf16[1,1,512,512]{3,2,1,0:T(8,128)(2,1)} %param.7), kind=kLoop, calls=%fused_computation.77 | loop fusion | bytes 1048576 | tf_op jit(solution)/shard_map/slice | solution.py:49
  10.0 2.1 %fusion.4 = f32[512]{0:T(512)S(1)} fusion(bf16[1,1,512,2048]{3,2,1,0:T(8,128)(2,1)} %param.5), kind=kLoop, calls=%fused_computation.6 | loop fusion | flops 3145216 | bytes 2099200 | tf_op jit(solution)/shard_map/reduce_sum | solution.py:41
  12.1 13.5 %psum.21 = f32[512,1]{0,1:T(1,128)S(1)} all-reduce(f32[512,1]{0,1:T(1,128)S(1)} %bitcast.54), channel_id=1, replica_groups=mesh['dp'=4,'pipe'=2,'tensor'=4] {'tensor'}, use_global_device_ids=true, to_apply=%region_1.2 | all-reduce | flops 512 | bytes 4096 | tf_op jit(solution)/shard_map/psum | solution.py:41
  25.6 3.3 %multiply_convert_fusion = (bf16[512,2048]{1,0:T(8,128)(2,1)}, f32[512,2048]{1,0:T(8,128)}) fusion(f32[2048]{0:T(1024)S(1)} %bitcast.47, f32[512]{0:T(512)S(1)} %bitcast.53, bf16[1,1,512,2048]{3,2,1,0:T(8,128)(2,1)S(1)} %copy-done.2), kind=kLoop, calls=%fused_computation.10 | loop fusion | flops 4194304 | bytes 8398848 | tf_op jit(solution)/shard_map/convert_element_type | solution.py:44
  29.0 11.9 %all-gather.5.cloned.1.call-done = bf16[1,1,256,2048]{3,2,1,0:T(8,128)(2,1)} async-done(((bf16[1,1,256,512]{3,2,1,0:T(8,128)(2,1)}), bf16[1,1,256,2048]{3,2,1,0:T(8,128)(2,1)}) %all-gather.5.cloned.1.call-update) | async-done | bytes 1048592 | tf_op jit(solution)/shard_map/all_gather | solution.py:49
  40.9 8.2 %multiply_reduce_fusion.1 = (f32[2048]{0:T(1024)S(1)}, f32[256]{0:T(256)S(1)}, f32[256,2048]{1,0:T(8,128)}) fusion(f32[512,2048]{1,0:T(8,128)} %get-tuple-element.20, f32[2048]{0:T(1024)S(1)} %bitcast.48, bf16[1,2048,2048]{2,1,0:T(8,128)(2,1)} %param.9, bf16[1,1,256,2048]{3,2,1,0:T(8,128)(2,1)} %all-gather.5.cloned.1.call-done), kind=kOutput, calls=%fused_computation.19 | convolution fusion | flops 2150102784 | bytes 13648896 | tf_op jit(solution)/shard_map/dot_general | solution.py:82
  49.0 10.5 %psum.22 = f32[256,1]{0,1:T(1,128)S(1)} all-reduce(f32[256,1]{0,1:T(1,128)S(1)} %bitcast.62), channel_id=1, replica_groups=mesh['dp'=4,'pipe'=2,'tensor'=4] {'tensor'}, use_global_device_ids=true, to_apply=%region_3.4 | all-reduce | flops 256 | bytes 2048 | tf_op jit(solution)/shard_map/psum | solution.py:87
  59.5 4.1 %fusion.7 = bf16[256,2048]{1,0:T(8,128)(2,1)} fusion(f32[256,2048]{1,0:T(8,128)} %get-tuple-element.33, f32[512,2048]{1,0:T(8,128)} %get-tuple-element.20, f32[256]{0:T(256)S(1)} %bitcast.58, f32[2048]{0:T(1024)S(1)} %bitcast.49, f32[256]{0:T(256)S(1)} %bitcast.60, bf16[1,1,512,2048]{3,2,1,0:T(8,128)(2,1)} %param.6), kind=kLoop, calls=%fused_computation.17 | loop fusion | flops 3670016 | bytes 6301696 | tf_op jit(solution)/shard_map/convert_element_type | solution.py:91
  63.6 1.3 collective-permute-start
  64.9 5.3 %all-gather.7.cloned.1.call-done = bf16[1,1,256,2048]{3,2,1,0:T(8,128)(2,1)} async-done(((bf16[1,1,256,512]{3,2,1,0:T(8,128)(2,1)}), bf16[1,1,256,2048]{3,2,1,0:T(8,128)(2,1)}) %all-gather.7.cloned.1.call-update) | async-done | bytes 1048592 | tf_op jit(solution)/shard_map/all_gather | solution.py:49
  70.1 1.4 constant_dynamic-slice_fusion.5
  72.4 2.0 %fusion.19 = f32[2048,512]{1,0:T(8,128)S(1)} fusion(bf16[512,2048]{1,0:T(8,128)(2,1)} %get-tuple-element.9, s32[]{:T(128)S(6)} %select_n.59, bf16[256,512]{1,0:T(8,128)(2,1)S(1)} %get-tuple-element.28, bf16[256,512]{1,0:T(8,128)(2,1)S(1)} %get-tuple-element.27), kind=kOutput, calls=%fused_computation.33 | convolution fusion | flops 537395200 | bytes 5767172 | tf_op jit(solution)/shard_map/dot_general | solution.py:60
  76.0 4.1 %add_convert_fusion.1 = bf16[2048,512]{1,0:T(8,128)(2,1)} fusion(f32[2048,512]{1,0:T(8,128)S(1)} %fusion.10, f32[2048,512]{1,0:T(8,128)S(1)} %fusion.19, f32[2048,512]{1,0:T(8,128)S(1)} %fusion.16, bf16[512,2048]{1,0:T(8,128)(2,1)} %get-tuple-element.9, s32[]{:T(128)S(6)} %select_n.59, bf16[256,512]{1,0:T(8,128)(2,1)S(1)} %get-tuple-element.24, ...), kind=kOutput, calls=%fused_computation.9 | convolution fusion | flops 541589504 | bytes 16252932 | tf_op jit(solution)/shard_map/dot_general | solution.py:60
  80.1 1.5 %collective-permute-start.5 = (bf16[2048,512]{1,0:T(8,128)(2,1)}, bf16[2048,512]{1,0:T(8,128)(2,1)}, u32[]{:S(2)}, u32[]{:S(2)}) collective-permute-start(bf16[2048,512]{1,0:T(8,128)(2,1)} %add_convert_fusion.1), channel_id=1, source_target_pairs={{0,16},{8,24},{16,0},{24,8},{1,17},{9,25},{17,1},{25,9},{2,18},{10... | collective-permute-start | bytes 6291464 | tf_op jit(solution)/shard_map/ppermute | solution.py:18
  81.6 4.0 %multiply_reduce_fusion = (f32[2048]{0:T(1024)S(1)}, f32[256]{0:T(256)S(1)}, f32[256,2048]{1,0:T(8,128)}) fusion(f32[512,2048]{1,0:T(8,128)S(1)} %copy-done, f32[2048]{0:T(1024)S(1)} %bitcast.50, bf16[256,2048]{1,0:T(8,128)(2,1)S(1)} %bitcast.45, bf16[1,2048,2048]{2,1,0:T(8,128)(2,1)S(1)} %bitcast.64), kind=kOutput, calls=%fused_computation.18 | convolution fusion | flops 2150102784 | bytes 13648896 | tf_op jit(solution)/shard_map/dot_general | solution.py:82
  85.6 10.3 %psum.23 = f32[256,1]{0,1:T(1,128)S(1)} all-reduce(f32[256,1]{0,1:T(1,128)S(1)} %bitcast.61), channel_id=1, replica_groups=mesh['dp'=4,'pipe'=2,'tensor'=4] {'tensor'}, use_global_device_ids=true, to_apply=%region_5.6 | all-reduce | flops 256 | bytes 2048 | tf_op jit(solution)/shard_map/psum | solution.py:87
  95.9 4.1 %fusion.6 = bf16[256,2048]{1,0:T(8,128)(2,1)} fusion(f32[256,2048]{1,0:T(8,128)} %get-tuple-element.34, f32[512,2048]{1,0:T(8,128)} %get-tuple-element.20, f32[256]{0:T(256)S(1)} %bitcast.57, f32[256]{0:T(256)S(1)} %bitcast.59, bf16[1,1,512,2048]{3,2,1,0:T(8,128)(2,1)} %param.6, f32[2048]{0:T(1024)S(1)} %bitcast.51), kind=kLoop, calls=%fused_computation.15 | loop fusion | flops 3670016 | bytes 6301696 | tf_op jit(solution)/shard_map/convert_element_type | solution.py:91
  100.0 1.5 %collective-permute-start.4 = (bf16[256,2048]{1,0:T(8,128)(2,1)}, bf16[256,2048]{1,0:T(8,128)(2,1)}, u32[]{:S(2)}, u32[]{:S(2)}) collective-permute-start(bf16[256,2048]{1,0:T(8,128)(2,1)} %fusion.6), channel_id=1, source_target_pairs={{4,0},{5,1},{6,2},{7,3},{12,8},{13,9},{14,10},{15,11},{20,16},{21,... | collective-permute-start | bytes 3145736 | tf_op jit(solution)/shard_map/ppermute | solution.py:13
  102.2 2.1 %convolution_add_fusion = f32[2048,512]{1,0:T(8,128)S(1)} fusion(f32[2048,512]{1,0:T(8,128)S(1)} %fusion.14, bf16[512,2048]{1,0:T(8,128)(2,1)} %get-tuple-element.9, s32[]{:T(128)S(6)} %select_n.62, bf16[256,512]{1,0:T(8,128)(2,1)S(1)} %get-tuple-element.28, bf16[256,512]{1,0:T(8,128)(2,1)S(1)} %get-tuple-element.27), kind=kOutput, calls=%fused_computation.11 | convolution fusion | flops 538443776 | bytes 9961476 | tf_op jit(solution)/shard_map/dot_general | solution.py:60
  105.1 1.2 collective-permute-start.7
  106.4 4.0 %add_add_fusion = f32[2048,512]{1,0:T(8,128)} fusion(f32[2048,512]{1,0:T(8,128)S(1)} %convolution_add_fusion, f32[2048,512]{1,0:T(8,128)S(1)} %fusion.8, bf16[512,2048]{1,0:T(8,128)(2,1)} %get-tuple-element.9, s32[]{:T(128)S(6)} %select_n.62, bf16[256,512]{1,0:T(8,128)(2,1)S(1)} %get-tuple-element.24, bf16[256,512]{1,0:T(8,128)(2,1)S(1)} %get-tuple-element.21), kind=kOutput, calls=%fused_computation.8 | convolution fusion | flops 539492352 | bytes 14155780 | tf_op jit(solution)/shard_map/dot_general | solution.py:60
  110.5 17.7 %collective-permute-done.7 = f32[2048]{0:T(1024)S(1)} collective-permute-done((f32[2048]{0:T(1024)S(1)}, f32[2048]{0:T(1024)S(1)}, u32[]{:S(2)}, u32[]{:S(2)}) %collective-permute-start.7) | collective-permute-done | bytes 8224 | tf_op jit(solution)/shard_map/ppermute | solution.py:18
  128.8 3.3 %maximum_bitcast_fusion = bf16[1,1,512,2048]{3,2,1,0:T(8,128)(2,1)} fusion(bf16[256,2048]{1,0:T(8,128)(2,1)} %collective-permute-done.4, bf16[256,2048]{1,0:T(8,128)(2,1)} %collective-permute-done), kind=kLoop, calls=%fused_computation.13 | loop fusion | flops 4194304 | bytes 4194304 | tf_op jit(solution)/shard_map/broadcast_in_dim | solution.py:127
  132.1 3.8 %fusion.5 = bf16[1,2048,512]{2,1,0:T(8,128)(2,1)} fusion(f32[2048,512]{1,0:T(8,128)S(1)} %copy-done.1, bf16[2048,512]{1,0:T(8,128)(2,1)} %collective-permute-done.5), kind=kLoop, calls=%fused_computation.12 | loop fusion | flops 3145728 | bytes 8388608 | tf_op jit(solution)/shard_map/broadcast_in_dim | solution.py:127
  (54 shorter events, 5.6 us)
Async XLA Ops:
  7.2 18.4 %copy-start.2 = (bf16[1,1,512,2048]{3,2,1,0:T(8,128)(2,1)S(1)}, bf16[1,1,512,2048]{3,2,1,0:T(8,128)(2,1)}, u32[]{:S(2)}) copy-start(bf16[1,1,512,2048]{3,2,1,0:T(8,128)(2,1)} %param.5) | copy-start | bytes 6291460
  7.2 33.7 %all-gather.5.cloned.1.call-start = ((), (), s32[]{:S(2)}) async-start(), calls=%async_computation | async-start | bytes 1310720 | tf_op jit(solution)/shard_map/all_gather | solution.py:49
  9.2 60.9 %all-gather.7.cloned.1.call-start = ((), (), s32[]{:S(2)}) async-start(), calls=%async_computation.1 | async-start | bytes 1310720 | tf_op jit(solution)/shard_map/all_gather | solution.py:49
  28.9 41.3 %collective-permute-start.1 = (bf16[512,2048]{1,0:T(8,128)(2,1)}, bf16[512,2048]{1,0:T(8,128)(2,1)S(1)}, u32[]{:S(2)}, u32[]{:S(2)}) collective-permute-start(bf16[512,2048]{1,0:T(8,128)(2,1)} %get-tuple-element.9), channel_id=1, source_target_pairs={{0,8},{8,0},{16,24},{24,16},{1,9},{9,1},{17,25},{25,17},{2,10},{10... | collective-permute-start | bytes 6291464 | tf_op jit(solution)/shard_map/ppermute | solution.py:23
  63.6 65.3 %collective-permute-start = (bf16[256,2048]{1,0:T(8,128)(2,1)}, bf16[256,2048]{1,0:T(8,128)(2,1)}, u32[]{:S(2)}, u32[]{:S(2)}) collective-permute-start(bf16[256,2048]{1,0:T(8,128)(2,1)} %fusion.7), channel_id=1, source_target_pairs={{4,0},{5,1},{6,2},{7,3},{12,8},{13,9},{14,10},{15,11},{20,16},{21,... | collective-permute-start | bytes 3145736 | tf_op jit(solution)/shard_map/ppermute | solution.py:13
  70.1 1.5 %copy-start.3 = (bf16[1,1,256,2048]{3,2,1,0:T(8,128)(2,1)S(1)}, bf16[1,1,256,2048]{3,2,1,0:T(8,128)(2,1)}, u32[]{:S(2)}) copy-start(bf16[1,1,256,2048]{3,2,1,0:T(8,128)(2,1)} %all-gather.7.cloned.1.call-done) | copy-start | bytes 3145732
  71.6 2.8 %collective-permute-start.2 = (bf16[256,1024]{1,0:T(8,128)(2,1)S(1)}, bf16[256,1024]{1,0:T(8,128)(2,1)S(1)}, u32[]{:S(2)}, u32[]{:S(2)}) collective-permute-start(bf16[256,1024]{1,0:T(8,128)(2,1)S(1)} %pad_maximum_fusion), channel_id=1, source_target_pairs={{0,8},{8,0},{16,24},{24,16},{1,9},{9,1},{17,25},{25,17},{2,10},{10... | collective-permute-start | bytes 1572872 | tf_op jit(solution)/shard_map/ppermute | solution.py:23
  71.8 3.4 %collective-permute-start.3 = (bf16[256,1024]{1,0:T(8,128)(2,1)S(1)}, bf16[256,1024]{1,0:T(8,128)(2,1)S(1)}, u32[]{:S(2)}, u32[]{:S(2)}) collective-permute-start(bf16[256,1024]{1,0:T(8,128)(2,1)S(1)} %pad_maximum_fusion.1), channel_id=1, source_target_pairs={{0,8},{8,0},{16,24},{24,16},{1,9},{9,1},{17,25},{25,17},{2,10},{10... | collective-permute-start | bytes 1572872 | tf_op jit(solution)/shard_map/ppermute | solution.py:23
  74.4 0.8 copy-start.4
  75.2 0.8 copy-start.6
  75.2 6.4 %slice-start = ((s8[8388608]{0:T(1024)(128)(4,1)}), s8[4194304]{0:T(1024)(128)(4,1)S(1)}, s32[]{:S(2)}) async-start(s8[8388608]{0:T(1024)(128)(4,1)} %bitcast.63), calls=%async_computation.2 | async-start | bytes 8388608
  76.0 5.6 %copy-start = (f32[512,2048]{1,0:T(8,128)S(1)}, f32[512,2048]{1,0:T(8,128)}, u32[]{:S(2)}) copy-start(f32[512,2048]{1,0:T(8,128)} %get-tuple-element.20) | copy-start | bytes 12582916
  76.0 5.6 %slice-start.1 = ((s8[8388608]{0:T(1024)(128)(4,1)}), s8[4194304]{0:T(1024)(128)(4,1)S(1)}, s32[]{:S(2)}) async-start(s8[8388608]{0:T(1024)(128)(4,1)} %bitcast.63), calls=%async_computation.3 | async-start | bytes 8388608
  80.1 52.0 %collective-permute-start.5 = (bf16[2048,512]{1,0:T(8,128)(2,1)}, bf16[2048,512]{1,0:T(8,128)(2,1)}, u32[]{:S(2)}, u32[]{:S(2)}) collective-permute-start(bf16[2048,512]{1,0:T(8,128)(2,1)} %add_convert_fusion.1), channel_id=1, source_target_pairs={{0,16},{8,24},{16,0},{24,8},{1,17},{9,25},{17,1},{25,9},{2,18},{10... | collective-permute-start | bytes 6291464 | tf_op jit(solution)/shard_map/ppermute | solution.py:18
  85.6 19.5 %collective-permute-start.6 = (f32[2048]{0:T(1024)S(1)}, f32[2048]{0:T(1024)S(1)}, u32[]{:S(2)}, u32[]{:S(2)}) collective-permute-start(f32[2048]{0:T(1024)S(1)} %add.125), channel_id=1, source_target_pairs={{0,8},{8,0},{16,24},{24,16},{1,9},{9,1},{17,25},{25,17},{2,10},{10... | collective-permute-start | bytes 24584 | tf_op jit(solution)/shard_map/ppermute | solution.py:23
  95.9 5.6 %copy-start.5 = (bf16[256,1024]{1,0:T(8,128)(2,1)S(1)}, bf16[256,1024]{1,0:T(8,128)(2,1)}, u32[]{:S(2)}) copy-start(bf16[256,1024]{1,0:T(8,128)(2,1)} %copy-done.4) | copy-start | bytes 1572868
  100.0 28.9 %collective-permute-start.4 = (bf16[256,2048]{1,0:T(8,128)(2,1)}, bf16[256,2048]{1,0:T(8,128)(2,1)}, u32[]{:S(2)}, u32[]{:S(2)}) collective-permute-start(bf16[256,2048]{1,0:T(8,128)(2,1)} %fusion.6), channel_id=1, source_target_pairs={{4,0},{5,1},{6,2},{7,3},{12,8},{13,9},{14,10},{15,11},{20,16},{21,... | collective-permute-start | bytes 3145736 | tf_op jit(solution)/shard_map/ppermute | solution.py:13
  102.2 2.1 %copy-start.7 = (bf16[256,1024]{1,0:T(8,128)(2,1)S(1)}, bf16[256,1024]{1,0:T(8,128)(2,1)}, u32[]{:S(2)}) copy-start(bf16[256,1024]{1,0:T(8,128)(2,1)} %copy-done.6) | copy-start | bytes 1572868
  105.1 23.0 %collective-permute-start.7 = (f32[2048]{0:T(1024)S(1)}, f32[2048]{0:T(1024)S(1)}, u32[]{:S(2)}, u32[]{:S(2)}) collective-permute-start(f32[2048]{0:T(1024)S(1)} %add.126), channel_id=1, source_target_pairs={{0,16},{8,24},{16,0},{24,8},{1,17},{9,25},{17,1},{25,9},{2,18},{10... | collective-permute-start | bytes 24584 | tf_op jit(solution)/shard_map/ppermute | solution.py:18
  128.8 3.3 %copy-start.1 = (f32[2048,512]{1,0:T(8,128)S(1)}, f32[2048,512]{1,0:T(8,128)}, u32[]{:S(2)}) copy-start(f32[2048,512]{1,0:T(8,128)} %add_add_fusion) | copy-start | bytes 12582916
Sparse Core Ops, SparseCore 0:
  10.2 30.6 all-gather.4
  42.4 27.6 all-gather.6

commit v19 on v18

--- a/solution.py
+++ b/solution.py
@@ -117,6 +117,7 @@
 
     upstream = jnp.concatenate(inputs_grad, axis=0)
     pair_gain = gain_part + to_partner(gain_part)
+    upstream, pair_gain = lax.optimization_barrier((upstream, pair_gain))
     own_g = me // 2
     stacked = jnp.zeros((groups, d_local), jnp.float32)
     stacked = lax.dynamic_update_slice_in_dim(stacked, pair_gain[None], own_g, axis=0)

time: 143 us -> 145 us (1.014)
  waiting for transfers between devices: 34.9 us -> 37.4 us
    ppermute x2, waiting for transfers between devices: 0.01 us -> 20.3 us  [from_behind(): return lax.ppermute(block, axis, route)]
    ppermute x2, waiting for transfers between devices: 17.7 us -> 0.01 us  [shifted(): return lax.ppermute(block, axis, [(i, (i + shift) % n) for i in range(n)])]
    concatenate x0 -> x1, other arithmetic: none -> 2.79 us  [on_device(): upstream = jnp.concatenate(inputs_grad, axis=0)]
    broadcast_in_dim x2 -> x1, other arithmetic: 7.07 us -> 4.9 us  [on_device(): return (upstream[None, None], weight_total[None], gain_total[None])]
  transfers between devices with their start and end apart: 10 -> 10, of which waited for: 3 -> 3; matrix products, arithmetic and copies ran while one was open for 33% -> 32% of each run, Pallas kernels for 0% -> 0%
where the time goes in v19:
time: 145 us
  waiting for transfers between devices  37.4 us (26%)
  blocking collectives  34.3 us (24%)
  matrix products  27.3 us (19%)
  other arithmetic  21.8 us (15%)
  between operations  14.3 us (10%)
  starting transfers between devices  6.08 us (4%)
  local copies, waits for them, and re-layouts  3.78 us (3%)
    psum x2, blocking collectives, on_device(): lax.psum(jnp.sum(scaled * normed_c, axis=1, keepdims=True), 'tensor')  20.7 us
    ppermute x2, waiting for transfers between devices, from_behind(): return lax.ppermute(block, axis, route)  20.3 us
    all_gather x2, waiting for transfers between devices, on_device(): lax.all_gather(grad_kv[c * step:(c + 1) * step], 'tensor', axis=1, tiled=...  17.1 us
    dot_general x8, matrix products, tn(): lax.dot_general(a, b, (((0,), (0,)), ((), ())), preferred_element_type=jn...  15.2 us
    psum x1, blocking collectives, on_device(): lax.psum(jnp.sum(values * values, axis=1, keepdims=True), 'tensor')  13.5 us
    dot_general x2, matrix products, on_device(): lax.dot_general(block, weight, (((1,), (1,)), ((), ())), preferred_elemen...  12.1 us
    convert_element_type x2, other arithmetic, on_device(): input_grad = (grad_out[lo:lo + step].astype(jnp.float32) + rstd[lo:lo + s...  7.27 us
    broadcast_in_dim x1, other arithmetic, on_device(): return (upstream[None, None], weight_total[None], gain_total[None])  4.9 us
  transfers between devices with their start and end apart: 10, of which 3 were waited for; matrix products, arithmetic and copies ran while one was open for 32% of the time, Pallas kernels for 0%

profile of v19, /device:TPU:0, one launch (start us, length us, event | category | flops | bytes accessed | tf_op | source)
XLA Modules:
  0.0 145.0 jit_solution(13685697116517623029)
XLA Ops:
  7.2 2.0 %fusion.46 = (bf16[1,1,256,512]{3,2,1,0:T(8,128)(2,1)}, bf16[1,1,256,512]{3,2,1,0:T(8,128)(2,1)}) fusion(bf16[1,1,512,512]{3,2,1,0:T(8,128)(2,1)} %param.7), kind=kLoop, calls=%fused_computation.77 | loop fusion | bytes 1048576 | tf_op jit(solution)/shard_map/slice | solution.py:49
  10.0 2.1 %fusion.4 = f32[512]{0:T(512)S(1)} fusion(bf16[1,1,512,2048]{3,2,1,0:T(8,128)(2,1)} %param.5), kind=kLoop, calls=%fused_computation.6 | loop fusion | flops 3145216 | bytes 2099200 | tf_op jit(solution)/shard_map/reduce_sum | solution.py:41
  12.1 13.5 %psum.21 = f32[512,1]{0,1:T(1,128)S(1)} all-reduce(f32[512,1]{0,1:T(1,128)S(1)} %bitcast.54), channel_id=1, replica_groups=mesh['dp'=4,'pipe'=2,'tensor'=4] {'tensor'}, use_global_device_ids=true, to_apply=%region_1.2 | all-reduce | flops 512 | bytes 4096 | tf_op jit(solution)/shard_map/psum | solution.py:41
  25.6 3.3 %multiply_convert_fusion = (bf16[512,2048]{1,0:T(8,128)(2,1)}, f32[512,2048]{1,0:T(8,128)}) fusion(f32[2048]{0:T(1024)S(1)} %bitcast.47, f32[512]{0:T(512)S(1)} %bitcast.53, bf16[1,1,512,2048]{3,2,1,0:T(8,128)(2,1)S(1)} %copy-done.1), kind=kLoop, calls=%fused_computation.10 | loop fusion | flops 4194304 | bytes 8398848 | tf_op jit(solution)/shard_map/convert_element_type | solution.py:44
  29.0 11.9 %all-gather.5.cloned.1.call-done = bf16[1,1,256,2048]{3,2,1,0:T(8,128)(2,1)} async-done(((bf16[1,1,256,512]{3,2,1,0:T(8,128)(2,1)}), bf16[1,1,256,2048]{3,2,1,0:T(8,128)(2,1)}) %all-gather.5.cloned.1.call-update) | async-done | bytes 1048592 | tf_op jit(solution)/shard_map/all_gather | solution.py:49
  40.9 8.2 %multiply_reduce_fusion.1 = (f32[2048]{0:T(1024)S(1)}, f32[256]{0:T(256)S(1)}, f32[256,2048]{1,0:T(8,128)}) fusion(f32[512,2048]{1,0:T(8,128)} %get-tuple-element.24, f32[2048]{0:T(1024)S(1)} %bitcast.48, bf16[1,2048,2048]{2,1,0:T(8,128)(2,1)} %param.9, bf16[1,1,256,2048]{3,2,1,0:T(8,128)(2,1)} %all-gather.5.cloned.1.call-done), kind=kOutput, calls=%fused_computation.19 | convolution fusion | flops 2150102784 | bytes 13648896 | tf_op jit(solution)/shard_map/dot_general | solution.py:82
  49.0 10.5 %psum.22 = f32[256,1]{0,1:T(1,128)S(1)} all-reduce(f32[256,1]{0,1:T(1,128)S(1)} %bitcast.62), channel_id=1, replica_groups=mesh['dp'=4,'pipe'=2,'tensor'=4] {'tensor'}, use_global_device_ids=true, to_apply=%region_3.4 | all-reduce | flops 256 | bytes 2048 | tf_op jit(solution)/shard_map/psum | solution.py:87
  59.5 4.1 %fusion.7 = bf16[256,2048]{1,0:T(8,128)(2,1)} fusion(f32[256,2048]{1,0:T(8,128)} %get-tuple-element.37, f32[512,2048]{1,0:T(8,128)} %get-tuple-element.24, f32[256]{0:T(256)S(1)} %bitcast.58, f32[2048]{0:T(1024)S(1)} %bitcast.49, f32[256]{0:T(256)S(1)} %bitcast.60, bf16[1,1,512,2048]{3,2,1,0:T(8,128)(2,1)} %param.6), kind=kLoop, calls=%fused_computation.17 | loop fusion | flops 3670016 | bytes 6301696 | tf_op jit(solution)/shard_map/convert_element_type | solution.py:91
  63.6 1.3 collective-permute-start
  64.9 5.2 %all-gather.7.cloned.1.call-done = bf16[1,1,256,2048]{3,2,1,0:T(8,128)(2,1)} async-done(((bf16[1,1,256,512]{3,2,1,0:T(8,128)(2,1)}), bf16[1,1,256,2048]{3,2,1,0:T(8,128)(2,1)}) %all-gather.7.cloned.1.call-update) | async-done | bytes 1048592 | tf_op jit(solution)/shard_map/all_gather | solution.py:49
  70.1 1.4 constant_dynamic-slice_fusion.5
  72.4 2.0 %fusion.19 = f32[2048,512]{1,0:T(8,128)S(1)} fusion(bf16[512,2048]{1,0:T(8,128)(2,1)} %get-tuple-element.11, s32[]{:T(128)S(6)} %select_n.59, bf16[256,512]{1,0:T(8,128)(2,1)S(1)} %get-tuple-element.32, bf16[256,512]{1,0:T(8,128)(2,1)S(1)} %get-tuple-element.31), kind=kOutput, calls=%fused_computation.33 | convolution fusion | flops 537395200 | bytes 5767172 | tf_op jit(solution)/shard_map/dot_general | solution.py:60
  76.0 4.1 %add_convert_fusion.1 = bf16[2048,512]{1,0:T(8,128)(2,1)} fusion(f32[2048,512]{1,0:T(8,128)S(1)} %fusion.10, f32[2048,512]{1,0:T(8,128)S(1)} %fusion.19, f32[2048,512]{1,0:T(8,128)S(1)} %fusion.16, bf16[512,2048]{1,0:T(8,128)(2,1)} %get-tuple-element.11, s32[]{:T(128)S(6)} %select_n.59, bf16[256,512]{1,0:T(8,128)(2,1)S(1)} %get-tuple-element.28, ...), kind=kOutput, calls=%fused_computation.9 | convolution fusion | flops 541589504 | bytes 16252932 | tf_op jit(solution)/shard_map/dot_general | solution.py:60
  80.1 1.5 %collective-permute-start.6 = (bf16[2048,512]{1,0:T(8,128)(2,1)}, bf16[2048,512]{1,0:T(8,128)(2,1)}, u32[]{:S(2)}, u32[]{:S(2)}) collective-permute-start(bf16[2048,512]{1,0:T(8,128)(2,1)} %add_convert_fusion.1), channel_id=1, source_target_pairs={{0,16},{8,24},{16,0},{24,8},{1,17},{9,25},{17,1},{25,9},{2,18},{10... | collective-permute-start | bytes 6291464 | tf_op jit(solution)/shard_map/ppermute | solution.py:18
  81.6 4.0 %multiply_reduce_fusion = (f32[2048]{0:T(1024)S(1)}, f32[256]{0:T(256)S(1)}, f32[256,2048]{1,0:T(8,128)}) fusion(f32[512,2048]{1,0:T(8,128)S(1)} %copy-done, f32[2048]{0:T(1024)S(1)} %bitcast.50, bf16[256,2048]{1,0:T(8,128)(2,1)S(1)} %bitcast.45, bf16[1,2048,2048]{2,1,0:T(8,128)(2,1)S(1)} %bitcast.64), kind=kOutput, calls=%fused_computation.18 | convolution fusion | flops 2150102784 | bytes 13648896 | tf_op jit(solution)/shard_map/dot_general | solution.py:82
  85.5 10.3 %psum.23 = f32[256,1]{0,1:T(1,128)S(1)} all-reduce(f32[256,1]{0,1:T(1,128)S(1)} %bitcast.61), channel_id=1, replica_groups=mesh['dp'=4,'pipe'=2,'tensor'=4] {'tensor'}, use_global_device_ids=true, to_apply=%region_5.6 | all-reduce | flops 256 | bytes 2048 | tf_op jit(solution)/shard_map/psum | solution.py:87
  95.8 3.1 %fusion.6 = bf16[256,2048]{1,0:T(8,128)(2,1)S(1)} fusion(f32[256,2048]{1,0:T(8,128)} %get-tuple-element.38, f32[512,2048]{1,0:T(8,128)} %get-tuple-element.24, f32[256]{0:T(256)S(1)} %bitcast.57, f32[256]{0:T(256)S(1)} %bitcast.59, bf16[1,1,512,2048]{3,2,1,0:T(8,128)(2,1)} %param.6, f32[2048]{0:T(1024)S(1)} %bitcast.51), kind=kLoop, calls=%fused_computation.15 | loop fusion | flops 3670016 | bytes 6301696 | tf_op jit(solution)/shard_map/convert_element_type | solution.py:91
  99.0 1.5 %collective-permute-start.4 = (bf16[256,2048]{1,0:T(8,128)(2,1)S(1)}, bf16[256,2048]{1,0:T(8,128)(2,1)S(1)}, u32[]{:S(2)}, u32[]{:S(2)}) collective-permute-start(bf16[256,2048]{1,0:T(8,128)(2,1)S(1)} %fusion.6), channel_id=1, source_target_pairs={{4,0},{5,1},{6,2},{7,3},{12,8},{13,9},{14,10},{15,11},{20,16},{21,... | collective-permute-start | bytes 3145736 | tf_op jit(solution)/shard_map/ppermute | solution.py:13
  101.2 2.1 %convolution_add_fusion = f32[2048,512]{1,0:T(8,128)S(1)} fusion(f32[2048,512]{1,0:T(8,128)S(1)} %fusion.14, bf16[512,2048]{1,0:T(8,128)(2,1)} %get-tuple-element.11, s32[]{:T(128)S(6)} %select_n.62, bf16[256,512]{1,0:T(8,128)(2,1)S(1)} %get-tuple-element.32, bf16[256,512]{1,0:T(8,128)(2,1)S(1)} %get-tuple-element.31), kind=kOutput, calls=%fused_computation.11 | convolution fusion | flops 538443776 | bytes 9961476 | tf_op jit(solution)/shard_map/dot_general | solution.py:60
  104.1 20.3 %collective-permute-done.4 = bf16[256,2048]{1,0:T(8,128)(2,1)S(1)} collective-permute-done((bf16[256,2048]{1,0:T(8,128)(2,1)S(1)}, bf16[256,2048]{1,0:T(8,128)(2,1)S(1)}, u32[]{:S(2)}, u32[]{:S(2)}) %collective-permute-start.4) | collective-permute-done | bytes 1048608 | tf_op jit(solution)/shard_map/ppermute | solution.py:13
  124.4 2.8 %pad_maximum_fusion = bf16[512,2048]{1,0:T(8,128)(2,1)} fusion(bf16[256,2048]{1,0:T(8,128)(2,1)S(1)} %collective-permute-done.4, bf16[256,2048]{1,0:T(8,128)(2,1)} %collective-permute-done), kind=kLoop, calls=%fused_computation.13 | loop fusion | flops 4194304 | bytes 4194304 | tf_op jit(solution)/shard_map/concatenate | solution.py:118
  127.2 1.2 collective-permute-start.7
  128.4 4.0 %add_add_fusion = f32[2048,512]{1,0:T(8,128)} fusion(f32[2048,512]{1,0:T(8,128)S(1)} %convolution_add_fusion, f32[2048,512]{1,0:T(8,128)S(1)} %fusion.8, bf16[512,2048]{1,0:T(8,128)(2,1)} %get-tuple-element.11, s32[]{:T(128)S(6)} %select_n.62, bf16[256,512]{1,0:T(8,128)(2,1)S(1)} %get-tuple-element.28, bf16[256,512]{1,0:T(8,128)(2,1)S(1)} %get-tuple-element.25), kind=kOutput, calls=%fused_computation.8 | convolution fusion | flops 539492352 | bytes 14155780 | tf_op jit(solution)/shard_map/dot_general | solution.py:60
  133.2 4.9 %fusion.5 = bf16[1,2048,512]{2,1,0:T(8,128)(2,1)} fusion(f32[2048,512]{1,0:T(8,128)} %add_add_fusion, bf16[2048,512]{1,0:T(8,128)(2,1)} %collective-permute-done.6), kind=kLoop, calls=%fused_computation.12 | loop fusion | flops 3145728 | bytes 8388608 | tf_op jit(solution)/shard_map/broadcast_in_dim | solution.py:128
  (52 shorter events, 5.6 us)
Async XLA Ops:
  7.2 18.4 %copy-start.1 = (bf16[1,1,512,2048]{3,2,1,0:T(8,128)(2,1)S(1)}, bf16[1,1,512,2048]{3,2,1,0:T(8,128)(2,1)}, u32[]{:S(2)}) copy-start(bf16[1,1,512,2048]{3,2,1,0:T(8,128)(2,1)} %param.5) | copy-start | bytes 6291460
  7.2 33.7 %all-gather.5.cloned.1.call-start = ((), (), s32[]{:S(2)}) async-start(), calls=%async_computation | async-start | bytes 1310720 | tf_op jit(solution)/shard_map/all_gather | solution.py:49
  9.2 60.9 %all-gather.7.cloned.1.call-start = ((), (), s32[]{:S(2)}) async-start(), calls=%async_computation.1 | async-start | bytes 1310720 | tf_op jit(solution)/shard_map/all_gather | solution.py:49
  28.9 41.3 %collective-permute-start.1 = (bf16[512,2048]{1,0:T(8,128)(2,1)}, bf16[512,2048]{1,0:T(8,128)(2,1)S(1)}, u32[]{:S(2)}, u32[]{:S(2)}) collective-permute-start(bf16[512,2048]{1,0:T(8,128)(2,1)} %get-tuple-element.11), channel_id=1, source_target_pairs={{0,8},{8,0},{16,24},{24,16},{1,9},{9,1},{17,25},{25,17},{2,10},{10... | collective-permute-start | bytes 6291464 | tf_op jit(solution)/shard_map/ppermute | solution.py:23
  63.6 40.5 %collective-permute-start = (bf16[256,2048]{1,0:T(8,128)(2,1)}, bf16[256,2048]{1,0:T(8,128)(2,1)}, u32[]{:S(2)}, u32[]{:S(2)}) collective-permute-start(bf16[256,2048]{1,0:T(8,128)(2,1)} %fusion.7), channel_id=1, source_target_pairs={{4,0},{5,1},{6,2},{7,3},{12,8},{13,9},{14,10},{15,11},{20,16},{21,... | collective-permute-start | bytes 3145736 | tf_op jit(solution)/shard_map/ppermute | solution.py:13
  70.1 1.5 %copy-start.2 = (bf16[1,1,256,2048]{3,2,1,0:T(8,128)(2,1)S(1)}, bf16[1,1,256,2048]{3,2,1,0:T(8,128)(2,1)}, u32[]{:S(2)}) copy-start(bf16[1,1,256,2048]{3,2,1,0:T(8,128)(2,1)} %all-gather.7.cloned.1.call-done) | copy-start | bytes 3145732
  71.6 2.8 %collective-permute-start.2 = (bf16[256,1024]{1,0:T(8,128)(2,1)S(1)}, bf16[256,1024]{1,0:T(8,128)(2,1)S(1)}, u32[]{:S(2)}, u32[]{:S(2)}) collective-permute-start(bf16[256,1024]{1,0:T(8,128)(2,1)S(1)} %pad_maximum_fusion.1), channel_id=1, source_target_pairs={{0,8},{8,0},{16,24},{24,16},{1,9},{9,1},{17,25},{25,17},{2,10},{10... | collective-permute-start | bytes 1572872 | tf_op jit(solution)/shard_map/ppermute | solution.py:23
  71.8 3.4 %collective-permute-start.3 = (bf16[256,1024]{1,0:T(8,128)(2,1)S(1)}, bf16[256,1024]{1,0:T(8,128)(2,1)S(1)}, u32[]{:S(2)}, u32[]{:S(2)}) collective-permute-start(bf16[256,1024]{1,0:T(8,128)(2,1)S(1)} %pad_maximum_fusion.2), channel_id=1, source_target_pairs={{0,8},{8,0},{16,24},{24,16},{1,9},{9,1},{17,25},{25,17},{2,10},{10... | collective-permute-start | bytes 1572872 | tf_op jit(solution)/shard_map/ppermute | solution.py:23
  74.4 0.8 copy-start.3
  75.2 0.8 copy-start.5
  75.2 6.3 %slice-start = ((s8[8388608]{0:T(1024)(128)(4,1)}), s8[4194304]{0:T(1024)(128)(4,1)S(1)}, s32[]{:S(2)}) async-start(s8[8388608]{0:T(1024)(128)(4,1)} %bitcast.63), calls=%async_computation.2 | async-start | bytes 8388608
  76.0 5.5 %copy-start = (f32[512,2048]{1,0:T(8,128)S(1)}, f32[512,2048]{1,0:T(8,128)}, u32[]{:S(2)}) copy-start(f32[512,2048]{1,0:T(8,128)} %get-tuple-element.24) | copy-start | bytes 12582916
  76.0 5.5 %slice-start.1 = ((s8[8388608]{0:T(1024)(128)(4,1)}), s8[4194304]{0:T(1024)(128)(4,1)S(1)}, s32[]{:S(2)}) async-start(s8[8388608]{0:T(1024)(128)(4,1)} %bitcast.63), calls=%async_computation.3 | async-start | bytes 8388608
  80.1 53.1 %collective-permute-start.6 = (bf16[2048,512]{1,0:T(8,128)(2,1)}, bf16[2048,512]{1,0:T(8,128)(2,1)}, u32[]{:S(2)}, u32[]{:S(2)}) collective-permute-start(bf16[2048,512]{1,0:T(8,128)(2,1)} %add_convert_fusion.1), channel_id=1, source_target_pairs={{0,16},{8,24},{16,0},{24,8},{1,17},{9,25},{17,1},{25,9},{2,18},{10... | collective-permute-start | bytes 6291464 | tf_op jit(solution)/shard_map/ppermute | solution.py:18
  85.5 18.6 %collective-permute-start.5 = (f32[2048]{0:T(1024)S(1)}, f32[2048]{0:T(1024)S(1)}, u32[]{:S(2)}, u32[]{:S(2)}) collective-permute-start(f32[2048]{0:T(1024)S(1)} %add.120), channel_id=1, source_target_pairs={{0,8},{8,0},{16,24},{24,16},{1,9},{9,1},{17,25},{25,17},{2,10},{10... | collective-permute-start | bytes 24584 | tf_op jit(solution)/shard_map/ppermute | solution.py:23
  95.8 4.6 %copy-start.4 = (bf16[256,1024]{1,0:T(8,128)(2,1)S(1)}, bf16[256,1024]{1,0:T(8,128)(2,1)}, u32[]{:S(2)}) copy-start(bf16[256,1024]{1,0:T(8,128)(2,1)} %copy-done.3) | copy-start | bytes 1572868
  99.0 25.4 %collective-permute-start.4 = (bf16[256,2048]{1,0:T(8,128)(2,1)S(1)}, bf16[256,2048]{1,0:T(8,128)(2,1)S(1)}, u32[]{:S(2)}, u32[]{:S(2)}) collective-permute-start(bf16[256,2048]{1,0:T(8,128)(2,1)S(1)} %fusion.6), channel_id=1, source_target_pairs={{4,0},{5,1},{6,2},{7,3},{12,8},{13,9},{14,10},{15,11},{20,16},{21,... | collective-permute-start | bytes 3145736 | tf_op jit(solution)/shard_map/ppermute | solution.py:13
  101.2 2.1 %copy-start.6 = (bf16[256,1024]{1,0:T(8,128)(2,1)S(1)}, bf16[256,1024]{1,0:T(8,128)(2,1)}, u32[]{:S(2)}) copy-start(bf16[256,1024]{1,0:T(8,128)(2,1)} %copy-done.5) | copy-start | bytes 1572868
  127.2 5.3 %collective-permute-start.7 = (f32[2048]{0:T(1024)S(1)}, f32[2048]{0:T(1024)S(1)}, u32[]{:S(2)}, u32[]{:S(2)}) collective-permute-start(f32[2048]{0:T(1024)S(1)} %add.121), channel_id=1, source_target_pairs={{0,16},{8,24},{16,0},{24,8},{1,17},{9,25},{17,1},{25,9},{2,18},{10... | collective-permute-start | bytes 24584 | tf_op jit(solution)/shard_map/ppermute | solution.py:18
Sparse Core Ops, SparseCore 0:
  10.2 30.6 all-gather.4
  42.4 27.6 all-gather.6

commit v20 on v19

--- a/solution.py
+++ b/solution.py
@@ -108,13 +108,11 @@
             total = first
             for k in range(1, CHUNKS):
                 total = total + chunk_blocks[k](own_g)
-            total = lax.optimization_barrier(total)
-            for got in received:
-                total = total + got.astype(jnp.float32)
-            weight_total = total.astype(jnp.bfloat16)
+            own_total = total
         if c + 1 < CHUNKS:
             _, block = lax.optimization_barrier(((input_grad, outs), parts[c + 1]))
 
+    inputs_grad, own_total = lax.optimization_barrier((inputs_grad, own_total))
     upstream = jnp.concatenate(inputs_grad, axis=0)
     pair_gain = gain_part + to_partner(gain_part)
     upstream, pair_gain = lax.optimization_barrier((upstream, pair_gain))
@@ -125,6 +123,10 @@
         got = shifted(pair_gain, "dp", 2 * d)
         stacked = lax.dynamic_update_slice_in_dim(stacked, got[None], (own_g - d) % groups, axis=0)
     gain_total = jnp.sum(stacked, axis=0)
+    total = own_total
+    for got in received:
+        total = total + got.astype(jnp.float32)
+    weight_total = total.astype(jnp.bfloat16)
     return (upstream[None, None], weight_total[None], gain_total[None])
 
 

time: 145 us -> 144 us (level)
  waiting for transfers between devices: 37.4 us -> 35.8 us
    ppermute x2, waiting for transfers between devices: 20.3 us -> 16.3 us  [from_behind(): return lax.ppermute(block, axis, route)]
    ppermute x2, waiting for transfers between devices: 0.01 us -> 2.39 us  [shifted(): return lax.ppermute(block, axis, [(i, (i + shift) % n) for i in range(n)])]
  transfers between devices with their start and end apart: 10 -> 10, of which waited for: 3 -> 4; matrix products, arithmetic and copies ran while one was open for 32% -> 32% of each run, Pallas kernels for 0% -> 0%
where the time goes in v20:
time: 144 us; the launch traced here: 143 us
  waiting for transfers between devices  35.8 us (25%)
  blocking collectives  34.3 us (24%)
  matrix products  27.3 us (19%)
  other arithmetic  21.8 us (15%)
  between operations  14.3 us (10%)
  starting transfers between devices  6.08 us (4%)
  local copies, waits for them, and re-layouts  3.76 us (3%)
    psum x2, blocking collectives, on_device(): lax.psum(jnp.sum(scaled * normed_c, axis=1, keepdims=True), 'tensor')  20.7 us
    all_gather x2, waiting for transfers between devices, on_device(): lax.all_gather(grad_kv[c * step:(c + 1) * step], 'tensor', axis=1, tiled=...  17.1 us
    ppermute x2, waiting for transfers between devices, from_behind(): return lax.ppermute(block, axis, route)  16.3 us
    dot_general x8, matrix products, tn(): lax.dot_general(a, b, (((0,), (0,)), ((), ())), preferred_element_type=jn...  15.2 us
    psum x1, blocking collectives, on_device(): lax.psum(jnp.sum(values * values, axis=1, keepdims=True), 'tensor')  13.5 us
    dot_general x2, matrix products, on_device(): lax.dot_general(block, weight, (((1,), (1,)), ((), ())), preferred_elemen...  12.1 us
    convert_element_type x2, other arithmetic, on_device(): input_grad = (grad_out[lo:lo + step].astype(jnp.float32) + rstd[lo:lo + s...  7.27 us
    broadcast_in_dim x1, other arithmetic, on_device(): return (upstream[None, None], weight_total[None], gain_total[None])  4.9 us
  transfers between devices with their start and end apart: 10, of which 4 were waited for; matrix products, arithmetic and copies ran while one was open for 32% of the time, Pallas kernels for 0%

profile of v20, /device:TPU:0, one launch (start us, length us, event | category | flops | bytes accessed | tf_op | source)
XLA Modules:
  0.0 143.3 jit_solution(5085904698234469464)
XLA Ops:
  7.2 2.0 %fusion.46 = (bf16[1,1,256,512]{3,2,1,0:T(8,128)(2,1)}, bf16[1,1,256,512]{3,2,1,0:T(8,128)(2,1)}) fusion(bf16[1,1,512,512]{3,2,1,0:T(8,128)(2,1)} %param.7), kind=kLoop, calls=%fused_computation.77 | loop fusion | bytes 1048576 | tf_op jit(solution)/shard_map/slice | solution.py:49
  10.0 2.1 %fusion.4 = f32[512]{0:T(512)S(1)} fusion(bf16[1,1,512,2048]{3,2,1,0:T(8,128)(2,1)} %param.5), kind=kLoop, calls=%fused_computation.6 | loop fusion | flops 3145216 | bytes 2099200 | tf_op jit(solution)/shard_map/reduce_sum | solution.py:41
  12.1 13.5 %psum.21 = f32[512,1]{0,1:T(1,128)S(1)} all-reduce(f32[512,1]{0,1:T(1,128)S(1)} %bitcast.54), channel_id=1, replica_groups=mesh['dp'=4,'pipe'=2,'tensor'=4] {'tensor'}, use_global_device_ids=true, to_apply=%region_1.2 | all-reduce | flops 512 | bytes 4096 | tf_op jit(solution)/shard_map/psum | solution.py:41
  25.6 3.3 %multiply_convert_fusion = (bf16[512,2048]{1,0:T(8,128)(2,1)}, f32[512,2048]{1,0:T(8,128)}) fusion(f32[2048]{0:T(1024)S(1)} %bitcast.47, f32[512]{0:T(512)S(1)} %bitcast.53, bf16[1,1,512,2048]{3,2,1,0:T(8,128)(2,1)S(1)} %copy-done.1), kind=kLoop, calls=%fused_computation.10 | loop fusion | flops 4194304 | bytes 8398848 | tf_op jit(solution)/shard_map/convert_element_type | solution.py:44
  29.0 11.9 %all-gather.5.cloned.1.call-done = bf16[1,1,256,2048]{3,2,1,0:T(8,128)(2,1)} async-done(((bf16[1,1,256,512]{3,2,1,0:T(8,128)(2,1)}), bf16[1,1,256,2048]{3,2,1,0:T(8,128)(2,1)}) %all-gather.5.cloned.1.call-update) | async-done | bytes 1048592 | tf_op jit(solution)/shard_map/all_gather | solution.py:49
  40.9 8.2 %multiply_reduce_fusion.1 = (f32[2048]{0:T(1024)S(1)}, f32[256]{0:T(256)S(1)}, f32[256,2048]{1,0:T(8,128)}) fusion(f32[512,2048]{1,0:T(8,128)} %get-tuple-element.30, f32[2048]{0:T(1024)S(1)} %bitcast.48, bf16[1,2048,2048]{2,1,0:T(8,128)(2,1)} %param.9, bf16[1,1,256,2048]{3,2,1,0:T(8,128)(2,1)} %all-gather.5.cloned.1.call-done), kind=kOutput, calls=%fused_computation.19 | convolution fusion | flops 2150102784 | bytes 13648896 | tf_op jit(solution)/shard_map/dot_general | solution.py:82
  49.0 10.5 %psum.22 = f32[256,1]{0,1:T(1,128)S(1)} all-reduce(f32[256,1]{0,1:T(1,128)S(1)} %bitcast.62), channel_id=1, replica_groups=mesh['dp'=4,'pipe'=2,'tensor'=4] {'tensor'}, use_global_device_ids=true, to_apply=%region_3.4 | all-reduce | flops 256 | bytes 2048 | tf_op jit(solution)/shard_map/psum | solution.py:87
  59.5 4.1 %fusion.7 = bf16[256,2048]{1,0:T(8,128)(2,1)} fusion(f32[256,2048]{1,0:T(8,128)} %get-tuple-element.43, f32[512,2048]{1,0:T(8,128)} %get-tuple-element.30, f32[256]{0:T(256)S(1)} %bitcast.58, f32[2048]{0:T(1024)S(1)} %bitcast.49, f32[256]{0:T(256)S(1)} %bitcast.60, bf16[1,1,512,2048]{3,2,1,0:T(8,128)(2,1)} %param.6), kind=kLoop, calls=%fused_computation.17 | loop fusion | flops 3670016 | bytes 6301696 | tf_op jit(solution)/shard_map/convert_element_type | solution.py:91
  63.6 1.3 collective-permute-start
  64.9 5.2 %all-gather.7.cloned.1.call-done = bf16[1,1,256,2048]{3,2,1,0:T(8,128)(2,1)} async-done(((bf16[1,1,256,512]{3,2,1,0:T(8,128)(2,1)}), bf16[1,1,256,2048]{3,2,1,0:T(8,128)(2,1)}) %all-gather.7.cloned.1.call-update) | async-done | bytes 1048592 | tf_op jit(solution)/shard_map/all_gather | solution.py:49
  70.1 1.4 constant_dynamic-slice_fusion.5
  72.4 2.0 %fusion.19 = f32[2048,512]{1,0:T(8,128)S(1)} fusion(bf16[512,2048]{1,0:T(8,128)(2,1)} %get-tuple-element.14, s32[]{:T(128)S(6)} %select_n.59, bf16[256,512]{1,0:T(8,128)(2,1)S(1)} %get-tuple-element.38, bf16[256,512]{1,0:T(8,128)(2,1)S(1)} %get-tuple-element.37), kind=kOutput, calls=%fused_computation.33 | convolution fusion | flops 537395200 | bytes 5767172 | tf_op jit(solution)/shard_map/dot_general | solution.py:60
  76.0 4.1 %add_convert_fusion.1 = bf16[2048,512]{1,0:T(8,128)(2,1)} fusion(f32[2048,512]{1,0:T(8,128)S(1)} %fusion.10, f32[2048,512]{1,0:T(8,128)S(1)} %fusion.19, f32[2048,512]{1,0:T(8,128)S(1)} %fusion.16, bf16[512,2048]{1,0:T(8,128)(2,1)} %get-tuple-element.14, s32[]{:T(128)S(6)} %select_n.59, bf16[256,512]{1,0:T(8,128)(2,1)S(1)} %get-tuple-element.34, ...), kind=kOutput, calls=%fused_computation.9 | convolution fusion | flops 541589504 | bytes 16252932 | tf_op jit(solution)/shard_map/dot_general | solution.py:60
  80.1 1.5 %collective-permute-start.6 = (bf16[2048,512]{1,0:T(8,128)(2,1)}, bf16[2048,512]{1,0:T(8,128)(2,1)}, u32[]{:S(2)}, u32[]{:S(2)}) collective-permute-start(bf16[2048,512]{1,0:T(8,128)(2,1)} %add_convert_fusion.1), channel_id=1, source_target_pairs={{0,16},{8,24},{16,0},{24,8},{1,17},{9,25},{17,1},{25,9},{2,18},{10... | collective-permute-start | bytes 6291464 | tf_op jit(solution)/shard_map/ppermute | solution.py:18
  81.6 4.0 %multiply_reduce_fusion = (f32[2048]{0:T(1024)S(1)}, f32[256]{0:T(256)S(1)}, f32[256,2048]{1,0:T(8,128)}) fusion(f32[512,2048]{1,0:T(8,128)S(1)} %copy-done, f32[2048]{0:T(1024)S(1)} %bitcast.50, bf16[256,2048]{1,0:T(8,128)(2,1)S(1)} %bitcast.45, bf16[1,2048,2048]{2,1,0:T(8,128)(2,1)S(1)} %bitcast.64), kind=kOutput, calls=%fused_computation.18 | convolution fusion | flops 2150102784 | bytes 13648896 | tf_op jit(solution)/shard_map/dot_general | solution.py:82
  85.5 10.3 %psum.23 = f32[256,1]{0,1:T(1,128)S(1)} all-reduce(f32[256,1]{0,1:T(1,128)S(1)} %bitcast.61), channel_id=1, replica_groups=mesh['dp'=4,'pipe'=2,'tensor'=4] {'tensor'}, use_global_device_ids=true, to_apply=%region_5.6 | all-reduce | flops 256 | bytes 2048 | tf_op jit(solution)/shard_map/psum | solution.py:87
  95.8 3.1 %fusion.6 = bf16[256,2048]{1,0:T(8,128)(2,1)S(1)} fusion(f32[256,2048]{1,0:T(8,128)} %get-tuple-element.44, f32[512,2048]{1,0:T(8,128)} %get-tuple-element.30, f32[256]{0:T(256)S(1)} %bitcast.57, f32[256]{0:T(256)S(1)} %bitcast.59, bf16[1,1,512,2048]{3,2,1,0:T(8,128)(2,1)} %param.6, f32[2048]{0:T(1024)S(1)} %bitcast.51), kind=kLoop, calls=%fused_computation.15 | loop fusion | flops 3670016 | bytes 6301696 | tf_op jit(solution)/shard_map/convert_element_type | solution.py:91
  99.0 1.5 %collective-permute-start.4 = (bf16[256,2048]{1,0:T(8,128)(2,1)S(1)}, bf16[256,2048]{1,0:T(8,128)(2,1)S(1)}, u32[]{:S(2)}, u32[]{:S(2)}) collective-permute-start(bf16[256,2048]{1,0:T(8,128)(2,1)S(1)} %fusion.6), channel_id=1, source_target_pairs={{4,0},{5,1},{6,2},{7,3},{12,8},{13,9},{14,10},{15,11},{20,16},{21,... | collective-permute-start | bytes 3145736 | tf_op jit(solution)/shard_map/ppermute | solution.py:13
  101.2 2.1 %convolution_add_fusion = f32[2048,512]{1,0:T(8,128)S(1)} fusion(f32[2048,512]{1,0:T(8,128)S(1)} %fusion.14, bf16[512,2048]{1,0:T(8,128)(2,1)} %get-tuple-element.14, s32[]{:T(128)S(6)} %select_n.62, bf16[256,512]{1,0:T(8,128)(2,1)S(1)} %get-tuple-element.38, bf16[256,512]{1,0:T(8,128)(2,1)S(1)} %get-tuple-element.37), kind=kOutput, calls=%fused_computation.11 | convolution fusion | flops 538443776 | bytes 9961476 | tf_op jit(solution)/shard_map/dot_general | solution.py:60
  104.1 4.0 %add_add_fusion = f32[2048,512]{1,0:T(8,128)} fusion(f32[2048,512]{1,0:T(8,128)S(1)} %convolution_add_fusion, f32[2048,512]{1,0:T(8,128)S(1)} %fusion.8, bf16[512,2048]{1,0:T(8,128)(2,1)} %get-tuple-element.14, s32[]{:T(128)S(6)} %select_n.62, bf16[256,512]{1,0:T(8,128)(2,1)S(1)} %get-tuple-element.34, bf16[256,512]{1,0:T(8,128)(2,1)S(1)} %get-tuple-element.31), kind=kOutput, calls=%fused_computation.8 | convolution fusion | flops 539492352 | bytes 14155780 | tf_op jit(solution)/shard_map/dot_general | solution.py:60
  108.1 16.3 %collective-permute-done.4 = bf16[256,2048]{1,0:T(8,128)(2,1)S(1)} collective-permute-done((bf16[256,2048]{1,0:T(8,128)(2,1)S(1)}, bf16[256,2048]{1,0:T(8,128)(2,1)S(1)}, u32[]{:S(2)}, u32[]{:S(2)}) %collective-permute-start.4) | collective-permute-done | bytes 1048608 | tf_op jit(solution)/shard_map/ppermute | solution.py:13
  124.4 2.8 %pad_maximum_fusion = bf16[512,2048]{1,0:T(8,128)(2,1)} fusion(bf16[256,2048]{1,0:T(8,128)(2,1)S(1)} %collective-permute-done.4, bf16[256,2048]{1,0:T(8,128)(2,1)} %collective-permute-done), kind=kLoop, calls=%fused_computation.13 | loop fusion | flops 4194304 | bytes 4194304 | tf_op jit(solution)/shard_map/concatenate | solution.py:116
  128.5 2.4 %collective-permute-done.7 = f32[2048]{0:T(1024)S(1)} collective-permute-done((f32[2048]{0:T(1024)S(1)}, f32[2048]{0:T(1024)S(1)}, u32[]{:S(2)}, u32[]{:S(2)}) %collective-permute-start.7) | collective-permute-done | bytes 8224 | tf_op jit(solution)/shard_map/ppermute | solution.py:18
  131.5 4.9 %fusion.5 = bf16[1,2048,512]{2,1,0:T(8,128)(2,1)} fusion(f32[2048,512]{1,0:T(8,128)} %add_add_fusion, bf16[2048,512]{1,0:T(8,128)(2,1)} %collective-permute-done.6), kind=kLoop, calls=%fused_computation.12 | loop fusion | flops 3145728 | bytes 8388608 | tf_op jit(solution)/shard_map/broadcast_in_dim | solution.py:130
  (52 shorter events, 6.8 us)
Async XLA Ops:
  7.2 18.4 %copy-start.1 = (bf16[1,1,512,2048]{3,2,1,0:T(8,128)(2,1)S(1)}, bf16[1,1,512,2048]{3,2,1,0:T(8,128)(2,1)}, u32[]{:S(2)}) copy-start(bf16[1,1,512,2048]{3,2,1,0:T(8,128)(2,1)} %param.5) | copy-start | bytes 6291460
  7.2 33.7 %all-gather.5.cloned.1.call-start = ((), (), s32[]{:S(2)}) async-start(), calls=%async_computation | async-start | bytes 1310720 | tf_op jit(solution)/shard_map/all_gather | solution.py:49
  9.2 60.9 %all-gather.7.cloned.1.call-start = ((), (), s32[]{:S(2)}) async-start(), calls=%async_computation.1 | async-start | bytes 1310720 | tf_op jit(solution)/shard_map/all_gather | solution.py:49
  28.9 41.3 %collective-permute-start.1 = (bf16[512,2048]{1,0:T(8,128)(2,1)}, bf16[512,2048]{1,0:T(8,128)(2,1)S(1)}, u32[]{:S(2)}, u32[]{:S(2)}) collective-permute-start(bf16[512,2048]{1,0:T(8,128)(2,1)} %get-tuple-element.14), channel_id=1, source_target_pairs={{0,8},{8,0},{16,24},{24,16},{1,9},{9,1},{17,25},{25,17},{2,10},{10... | collective-permute-start | bytes 6291464 | tf_op jit(solution)/shard_map/ppermute | solution.py:23
  63.6 44.5 %collective-permute-start = (bf16[256,2048]{1,0:T(8,128)(2,1)}, bf16[256,2048]{1,0:T(8,128)(2,1)}, u32[]{:S(2)}, u32[]{:S(2)}) collective-permute-start(bf16[256,2048]{1,0:T(8,128)(2,1)} %fusion.7), channel_id=1, source_target_pairs={{4,0},{5,1},{6,2},{7,3},{12,8},{13,9},{14,10},{15,11},{20,16},{21,... | collective-permute-start | bytes 3145736 | tf_op jit(solution)/shard_map/ppermute | solution.py:13
  70.1 1.5 %copy-start.2 = (bf16[1,1,256,2048]{3,2,1,0:T(8,128)(2,1)S(1)}, bf16[1,1,256,2048]{3,2,1,0:T(8,128)(2,1)}, u32[]{:S(2)}) copy-start(bf16[1,1,256,2048]{3,2,1,0:T(8,128)(2,1)} %all-gather.7.cloned.1.call-done) | copy-start | bytes 3145732
  71.6 2.8 %collective-permute-start.2 = (bf16[256,1024]{1,0:T(8,128)(2,1)S(1)}, bf16[256,1024]{1,0:T(8,128)(2,1)S(1)}, u32[]{:S(2)}, u32[]{:S(2)}) collective-permute-start(bf16[256,1024]{1,0:T(8,128)(2,1)S(1)} %pad_maximum_fusion.1), channel_id=1, source_target_pairs={{0,8},{8,0},{16,24},{24,16},{1,9},{9,1},{17,25},{25,17},{2,10},{10... | collective-permute-start | bytes 1572872 | tf_op jit(solution)/shard_map/ppermute | solution.py:23
  71.8 3.4 %collective-permute-start.3 = (bf16[256,1024]{1,0:T(8,128)(2,1)S(1)}, bf16[256,1024]{1,0:T(8,128)(2,1)S(1)}, u32[]{:S(2)}, u32[]{:S(2)}) collective-permute-start(bf16[256,1024]{1,0:T(8,128)(2,1)S(1)} %pad_maximum_fusion.2), channel_id=1, source_target_pairs={{0,8},{8,0},{16,24},{24,16},{1,9},{9,1},{17,25},{25,17},{2,10},{10... | collective-permute-start | bytes 1572872 | tf_op jit(solution)/shard_map/ppermute | solution.py:23
  74.4 0.8 copy-start.3
  75.2 0.8 copy-start.5
  75.2 6.3 %slice-start = ((s8[8388608]{0:T(1024)(128)(4,1)}), s8[4194304]{0:T(1024)(128)(4,1)S(1)}, s32[]{:S(2)}) async-start(s8[8388608]{0:T(1024)(128)(4,1)} %bitcast.63), calls=%async_computation.2 | async-start | bytes 8388608
  76.0 5.5 %copy-start = (f32[512,2048]{1,0:T(8,128)S(1)}, f32[512,2048]{1,0:T(8,128)}, u32[]{:S(2)}) copy-start(f32[512,2048]{1,0:T(8,128)} %get-tuple-element.30) | copy-start | bytes 12582916
  76.0 5.5 %slice-start.1 = ((s8[8388608]{0:T(1024)(128)(4,1)}), s8[4194304]{0:T(1024)(128)(4,1)S(1)}, s32[]{:S(2)}) async-start(s8[8388608]{0:T(1024)(128)(4,1)} %bitcast.63), calls=%async_computation.3 | async-start | bytes 8388608
  80.1 51.4 %collective-permute-start.6 = (bf16[2048,512]{1,0:T(8,128)(2,1)}, bf16[2048,512]{1,0:T(8,128)(2,1)}, u32[]{:S(2)}, u32[]{:S(2)}) collective-permute-start(bf16[2048,512]{1,0:T(8,128)(2,1)} %add_convert_fusion.1), channel_id=1, source_target_pairs={{0,16},{8,24},{16,0},{24,8},{1,17},{9,25},{17,1},{25,9},{2,18},{10... | collective-permute-start | bytes 6291464 | tf_op jit(solution)/shard_map/ppermute | solution.py:18
  85.5 22.6 %collective-permute-start.5 = (f32[2048]{0:T(1024)S(1)}, f32[2048]{0:T(1024)S(1)}, u32[]{:S(2)}, u32[]{:S(2)}) collective-permute-start(f32[2048]{0:T(1024)S(1)} %add.124), channel_id=1, source_target_pairs={{0,8},{8,0},{16,24},{24,16},{1,9},{9,1},{17,25},{25,17},{2,10},{10... | collective-permute-start | bytes 24584 | tf_op jit(solution)/shard_map/ppermute | solution.py:23
  95.8 4.6 %copy-start.4 = (bf16[256,1024]{1,0:T(8,128)(2,1)S(1)}, bf16[256,1024]{1,0:T(8,128)(2,1)}, u32[]{:S(2)}) copy-start(bf16[256,1024]{1,0:T(8,128)(2,1)} %copy-done.3) | copy-start | bytes 1572868
  99.0 25.4 %collective-permute-start.4 = (bf16[256,2048]{1,0:T(8,128)(2,1)S(1)}, bf16[256,2048]{1,0:T(8,128)(2,1)S(1)}, u32[]{:S(2)}, u32[]{:S(2)}) collective-permute-start(bf16[256,2048]{1,0:T(8,128)(2,1)S(1)} %fusion.6), channel_id=1, source_target_pairs={{4,0},{5,1},{6,2},{7,3},{12,8},{13,9},{14,10},{15,11},{20,16},{21,... | collective-permute-start | bytes 3145736 | tf_op jit(solution)/shard_map/ppermute | solution.py:13
  101.2 2.1 %copy-start.6 = (bf16[256,1024]{1,0:T(8,128)(2,1)S(1)}, bf16[256,1024]{1,0:T(8,128)(2,1)}, u32[]{:S(2)}) copy-start(bf16[256,1024]{1,0:T(8,128)(2,1)} %copy-done.5) | copy-start | bytes 1572868
  127.2 3.7 %collective-permute-start.7 = (f32[2048]{0:T(1024)S(1)}, f32[2048]{0:T(1024)S(1)}, u32[]{:S(2)}, u32[]{:S(2)}) collective-permute-start(f32[2048]{0:T(1024)S(1)} %add.125), channel_id=1, source_target_pairs={{0,16},{8,24},{16,0},{24,8},{1,17},{9,25},{17,1},{25,9},{2,18},{10... | collective-permute-start | bytes 24584 | tf_op jit(solution)/shard_map/ppermute | solution.py:18
Sparse Core Ops, SparseCore 0:
  10.2 30.6 all-gather.4
  42.4 27.6 all-gather.6

commit v21 on v13

--- a/solution.py
+++ b/solution.py
@@ -108,6 +108,7 @@
             total = first
             for k in range(1, CHUNKS):
                 total = total + chunk_blocks[k](own_g)
+            total = lax.optimization_barrier(total.astype(jnp.bfloat16)).astype(jnp.float32)
             for got in received:
                 total = total + got.astype(jnp.float32)
             weight_total = total.astype(jnp.bfloat16)

time: 146 us -> 143 us (0.979)
  matrix products: 32.9 us -> 25.3 us
  other arithmetic: 18.3 us -> 21.6 us
    dot_general x8, matrix products: 20.8 us -> 13.2 us  [tn(): lax.dot_general(a, b, (((0,), (0,)), ((), ())), preferred_element_type=jn...]
    broadcast_in_dim x1 -> x2, other arithmetic: 3.26 us -> 6.61 us  [on_device(): return (upstream[None, None], weight_total[None], gain_total[None])]
    ppermute x2, waiting for transfers between devices: 17.9 us -> 19.6 us  [shifted(): return lax.ppermute(block, axis, [(i, (i + shift) % n) for i in range(n)])]
where the time goes in v21:
time: 143 us; the launch traced here: 142 us
  waiting for transfers between devices  36.8 us (26%)
  blocking collectives  34.3 us (24%)
  matrix products  25.3 us (18%)
  other arithmetic  21.6 us (15%)
  between operations  14.3 us (10%)
  starting transfers between devices  6.16 us (4%)
  local copies, waits for them, and re-layouts  3.73 us (3%)
    psum x2, blocking collectives, on_device(): lax.psum(jnp.sum(scaled * normed_c, axis=1, keepdims=True), 'tensor')  20.7 us
    ppermute x2, waiting for transfers between devices, shifted(): return lax.ppermute(block, axis, [(i, (i + shift) % n) for i in range(n)])  19.6 us
    all_gather x2, waiting for transfers between devices, on_device(): lax.all_gather(grad_kv[c * step:(c + 1) * step], 'tensor', axis=1, tiled=...  17.2 us
    psum x1, blocking collectives, on_device(): lax.psum(jnp.sum(values * values, axis=1, keepdims=True), 'tensor')  13.5 us
    dot_general x8, matrix products, tn(): lax.dot_general(a, b, (((0,), (0,)), ((), ())), preferred_element_type=jn...  13.2 us
    dot_general x2, matrix products, on_device(): lax.dot_general(block, weight, (((1,), (1,)), ((), ())), preferred_elemen...  12.1 us
    convert_element_type x2, other arithmetic, on_device(): input_grad = (grad_out[lo:lo + step].astype(jnp.float32) + rstd[lo:lo + s...  8.17 us
    broadcast_in_dim x2, other arithmetic, on_device(): return (upstream[None, None], weight_total[None], gain_total[None])  6.61 us
  transfers between devices with their start and end apart: 10, of which 3 were waited for; matrix products, arithmetic and copies ran while one was open for 32% of the time, Pallas kernels for 0%

profile of v21, /device:TPU:0, one launch (start us, length us, event | category | flops | bytes accessed | tf_op | source)
XLA Modules:
  0.0 142.2 jit_solution(9575622211803400236)
XLA Ops:
  7.2 2.0 %fusion.46 = (bf16[1,1,256,512]{3,2,1,0:T(8,128)(2,1)}, bf16[1,1,256,512]{3,2,1,0:T(8,128)(2,1)}) fusion(bf16[1,1,512,512]{3,2,1,0:T(8,128)(2,1)} %param.7), kind=kLoop, calls=%fused_computation.77 | loop fusion | bytes 1048576 | tf_op jit(solution)/shard_map/slice | solution.py:49
  10.0 2.1 %fusion.4 = f32[512]{0:T(512)S(1)} fusion(bf16[1,1,512,2048]{3,2,1,0:T(8,128)(2,1)} %param.5), kind=kLoop, calls=%fused_computation.6 | loop fusion | flops 3145216 | bytes 2099200 | tf_op jit(solution)/shard_map/reduce_sum | solution.py:41
  12.1 13.5 %psum.21 = f32[512,1]{0,1:T(1,128)S(1)} all-reduce(f32[512,1]{0,1:T(1,128)S(1)} %bitcast.54), channel_id=1, replica_groups=mesh['dp'=4,'pipe'=2,'tensor'=4] {'tensor'}, use_global_device_ids=true, to_apply=%region_1.2 | all-reduce | flops 512 | bytes 4096 | tf_op jit(solution)/shard_map/psum | solution.py:41
  25.6 3.3 %multiply_convert_fusion = (bf16[512,2048]{1,0:T(8,128)(2,1)}, f32[512,2048]{1,0:T(8,128)}) fusion(f32[2048]{0:T(1024)S(1)} %bitcast.47, f32[512]{0:T(512)S(1)} %bitcast.53, bf16[1,1,512,2048]{3,2,1,0:T(8,128)(2,1)S(1)} %copy-done.1), kind=kLoop, calls=%fused_computation.10 | loop fusion | flops 4194304 | bytes 8398848 | tf_op jit(solution)/shard_map/convert_element_type | solution.py:44
  29.0 11.9 %all-gather.5.cloned.1.call-done = bf16[1,1,256,2048]{3,2,1,0:T(8,128)(2,1)} async-done(((bf16[1,1,256,512]{3,2,1,0:T(8,128)(2,1)}), bf16[1,1,256,2048]{3,2,1,0:T(8,128)(2,1)}) %all-gather.5.cloned.1.call-update) | async-done | bytes 1048592 | tf_op jit(solution)/shard_map/all_gather | solution.py:49
  40.9 8.2 %multiply_reduce_fusion.1 = (f32[2048]{0:T(1024)S(1)}, f32[256]{0:T(256)S(1)}, f32[256,2048]{1,0:T(8,128)}) fusion(f32[512,2048]{1,0:T(8,128)} %get-tuple-element.20, f32[2048]{0:T(1024)S(1)} %bitcast.48, bf16[1,2048,2048]{2,1,0:T(8,128)(2,1)} %param.9, bf16[1,1,256,2048]{3,2,1,0:T(8,128)(2,1)} %all-gather.5.cloned.1.call-done), kind=kOutput, calls=%fused_computation.19 | convolution fusion | flops 2150102784 | bytes 13648896 | tf_op jit(solution)/shard_map/dot_general | solution.py:82
  49.0 10.5 %psum.22 = f32[256,1]{0,1:T(1,128)S(1)} all-reduce(f32[256,1]{0,1:T(1,128)S(1)} %bitcast.62), channel_id=1, replica_groups=mesh['dp'=4,'pipe'=2,'tensor'=4] {'tensor'}, use_global_device_ids=true, to_apply=%region_3.4 | all-reduce | flops 256 | bytes 2048 | tf_op jit(solution)/shard_map/psum | solution.py:87
  59.5 4.1 %fusion.7 = bf16[256,2048]{1,0:T(8,128)(2,1)} fusion(f32[256,2048]{1,0:T(8,128)} %get-tuple-element.33, f32[512,2048]{1,0:T(8,128)} %get-tuple-element.20, f32[256]{0:T(256)S(1)} %bitcast.58, f32[2048]{0:T(1024)S(1)} %bitcast.49, f32[256]{0:T(256)S(1)} %bitcast.60, bf16[1,1,512,2048]{3,2,1,0:T(8,128)(2,1)} %param.6), kind=kLoop, calls=%fused_computation.17 | loop fusion | flops 3670016 | bytes 6301696 | tf_op jit(solution)/shard_map/convert_element_type | solution.py:91
  63.6 1.3 collective-permute-start
  64.8 5.3 %all-gather.7.cloned.1.call-done = bf16[1,1,256,2048]{3,2,1,0:T(8,128)(2,1)} async-done(((bf16[1,1,256,512]{3,2,1,0:T(8,128)(2,1)}), bf16[1,1,256,2048]{3,2,1,0:T(8,128)(2,1)}) %all-gather.7.cloned.1.call-update) | async-done | bytes 1048592 | tf_op jit(solution)/shard_map/all_gather | solution.py:49
  70.1 1.4 constant_dynamic-slice_fusion.5
  72.4 2.0 %fusion.19 = f32[2048,512]{1,0:T(8,128)S(1)} fusion(bf16[512,2048]{1,0:T(8,128)(2,1)} %get-tuple-element.9, s32[]{:T(128)S(6)} %select_n.59, bf16[256,512]{1,0:T(8,128)(2,1)S(1)} %get-tuple-element.28, bf16[256,512]{1,0:T(8,128)(2,1)S(1)} %get-tuple-element.27), kind=kOutput, calls=%fused_computation.33 | convolution fusion | flops 537395200 | bytes 5767172 | tf_op jit(solution)/shard_map/dot_general | solution.py:60
  76.0 4.1 %add_convert_fusion.2 = bf16[2048,512]{1,0:T(8,128)(2,1)} fusion(f32[2048,512]{1,0:T(8,128)S(1)} %fusion.10, f32[2048,512]{1,0:T(8,128)S(1)} %fusion.19, f32[2048,512]{1,0:T(8,128)S(1)} %fusion.16, bf16[512,2048]{1,0:T(8,128)(2,1)} %get-tuple-element.9, s32[]{:T(128)S(6)} %select_n.59, bf16[256,512]{1,0:T(8,128)(2,1)S(1)} %get-tuple-element.24, ...), kind=kOutput, calls=%fused_computation.9 | convolution fusion | flops 541589504 | bytes 16252932 | tf_op jit(solution)/shard_map/dot_general | solution.py:60
  80.1 1.5 %collective-permute-start.5 = (bf16[2048,512]{1,0:T(8,128)(2,1)}, bf16[2048,512]{1,0:T(8,128)(2,1)}, u32[]{:S(2)}, u32[]{:S(2)}) collective-permute-start(bf16[2048,512]{1,0:T(8,128)(2,1)} %add_convert_fusion.2), channel_id=1, source_target_pairs={{0,16},{8,24},{16,0},{24,8},{1,17},{9,25},{17,1},{25,9},{2,18},{10... | collective-permute-start | bytes 6291464 | tf_op jit(solution)/shard_map/ppermute | solution.py:18
  81.6 4.0 %multiply_reduce_fusion = (f32[2048]{0:T(1024)S(1)}, f32[256]{0:T(256)S(1)}, f32[256,2048]{1,0:T(8,128)}) fusion(f32[512,2048]{1,0:T(8,128)S(1)} %copy-done, f32[2048]{0:T(1024)S(1)} %bitcast.50, bf16[256,2048]{1,0:T(8,128)(2,1)S(1)} %bitcast.45, bf16[1,2048,2048]{2,1,0:T(8,128)(2,1)S(1)} %bitcast.64), kind=kOutput, calls=%fused_computation.18 | convolution fusion | flops 2150102784 | bytes 13648896 | tf_op jit(solution)/shard_map/dot_general | solution.py:82
  85.5 10.3 %psum.23 = f32[256,1]{0,1:T(1,128)S(1)} all-reduce(f32[256,1]{0,1:T(1,128)S(1)} %bitcast.61), channel_id=1, replica_groups=mesh['dp'=4,'pipe'=2,'tensor'=4] {'tensor'}, use_global_device_ids=true, to_apply=%region_5.6 | all-reduce | flops 256 | bytes 2048 | tf_op jit(solution)/shard_map/psum | solution.py:87
  95.8 4.1 %fusion.6 = bf16[256,2048]{1,0:T(8,128)(2,1)} fusion(f32[256,2048]{1,0:T(8,128)} %get-tuple-element.34, f32[512,2048]{1,0:T(8,128)} %get-tuple-element.20, f32[256]{0:T(256)S(1)} %bitcast.57, f32[256]{0:T(256)S(1)} %bitcast.59, bf16[1,1,512,2048]{3,2,1,0:T(8,128)(2,1)} %param.6, f32[2048]{0:T(1024)S(1)} %bitcast.51), kind=kLoop, calls=%fused_computation.15 | loop fusion | flops 3670016 | bytes 6301696 | tf_op jit(solution)/shard_map/convert_element_type | solution.py:91
  99.9 1.5 %collective-permute-start.4 = (bf16[256,2048]{1,0:T(8,128)(2,1)}, bf16[256,2048]{1,0:T(8,128)(2,1)}, u32[]{:S(2)}, u32[]{:S(2)}) collective-permute-start(bf16[256,2048]{1,0:T(8,128)(2,1)} %fusion.6), channel_id=1, source_target_pairs={{4,0},{5,1},{6,2},{7,3},{12,8},{13,9},{14,10},{15,11},{20,16},{21,... | collective-permute-start | bytes 3145736 | tf_op jit(solution)/shard_map/ppermute | solution.py:13
  102.2 2.1 %convolution_add_fusion = f32[2048,512]{1,0:T(8,128)S(1)} fusion(f32[2048,512]{1,0:T(8,128)S(1)} %fusion.14, bf16[512,2048]{1,0:T(8,128)(2,1)} %get-tuple-element.9, s32[]{:T(128)S(6)} %select_n.62, bf16[256,512]{1,0:T(8,128)(2,1)S(1)} %get-tuple-element.28, bf16[256,512]{1,0:T(8,128)(2,1)S(1)} %get-tuple-element.27), kind=kOutput, calls=%fused_computation.11 | convolution fusion | flops 538443776 | bytes 9961476 | tf_op jit(solution)/shard_map/dot_general | solution.py:60
  105.1 1.3 collective-permute-start.7
  106.3 2.0 %add_convert_fusion.1 = bf16[2048,512]{1,0:T(8,128)(2,1)S(1)} fusion(f32[2048,512]{1,0:T(8,128)S(1)} %convolution_add_fusion, f32[2048,512]{1,0:T(8,128)S(1)} %fusion.8, bf16[512,2048]{1,0:T(8,128)(2,1)} %get-tuple-element.9, s32[]{:T(128)S(6)} %select_n.62, bf16[256,512]{1,0:T(8,128)(2,1)S(1)} %get-tuple-element.24, bf16[256,512]{1,0:T(8,128)(2,1)S(1)} %get-tuple-element.21), kind=kOutput, calls=%fused_computation.8 | convolution fusion | flops 540540928 | bytes 12058628 | tf_op jit(solution)/shard_map/dot_general | solution.py:60
  108.5 19.6 %collective-permute-done.7 = f32[2048]{0:T(1024)S(1)} collective-permute-done((f32[2048]{0:T(1024)S(1)}, f32[2048]{0:T(1024)S(1)}, u32[]{:S(2)}, u32[]{:S(2)}) %collective-permute-start.7) | collective-permute-done | bytes 8224 | tf_op jit(solution)/shard_map/ppermute | solution.py:18
  128.8 3.1 %maximum_bitcast_fusion = bf16[1,1,512,2048]{3,2,1,0:T(8,128)(2,1)} fusion(bf16[256,2048]{1,0:T(8,128)(2,1)} %collective-permute-done.4, bf16[256,2048]{1,0:T(8,128)(2,1)} %collective-permute-done), kind=kLoop, calls=%fused_computation.13 | loop fusion | flops 4194304 | bytes 4194304 | tf_op jit(solution)/shard_map/broadcast_in_dim | solution.py:127
  131.9 3.5 %fusion.5 = bf16[1,2048,512]{2,1,0:T(8,128)(2,1)} fusion(bf16[2048,512]{1,0:T(8,128)(2,1)} %collective-permute-done.5, bf16[2048,512]{1,0:T(8,128)(2,1)S(1)} %add_convert_fusion.1), kind=kLoop, calls=%fused_computation.12 | loop fusion | flops 4194304 | bytes 6291456 | tf_op jit(solution)/shard_map/broadcast_in_dim | solution.py:127
  (52 shorter events, 5.6 us)
Async XLA Ops:
  7.2 18.4 %copy-start.1 = (bf16[1,1,512,2048]{3,2,1,0:T(8,128)(2,1)S(1)}, bf16[1,1,512,2048]{3,2,1,0:T(8,128)(2,1)}, u32[]{:S(2)}) copy-start(bf16[1,1,512,2048]{3,2,1,0:T(8,128)(2,1)} %param.5) | copy-start | bytes 6291460
  7.2 33.7 %all-gather.5.cloned.1.call-start = ((), (), s32[]{:S(2)}) async-start(), calls=%async_computation | async-start | bytes 1310720 | tf_op jit(solution)/shard_map/all_gather | solution.py:49
  9.2 60.9 %all-gather.7.cloned.1.call-start = ((), (), s32[]{:S(2)}) async-start(), calls=%async_computation.1 | async-start | bytes 1310720 | tf_op jit(solution)/shard_map/all_gather | solution.py:49
  28.9 41.3 %collective-permute-start.1 = (bf16[512,2048]{1,0:T(8,128)(2,1)}, bf16[512,2048]{1,0:T(8,128)(2,1)S(1)}, u32[]{:S(2)}, u32[]{:S(2)}) collective-permute-start(bf16[512,2048]{1,0:T(8,128)(2,1)} %get-tuple-element.9), channel_id=1, source_target_pairs={{0,8},{8,0},{16,24},{24,16},{1,9},{9,1},{17,25},{25,17},{2,10},{10... | collective-permute-start | bytes 6291464 | tf_op jit(solution)/shard_map/ppermute | solution.py:23
  63.6 65.2 %collective-permute-start = (bf16[256,2048]{1,0:T(8,128)(2,1)}, bf16[256,2048]{1,0:T(8,128)(2,1)}, u32[]{:S(2)}, u32[]{:S(2)}) collective-permute-start(bf16[256,2048]{1,0:T(8,128)(2,1)} %fusion.7), channel_id=1, source_target_pairs={{4,0},{5,1},{6,2},{7,3},{12,8},{13,9},{14,10},{15,11},{20,16},{21,... | collective-permute-start | bytes 3145736 | tf_op jit(solution)/shard_map/ppermute | solution.py:13
  70.1 1.5 %copy-start.2 = (bf16[1,1,256,2048]{3,2,1,0:T(8,128)(2,1)S(1)}, bf16[1,1,256,2048]{3,2,1,0:T(8,128)(2,1)}, u32[]{:S(2)}) copy-start(bf16[1,1,256,2048]{3,2,1,0:T(8,128)(2,1)} %all-gather.7.cloned.1.call-done) | copy-start | bytes 3145732
  71.6 2.8 %collective-permute-start.2 = (bf16[256,1024]{1,0:T(8,128)(2,1)S(1)}, bf16[256,1024]{1,0:T(8,128)(2,1)S(1)}, u32[]{:S(2)}, u32[]{:S(2)}) collective-permute-start(bf16[256,1024]{1,0:T(8,128)(2,1)S(1)} %pad_maximum_fusion), channel_id=1, source_target_pairs={{0,8},{8,0},{16,24},{24,16},{1,9},{9,1},{17,25},{25,17},{2,10},{10... | collective-permute-start | bytes 1572872 | tf_op jit(solution)/shard_map/ppermute | solution.py:23
  71.8 3.3 %collective-permute-start.3 = (bf16[256,1024]{1,0:T(8,128)(2,1)S(1)}, bf16[256,1024]{1,0:T(8,128)(2,1)S(1)}, u32[]{:S(2)}, u32[]{:S(2)}) collective-permute-start(bf16[256,1024]{1,0:T(8,128)(2,1)S(1)} %pad_maximum_fusion.1), channel_id=1, source_target_pairs={{0,8},{8,0},{16,24},{24,16},{1,9},{9,1},{17,25},{25,17},{2,10},{10... | collective-permute-start | bytes 1572872 | tf_op jit(solution)/shard_map/ppermute | solution.py:23
  74.4 0.8 copy-start.3
  75.2 0.8 copy-start.5
  75.2 6.4 %slice-start = ((s8[8388608]{0:T(1024)(128)(4,1)}), s8[4194304]{0:T(1024)(128)(4,1)S(1)}, s32[]{:S(2)}) async-start(s8[8388608]{0:T(1024)(128)(4,1)} %bitcast.63), calls=%async_computation.2 | async-start | bytes 8388608
  76.0 5.6 %copy-start = (f32[512,2048]{1,0:T(8,128)S(1)}, f32[512,2048]{1,0:T(8,128)}, u32[]{:S(2)}) copy-start(f32[512,2048]{1,0:T(8,128)} %get-tuple-element.20) | copy-start | bytes 12582916
  76.0 5.6 %slice-start.1 = ((s8[8388608]{0:T(1024)(128)(4,1)}), s8[4194304]{0:T(1024)(128)(4,1)S(1)}, s32[]{:S(2)}) async-start(s8[8388608]{0:T(1024)(128)(4,1)} %bitcast.63), calls=%async_computation.3 | async-start | bytes 8388608
  80.1 51.8 %collective-permute-start.5 = (bf16[2048,512]{1,0:T(8,128)(2,1)}, bf16[2048,512]{1,0:T(8,128)(2,1)}, u32[]{:S(2)}, u32[]{:S(2)}) collective-permute-start(bf16[2048,512]{1,0:T(8,128)(2,1)} %add_convert_fusion.2), channel_id=1, source_target_pairs={{0,16},{8,24},{16,0},{24,8},{1,17},{9,25},{17,1},{25,9},{2,18},{10... | collective-permute-start | bytes 6291464 | tf_op jit(solution)/shard_map/ppermute | solution.py:18
  85.5 19.5 %collective-permute-start.6 = (f32[2048]{0:T(1024)S(1)}, f32[2048]{0:T(1024)S(1)}, u32[]{:S(2)}, u32[]{:S(2)}) collective-permute-start(f32[2048]{0:T(1024)S(1)} %add.125), channel_id=1, source_target_pairs={{0,8},{8,0},{16,24},{24,16},{1,9},{9,1},{17,25},{25,17},{2,10},{10... | collective-permute-start | bytes 24584 | tf_op jit(solution)/shard_map/ppermute | solution.py:23
  95.8 5.6 %copy-start.4 = (bf16[256,1024]{1,0:T(8,128)(2,1)S(1)}, bf16[256,1024]{1,0:T(8,128)(2,1)}, u32[]{:S(2)}) copy-start(bf16[256,1024]{1,0:T(8,128)(2,1)} %copy-done.3) | copy-start | bytes 1572868
  99.9 28.8 %collective-permute-start.4 = (bf16[256,2048]{1,0:T(8,128)(2,1)}, bf16[256,2048]{1,0:T(8,128)(2,1)}, u32[]{:S(2)}, u32[]{:S(2)}) collective-permute-start(bf16[256,2048]{1,0:T(8,128)(2,1)} %fusion.6), channel_id=1, source_target_pairs={{4,0},{5,1},{6,2},{7,3},{12,8},{13,9},{14,10},{15,11},{20,16},{21,... | collective-permute-start | bytes 3145736 | tf_op jit(solution)/shard_map/ppermute | solution.py:13
  102.2 2.1 %copy-start.6 = (bf16[256,1024]{1,0:T(8,128)(2,1)S(1)}, bf16[256,1024]{1,0:T(8,128)(2,1)}, u32[]{:S(2)}) copy-start(bf16[256,1024]{1,0:T(8,128)(2,1)} %copy-done.5) | copy-start | bytes 1572868
  105.1 23.0 %collective-permute-start.7 = (f32[2048]{0:T(1024)S(1)}, f32[2048]{0:T(1024)S(1)}, u32[]{:S(2)}, u32[]{:S(2)}) collective-permute-start(f32[2048]{0:T(1024)S(1)} %add.126), channel_id=1, source_target_pairs={{0,16},{8,24},{16,0},{24,8},{1,17},{9,25},{17,1},{25,9},{2,18},{10... | collective-permute-start | bytes 24584 | tf_op jit(solution)/shard_map/ppermute | solution.py:18
Sparse Core Ops, SparseCore 0:
  10.2 30.6 all-gather.4
  42.4 27.6 all-gather.6
